TPU v7x, 32 devices: a whole 2x2x4 slice. The times are simulated.
32 devices in a mesh: groups: 2 (over y), tile: 4 (over z), depth: 2 (over x), batch: 2 (over core).
Axes of the slice: x: 2, y: 2, z: 4, core: 2. Of those that a mesh axis runs over, the one named last changes fastest.
Arguments:
- object_field: float32 [4, 2, 1024, 512], P(('groups', 'depth'), None, 'tile'), parts along dimension 0, may hold values from -1 to 1, as said below
- probe: bfloat16 [4, 256, 256], P('groups'), parts along dimension 0, may hold values from -6 to 6
- positions: int32 [32, 2], P(('groups', 'tile', 'batch')), parts along dimension 0, may hold values from 0 to 768, as said below
- counts: int32 [16], P(('groups', 'tile', 'batch')), parts along dimension 0, may hold values from 0 to 2, as said below
- measured: float32 [32, 256, 256], P(('groups', 'tile', 'batch')), parts along dimension 0, may hold values from 0.1 to 8
Outputs:
- object_grad: float32 [4, 2, 1024, 512], P(('groups', 'depth'), None, 'tile'), parts along dimension 0
There are 2 independent parts, one for each index of `groups`. A program takes and returns all parts, laid end to end along the dimension named above; each array names one. Nothing has to cross between parts.
Inputs may be any that keep to these rules, and one draw needn't show every extreme that they name: `positions`: slot i belongs to tile (i // 2) // 2; its row offset lies within that tile's rows, from its first row to 255 rows later, and its patch ends inside the object; its column offset is at most 256. Some slot starts at row 768. counts[2 t] and counts[2 t + 1] are the live first slots of the two devices of tile t along the batch axis; their sum is at least 1 and at most 2, and equals 2 for some tile. `object_field`: each entry pair is a complex number of magnitude at most 1.
All inputs are finite; a program needn't handle non-finite values.
Results may differ from a plain program's by a relative error of at most 0.03.
Values may be sent and summed in bfloat16 or wider, within the bound.
No kernel may reach another device: no remote copies, remote signals or barrier semaphores. Data moves between devices by JAX's collectives and lax.ppermute only.
A program may use at most 64 MiB of HBM per device.

v0:
```python
import math

import jax
import jax.numpy as jnp
from jax import lax
from jax.sharding import PartitionSpec as P
from jax.experimental import pallas as pl

SLICE_COEF = 0.002
DETECTOR_COEF = 0.006
RESIDUAL_SCALE = 0.125


def from_behind(block, axis, distance):
    devices = range(lax.axis_size(axis))
    route = [(i - distance, i) for i in devices if i - distance in devices]
    return lax.ppermute(block, axis, route)


def dft_block(width, sign):
    freq = jnp.arange(width, dtype=jnp.int32)
    product = freq[:, None] * freq[None, :] % width
    angle = 2.0 * math.pi / width * product.astype(jnp.float32)
    scale = 1.0 / math.sqrt(width)
    real_part = (jnp.cos(angle) * scale).astype(jnp.bfloat16)
    imag_part = (sign * jnp.sin(angle) * scale).astype(jnp.bfloat16)
    upper = jnp.concatenate([real_part, -imag_part], axis=1)
    lower = jnp.concatenate([imag_part, real_part], axis=1)
    return jnp.concatenate([upper, lower], axis=0)


def chirp_parts(width, coef):
    freq = jnp.arange(width, dtype=jnp.int32)
    shifted = (freq + width // 2) % width - width // 2
    square = shifted * shifted
    total = (square[:, None] + square[None, :]).astype(jnp.float32)
    phase = -coef * total
    return (jnp.cos(phase), jnp.sin(phase))


def left_apply(block, waves):
    number = waves.shape[0]
    width = waves.shape[2]
    stacked = waves.reshape(number, 2 * width, width)
    result = jnp.einsum("ij,gjk->gik", block, stacked, preferred_element_type=jnp.float32)
    return result.reshape(number, 2, width, width)


def propagate(waves, forward_block, inverse_block, chirp_re, chirp_im):
    first = left_apply(forward_block, waves).astype(jnp.bfloat16)
    spectrum = left_apply(forward_block, jnp.swapaxes(first, -1, -2))
    spec_re = spectrum[:, 0]
    spec_im = spectrum[:, 1]
    filtered = jnp.stack(
        [spec_re * chirp_re - spec_im * chirp_im, spec_re * chirp_im + spec_im * chirp_re], axis=1
    ).astype(jnp.bfloat16)
    back = left_apply(inverse_block, filtered).astype(jnp.bfloat16)
    return left_apply(inverse_block, jnp.swapaxes(back, -1, -2)).astype(jnp.bfloat16)


def transmit(waves, patch):
    values = waves.astype(jnp.float32)
    wave_re = values[:, 0]
    wave_im = values[:, 1]
    return jnp.stack(
        [
            patch[:, 0] * wave_re - patch[:, 1] * wave_im,
            patch[:, 0] * wave_im + patch[:, 1] * wave_re,
        ],
        axis=1,
    ).astype(jnp.bfloat16)


def residual_wave(waves, measured):
    values = waves.astype(jnp.float32)
    intensity = values[:, 0] * values[:, 0] + values[:, 1] * values[:, 1]
    weight = RESIDUAL_SCALE * (intensity - measured)
    return jnp.stack([weight * values[:, 0], weight * values[:, 1]], axis=1).astype(jnp.bfloat16)


def adjoint_terms(incoming, forward_block, inverse_block, chirp_re, chirp_im, inputs, patch):
    spread = propagate(incoming, forward_block, inverse_block, chirp_re, -chirp_im).astype(
        jnp.float32
    )
    source = inputs.astype(jnp.float32)
    term = jnp.stack(
        [
            source[:, 0] * spread[:, 0] + source[:, 1] * spread[:, 1],
            source[:, 0] * spread[:, 1] - source[:, 1] * spread[:, 0],
        ],
        axis=1,
    )
    passed = jnp.stack(
        [
            patch[:, 0] * spread[:, 0] + patch[:, 1] * spread[:, 1],
            patch[:, 0] * spread[:, 1] - patch[:, 1] * spread[:, 0],
        ],
        axis=1,
    ).astype(jnp.bfloat16)
    return (passed, term)


def wave_kernel(transmit_first, residual_after, backward):
    def kernel(*refs):
        refs = list(refs)
        wave_ref = refs.pop(0)
        patch_ref = refs.pop(0)
        chirp_ref = refs.pop(0)
        fl_ref, fr_ref, gl_ref, gr_ref = refs[:4]
        refs = refs[4:]
        extra_ref = refs.pop(0) if (residual_after or backward) else None
        width = wave_ref.shape[2]
        wave = wave_ref[0].astype(jnp.float32)
        patch_re = patch_ref[0, 0]
        patch_im = patch_ref[0, 1]
        if transmit_first:
            wave_re = patch_re * wave[0] - patch_im * wave[1]
            wave_im = patch_re * wave[1] + patch_im * wave[0]
        else:
            wave_re = wave[0]
            wave_im = wave[1]
        stacked = jnp.concatenate([wave_re, wave_im], axis=0).astype(jnp.bfloat16)
        first = jnp.dot(fl_ref[...], stacked, preferred_element_type=jnp.float32).astype(jnp.bfloat16)
        rowwise = jnp.concatenate([first[:width], first[width:]], axis=1)
        spectrum = jnp.dot(rowwise, fr_ref[...], preferred_element_type=jnp.float32)
        spec_re = spectrum[:, :width]
        spec_im = spectrum[:, width:]
        chirp_re = chirp_ref[0]
        chirp_im = chirp_ref[1]
        if backward:
            chirp_im = -chirp_im
        filtered = jnp.concatenate(
            [spec_re * chirp_re - spec_im * chirp_im, spec_re * chirp_im + spec_im * chirp_re],
            axis=1,
        ).astype(jnp.bfloat16)
        back = jnp.dot(filtered, gr_ref[...], preferred_element_type=jnp.float32).astype(jnp.bfloat16)
        columnwise = jnp.concatenate([back[:, :width], back[:, width:]], axis=0)
        out = jnp.dot(gl_ref[...], columnwise, preferred_element_type=jnp.float32).astype(jnp.bfloat16)
        values = out.astype(jnp.float32)
        out_re = values[:width]
        out_im = values[width:]
        if residual_after:
            measured = extra_ref[0]
            weight = RESIDUAL_SCALE * (out_re * out_re + out_im * out_im - measured)
            result_ref = refs[0]
            result_ref[0, 0] = (weight * out_re).astype(jnp.bfloat16)
            result_ref[0, 1] = (weight * out_im).astype(jnp.bfloat16)
        elif backward:
            source = extra_ref[0].astype(jnp.float32)
            passed_ref, term_ref = refs[0], refs[1]
            passed_ref[0, 0] = (patch_re * out_re + patch_im * out_im).astype(jnp.bfloat16)
            passed_ref[0, 1] = (patch_re * out_im - patch_im * out_re).astype(jnp.bfloat16)
            term_ref[0, 0] = source[0] * out_re + source[1] * out_im
            term_ref[0, 1] = source[0] * out_im - source[1] * out_re
        else:
            result_ref = refs[0]
            result_ref[0, 0] = out[:width]
            result_ref[0, 1] = out[width:]

    return kernel


def run_waves(waves, patches, chirps, blocks, extra=None, transmit_first=True, residual_after=False, backward=False):
    number, _, width, _ = waves.shape
    wave_spec = pl.BlockSpec((1, 2, width, width), lambda i: (i, 0, 0, 0))
    chirp_spec = pl.BlockSpec((2, width, width), lambda i: (0, 0, 0))
    block_spec = pl.BlockSpec((2 * width, 2 * width), lambda i: (0, 0))
    in_specs = [wave_spec, wave_spec, chirp_spec] + [block_spec] * 4
    args = [waves, patches, chirps] + list(blocks)
    if residual_after:
        in_specs.append(pl.BlockSpec((1, width, width), lambda i: (i, 0, 0)))
        args.append(extra)
    if backward:
        in_specs.append(wave_spec)
        args.append(extra)
        out_shape = (
            jax.ShapeDtypeStruct(waves.shape, jnp.bfloat16),
            jax.ShapeDtypeStruct(waves.shape, jnp.float32),
        )
        out_specs = (wave_spec, wave_spec)
    else:
        out_shape = jax.ShapeDtypeStruct(waves.shape, jnp.bfloat16)
        out_specs = wave_spec
    return pl.pallas_call(
        wave_kernel(transmit_first, residual_after, backward),
        grid=(number,),
        in_specs=in_specs,
        out_specs=out_specs,
        out_shape=out_shape,
    )(*args)


def local(object_field, probe, positions, counts, measured):
    width = probe.shape[1]
    tile_rows = object_field.shape[2]
    columns_all = object_field.shape[3]
    tile_index = lax.axis_index("tile")
    tile_count = lax.axis_size("tile")
    segment = lax.axis_index("depth")
    depth_count = lax.axis_size("depth")
    batch_index = lax.axis_index("batch")
    batch_count = lax.axis_size("batch")
    rim = from_behind(object_field[:, :, :width, :], "tile", -1)
    extended = jnp.concatenate([object_field, rim], axis=2)[0]
    capacity = positions.shape[0]
    live = jnp.arange(capacity, dtype=jnp.int32) < counts[0]
    local_rows = positions[:, 0] - tile_index * tile_rows
    local_columns = positions[:, 1]
    anchor = jnp.zeros((), jnp.int32)

    def cut_patch(row, column):
        return lax.dynamic_slice(extended, (anchor, row, column), (2, width, width))

    patches = jax.vmap(cut_patch)(local_rows, local_columns)
    number = patches.shape[0]
    forward_block = dft_block(width, -1.0)
    inverse_block = dft_block(width, 1.0)
    coef = jnp.where(
        segment == depth_count - 1, jnp.float32(DETECTOR_COEF), jnp.float32(SLICE_COEF)
    )
    chirp_re, chirp_im = chirp_parts(width, coef)
    start = jnp.broadcast_to(probe[None], (number, 2, width, width))

    chirps = jnp.stack([chirp_re, chirp_im])
    blocks = (forward_block, forward_block.T, inverse_block, inverse_block.T)

    def forward_all(waves):
        return run_waves(waves, patches, chirps, blocks)

    def forward_last(waves):
        return run_waves(waves, patches, chirps, blocks, measured, residual_after=True)

    def silent(waves):
        return jnp.zeros_like(waves)

    carry = start
    inputs = start
    for turn in range(depth_count):
        if turn > 0:
            carry = lax.ppermute(carry, "depth", [(turn - 1, turn)])
            inputs = jnp.where(segment == turn, carry, inputs)
        step = forward_last if turn == depth_count - 1 else forward_all
        carry = lax.cond(segment == turn, step, silent, carry)

    def back_pass(incoming):
        return run_waves(
            incoming, patches, chirps, blocks, inputs, transmit_first=False, backward=True
        )

    def back_silent(incoming):
        return (jnp.zeros_like(incoming), jnp.zeros(incoming.shape, jnp.float32))

    terms = jnp.zeros(start.shape, jnp.float32)
    for turn in reversed(range(depth_count)):
        if turn < depth_count - 1:
            carry = lax.ppermute(carry, "depth", [(turn + 1, turn)])
        carry, got = lax.cond(segment == turn, back_pass, back_silent, carry)
        terms = jnp.where(segment == turn, got, terms)

    weighted = jnp.where(live[:, None, None, None], terms, 0.0)
    gradient = jnp.zeros((2, tile_rows + width, columns_all), jnp.float32)
    for index in range(number):
        place = (anchor, local_rows[index], local_columns[index])
        current = lax.dynamic_slice(gradient, place, (2, width, width))
        gradient = lax.dynamic_update_slice(gradient, current + weighted[index], place)

    own = gradient[:, :tile_rows, :].astype(jnp.bfloat16)
    spill = gradient[:, tile_rows:, :].astype(jnp.bfloat16)
    pairs = [(b, (b + 1) % batch_count) for b in range(batch_count)]
    partner = lax.ppermute(own, "batch", pairs)
    same_core = lax.ppermute(
        spill, "tile", [(t, t + 1) for t in range(tile_count - 1)]
    )
    diagonal = lax.ppermute(
        spill,
        ("tile", "batch"),
        [
            (t * batch_count + b, (t + 1) * batch_count + (b + 1) % batch_count)
            for t in range(tile_count - 1)
            for b in range(batch_count)
        ],
    )
    summed = own.astype(jnp.float32) + partner.astype(jnp.float32)
    spilled = same_core.astype(jnp.float32) + diagonal.astype(jnp.float32)
    summed = summed.at[:, :width, :].add(spilled)
    return summed[None]


def solution(mesh):
    placed = (
        P(("groups", "depth"), None, "tile", None),
        P("groups", None, None),
        P(("groups", "tile", "batch"), None),
        P(("groups", "tile", "batch")),
        P(("groups", "tile", "batch"), None, None),
    )
    return jax.shard_map(
        local,
        mesh=mesh,
        in_specs=placed,
        out_specs=P(("groups", "depth"), None, "tile", None),
        check_vma=False,
    )
```

profile of v0, /device:TPU:0, one launch (start us, length us, event | category | flops | bytes accessed | tf_op | source)
XLA Modules:
  0.0 141.7 jit_solution(600896033931696984)
XLA Ops:
  0.0 1.4 collective-permute-start
  1.4 1.0 multiply_convert_fusion
  2.4 1.0 fusion.12
  3.5 1.0 multiply_convert_fusion.2
  4.4 0.9 fusion.17
  5.8 1.0 fusion.9
  6.9 21.7 %collective-permute-done = f32[1,2,256,512]{3,2,1,0:T(8,128)} collective-permute-done((f32[1,2,256,512]{3,2,1,0:T(8,128)}, f32[1,2,256,512]{3,2,1,0:T(8,128)}, u32[]{:S(2)}, u32[]{:S(2)}) %collective-permute-start) | collective-permute-done | bytes 1048608 | tf_op jit(solution)/shard_map/ppermute | solution.py:17
  28.5 2.7 %maximum_bitcast_fusion = f32[2,512,512]{2,1,0:T(8,128)} fusion(f32[1,2,256,512]{3,2,1,0:T(8,128)} %collective-permute-done, f32[1,2,256,512]{3,2,1,0:T(8,128)S(1)} %copy-done.1), kind=kLoop, calls=%fused_computation.2 | loop fusion | flops 524288 | bytes 4194304 | tf_op jit(solution)/shard_map/squeeze | solution.py:204
  31.3 6.3 %while.4 = (s32[]{:T(128)}, f32[2,512,512]{2,1,0:T(8,128)}, s32[2,3]{1,0:T(2,128)S(1)}, f32[2,2,256,256]{3,2,1,0:T(8,128)S(1)}) while((s32[]{:T(128)}, f32[2,512,512]{2,1,0:T(8,128)}, s32[2,3]{1,0:T(2,128)S(1)}, f32[2,2,256,256]{3,2,1,0:T(8,128)S(1)}) %tuple.77), condition=%wide.while_cond.1.clone, body=%wide.while_body.1.sunk.clone | while | flops 2 | bytes 1048685 | solution.py:212
  31.9 2.6 %bitcast_dynamic-update-slice_fusion.3 = f32[2,2,256,256]{3,2,1,0:T(8,128)S(1)} fusion(f32[2,2,256,256]{3,2,1,0:T(8,128)S(1)} %get-tuple-element.249, s32[]{:T(128)} %get-tuple-element.246, f32[2,512,512]{2,1,0:T(8,128)} %get-tuple-element.251, s32[]{:T(128)} %bitcast.29, s32[]{:T(128)} %bitcast.30), kind=kLoop, calls=%fused_computation.clone.1.clone | loop fusion | bytes 1048588 | tf_op jit(solution)/shard_map/vmap()/gather
  35.1 2.6 %bitcast_dynamic-update-slice_fusion.3 = f32[2,2,256,256]{3,2,1,0:T(8,128)S(1)} fusion(f32[2,2,256,256]{3,2,1,0:T(8,128)S(1)} %get-tuple-element.249, s32[]{:T(128)} %get-tuple-element.246, f32[2,512,512]{2,1,0:T(8,128)} %get-tuple-element.251, s32[]{:T(128)} %bitcast.29, s32[]{:T(128)} %bitcast.30), kind=kLoop, calls=%fused_computation.clone.1.clone | loop fusion | bytes 1048588 | tf_op jit(solution)/shard_map/vmap()/gather
  38.5 6.4 %conditional.4 = (bf16[2,2,256,256]{3,2,1,0:T(8,128)(2,1)}) conditional(s32[]{:T(128)} %convert_element_type.74, () %tuple.40, (bf16[2,2,256,256]{3,2,1,0:T(8,128)(2,1)}, f32[2,2,256,256]{3,2,1,0:T(8,128)S(1)}, f32[2,256,256]{2,1,0:T(8,128)S(1)}, bf16[512,512]{1,0:T(8,128)(2,1)S(1)}, bf16[512,512]{0,1:T(8,128)(2,1)}, ...), branch_computations={%region_0.1_spmd, %region_1.2_spmd} | conditional | bytes 1048584 | solution.py:243
  38.5 2.1 %copy.8.refs_4_ = bf16[512,512]{1,0:T(8,128)(2,1)} copy(bf16[512,512]{0,1:T(8,128)(2,1)} %get-tuple-element.146) | data formatting | bytes 1048576 | tf_op jit(solution)/shard_map
  40.5 4.3 %branch_1_fun.4 = bf16[2,2,256,256]{3,2,1,0:T(8,128)(2,1)} custom-call(bf16[2,2,256,256]{3,2,1,0:T(8,128)(2,1)} %get-tuple-element.96.refs_0_, f32[2,2,256,256]{3,2,1,0:T(8,128)S(1)} %get-tuple-element.97.refs_1_, f32[2,256,256]{2,1,0:T(8,128)S(1)} %get-tuple-element.98.refs_2_, bf16[512,512]{1,0:T(8,128)(2,1)S(1)} %get-tuple-element.99.refs_3_, ...), custom_call_target="tpu_custom_call" | custom-call | tf_op jit(solution)/shard_map/cond/branch_1_fun/pallas_call | solution.py:184
  44.8 2.1 %collective-permute-start.1 = (bf16[2,2,256,256]{3,2,1,0:T(8,128)(2,1)}, bf16[2,2,256,256]{3,2,1,0:T(8,128)(2,1)}, u32[]{:S(2)}, u32[]{:S(2)}) collective-permute-start(bf16[2,2,256,256]{3,2,1,0:T(8,128)(2,1)} %get-tuple-element.258), channel_id=1, source_target_pairs={{0,2},{1,3},{4,6},{5,7},{8,10},{9,11},{12,14},{13,15},{16,18},{17,... | collective-permute-start | bytes 1572872 | tf_op jit(solution)/shard_map/ppermute | solution.py:240
  46.9 10.4 %collective-permute-done.1 = bf16[2,2,256,256]{3,2,1,0:T(8,128)(2,1)} collective-permute-done((bf16[2,2,256,256]{3,2,1,0:T(8,128)(2,1)}, bf16[2,2,256,256]{3,2,1,0:T(8,128)(2,1)}, u32[]{:S(2)}, u32[]{:S(2)}) %collective-permute-start.1) | collective-permute-done | bytes 524320 | tf_op jit(solution)/shard_map/ppermute | solution.py:240
  59.0 1.9 %conditional.6 = ((bf16[2,2,256,256]{3,2,1,0:T(8,128)(2,1)}, f32[2,2,256,256]{3,2,1,0:T(8,128)})) conditional(s32[]{:T(128)} %convert_element_type.75, () %tuple.38, (bf16[2,2,256,256]{3,2,1,0:T(8,128)(2,1)}, f32[2,2,256,256]{3,2,1,0:T(8,128)S(1)}, f32[2,256,256]{2,1,0:T(8,128)S(1)}, bf16[512,512]{1,0:T(8,128)(2,1)S(1)}, bf16[512,512]{0,1:T(8,128)(2,1)}, ...), branch_computations={%region_4.5_spmd, %region_5.6_spmd} | conditional | bytes 1572894 | solution.py:257
  59.0 1.1 broadcast.222
  60.9 1.3 collective-permute-start.2
  71.7 15.5 %collective-permute-done.2 = bf16[2,2,256,256]{3,2,1,0:T(8,128)(2,1)} collective-permute-done((bf16[2,2,256,256]{3,2,1,0:T(8,128)(2,1)}, bf16[2,2,256,256]{3,2,1,0:T(8,128)(2,1)}, u32[]{:S(2)}, u32[]{:S(2)}) %collective-permute-start.2) | collective-permute-done | bytes 524320 | tf_op jit(solution)/shard_map/ppermute | solution.py:256
  87.2 6.7 %conditional.7 = (f32[2,2,256,256]{3,2,1,0:T(8,128)}) conditional(s32[]{:T(128)} %convert_element_type.74, () %tuple.37, (bf16[2,2,256,256]{3,2,1,0:T(8,128)(2,1)}, f32[2,2,256,256]{3,2,1,0:T(8,128)S(1)}, f32[2,256,256]{2,1,0:T(8,128)S(1)}, bf16[512,512]{1,0:T(8,128)(2,1)S(1)}, bf16[512,512]{0,1:T(8,128)(2,1)}, ...), branch_computations={%region_6.7_spmd, %region_7.8_spmd} | conditional | bytes 1048588 | solution.py:257
  87.2 2.1 %copy.11.refs_4_ = bf16[512,512]{1,0:T(8,128)(2,1)} copy(bf16[512,512]{0,1:T(8,128)(2,1)} %get-tuple-element.169) | data formatting | bytes 1048576 | tf_op jit(solution)/shard_map
  89.2 4.6 %branch_1_fun.7 = (bf16[2,2,256,256]{3,2,1,0:T(8,128)(2,1)}, f32[2,2,256,256]{3,2,1,0:T(8,128)}) custom-call(bf16[2,2,256,256]{3,2,1,0:T(8,128)(2,1)} %get-tuple-element.119.refs_0_, f32[2,2,256,256]{3,2,1,0:T(8,128)S(1)} %get-tuple-element.120.refs_1_, f32[2,256,256]{2,1,0:T(8,128)S(1)} %get-tuple-element.121.refs_2_, ...), custom_call_target="tpu_custom_call" | custom-call | tf_op jit(solution)/shard_map/cond/branch_1_fun/pallas_call | solution.py:184
  93.9 1.4 %select_select_fusion = f32[2,2,256,256]{3,2,1,0:T(8,128)S(1)} fusion(f32[2,2,256,256]{3,2,1,0:T(8,128)} %get-tuple-element.261, f32[2,2,256,256]{3,2,1,0:T(8,128)} %get-tuple-element.131, pred[2]{0:T(512)(128)(4,1)S(1)} %iota_compare_fusion, pred[]{:T(512)S(6)} %eq.10, pred[]{:T(512)S(6)} %eq.9), kind=kLoop, calls=%fused_computation.4 | loop fusion | flops 786432 | bytes 3145732 | tf_op jit(solution)/shard_map/jit(_where)/select_n | solution.py:260
  96.4 7.4 %dynamic_update_slice.6 = f32[2,512,512]{2,1,0:T(8,128)S(1)} dynamic-update-slice(f32[2,512,512]{2,1,0:T(8,128)S(1)} %broadcast_in_dim.12, f32[2,256,256]{2,1,0:T(8,128)} %slice_bitcast_fusion.1, s32[]{:T(128)} %constant.95.clone.1, s32[]{:T(128)S(6)} %select_n.98, s32[]{:T(128)S(6)} %select_n.99) | dynamic-update-slice | bytes 1048580 | tf_op jit(solution)/shard_map/dynamic_update_slice | solution.py:265
  103.8 1.0 fusion.2
  104.8 7.7 %dynamic_update_slice.7 = f32[2,512,512]{2,1,0:T(8,128)S(1)} dynamic-update-slice(f32[2,512,512]{2,1,0:T(8,128)S(1)} %dynamic_update_slice.6, f32[2,256,256]{2,1,0:T(8,128)} %fusion.2, s32[]{:T(128)} %constant.95.clone.1, s32[]{:T(128)S(6)} %select_n.100, s32[]{:T(128)S(6)} %select_n.101) | dynamic-update-slice | bytes 1048580 | tf_op jit(solution)/shard_map/dynamic_update_slice | solution.py:265
  112.8 4.9 %collective-permute-start.4 = (bf16[2,256,512]{2,1,0:T(8,128)(2,1)S(1)}, bf16[2,256,512]{2,1,0:T(8,128)(2,1)S(1)}, u32[]{:S(2)}, u32[]{:S(2)}) collective-permute-start(bf16[2,256,512]{2,1,0:T(8,128)(2,1)S(1)} %get-tuple-element.186), channel_id=1, source_target_pairs={{0,4},{4,8},{8,12},{1,5},{5,9},{9,13},{2,6},{6,10},{10,14},{3,7},{... | collective-permute-start | bytes 1572872 | tf_op jit(solution)/shard_map/ppermute | solution.py:271
  117.6 2.8 %collective-permute-start.5 = (bf16[2,256,512]{2,1,0:T(8,128)(2,1)S(1)}, bf16[2,256,512]{2,1,0:T(8,128)(2,1)S(1)}, u32[]{:S(2)}, u32[]{:S(2)}) collective-permute-start(bf16[2,256,512]{2,1,0:T(8,128)(2,1)S(1)} %get-tuple-element.186), channel_id=1, source_target_pairs={{0,5},{1,4},{4,9},{5,8},{8,13},{9,12},{2,7},{3,6},{6,11},{7,10},{1... | collective-permute-start | bytes 1572872 | tf_op jit(solution)/shard_map/ppermute | solution.py:274
  120.4 9.4 %collective-permute-done.4 = bf16[2,256,512]{2,1,0:T(8,128)(2,1)S(1)} collective-permute-done((bf16[2,256,512]{2,1,0:T(8,128)(2,1)S(1)}, bf16[2,256,512]{2,1,0:T(8,128)(2,1)S(1)}, u32[]{:S(2)}, u32[]{:S(2)}) %collective-permute-start.4) | collective-permute-done | bytes 524320 | tf_op jit(solution)/shard_map/ppermute | solution.py:271
  129.9 10.5 %collective-permute-done.5 = bf16[2,256,512]{2,1,0:T(8,128)(2,1)S(1)} collective-permute-done((bf16[2,256,512]{2,1,0:T(8,128)(2,1)S(1)}, bf16[2,256,512]{2,1,0:T(8,128)(2,1)S(1)}, u32[]{:S(2)}, u32[]{:S(2)}) %collective-permute-start.5) | collective-permute-done | bytes 524320 | tf_op jit(solution)/shard_map/ppermute | solution.py:274
  140.4 1.2 add_bitcast_fusion
  (31 shorter events, 8.4 us)
Async XLA Ops:
  0.0 5.6 %copy-start.2 = (s32[2,2]{1,0:T(2,128)S(1)}, s32[2,2]{1,0:T(2,128)}, u32[]{:S(2)}) copy-start(s32[2,2]{1,0:T(2,128)} %param.19) | copy-start | bytes 52
  0.0 28.5 %collective-permute-start = (f32[1,2,256,512]{3,2,1,0:T(8,128)}, f32[1,2,256,512]{3,2,1,0:T(8,128)}, u32[]{:S(2)}, u32[]{:S(2)}) collective-permute-start(f32[1,2,256,512]{3,2,1,0:T(8,128)} %param.17), channel_id=1, source_target_pairs={{4,0},{8,4},{12,8},{5,1},{9,5},{13,9},{6,2},{10,6},{14,10},{7,3},{... | collective-permute-start | bytes 3145736 | tf_op jit(solution)/shard_map/ppermute | solution.py:17
  5.6 22.9 %copy-start.1 = (f32[1,2,256,512]{3,2,1,0:T(8,128)S(1)}, f32[1,2,256,512]{3,2,1,0:T(8,128)}, u32[]{:S(2)}) copy-start(f32[1,2,256,512]{3,2,1,0:T(8,128)} %param.17) | copy-start | bytes 3145732
  31.3 6.3 %copy-start = (bf16[2,256,256]{2,1,0:T(8,128)(2,1)S(1)}, bf16[2,256,256]{2,1,0:T(8,128)(2,1)}, u32[]{:S(2)}) copy-start(bf16[2,256,256]{2,1,0:T(8,128)(2,1)} %param.18) | copy-start | bytes 786436
  44.8 12.5 %collective-permute-start.1 = (bf16[2,2,256,256]{3,2,1,0:T(8,128)(2,1)}, bf16[2,2,256,256]{3,2,1,0:T(8,128)(2,1)}, u32[]{:S(2)}, u32[]{:S(2)}) collective-permute-start(bf16[2,2,256,256]{3,2,1,0:T(8,128)(2,1)} %get-tuple-element.258), channel_id=1, source_target_pairs={{0,2},{1,3},{4,6},{5,7},{8,10},{9,11},{12,14},{13,15},{16,18},{17,... | collective-permute-start | bytes 1572872 | tf_op jit(solution)/shard_map/ppermute | solution.py:240
  60.9 26.2 %collective-permute-start.2 = (bf16[2,2,256,256]{3,2,1,0:T(8,128)(2,1)}, bf16[2,2,256,256]{3,2,1,0:T(8,128)(2,1)}, u32[]{:S(2)}, u32[]{:S(2)}) collective-permute-start(bf16[2,2,256,256]{3,2,1,0:T(8,128)(2,1)} %get-tuple-element.130), channel_id=1, source_target_pairs={{2,0},{3,1},{6,4},{7,5},{10,8},{11,9},{14,12},{15,13},{18,16},{19,... | collective-permute-start | bytes 1572872 | tf_op jit(solution)/shard_map/ppermute | solution.py:256
  112.7 7.7 %collective-permute-start.3 = (bf16[2,256,512]{2,1,0:T(8,128)(2,1)S(1)}, bf16[2,256,512]{2,1,0:T(8,128)(2,1)S(1)}, u32[]{:S(2)}, u32[]{:S(2)}) collective-permute-start(bf16[2,256,512]{2,1,0:T(8,128)(2,1)S(1)} %get-tuple-element.185), channel_id=1, source_target_pairs={{0,1},{1,0},{2,3},{3,2},{4,5},{5,4},{6,7},{7,6},{8,9},{9,8},{10,11... | collective-permute-start | bytes 1572872 | tf_op jit(solution)/shard_map/ppermute | solution.py:270
  112.8 17.1 %collective-permute-start.4 = (bf16[2,256,512]{2,1,0:T(8,128)(2,1)S(1)}, bf16[2,256,512]{2,1,0:T(8,128)(2,1)S(1)}, u32[]{:S(2)}, u32[]{:S(2)}) collective-permute-start(bf16[2,256,512]{2,1,0:T(8,128)(2,1)S(1)} %get-tuple-element.186), channel_id=1, source_target_pairs={{0,4},{4,8},{8,12},{1,5},{5,9},{9,13},{2,6},{6,10},{10,14},{3,7},{... | collective-permute-start | bytes 1572872 | tf_op jit(solution)/shard_map/ppermute | solution.py:271
  117.6 22.8 %collective-permute-start.5 = (bf16[2,256,512]{2,1,0:T(8,128)(2,1)S(1)}, bf16[2,256,512]{2,1,0:T(8,128)(2,1)S(1)}, u32[]{:S(2)}, u32[]{:S(2)}) collective-permute-start(bf16[2,256,512]{2,1,0:T(8,128)(2,1)S(1)} %get-tuple-element.186), channel_id=1, source_target_pairs={{0,5},{1,4},{4,9},{5,8},{8,13},{9,12},{2,7},{3,6},{6,11},{7,10},{1... | collective-permute-start | bytes 1572872 | tf_op jit(solution)/shard_map/ppermute | solution.py:274
where the time goes:
time: 143 us; the launch traced here: 142 us
  waiting for transfers between devices  67.6 us (47%)
  local copies, waits for them, and re-layouts  31.7 us (22%)
  starting transfers between devices  12.5 us (9%)
  other arithmetic  12.5 us (9%)
  Pallas kernels  8.93 us (6%)
  between operations  8.46 us (6%)
    ppermute x1, waiting for transfers between devices, from_behind(): return lax.ppermute(block, axis, route)  21.7 us
    ppermute x1, waiting for transfers between devices, local(): carry = lax.ppermute(carry, 'depth', [(turn + 1, turn)])  15.5 us
    dynamic_update_slice x2, local copies, waits for them, and re-layouts, local(): lax.dynamic_update_slice(gradient, current + weighted[index], place)  15.1 us
    ppermute x1, waiting for transfers between devices, local(): lax.ppermute(spill, ('tile', 'batch'), [(t * batch_count + b, (t + 1) * b...  10.5 us
    ppermute x1, waiting for transfers between devices, local(): carry = lax.ppermute(carry, 'depth', [(turn - 1, turn)])  10.4 us
    ppermute x1, waiting for transfers between devices, local(): lax.ppermute(spill, 'tile', [(t, t + 1) for t in range(tile_count - 1)])  9.44 us
    pallas_call x2, Pallas kernels, run_waves(): pl.pallas_call(wave_kernel(transmit_first, residual_after, backward), gri...  8.93 us
    another operation x6, local copies, waits for them, and re-layouts  6.88 us
  transfers between devices with their start and end apart: 6, of which 5 were waited for; matrix products, arithmetic and copies ran while one was open for 5% of the time, Pallas kernels for 0%

commit v1 on v0

--- a/solution.py
+++ b/solution.py
@@ -5,6 +5,7 @@
 from jax import lax
 from jax.sharding import PartitionSpec as P
 from jax.experimental import pallas as pl
+from jax.experimental.pallas import tpu as pltpu
 
 SLICE_COEF = 0.002
 DETECTOR_COEF = 0.006
@@ -26,6 +27,18 @@
     imag_part = (sign * jnp.sin(angle) * scale).astype(jnp.bfloat16)
     upper = jnp.concatenate([real_part, -imag_part], axis=1)
     lower = jnp.concatenate([imag_part, real_part], axis=1)
+    return jnp.concatenate([upper, lower], axis=0)
+
+
+def dft_right(width, sign):
+    freq = jnp.arange(width, dtype=jnp.int32)
+    product = freq[:, None] * freq[None, :] % width
+    angle = 2.0 * math.pi / width * product.astype(jnp.float32)
+    scale = 1.0 / math.sqrt(width)
+    real_part = (jnp.cos(angle) * scale).astype(jnp.bfloat16)
+    imag_part = (sign * jnp.sin(angle) * scale).astype(jnp.bfloat16)
+    upper = jnp.concatenate([real_part, imag_part], axis=1)
+    lower = jnp.concatenate([-imag_part, real_part], axis=1)
     return jnp.concatenate([upper, lower], axis=0)
 
 
@@ -190,6 +203,47 @@
     )(*args)
 
 
+def scatter_kernel(rows_ref, columns_ref, live_ref, terms_ref, out_ref):
+    index = pl.program_id(0)
+
+    @pl.when(index == 0)
+    def _():
+        out_ref[...] = jnp.zeros(out_ref.shape, out_ref.dtype)
+
+    width = terms_ref.shape[2]
+    height = out_ref.shape[1]
+    columns_all = out_ref.shape[2]
+    row = rows_ref[index]
+    column = columns_ref[index]
+    alive = live_ref[index] > 0
+    for part in range(2):
+        term = jnp.where(alive, terms_ref[0, part], 0.0)
+        wide = jnp.concatenate(
+            [term, jnp.zeros((width, columns_all - width), jnp.float32)], axis=1
+        )
+        wide = pltpu.roll(wide, column, 1)
+        tall = jnp.concatenate(
+            [wide, jnp.zeros((height - width, columns_all), jnp.float32)], axis=0
+        )
+        tall = pltpu.roll(tall, row, 0)
+        out_ref[part] = out_ref[part] + tall
+
+
+def scatter_terms(terms, rows, columns, live, height, columns_all):
+    number, _, width, _ = terms.shape
+    grid_spec = pltpu.PrefetchScalarGridSpec(
+        num_scalar_prefetch=3,
+        grid=(number,),
+        in_specs=[pl.BlockSpec((1, 2, width, width), lambda i, r, c, a: (i, 0, 0, 0))],
+        out_specs=pl.BlockSpec((2, height, columns_all), lambda i, r, c, a: (0, 0, 0)),
+    )
+    return pl.pallas_call(
+        scatter_kernel,
+        grid_spec=grid_spec,
+        out_shape=jax.ShapeDtypeStruct((2, height, columns_all), jnp.float32),
+    )(rows, columns, live.astype(jnp.int32), terms)
+
+
 def local(object_field, probe, positions, counts, measured):
     width = probe.shape[1]
     tile_rows = object_field.shape[2]
@@ -222,7 +276,7 @@
     start = jnp.broadcast_to(probe[None], (number, 2, width, width))
 
     chirps = jnp.stack([chirp_re, chirp_im])
-    blocks = (forward_block, forward_block.T, inverse_block, inverse_block.T)
+    blocks = (forward_block, dft_right(width, -1.0), inverse_block, dft_right(width, 1.0))
 
     def forward_all(waves):
         return run_waves(waves, patches, chirps, blocks)
@@ -257,32 +311,16 @@
         carry, got = lax.cond(segment == turn, back_pass, back_silent, carry)
         terms = jnp.where(segment == turn, got, terms)
 
-    weighted = jnp.where(live[:, None, None, None], terms, 0.0)
-    gradient = jnp.zeros((2, tile_rows + width, columns_all), jnp.float32)
-    for index in range(number):
-        place = (anchor, local_rows[index], local_columns[index])
-        current = lax.dynamic_slice(gradient, place, (2, width, width))
-        gradient = lax.dynamic_update_slice(gradient, current + weighted[index], place)
-
-    own = gradient[:, :tile_rows, :].astype(jnp.bfloat16)
+    gradient = scatter_terms(
+        terms, local_rows, local_columns, live, tile_rows + width, columns_all
+    )
     spill = gradient[:, tile_rows:, :].astype(jnp.bfloat16)
+    arrived = lax.ppermute(spill, "tile", [(t, t + 1) for t in range(tile_count - 1)])
+    own = gradient[:, :tile_rows, :]
+    own = own.at[:, :width, :].add(arrived.astype(jnp.float32)).astype(jnp.bfloat16)
     pairs = [(b, (b + 1) % batch_count) for b in range(batch_count)]
     partner = lax.ppermute(own, "batch", pairs)
-    same_core = lax.ppermute(
-        spill, "tile", [(t, t + 1) for t in range(tile_count - 1)]
-    )
-    diagonal = lax.ppermute(
-        spill,
-        ("tile", "batch"),
-        [
-            (t * batch_count + b, (t + 1) * batch_count + (b + 1) % batch_count)
-            for t in range(tile_count - 1)
-            for b in range(batch_count)
-        ],
-    )
     summed = own.astype(jnp.float32) + partner.astype(jnp.float32)
-    spilled = same_core.astype(jnp.float32) + diagonal.astype(jnp.float32)
-    summed = summed.at[:, :width, :].add(spilled)
     return summed[None]
 
 

time: 143 us -> 112 us (0.78)
  local copies, waits for them, and re-layouts: 31.7 us -> 11.4 us
  between operations: 8.46 us -> 0.75 us
  waiting for transfers between devices: 67.6 us -> 61.4 us
  Pallas kernels: 8.93 us -> 14.3 us
  starting transfers between devices: 12.5 us -> 7.74 us
  other arithmetic: 12.5 us -> 15.6 us
    dynamic_update_slice x2 -> x0, local copies, waits for them, and re-layouts: 15.1 us -> none  [local(): lax.dynamic_update_slice(gradient, current + weighted[index], place)]
    ppermute x1 -> x0, waiting for transfers between devices: 10.5 us -> none  [local(): lax.ppermute(spill, ('tile', 'batch'), [(t * batch_count + b, (t + 1) * b...]
    pallas_call x0 -> x1, Pallas kernels: none -> 5.4 us  [scatter_terms(): pl.pallas_call(scatter_kernel, grid_spec=grid_spec, out_shape=jax.ShapeDt...]
    another operation x6 -> x4, local copies, waits for them, and re-layouts: 6.88 us -> 2.74 us
    ppermute x1, waiting for transfers between devices: 15.5 us -> 19.6 us  [local(): carry = lax.ppermute(carry, 'depth', [(turn + 1, turn)])]
    ppermute x1 -> x0, starting transfers between devices: 2.77 us -> none  [local(): lax.ppermute(spill, ('tile', 'batch'), [(t * batch_count + b, (t + 1) * b...]
    convert_element_type x0 -> x2, other arithmetic: none -> 1.92 us  [the longest x1 1.39 us: local(): own.at[:, :width, :].add(arrived.astype(jnp.float32)).astype(jnp.bfloat16)]
    ppermute x1, waiting for transfers between devices: 0.01 us -> 1.9 us  [local(): partner = lax.ppermute(own, 'batch', pairs)]
  transfers between devices with their start and end apart: 6 -> 5, of which waited for: 5 -> 5; matrix products, arithmetic and copies ran while one was open for 5% -> 6% of each run, Pallas kernels for 0% -> 0%
where the time goes in v1:
time: 112 us; the launch traced here: 111 us
  waiting for transfers between devices  61.4 us (55%)
  other arithmetic  15.6 us (14%)
  Pallas kernels  14.3 us (13%)
  local copies, waits for them, and re-layouts  11.4 us (10%)
  starting transfers between devices  7.74 us (7%)
    ppermute x1, waiting for transfers between devices, from_behind(): return lax.ppermute(block, axis, route)  20.5 us
    ppermute x1, waiting for transfers between devices, local(): carry = lax.ppermute(carry, 'depth', [(turn + 1, turn)])  19.6 us
    ppermute x1, waiting for transfers between devices, local(): carry = lax.ppermute(carry, 'depth', [(turn - 1, turn)])  10.4 us
    ppermute x1, waiting for transfers between devices, local(): lax.ppermute(spill, 'tile', [(t, t + 1) for t in range(tile_count - 1)])  8.97 us
    pallas_call x2, Pallas kernels, run_waves(): pl.pallas_call(wave_kernel(transmit_first, residual_after, backward), gri...  8.94 us
    gather x6, local copies, waits for them, and re-layouts  6.53 us
    pallas_call x1, Pallas kernels, scatter_terms(): pl.pallas_call(scatter_kernel, grid_spec=grid_spec, out_shape=jax.ShapeDt...  5.4 us
    ppermute x1, starting transfers between devices, local(): lax.ppermute(spill, 'tile', [(t, t + 1) for t in range(tile_count - 1)])  3.01 us
  transfers between devices with their start and end apart: 5, of which 5 were waited for; matrix products, arithmetic and copies ran while one was open for 6% of the time, Pallas kernels for 0%

profile of v1, /device:TPU:0, one launch (start us, length us, event | category | flops | bytes accessed | tf_op | source)
XLA Modules:
  0.0 111.2 jit_solution(12823780679777263160)
XLA Ops:
  0.0 1.3 %collective-permute-start = (f32[1,2,256,512]{3,2,1,0:T(8,128)}, f32[1,2,256,512]{3,2,1,0:T(8,128)}, u32[]{:S(2)}, u32[]{:S(2)}) collective-permute-start(f32[1,2,256,512]{3,2,1,0:T(8,128)} %param.17), channel_id=1, source_target_pairs={{4,0},{8,4},{12,8},{5,1},{9,5},{13,9},{6,2},{10,6},{14,10},{7,3},{... | collective-permute-start | bytes 3145736 | tf_op jit(solution)/shard_map/ppermute | solution.py:18
  1.3 1.5 %compare_select_fusion.1 = (s32[2,1]{1,0:T(2,128)S(1)}, s32[2,1]{1,0:T(2,128)S(1)}, s32[2]{0:T(128)}, s32[2]{0:T(128)}) fusion(s32[2,2]{1,0:T(2,128)} %param.19, s32[]{:T(128)S(6)} %mul.235), kind=kLoop, calls=%fused_computation.41 | loop fusion | flops 14 | bytes 52 | tf_op jit(solution)/shard_map/vmap()/select_n | solution.py:266
  2.9 1.0 multiply_convert_fusion.2
  3.9 1.0 multiply_convert_fusion
  4.9 1.0 fusion.14
  5.9 1.0 fusion.11
  6.9 1.0 fusion.4
  7.9 20.5 %collective-permute-done = f32[1,2,256,512]{3,2,1,0:T(8,128)} collective-permute-done((f32[1,2,256,512]{3,2,1,0:T(8,128)}, f32[1,2,256,512]{3,2,1,0:T(8,128)}, u32[]{:S(2)}, u32[]{:S(2)}) %collective-permute-start) | collective-permute-done | bytes 1048608 | tf_op jit(solution)/shard_map/ppermute | solution.py:18
  28.4 2.7 %maximum_bitcast_fusion = f32[2,512,512]{2,1,0:T(8,128)} fusion(f32[1,2,256,512]{3,2,1,0:T(8,128)} %collective-permute-done, f32[1,2,256,512]{3,2,1,0:T(8,128)S(1)} %copy-done.1), kind=kLoop, calls=%fused_computation.2 | loop fusion | flops 524288 | bytes 4194304 | tf_op jit(solution)/shard_map/squeeze | solution.py:258
  31.1 6.6 %while.4 = (s32[]{:T(128)}, f32[2,512,512]{2,1,0:T(8,128)}, s32[2,3]{1,0:T(2,128)S(1)}, f32[2,2,256,256]{3,2,1,0:T(8,128)S(1)}) while((s32[]{:T(128)}, f32[2,512,512]{2,1,0:T(8,128)}, s32[2,3]{1,0:T(2,128)S(1)}, f32[2,2,256,256]{3,2,1,0:T(8,128)S(1)}) %tuple.74), condition=%wide.while_cond.1.clone, body=%wide.while_body.1.sunk.clone | while | flops 2 | bytes 1048685 | solution.py:266
  31.8 2.6 %bitcast_dynamic-update-slice_fusion.3 = f32[2,2,256,256]{3,2,1,0:T(8,128)S(1)} fusion(f32[2,2,256,256]{3,2,1,0:T(8,128)S(1)} %get-tuple-element.218, s32[]{:T(128)} %get-tuple-element.215, f32[2,512,512]{2,1,0:T(8,128)} %get-tuple-element.220, s32[]{:T(128)} %bitcast.16, s32[]{:T(128)} %bitcast.17), kind=kLoop, calls=%fused_computation.clone.1.clone | loop fusion | bytes 1048588 | tf_op jit(solution)/shard_map/vmap()/gather
  35.1 2.6 %bitcast_dynamic-update-slice_fusion.3 = f32[2,2,256,256]{3,2,1,0:T(8,128)S(1)} fusion(f32[2,2,256,256]{3,2,1,0:T(8,128)S(1)} %get-tuple-element.218, s32[]{:T(128)} %get-tuple-element.215, f32[2,512,512]{2,1,0:T(8,128)} %get-tuple-element.220, s32[]{:T(128)} %bitcast.16, s32[]{:T(128)} %bitcast.17), kind=kLoop, calls=%fused_computation.clone.1.clone | loop fusion | bytes 1048588 | tf_op jit(solution)/shard_map/vmap()/gather
  38.5 4.3 %conditional.4 = (bf16[2,2,256,256]{3,2,1,0:T(8,128)(2,1)}) conditional(s32[]{:T(128)} %convert_element_type.115, () %tuple.40, (bf16[2,2,256,256]{3,2,1,0:T(8,128)(2,1)}, f32[2,2,256,256]{3,2,1,0:T(8,128)S(1)}, f32[2,256,256]{2,1,0:T(8,128)S(1)}, bf16[512,512]{1,0:T(8,128)(2,1)S(1)}, bf16[512,512]{1,0:T(8,128)(2,1)}, ...), branch_computations={%region_0.1_spmd, %region_1.2_spmd} | conditional | bytes 524298 | solution.py:297
  38.5 4.3 %branch_1_fun.4 = bf16[2,2,256,256]{3,2,1,0:T(8,128)(2,1)} custom-call(bf16[2,2,256,256]{3,2,1,0:T(8,128)(2,1)} %get-tuple-element.96.refs_0_, f32[2,2,256,256]{3,2,1,0:T(8,128)S(1)} %get-tuple-element.97.refs_1_, f32[2,256,256]{2,1,0:T(8,128)S(1)} %get-tuple-element.98.refs_2_, bf16[512,512]{1,0:T(8,128)(2,1)S(1)} %get-tuple-element.99.refs_3_, ...), custom_call_target="tpu_custom_call" | custom-call | tf_op jit(solution)/shard_map/cond/branch_1_fun/pallas_call | solution.py:197
  42.8 2.1 %collective-permute-start.1 = (bf16[2,2,256,256]{3,2,1,0:T(8,128)(2,1)}, bf16[2,2,256,256]{3,2,1,0:T(8,128)(2,1)}, u32[]{:S(2)}, u32[]{:S(2)}) collective-permute-start(bf16[2,2,256,256]{3,2,1,0:T(8,128)(2,1)} %get-tuple-element.227), channel_id=1, source_target_pairs={{0,2},{1,3},{4,6},{5,7},{8,10},{9,11},{12,14},{13,15},{16,18},{17,... | collective-permute-start | bytes 1572872 | tf_op jit(solution)/shard_map/ppermute | solution.py:294
  44.9 10.4 %collective-permute-done.1 = bf16[2,2,256,256]{3,2,1,0:T(8,128)(2,1)} collective-permute-done((bf16[2,2,256,256]{3,2,1,0:T(8,128)(2,1)}, bf16[2,2,256,256]{3,2,1,0:T(8,128)(2,1)}, u32[]{:S(2)}, u32[]{:S(2)}) %collective-permute-start.1) | collective-permute-done | bytes 524320 | tf_op jit(solution)/shard_map/ppermute | solution.py:294
  56.2 0.9 broadcast_select_fusion
  57.0 1.9 %conditional.6 = ((bf16[2,2,256,256]{3,2,1,0:T(8,128)(2,1)}, f32[2,2,256,256]{3,2,1,0:T(8,128)})) conditional(s32[]{:T(128)} %convert_element_type.116, () %tuple.38, (bf16[2,2,256,256]{3,2,1,0:T(8,128)(2,1)}, f32[2,2,256,256]{3,2,1,0:T(8,128)S(1)}, f32[2,256,256]{2,1,0:T(8,128)S(1)}, bf16[512,512]{1,0:T(8,128)(2,1)S(1)}, bf16[512,512]{1,0:T(8,128)(2,1)}, ...), branch_computations={%region_4.5_spmd, %region_5.6_spmd} | conditional | bytes 1572894 | solution.py:311
  57.0 1.1 broadcast.221
  58.1 0.8 broadcast.220
  58.9 1.3 %collective-permute-start.2 = (bf16[2,2,256,256]{3,2,1,0:T(8,128)(2,1)}, bf16[2,2,256,256]{3,2,1,0:T(8,128)(2,1)}, u32[]{:S(2)}, u32[]{:S(2)}) collective-permute-start(bf16[2,2,256,256]{3,2,1,0:T(8,128)(2,1)} %get-tuple-element.130), channel_id=1, source_target_pairs={{2,0},{3,1},{6,4},{7,5},{10,8},{11,9},{14,12},{15,13},{18,16},{19,... | collective-permute-start | bytes 1572872 | tf_op jit(solution)/shard_map/ppermute | solution.py:310
  61.4 19.6 %collective-permute-done.2 = bf16[2,2,256,256]{3,2,1,0:T(8,128)(2,1)} collective-permute-done((bf16[2,2,256,256]{3,2,1,0:T(8,128)(2,1)}, bf16[2,2,256,256]{3,2,1,0:T(8,128)(2,1)}, u32[]{:S(2)}, u32[]{:S(2)}) %collective-permute-start.2) | collective-permute-done | bytes 524320 | tf_op jit(solution)/shard_map/ppermute | solution.py:310
  81.1 4.6 %conditional.7 = (f32[2,2,256,256]{3,2,1,0:T(8,128)}) conditional(s32[]{:T(128)} %convert_element_type.115, () %tuple.37, (bf16[2,2,256,256]{3,2,1,0:T(8,128)(2,1)}, f32[2,2,256,256]{3,2,1,0:T(8,128)S(1)}, f32[2,256,256]{2,1,0:T(8,128)S(1)}, bf16[512,512]{1,0:T(8,128)(2,1)S(1)}, bf16[512,512]{1,0:T(8,128)(2,1)}, ...), branch_computations={%region_6.7_spmd, %region_7.8_spmd} | conditional | bytes 1048588 | solution.py:311
  81.1 4.6 %branch_1_fun.7 = (bf16[2,2,256,256]{3,2,1,0:T(8,128)(2,1)}, f32[2,2,256,256]{3,2,1,0:T(8,128)}) custom-call(bf16[2,2,256,256]{3,2,1,0:T(8,128)(2,1)} %get-tuple-element.119.refs_0_, f32[2,2,256,256]{3,2,1,0:T(8,128)S(1)} %get-tuple-element.120.refs_1_, f32[2,256,256]{2,1,0:T(8,128)S(1)} %get-tuple-element.121.refs_2_, ...), custom_call_target="tpu_custom_call" | custom-call | tf_op jit(solution)/shard_map/cond/branch_1_fun/pallas_call | solution.py:197
  85.7 2.3 %select_select_fusion.terms_ref = f32[2,2,256,256]{3,2,1,0:T(8,128)} fusion(f32[2,2,256,256]{3,2,1,0:T(8,128)} %get-tuple-element.230, f32[2,2,256,256]{3,2,1,0:T(8,128)} %get-tuple-element.131, pred[]{:T(512)S(6)} %eq.20, pred[]{:T(512)S(6)} %eq.11), kind=kLoop, calls=%fused_computation.7 | loop fusion | flops 524288 | bytes 3145730 | tf_op jit(solution)/shard_map/jit(_where)/select_n | solution.py:312
  88.0 5.4 %shard_map.61 = f32[2,512,512]{2,1,0:T(8,128)} custom-call(s32[2]{0:T(128)} %get-tuple-element.164.rows_ref, s32[2]{0:T(128)} %get-tuple-element.165.columns_ref, s32[2]{0:T(128)} %compare_convert_fusion.live_ref, f32[2,2,256,256]{3,2,1,0:T(8,128)} %select_select_fusion.terms_ref), custom_call_target="tpu_custom_call" | custom-call | tf_op jit(solution)/shard_map/pallas_call | solution.py:240
  93.4 1.3 %slice.64 = bf16[2,256,512]{2,1,0:T(8,128)(2,1)S(1)} slice(f32[2,512,512]{2,1,0:T(8,128)} %shard_map.61), slice={[0:2], [256:512], [0:512]} | slice | bytes 1048576 | tf_op jit(solution)/shard_map/slice | solution.py:317
  94.7 3.0 %collective-permute-start.3 = (bf16[2,256,512]{2,1,0:T(8,128)(2,1)S(1)}, bf16[2,256,512]{2,1,0:T(8,128)(2,1)S(1)}, u32[]{:S(2)}, u32[]{:S(2)}) collective-permute-start(bf16[2,256,512]{2,1,0:T(8,128)(2,1)S(1)} %slice.64), channel_id=1, source_target_pairs={{0,4},{4,8},{8,12},{1,5},{5,9},{9,13},{2,6},{6,10},{10,14},{3,7},{... | collective-permute-start | bytes 1572872 | tf_op jit(solution)/shard_map/ppermute | solution.py:318
  97.8 9.0 %collective-permute-done.3 = bf16[2,256,512]{2,1,0:T(8,128)(2,1)S(1)} collective-permute-done((bf16[2,256,512]{2,1,0:T(8,128)(2,1)S(1)}, bf16[2,256,512]{2,1,0:T(8,128)(2,1)S(1)}, u32[]{:S(2)}, u32[]{:S(2)}) %collective-permute-start.3) | collective-permute-done | bytes 524320 | tf_op jit(solution)/shard_map/ppermute | solution.py:318
  106.7 1.4 %fusion = bf16[2,256,512]{2,1,0:T(8,128)(2,1)S(1)} fusion(f32[2,512,512]{2,1,0:T(8,128)} %shard_map.61, bf16[2,256,512]{2,1,0:T(8,128)(2,1)S(1)} %collective-permute-done.3), kind=kLoop, calls=%fused_computation.5 | loop fusion | flops 786432 | bytes 2097152 | tf_op jit(solution)/shard_map/convert_element_type | solution.py:320
  108.2 1.9 %collective-permute-done.4 = bf16[2,256,512]{2,1,0:T(8,128)(2,1)S(1)} collective-permute-done((bf16[2,256,512]{2,1,0:T(8,128)(2,1)S(1)}, bf16[2,256,512]{2,1,0:T(8,128)(2,1)S(1)}, u32[]{:S(2)}, u32[]{:S(2)}) %collective-permute-start.4) | collective-permute-done | bytes 524320 | tf_op jit(solution)/shard_map/ppermute | solution.py:322
  110.1 1.1 %add_bitcast_fusion = f32[1,2,256,512]{3,2,1,0:T(8,128)} fusion(bf16[2,256,512]{2,1,0:T(8,128)(2,1)S(1)} %collective-permute-done.4, bf16[2,256,512]{2,1,0:T(8,128)(2,1)S(1)} %fusion), kind=kLoop, calls=%fused_computation.6 | loop fusion | flops 786432 | bytes 2097152 | tf_op jit(solution)/shard_map/broadcast_in_dim | solution.py:324
  (18 shorter events, 4.6 us)
Async XLA Ops:
  0.0 28.4 %collective-permute-start = (f32[1,2,256,512]{3,2,1,0:T(8,128)}, f32[1,2,256,512]{3,2,1,0:T(8,128)}, u32[]{:S(2)}, u32[]{:S(2)}) collective-permute-start(f32[1,2,256,512]{3,2,1,0:T(8,128)} %param.17), channel_id=1, source_target_pairs={{4,0},{8,4},{12,8},{5,1},{9,5},{13,9},{6,2},{10,6},{14,10},{7,3},{... | collective-permute-start | bytes 3145736 | tf_op jit(solution)/shard_map/ppermute | solution.py:18
  5.9 22.5 %copy-start.1 = (f32[1,2,256,512]{3,2,1,0:T(8,128)S(1)}, f32[1,2,256,512]{3,2,1,0:T(8,128)}, u32[]{:S(2)}) copy-start(f32[1,2,256,512]{3,2,1,0:T(8,128)} %param.17) | copy-start | bytes 3145732
  31.1 6.6 %copy-start = (bf16[2,256,256]{2,1,0:T(8,128)(2,1)S(1)}, bf16[2,256,256]{2,1,0:T(8,128)(2,1)}, u32[]{:S(2)}) copy-start(bf16[2,256,256]{2,1,0:T(8,128)(2,1)} %param.18) | copy-start | bytes 786436
  42.8 12.5 %collective-permute-start.1 = (bf16[2,2,256,256]{3,2,1,0:T(8,128)(2,1)}, bf16[2,2,256,256]{3,2,1,0:T(8,128)(2,1)}, u32[]{:S(2)}, u32[]{:S(2)}) collective-permute-start(bf16[2,2,256,256]{3,2,1,0:T(8,128)(2,1)} %get-tuple-element.227), channel_id=1, source_target_pairs={{0,2},{1,3},{4,6},{5,7},{8,10},{9,11},{12,14},{13,15},{16,18},{17,... | collective-permute-start | bytes 1572872 | tf_op jit(solution)/shard_map/ppermute | solution.py:294
  58.9 22.1 %collective-permute-start.2 = (bf16[2,2,256,256]{3,2,1,0:T(8,128)(2,1)}, bf16[2,2,256,256]{3,2,1,0:T(8,128)(2,1)}, u32[]{:S(2)}, u32[]{:S(2)}) collective-permute-start(bf16[2,2,256,256]{3,2,1,0:T(8,128)(2,1)} %get-tuple-element.130), channel_id=1, source_target_pairs={{2,0},{3,1},{6,4},{7,5},{10,8},{11,9},{14,12},{15,13},{18,16},{19,... | collective-permute-start | bytes 1572872 | tf_op jit(solution)/shard_map/ppermute | solution.py:310
  94.7 12.0 %collective-permute-start.3 = (bf16[2,256,512]{2,1,0:T(8,128)(2,1)S(1)}, bf16[2,256,512]{2,1,0:T(8,128)(2,1)S(1)}, u32[]{:S(2)}, u32[]{:S(2)}) collective-permute-start(bf16[2,256,512]{2,1,0:T(8,128)(2,1)S(1)} %slice.64), channel_id=1, source_target_pairs={{0,4},{4,8},{8,12},{1,5},{5,9},{9,13},{2,6},{6,10},{10,14},{3,7},{... | collective-permute-start | bytes 1572872 | tf_op jit(solution)/shard_map/ppermute | solution.py:318
  108.1 2.0 %collective-permute-start.4 = (bf16[2,256,512]{2,1,0:T(8,128)(2,1)S(1)}, bf16[2,256,512]{2,1,0:T(8,128)(2,1)S(1)}, u32[]{:S(2)}, u32[]{:S(2)}) collective-permute-start(bf16[2,256,512]{2,1,0:T(8,128)(2,1)S(1)} %fusion), channel_id=1, source_target_pairs={{0,1},{1,0},{2,3},{3,2},{4,5},{5,4},{6,7},{7,6},{8,9},{9,8},{10,11... | collective-permute-start | bytes 1572872 | tf_op jit(solution)/shard_map/ppermute | solution.py:322

commit v2 on v1

--- a/solution.py
+++ b/solution.py
@@ -244,6 +244,45 @@
     )(rows, columns, live.astype(jnp.int32), terms)
 
 
+def cut_kernel(rows_ref, columns_ref, order_ref, tile_ref, mine_ref, partner_ref, out_ref):
+    index = pl.program_id(0)
+    width = out_ref.shape[2]
+    height = tile_ref.shape[2] + mine_ref.shape[2]
+    columns_all = tile_ref.shape[3]
+    row_shift = (height - rows_ref[index]) % height
+    column_shift = (columns_all - columns_ref[index]) % columns_all
+    first = order_ref[0] == 0
+    for part in range(2):
+        mine = mine_ref[0, part]
+        partner = partner_ref[0, part]
+        rim = jnp.concatenate(
+            [jnp.where(first, mine, partner), jnp.where(first, partner, mine)], axis=1
+        )
+        full = jnp.concatenate([tile_ref[0, part], rim], axis=0)
+        full = pltpu.roll(full, row_shift, 0)[:width]
+        full = pltpu.roll(full, column_shift, 1)[:, :width]
+        out_ref[0, part] = full
+
+
+def cut_patches(tile, mine, partner, rows, columns, order, width):
+    number = rows.shape[0]
+    grid_spec = pltpu.PrefetchScalarGridSpec(
+        num_scalar_prefetch=3,
+        grid=(number,),
+        in_specs=[
+            pl.BlockSpec(tile.shape, lambda i, r, c, o: (0, 0, 0, 0)),
+            pl.BlockSpec(mine.shape, lambda i, r, c, o: (0, 0, 0, 0)),
+            pl.BlockSpec(partner.shape, lambda i, r, c, o: (0, 0, 0, 0)),
+        ],
+        out_specs=pl.BlockSpec((1, 2, width, width), lambda i, r, c, o: (i, 0, 0, 0)),
+    )
+    return pl.pallas_call(
+        cut_kernel,
+        grid_spec=grid_spec,
+        out_shape=jax.ShapeDtypeStruct((number, 2, width, width), jnp.float32),
+    )(rows, columns, order, tile, mine, partner)
+
+
 def local(object_field, probe, positions, counts, measured):
     width = probe.shape[1]
     tile_rows = object_field.shape[2]
@@ -254,18 +293,17 @@
     depth_count = lax.axis_size("depth")
     batch_index = lax.axis_index("batch")
     batch_count = lax.axis_size("batch")
-    rim = from_behind(object_field[:, :, :width, :], "tile", -1)
-    extended = jnp.concatenate([object_field, rim], axis=2)[0]
+    half = columns_all // batch_count
+    wanted = lax.dynamic_slice_in_dim(object_field[:, :, :width, :], batch_index * half, half, 3)
+    mine = from_behind(wanted, "tile", -1)
+    pairs = [(b, (b + 1) % batch_count) for b in range(batch_count)]
+    partner = lax.ppermute(mine, "batch", pairs)
     capacity = positions.shape[0]
     live = jnp.arange(capacity, dtype=jnp.int32) < counts[0]
     local_rows = positions[:, 0] - tile_index * tile_rows
     local_columns = positions[:, 1]
-    anchor = jnp.zeros((), jnp.int32)
-
-    def cut_patch(row, column):
-        return lax.dynamic_slice(extended, (anchor, row, column), (2, width, width))
-
-    patches = jax.vmap(cut_patch)(local_rows, local_columns)
+    order = jnp.reshape(batch_index, (1,)).astype(jnp.int32)
+    patches = cut_patches(object_field, mine, partner, local_rows, local_columns, order, width)
     number = patches.shape[0]
     forward_block = dft_block(width, -1.0)
     inverse_block = dft_block(width, 1.0)
@@ -318,7 +356,6 @@
     arrived = lax.ppermute(spill, "tile", [(t, t + 1) for t in range(tile_count - 1)])
     own = gradient[:, :tile_rows, :]
     own = own.at[:, :width, :].add(arrived.astype(jnp.float32)).astype(jnp.bfloat16)
-    pairs = [(b, (b + 1) % batch_count) for b in range(batch_count)]
     partner = lax.ppermute(own, "batch", pairs)
     summed = own.astype(jnp.float32) + partner.astype(jnp.float32)
     return summed[None]

time: 112 us -> 104 us (0.929)
  waiting for transfers between devices: 61.4 us -> 56.1 us
  local copies, waits for them, and re-layouts: 11.4 us -> 6.74 us
  Pallas kernels: 14.3 us -> 18.5 us
  other arithmetic: 15.6 us -> 12.9 us
    ppermute x1, waiting for transfers between devices: 20.5 us -> 11 us  [from_behind(): return lax.ppermute(block, axis, route)]
    gather x6 -> x0, local copies, waits for them, and re-layouts: 6.53 us -> none
    pallas_call x0 -> x1, Pallas kernels: none -> 4.18 us  [cut_patches(): pl.pallas_call(cut_kernel, grid_spec=grid_spec, out_shape=jax.ShapeDtypeS...]
    squeeze x1 -> x0, other arithmetic: 2.73 us -> none  [local(): extended = jnp.concatenate([object_field, rim], axis=2)[0]]
    ppermute x1, waiting for transfers between devices: 8.97 us -> 10.7 us  [local(): lax.ppermute(spill, 'tile', [(t, t + 1) for t in range(tile_count - 1)])]
    slice x0 -> x1, other arithmetic: none -> 1.52 us  [local(): local_columns = positions[:, 1]]
    select_n x1 -> x0, other arithmetic: 1.49 us -> none  [cut_patch(): return lax.dynamic_slice(extended, (anchor, row, column), (2, width, width))]
    ppermute x1, waiting for transfers between devices: 19.6 us -> 20.9 us  [local(): carry = lax.ppermute(carry, 'depth', [(turn + 1, turn)])]
  transfers between devices with their start and end apart: 5 -> 6, of which waited for: 5 -> 5; matrix products, arithmetic and copies ran while one was open for 6% -> 7% of each run, Pallas kernels for 0% -> 0%
where the time goes in v2:
time: 104 us; the launch traced here: 103 us
  waiting for transfers between devices  56.1 us (54%)
  Pallas kernels  18.5 us (18%)
  other arithmetic  12.9 us (12%)
  starting transfers between devices  8.41 us (8%)
  local copies, waits for them, and re-layouts  6.74 us (6%)
    ppermute x1, waiting for transfers between devices, local(): carry = lax.ppermute(carry, 'depth', [(turn + 1, turn)])  20.9 us
    ppermute x1, waiting for transfers between devices, local(): carry = lax.ppermute(carry, 'depth', [(turn - 1, turn)])  11.6 us
    ppermute x1, waiting for transfers between devices, from_behind(): return lax.ppermute(block, axis, route)  11 us
    ppermute x1, waiting for transfers between devices, local(): lax.ppermute(spill, 'tile', [(t, t + 1) for t in range(tile_count - 1)])  10.7 us
    pallas_call x2, Pallas kernels, run_waves(): pl.pallas_call(wave_kernel(transmit_first, residual_after, backward), gri...  8.9 us
    pallas_call x1, Pallas kernels, scatter_terms(): pl.pallas_call(scatter_kernel, grid_spec=grid_spec, out_shape=jax.ShapeDt...  5.4 us
    pallas_call x1, Pallas kernels, cut_patches(): pl.pallas_call(cut_kernel, grid_spec=grid_spec, out_shape=jax.ShapeDtypeS...  4.18 us
    ppermute x1, starting transfers between devices, local(): lax.ppermute(spill, 'tile', [(t, t + 1) for t in range(tile_count - 1)])  3.67 us
  transfers between devices with their start and end apart: 6, of which 5 were waited for; matrix products, arithmetic and copies ran while one was open for 7% of the time, Pallas kernels for 0%

profile of v2, /device:TPU:0, one launch (start us, length us, event | category | flops | bytes accessed | tf_op | source)
XLA Modules:
  0.0 103.3 jit_solution(547324250850739728)
XLA Ops:
  0.0 1.1 %constant_dynamic-slice_fusion = f32[1,2,256,256]{3,2,1,0:T(8,128)S(1)} fusion(f32[1,2,256,512]{3,2,1,0:T(8,128)} %tile_ref.1, s32[]{:T(128)S(6)} %select_n.85), kind=kLoop, calls=%fused_computation.46 | loop fusion | bytes 1048580 | tf_op jit(solution)/shard_map/dynamic_slice | solution.py:297
  1.1 1.3 %collective-permute-start = (f32[1,2,256,256]{3,2,1,0:T(8,128)S(1)}, f32[1,2,256,256]{3,2,1,0:T(8,128)S(1)}, u32[]{:S(2)}, u32[]{:S(2)}) collective-permute-start(f32[1,2,256,256]{3,2,1,0:T(8,128)S(1)} %constant_dynamic-slice_fusion), channel_id=1, source_target_pairs={{4,0},{8,4},{12,8},{5,1},{9,5},{13,9},{6,2},{10,6},{14,10},{7,3},{... | collective-permute-start | bytes 1572872 | tf_op jit(solution)/shard_map/ppermute | solution.py:18
  2.4 1.5 %slice_reduce_fusion = (s32[2]{0:T(128)}, s32[2]{0:T(128)}) fusion(s32[2,2]{1,0:T(2,128)} %param.19, s32[]{:T(128)S(6)} %mul.238), kind=kLoop, calls=%fused_computation.44 | loop fusion | flops 2 | bytes 36 | tf_op jit(solution)/shard_map/slice | solution.py:304
  3.9 1.0 multiply_convert_fusion.2
  4.9 1.0 multiply_convert_fusion
  5.9 1.0 fusion.14
  6.9 11.0 %collective-permute-done.mine_ref = f32[1,2,256,256]{3,2,1,0:T(8,128)S(1)} collective-permute-done((f32[1,2,256,256]{3,2,1,0:T(8,128)S(1)}, f32[1,2,256,256]{3,2,1,0:T(8,128)S(1)}, u32[]{:S(2)}, u32[]{:S(2)}) %collective-permute-start) | collective-permute-done | bytes 524320 | tf_op jit(solution)/shard_map/ppermute | solution.py:18
  17.9 1.0 fusion.11
  19.0 1.0 fusion.4
  20.8 4.2 %shard_map.61 = f32[2,2,256,256]{3,2,1,0:T(8,128)S(1)} custom-call(s32[2]{0:T(128)} %get-tuple-element.135.rows_ref, s32[2]{0:T(128)} %get-tuple-element.134.columns_ref, s32[1]{0:T(128)} %bitcast.1.order_ref, f32[1,2,256,512]{3,2,1,0:T(8,128)} %tile_ref.1, f32[1,2,256,256]{3,2,1,0:T(8,128)} %copy-done.1, f32[1,2,256,256]{3,2,1,0:T(8,128)} %copy-done.2), custom_call_target="tpu_custom_call" | custom-call | tf_op jit(solution)/shard_map/pallas_call | solution.py:279
  25.8 4.3 %conditional.4 = (bf16[2,2,256,256]{3,2,1,0:T(8,128)(2,1)}) conditional(s32[]{:T(128)} %convert_element_type.115, () %tuple.40, (bf16[2,2,256,256]{3,2,1,0:T(8,128)(2,1)}, f32[2,2,256,256]{3,2,1,0:T(8,128)S(1)}, f32[2,256,256]{2,1,0:T(8,128)S(1)}, bf16[512,512]{1,0:T(8,128)(2,1)S(1)}, bf16[512,512]{1,0:T(8,128)(2,1)}, ...), branch_computations={%region_0.1_spmd, %region_1.2_spmd} | conditional | bytes 524298 | solution.py:335
  25.8 4.3 %branch_1_fun.4 = bf16[2,2,256,256]{3,2,1,0:T(8,128)(2,1)} custom-call(bf16[2,2,256,256]{3,2,1,0:T(8,128)(2,1)} %get-tuple-element.96.refs_0_, f32[2,2,256,256]{3,2,1,0:T(8,128)S(1)} %get-tuple-element.97.refs_1_, f32[2,256,256]{2,1,0:T(8,128)S(1)} %get-tuple-element.98.refs_2_, bf16[512,512]{1,0:T(8,128)(2,1)S(1)} %get-tuple-element.99.refs_3_, ...), custom_call_target="tpu_custom_call" | custom-call | tf_op jit(solution)/shard_map/cond/branch_1_fun/pallas_call | solution.py:197
  30.1 2.1 %collective-permute-start.2 = (bf16[2,2,256,256]{3,2,1,0:T(8,128)(2,1)}, bf16[2,2,256,256]{3,2,1,0:T(8,128)(2,1)}, u32[]{:S(2)}, u32[]{:S(2)}) collective-permute-start(bf16[2,2,256,256]{3,2,1,0:T(8,128)(2,1)} %get-tuple-element.152), channel_id=1, source_target_pairs={{0,2},{1,3},{4,6},{5,7},{8,10},{9,11},{12,14},{13,15},{16,18},{17,... | collective-permute-start | bytes 1572872 | tf_op jit(solution)/shard_map/ppermute | solution.py:332
  32.2 11.6 %collective-permute-done.2 = bf16[2,2,256,256]{3,2,1,0:T(8,128)(2,1)} collective-permute-done((bf16[2,2,256,256]{3,2,1,0:T(8,128)(2,1)}, bf16[2,2,256,256]{3,2,1,0:T(8,128)(2,1)}, u32[]{:S(2)}, u32[]{:S(2)}) %collective-permute-start.2) | collective-permute-done | bytes 524320 | tf_op jit(solution)/shard_map/ppermute | solution.py:332
  43.8 0.8 conditional.5
  43.8 0.8 broadcast.209
  44.7 0.9 broadcast_select_fusion
  45.5 1.9 %conditional.6 = ((bf16[2,2,256,256]{3,2,1,0:T(8,128)(2,1)}, f32[2,2,256,256]{3,2,1,0:T(8,128)})) conditional(s32[]{:T(128)} %convert_element_type.116, () %tuple.38, (bf16[2,2,256,256]{3,2,1,0:T(8,128)(2,1)}, f32[2,2,256,256]{3,2,1,0:T(8,128)S(1)}, f32[2,256,256]{2,1,0:T(8,128)S(1)}, bf16[512,512]{1,0:T(8,128)(2,1)S(1)}, bf16[512,512]{1,0:T(8,128)(2,1)}, ...), branch_computations={%region_4.5_spmd, %region_5.6_spmd} | conditional | bytes 1572894 | solution.py:349
  45.5 1.1 %broadcast.211 = f32[2,2,256,256]{3,2,1,0:T(8,128)} broadcast(f32[]{:T(128)} %constant.94.clone), dimensions={} | broadcast | bytes 1048580 | tf_op jit(solution)/shard_map/broadcast.15
  46.6 0.8 broadcast.210
  47.5 1.3 %collective-permute-start.3 = (bf16[2,2,256,256]{3,2,1,0:T(8,128)(2,1)}, bf16[2,2,256,256]{3,2,1,0:T(8,128)(2,1)}, u32[]{:S(2)}, u32[]{:S(2)}) collective-permute-start(bf16[2,2,256,256]{3,2,1,0:T(8,128)(2,1)} %get-tuple-element.130), channel_id=1, source_target_pairs={{2,0},{3,1},{6,4},{7,5},{10,8},{11,9},{14,12},{15,13},{18,16},{19,... | collective-permute-start | bytes 1572872 | tf_op jit(solution)/shard_map/ppermute | solution.py:348
  50.0 20.9 %collective-permute-done.3 = bf16[2,2,256,256]{3,2,1,0:T(8,128)(2,1)} collective-permute-done((bf16[2,2,256,256]{3,2,1,0:T(8,128)(2,1)}, bf16[2,2,256,256]{3,2,1,0:T(8,128)(2,1)}, u32[]{:S(2)}, u32[]{:S(2)}) %collective-permute-start.3) | collective-permute-done | bytes 524320 | tf_op jit(solution)/shard_map/ppermute | solution.py:348
  70.8 4.6 %conditional.7 = (f32[2,2,256,256]{3,2,1,0:T(8,128)}) conditional(s32[]{:T(128)} %convert_element_type.115, () %tuple.37, (bf16[2,2,256,256]{3,2,1,0:T(8,128)(2,1)}, f32[2,2,256,256]{3,2,1,0:T(8,128)S(1)}, f32[2,256,256]{2,1,0:T(8,128)S(1)}, bf16[512,512]{1,0:T(8,128)(2,1)S(1)}, bf16[512,512]{1,0:T(8,128)(2,1)}, ...), branch_computations={%region_6.7_spmd, %region_7.8_spmd} | conditional | bytes 1048588 | solution.py:349
  70.8 4.6 %branch_1_fun.7 = (bf16[2,2,256,256]{3,2,1,0:T(8,128)(2,1)}, f32[2,2,256,256]{3,2,1,0:T(8,128)}) custom-call(bf16[2,2,256,256]{3,2,1,0:T(8,128)(2,1)} %get-tuple-element.119.refs_0_, f32[2,2,256,256]{3,2,1,0:T(8,128)S(1)} %get-tuple-element.120.refs_1_, f32[2,256,256]{2,1,0:T(8,128)S(1)} %get-tuple-element.121.refs_2_, ...), custom_call_target="tpu_custom_call" | custom-call | tf_op jit(solution)/shard_map/cond/branch_1_fun/pallas_call | solution.py:197
  75.4 2.3 %select_select_fusion.terms_ref = f32[2,2,256,256]{3,2,1,0:T(8,128)} fusion(f32[2,2,256,256]{3,2,1,0:T(8,128)} %get-tuple-element.155, f32[2,2,256,256]{3,2,1,0:T(8,128)} %get-tuple-element.131, pred[]{:T(512)S(6)} %eq.20, pred[]{:T(512)S(6)} %eq.11), kind=kLoop, calls=%fused_computation.4 | loop fusion | flops 524288 | bytes 3145730 | tf_op jit(solution)/shard_map/jit(_where)/select_n | solution.py:350
  77.8 5.4 %shard_map.62 = f32[2,512,512]{2,1,0:T(8,128)} custom-call(s32[2]{0:T(128)} %get-tuple-element.135.rows_ref, s32[2]{0:T(128)} %get-tuple-element.134.columns_ref, s32[2]{0:T(128)} %compare_convert_fusion.live_ref, f32[2,2,256,256]{3,2,1,0:T(8,128)} %select_select_fusion.terms_ref), custom_call_target="tpu_custom_call" | custom-call | tf_op jit(solution)/shard_map/pallas_call | solution.py:240
  83.2 1.3 %slice.44 = bf16[2,256,512]{2,1,0:T(8,128)(2,1)S(1)} slice(f32[2,512,512]{2,1,0:T(8,128)} %shard_map.62), slice={[0:2], [256:512], [0:512]} | slice | bytes 1048576 | tf_op jit(solution)/shard_map/slice | solution.py:355
  84.5 3.7 %collective-permute-start.4 = (bf16[2,256,512]{2,1,0:T(8,128)(2,1)S(1)}, bf16[2,256,512]{2,1,0:T(8,128)(2,1)S(1)}, u32[]{:S(2)}, u32[]{:S(2)}) collective-permute-start(bf16[2,256,512]{2,1,0:T(8,128)(2,1)S(1)} %slice.44), channel_id=1, source_target_pairs={{0,4},{4,8},{8,12},{1,5},{5,9},{9,13},{2,6},{6,10},{10,14},{3,7},{... | collective-permute-start | bytes 1572872 | tf_op jit(solution)/shard_map/ppermute | solution.py:356
  88.2 10.7 %collective-permute-done.4 = bf16[2,256,512]{2,1,0:T(8,128)(2,1)S(1)} collective-permute-done((bf16[2,256,512]{2,1,0:T(8,128)(2,1)S(1)}, bf16[2,256,512]{2,1,0:T(8,128)(2,1)S(1)}, u32[]{:S(2)}, u32[]{:S(2)}) %collective-permute-start.4) | collective-permute-done | bytes 524320 | tf_op jit(solution)/shard_map/ppermute | solution.py:356
  98.8 1.4 %fusion = bf16[2,256,512]{2,1,0:T(8,128)(2,1)S(1)} fusion(f32[2,512,512]{2,1,0:T(8,128)} %shard_map.62, bf16[2,256,512]{2,1,0:T(8,128)(2,1)S(1)} %collective-permute-done.4), kind=kLoop, calls=%fused_computation.2 | loop fusion | flops 786432 | bytes 2097152 | tf_op jit(solution)/shard_map/convert_element_type | solution.py:358
  100.3 1.9 %collective-permute-done.5 = bf16[2,256,512]{2,1,0:T(8,128)(2,1)S(1)} collective-permute-done((bf16[2,256,512]{2,1,0:T(8,128)(2,1)S(1)}, bf16[2,256,512]{2,1,0:T(8,128)(2,1)S(1)}, u32[]{:S(2)}, u32[]{:S(2)}) %collective-permute-start.5) | collective-permute-done | bytes 524320 | tf_op jit(solution)/shard_map/ppermute | solution.py:359
  102.2 1.1 %add_bitcast_fusion = f32[1,2,256,512]{3,2,1,0:T(8,128)} fusion(bf16[2,256,512]{2,1,0:T(8,128)(2,1)S(1)} %collective-permute-done.5, bf16[2,256,512]{2,1,0:T(8,128)(2,1)S(1)} %fusion), kind=kLoop, calls=%fused_computation.3 | loop fusion | flops 786432 | bytes 2097152 | tf_op jit(solution)/shard_map/broadcast_in_dim | solution.py:361
  (13 shorter events, 2.3 us)
Async XLA Ops:
  1.1 16.8 %collective-permute-start = (f32[1,2,256,256]{3,2,1,0:T(8,128)S(1)}, f32[1,2,256,256]{3,2,1,0:T(8,128)S(1)}, u32[]{:S(2)}, u32[]{:S(2)}) collective-permute-start(f32[1,2,256,256]{3,2,1,0:T(8,128)S(1)} %constant_dynamic-slice_fusion), channel_id=1, source_target_pairs={{4,0},{8,4},{12,8},{5,1},{9,5},{13,9},{6,2},{10,6},{14,10},{7,3},{... | collective-permute-start | bytes 1572872 | tf_op jit(solution)/shard_map/ppermute | solution.py:18
  17.9 2.1 %copy-start.1 = (f32[1,2,256,256]{3,2,1,0:T(8,128)}, f32[1,2,256,256]{3,2,1,0:T(8,128)S(1)}, u32[]{:S(2)}) copy-start(f32[1,2,256,256]{3,2,1,0:T(8,128)S(1)} %collective-permute-done.mine_ref) | copy-start | bytes 1572868
  17.9 2.1 %collective-permute-start.1 = (f32[1,2,256,256]{3,2,1,0:T(8,128)S(1)}, f32[1,2,256,256]{3,2,1,0:T(8,128)S(1)}, u32[]{:S(2)}, u32[]{:S(2)}) collective-permute-start(f32[1,2,256,256]{3,2,1,0:T(8,128)S(1)} %collective-permute-done.mine_ref), channel_id=1, source_target_pairs={{0,1},{1,0},{2,3},{3,2},{4,5},{5,4},{6,7},{7,6},{8,9},{9,8},{10,11... | collective-permute-start | bytes 1572872 | tf_op jit(solution)/shard_map/ppermute | solution.py:300
  20.0 5.0 %copy-start = (bf16[2,256,256]{2,1,0:T(8,128)(2,1)S(1)}, bf16[2,256,256]{2,1,0:T(8,128)(2,1)}, u32[]{:S(2)}) copy-start(bf16[2,256,256]{2,1,0:T(8,128)(2,1)} %param.18) | copy-start | bytes 786436
  20.0 0.8 copy-start.2
  30.1 13.7 %collective-permute-start.2 = (bf16[2,2,256,256]{3,2,1,0:T(8,128)(2,1)}, bf16[2,2,256,256]{3,2,1,0:T(8,128)(2,1)}, u32[]{:S(2)}, u32[]{:S(2)}) collective-permute-start(bf16[2,2,256,256]{3,2,1,0:T(8,128)(2,1)} %get-tuple-element.152), channel_id=1, source_target_pairs={{0,2},{1,3},{4,6},{5,7},{8,10},{9,11},{12,14},{13,15},{16,18},{17,... | collective-permute-start | bytes 1572872 | tf_op jit(solution)/shard_map/ppermute | solution.py:332
  47.5 23.4 %collective-permute-start.3 = (bf16[2,2,256,256]{3,2,1,0:T(8,128)(2,1)}, bf16[2,2,256,256]{3,2,1,0:T(8,128)(2,1)}, u32[]{:S(2)}, u32[]{:S(2)}) collective-permute-start(bf16[2,2,256,256]{3,2,1,0:T(8,128)(2,1)} %get-tuple-element.130), channel_id=1, source_target_pairs={{2,0},{3,1},{6,4},{7,5},{10,8},{11,9},{14,12},{15,13},{18,16},{19,... | collective-permute-start | bytes 1572872 | tf_op jit(solution)/shard_map/ppermute | solution.py:348
  84.5 14.4 %collective-permute-start.4 = (bf16[2,256,512]{2,1,0:T(8,128)(2,1)S(1)}, bf16[2,256,512]{2,1,0:T(8,128)(2,1)S(1)}, u32[]{:S(2)}, u32[]{:S(2)}) collective-permute-start(bf16[2,256,512]{2,1,0:T(8,128)(2,1)S(1)} %slice.44), channel_id=1, source_target_pairs={{0,4},{4,8},{8,12},{1,5},{5,9},{9,13},{2,6},{6,10},{10,14},{3,7},{... | collective-permute-start | bytes 1572872 | tf_op jit(solution)/shard_map/ppermute | solution.py:356
  100.2 2.0 %collective-permute-start.5 = (bf16[2,256,512]{2,1,0:T(8,128)(2,1)S(1)}, bf16[2,256,512]{2,1,0:T(8,128)(2,1)S(1)}, u32[]{:S(2)}, u32[]{:S(2)}) collective-permute-start(bf16[2,256,512]{2,1,0:T(8,128)(2,1)S(1)} %fusion), channel_id=1, source_target_pairs={{0,1},{1,0},{2,3},{3,2},{4,5},{5,4},{6,7},{7,6},{8,9},{9,8},{10,11... | collective-permute-start | bytes 1572872 | tf_op jit(solution)/shard_map/ppermute | solution.py:359

commit v3 on v2

--- a/solution.py
+++ b/solution.py
@@ -299,9 +299,33 @@
     pairs = [(b, (b + 1) % batch_count) for b in range(batch_count)]
     partner = lax.ppermute(mine, "batch", pairs)
     capacity = positions.shape[0]
-    live = jnp.arange(capacity, dtype=jnp.int32) < counts[0]
-    local_rows = positions[:, 0] - tile_index * tile_rows
-    local_columns = positions[:, 1]
+    share = -(-capacity // batch_count)
+    first_core = batch_index == 0
+    both_positions = lax.ppermute(positions, "batch", pairs)
+    both_counts = lax.ppermute(counts, "batch", pairs)
+    both_measured = lax.ppermute(measured, "batch", pairs)
+    all_positions = jnp.where(
+        first_core,
+        jnp.concatenate([positions, both_positions]),
+        jnp.concatenate([both_positions, positions]),
+    )
+    all_counts = jnp.where(
+        first_core, jnp.concatenate([counts, both_counts]), jnp.concatenate([both_counts, counts])
+    )
+    all_measured = jnp.where(
+        first_core,
+        jnp.concatenate([measured, both_measured]),
+        jnp.concatenate([both_measured, measured]),
+    )
+    entry = batch_index * share + jnp.arange(share, dtype=jnp.int32)
+    live = entry < all_counts[0] + all_counts[1]
+    later = entry >= all_counts[0]
+    slot = jnp.clip(jnp.where(later, entry - all_counts[0], entry), 0, capacity - 1)
+    flat = jnp.where(later, capacity, 0) + slot
+    chosen = all_positions[flat]
+    measured = all_measured[flat]
+    local_rows = chosen[:, 0] - tile_index * tile_rows
+    local_columns = chosen[:, 1]
     order = jnp.reshape(batch_index, (1,)).astype(jnp.int32)
     patches = cut_patches(object_field, mine, partner, local_rows, local_columns, order, width)
     number = patches.shape[0]

time: 104 us -> 87.8 us (0.84)
  waiting for transfers between devices: 56.1 us -> 38.1 us
  Pallas kernels: 18.5 us -> 12.2 us
  other arithmetic: 12.9 us -> 16.1 us
  between operations: 0.76 us -> 3.89 us
  starting transfers between devices: 8.41 us -> 9.46 us
    ppermute x1, waiting for transfers between devices: 11.6 us -> 3.48 us  [local(): carry = lax.ppermute(carry, 'depth', [(turn - 1, turn)])]
    ppermute x1, waiting for transfers between devices: 20.9 us -> 14 us  [local(): carry = lax.ppermute(carry, 'depth', [(turn + 1, turn)])]
    pallas_call x2, Pallas kernels: 8.9 us -> 5.04 us  [run_waves(): pl.pallas_call(wave_kernel(transmit_first, residual_after, backward), gri...]
    concatenate x0 -> x1, other arithmetic: none -> 3.02 us  [local(): jnp.concatenate([both_measured, measured])]
    ppermute x1, waiting for transfers between devices: 11 us -> 8.26 us  [from_behind(): return lax.ppermute(block, axis, route)]
    slice x1 -> x0, other arithmetic: 1.52 us -> none  [local(): local_columns = positions[:, 1]]
    pallas_call x1, Pallas kernels: 5.4 us -> 4 us  [scatter_terms(): pl.pallas_call(scatter_kernel, grid_spec=grid_spec, out_shape=jax.ShapeDt...]
    unnamed x6 -> x10, local copies, waits for them, and re-layouts: 0.81 us -> 2.19 us
  transfers between devices with their start and end apart: 6 -> 9, of which waited for: 5 -> 5; matrix products, arithmetic and copies ran while one was open for 7% -> 15% of each run, Pallas kernels for 0% -> 6%
where the time goes in v3:
time: 87.8 us; the launch traced here: 87.1 us
  waiting for transfers between devices  38.1 us (43%)
  other arithmetic  16.1 us (18%)
  Pallas kernels  12.2 us (14%)
  starting transfers between devices  9.46 us (11%)
  local copies, waits for them, and re-layouts  7.4 us (8%)
  between operations  3.89 us (4%)
    ppermute x1, waiting for transfers between devices, local(): carry = lax.ppermute(carry, 'depth', [(turn + 1, turn)])  14 us
    ppermute x1, waiting for transfers between devices, local(): lax.ppermute(spill, 'tile', [(t, t + 1) for t in range(tile_count - 1)])  10.5 us
    ppermute x1, waiting for transfers between devices, from_behind(): return lax.ppermute(block, axis, route)  8.26 us
    pallas_call x2, Pallas kernels, run_waves(): pl.pallas_call(wave_kernel(transmit_first, residual_after, backward), gri...  5.04 us
    pallas_call x1, Pallas kernels, scatter_terms(): pl.pallas_call(scatter_kernel, grid_spec=grid_spec, out_shape=jax.ShapeDt...  4 us
    ppermute x1, starting transfers between devices, local(): lax.ppermute(spill, 'tile', [(t, t + 1) for t in range(tile_count - 1)])  3.51 us
    ppermute x1, waiting for transfers between devices, local(): carry = lax.ppermute(carry, 'depth', [(turn - 1, turn)])  3.48 us
    pallas_call x1, Pallas kernels, cut_patches(): pl.pallas_call(cut_kernel, grid_spec=grid_spec, out_shape=jax.ShapeDtypeS...  3.13 us
  transfers between devices with their start and end apart: 9, of which 5 were waited for; matrix products, arithmetic and copies ran while one was open for 15% of the time, Pallas kernels for 6%

profile of v3, /device:TPU:0, one launch (start us, length us, event | category | flops | bytes accessed | tf_op | source)
XLA Modules:
  0.0 87.1 jit_solution(3240657902633121047)
XLA Ops:
  1.0 1.1 %constant_dynamic-slice_fusion.1 = f32[1,2,256,256]{3,2,1,0:T(8,128)S(1)} fusion(f32[1,2,256,512]{3,2,1,0:T(8,128)} %tile_ref.1, s32[]{:T(128)S(6)} %select_n.130), kind=kLoop, calls=%fused_computation.49 | loop fusion | bytes 1048580 | tf_op jit(solution)/shard_map/dynamic_slice | solution.py:297
  2.0 1.3 %collective-permute-start.3 = (f32[1,2,256,256]{3,2,1,0:T(8,128)S(1)}, f32[1,2,256,256]{3,2,1,0:T(8,128)}, u32[]{:S(2)}, u32[]{:S(2)}) collective-permute-start(f32[1,2,256,256]{3,2,1,0:T(8,128)S(1)} %constant_dynamic-slice_fusion.1), channel_id=1, source_target_pairs={{4,0},{8,4},{12,8},{5,1},{9,5},{13,9},{6,2},{10,6},{14,10},{7,3},{... | collective-permute-start | bytes 1572872 | tf_op jit(solution)/shard_map/ppermute | solution.py:18
  4.0 1.0 %multiply_convert_fusion.2 = bf16[256,256]{1,0:T(8,128)(2,1)S(1)} fusion(), kind=kLoop, calls=%fused_computation.29 | loop fusion | flops 1048576 | bytes 131072 | tf_op jit(solution)/shard_map/convert_element_type | solution.py:26
  5.0 1.7 %fusion.14 = (bf16[256,256]{1,0:T(8,128)(2,1)}, bf16[256,256]{1,0:T(8,128)(2,1)}) fusion(), kind=kLoop, calls=%fused_computation.38 | loop fusion | flops 1572864 | bytes 262144 | tf_op jit(solution)/shard_map/neg | solution.py:28
  6.7 1.7 %multiply_convert_fusion = (bf16[256,256]{1,0:T(8,128)(2,1)}, bf16[256,256]{1,0:T(8,128)(2,1)}) fusion(), kind=kLoop, calls=%fused_computation.27 | loop fusion | flops 1179648 | bytes 262144 | tf_op jit(solution)/shard_map/convert_element_type | solution.py:27
  8.4 1.0 %fusion.11 = (f32[1,256,256]{2,1,0:T(8,128)S(1)}, f32[1,256,256]{2,1,0:T(8,128)S(1)}) fusion(s32[256]{0:T(256)S(1)} %fusion.17, f32[]{:T(128)S(6)} %neg.15), kind=kLoop, calls=%fused_computation.34 | loop fusion | flops 196608 | bytes 525316 | tf_op jit(solution)/shard_map/cos | solution.py:51
  9.5 1.5 %fusion.4 = (bf16[512,512]{1,0:T(8,128)(2,1)S(1)}, bf16[512,512]{1,0:T(8,128)(2,1)S(1)}, bf16[512,512]{1,0:T(8,128)(2,1)S(1)}, bf16[512,512]{1,0:T(8,128)(2,1)S(1)}) fusion(bf16[256,256]{1,0:T(8,128)(2,1)S(1)} %multiply_convert_fusion.2, bf16[256,256]{1,0:T(8,128)(2,1)} %get-tuple-element.184, bf16[256,256]{1,0:T(8,128)(2,1)} %get-tuple-element.181, ...), kind=kLoop, calls=%fused_computation.18 | loop fusion | flops 6815744 | bytes 2752512 | tf_op jit(solution)/shard_map/concatenate | solution.py:42
  11.0 8.3 %collective-permute-done.3.mine_ref = f32[1,2,256,256]{3,2,1,0:T(8,128)} collective-permute-done((f32[1,2,256,256]{3,2,1,0:T(8,128)S(1)}, f32[1,2,256,256]{3,2,1,0:T(8,128)}, u32[]{:S(2)}, u32[]{:S(2)}) %collective-permute-start.3) | collective-permute-done | bytes 524320 | tf_op jit(solution)/shard_map/ppermute | solution.py:18
  19.2 0.8 broadcast_select_fusion.1
  23.1 0.8 copy-done.4
  23.9 3.1 %shard_map.60 = f32[1,2,256,256]{3,2,1,0:T(8,128)S(1)} custom-call(s32[1]{0:T(128)S(6)} %sub.14.rows_ref, s32[1]{0:T(128)} %bitcast.7.columns_ref, s32[1]{0:T(128)} %bitcast.3.order_ref, f32[1,2,256,512]{3,2,1,0:T(8,128)} %tile_ref.1, f32[1,2,256,256]{3,2,1,0:T(8,128)} %collective-permute-done.3.mine_ref, f32[1,2,256,256]{3,2,1,0:T(8,128)} %copy-done.4), custom_call_target="tpu_custom_call" | custom-call | tf_op jit(solution)/shard_map/pallas_call | solution.py:279
  27.0 2.0 %conditional.4 = (bf16[1,2,256,256]{3,2,1,0:T(8,128)(2,1)}) conditional(s32[]{:T(128)} %convert_element_type.115, () %tuple.40, (bf16[1,2,256,256]{3,2,1,0:T(8,128)(2,1)S(1)}, f32[1,2,256,256]{3,2,1,0:T(8,128)S(1)}, f32[2,256,256]{2,1,0:T(8,128)S(1)}, bf16[512,512]{1,0:T(8,128)(2,1)S(1)}, bf16[512,512]{1,0:T(8,128)(2,1)S(1)}, ...), branch_computations={%region_0.1_spmd, %region_1.2_spmd} | conditional | bytes 262154 | solution.py:359
  27.1 2.0 %branch_1_fun.4 = bf16[1,2,256,256]{3,2,1,0:T(8,128)(2,1)} custom-call(bf16[1,2,256,256]{3,2,1,0:T(8,128)(2,1)S(1)} %get-tuple-element.105.refs_0_, f32[1,2,256,256]{3,2,1,0:T(8,128)S(1)} %get-tuple-element.106.refs_1_, f32[2,256,256]{2,1,0:T(8,128)S(1)} %get-tuple-element.107.refs_2_, bf16[512,512]{1,0:T(8,128)(2,1)S(1)} %get-tuple-element.108.refs_3_, ...), custom_call_target="tpu_custom_call" | custom-call | tf_op jit(solution)/shard_map/cond/branch_1_fun/pallas_call | solution.py:197
  29.0 2.3 %collective-permute-start.5 = (bf16[1,2,256,256]{3,2,1,0:T(8,128)(2,1)}, bf16[1,2,256,256]{3,2,1,0:T(8,128)(2,1)S(1)}, u32[]{:S(2)}, u32[]{:S(2)}) collective-permute-start(bf16[1,2,256,256]{3,2,1,0:T(8,128)(2,1)} %get-tuple-element.189), channel_id=1, source_target_pairs={{0,2},{1,3},{4,6},{5,7},{8,10},{9,11},{12,14},{13,15},{16,18},{17,... | collective-permute-start | bytes 786440 | tf_op jit(solution)/shard_map/ppermute | solution.py:356
  31.4 3.0 %pad_maximum_fusion.1 = (f32[4,256,256]{2,1,0:T(8,128)}, f32[4,256,256]{2,1,0:T(8,128)}) fusion(f32[2,256,256]{2,1,0:T(8,128)} %param.21, f32[2,256,256]{2,1,0:T(8,128)} %collective-permute-done.2), kind=kLoop, calls=%fused_computation.5 | loop fusion | flops 524288 | bytes 3145728 | tf_op jit(solution)/shard_map/concatenate | solution.py:318
  34.4 3.5 %collective-permute-done.5 = bf16[1,2,256,256]{3,2,1,0:T(8,128)(2,1)S(1)} collective-permute-done((bf16[1,2,256,256]{3,2,1,0:T(8,128)(2,1)}, bf16[1,2,256,256]{3,2,1,0:T(8,128)(2,1)S(1)}, u32[]{:S(2)}, u32[]{:S(2)}) %collective-permute-start.5) | collective-permute-done | bytes 262176 | tf_op jit(solution)/shard_map/ppermute | solution.py:356
  39.3 1.0 %broadcast_select_fusion = bf16[1,2,256,256]{3,2,1,0:T(8,128)(2,1)S(1)} fusion(bf16[1,2,256,256]{3,2,1,0:T(8,128)(2,1)} %copy-done.2, pred[]{:T(512)S(6)} %eq.24, bf16[2,256,256]{2,1,0:T(8,128)(2,1)} %param.18), kind=kLoop, calls=%fused_computation.36 | loop fusion | flops 131072 | bytes 786433 | tf_op jit(solution)/shard_map/jit(_where)/select_n | solution.py:357
  40.3 1.6 %conditional.6 = ((bf16[1,2,256,256]{3,2,1,0:T(8,128)(2,1)}, f32[1,2,256,256]{3,2,1,0:T(8,128)})) conditional(s32[]{:T(128)} %convert_element_type.116, () %tuple.38, (bf16[1,2,256,256]{3,2,1,0:T(8,128)(2,1)}, f32[1,2,256,256]{3,2,1,0:T(8,128)S(1)}, f32[2,256,256]{2,1,0:T(8,128)S(1)}, bf16[512,512]{1,0:T(8,128)(2,1)S(1)}, ...), branch_computations={%region_4.5_spmd, %region_5.6_spmd} | conditional | bytes 786462 | solution.py:373
  40.3 0.7 broadcast.207
  41.1 0.8 broadcast.208
  41.9 1.3 %collective-permute-start.6 = (bf16[1,2,256,256]{3,2,1,0:T(8,128)(2,1)}, bf16[1,2,256,256]{3,2,1,0:T(8,128)(2,1)}, u32[]{:S(2)}, u32[]{:S(2)}) collective-permute-start(bf16[1,2,256,256]{3,2,1,0:T(8,128)(2,1)} %get-tuple-element.142), channel_id=1, source_target_pairs={{2,0},{3,1},{6,4},{7,5},{10,8},{11,9},{14,12},{15,13},{18,16},{19,... | collective-permute-start | bytes 786440 | tf_op jit(solution)/shard_map/ppermute | solution.py:372
  44.4 14.0 %collective-permute-done.6 = bf16[1,2,256,256]{3,2,1,0:T(8,128)(2,1)} collective-permute-done((bf16[1,2,256,256]{3,2,1,0:T(8,128)(2,1)}, bf16[1,2,256,256]{3,2,1,0:T(8,128)(2,1)}, u32[]{:S(2)}, u32[]{:S(2)}) %collective-permute-start.6) | collective-permute-done | bytes 262176 | tf_op jit(solution)/shard_map/ppermute | solution.py:372
  58.4 3.1 %conditional.7 = (f32[1,2,256,256]{3,2,1,0:T(8,128)}) conditional(s32[]{:T(128)} %convert_element_type.115, () %tuple.37, (bf16[1,2,256,256]{3,2,1,0:T(8,128)(2,1)}, f32[1,2,256,256]{3,2,1,0:T(8,128)S(1)}, f32[2,256,256]{2,1,0:T(8,128)S(1)}, bf16[512,512]{1,0:T(8,128)(2,1)S(1)}, bf16[512,512]{1,0:T(8,128)(2,1)S(1)}, ...), branch_computations={%region_6.7_spmd, %region_7.8_spmd} | conditional | bytes 524300 | solution.py:373
  58.4 3.1 %branch_1_fun.7 = (bf16[1,2,256,256]{3,2,1,0:T(8,128)(2,1)}, f32[1,2,256,256]{3,2,1,0:T(8,128)}) custom-call(bf16[1,2,256,256]{3,2,1,0:T(8,128)(2,1)} %get-tuple-element.131.refs_0_, f32[1,2,256,256]{3,2,1,0:T(8,128)S(1)} %get-tuple-element.132.refs_1_, f32[2,256,256]{2,1,0:T(8,128)S(1)} %get-tuple-element.133.refs_2_, ...), custom_call_target="tpu_custom_call" | custom-call | tf_op jit(solution)/shard_map/cond/branch_1_fun/pallas_call | solution.py:197
  61.5 1.9 %select_select_fusion.terms_ref = f32[1,2,256,256]{3,2,1,0:T(8,128)} fusion(f32[1,2,256,256]{3,2,1,0:T(8,128)} %get-tuple-element.192, f32[1,2,256,256]{3,2,1,0:T(8,128)} %get-tuple-element.143, pred[]{:T(512)S(6)} %eq.24, pred[]{:T(512)S(6)} %eq.23), kind=kLoop, calls=%fused_computation.20 | loop fusion | flops 262144 | bytes 1572866 | tf_op jit(solution)/shard_map/jit(_where)/select_n | solution.py:374
  63.4 4.0 %shard_map.61 = f32[2,512,512]{2,1,0:T(8,128)} custom-call(s32[1]{0:T(128)S(6)} %sub.14.rows_ref, s32[1]{0:T(128)} %bitcast.7.columns_ref, s32[1]{0:T(128)S(6)} %convert_element_type.114.live_ref, f32[1,2,256,256]{3,2,1,0:T(8,128)} %select_select_fusion.terms_ref), custom_call_target="tpu_custom_call" | custom-call | tf_op jit(solution)/shard_map/pallas_call | solution.py:240
  67.4 1.3 %slice.68 = bf16[2,256,512]{2,1,0:T(8,128)(2,1)S(1)} slice(f32[2,512,512]{2,1,0:T(8,128)} %shard_map.61), slice={[0:2], [256:512], [0:512]} | slice | bytes 1048576 | tf_op jit(solution)/shard_map/slice | solution.py:379
  68.7 3.5 %collective-permute-start.7 = (bf16[2,256,512]{2,1,0:T(8,128)(2,1)S(1)}, bf16[2,256,512]{2,1,0:T(8,128)(2,1)S(1)}, u32[]{:S(2)}, u32[]{:S(2)}) collective-permute-start(bf16[2,256,512]{2,1,0:T(8,128)(2,1)S(1)} %slice.68), channel_id=1, source_target_pairs={{0,4},{4,8},{8,12},{1,5},{5,9},{9,13},{2,6},{6,10},{10,14},{3,7},{... | collective-permute-start | bytes 1572872 | tf_op jit(solution)/shard_map/ppermute | solution.py:380
  72.2 10.5 %collective-permute-done.7 = bf16[2,256,512]{2,1,0:T(8,128)(2,1)S(1)} collective-permute-done((bf16[2,256,512]{2,1,0:T(8,128)(2,1)S(1)}, bf16[2,256,512]{2,1,0:T(8,128)(2,1)S(1)}, u32[]{:S(2)}, u32[]{:S(2)}) %collective-permute-start.7) | collective-permute-done | bytes 524320 | tf_op jit(solution)/shard_map/ppermute | solution.py:380
  82.7 1.4 %fusion = bf16[2,256,512]{2,1,0:T(8,128)(2,1)S(1)} fusion(f32[2,512,512]{2,1,0:T(8,128)} %shard_map.61, bf16[2,256,512]{2,1,0:T(8,128)(2,1)S(1)} %collective-permute-done.7), kind=kLoop, calls=%fused_computation.3 | loop fusion | flops 786432 | bytes 2097152 | tf_op jit(solution)/shard_map/convert_element_type | solution.py:382
  84.1 1.9 %collective-permute-done.8 = bf16[2,256,512]{2,1,0:T(8,128)(2,1)S(1)} collective-permute-done((bf16[2,256,512]{2,1,0:T(8,128)(2,1)S(1)}, bf16[2,256,512]{2,1,0:T(8,128)(2,1)S(1)}, u32[]{:S(2)}, u32[]{:S(2)}) %collective-permute-start.8) | collective-permute-done | bytes 524320 | tf_op jit(solution)/shard_map/ppermute | solution.py:383
  86.0 1.1 %add_bitcast_fusion = f32[1,2,256,512]{3,2,1,0:T(8,128)} fusion(bf16[2,256,512]{2,1,0:T(8,128)(2,1)S(1)} %collective-permute-done.8, bf16[2,256,512]{2,1,0:T(8,128)(2,1)S(1)} %fusion), kind=kLoop, calls=%fused_computation.6 | loop fusion | flops 786432 | bytes 2097152 | tf_op jit(solution)/shard_map/broadcast_in_dim | solution.py:385
  (26 shorter events, 3.8 us)
Async XLA Ops:
  0.0 21.8 %collective-permute-start = (s32[2,2]{1,0:T(2,128)}, s32[2,2]{1,0:T(2,128)S(1)}, u32[]{:S(2)}, u32[]{:S(2)}) collective-permute-start(s32[2,2]{1,0:T(2,128)} %param.19), channel_id=1, source_target_pairs={{0,1},{1,0},{2,3},{3,2},{4,5},{5,4},{6,7},{7,6},{8,9},{9,8},{10,11... | collective-permute-start | bytes 56 | tf_op jit(solution)/shard_map/ppermute | solution.py:304
  0.5 18.8 %collective-permute-start.1 = (s32[1]{0:T(128)}, s32[1]{0:T(128)}, u32[]{:S(2)}, u32[]{:S(2)}) collective-permute-start(s32[1]{0:T(128)} %param.20), channel_id=1, source_target_pairs={{0,1},{1,0},{2,3},{3,2},{4,5},{5,4},{6,7},{7,6},{8,9},{9,8},{10,11... | collective-permute-start | bytes 20 | tf_op jit(solution)/shard_map/ppermute | solution.py:305
  0.5 30.9 %collective-permute-start.2 = (f32[2,256,256]{2,1,0:T(8,128)}, f32[2,256,256]{2,1,0:T(8,128)}, u32[]{:S(2)}, u32[]{:S(2)}) collective-permute-start(f32[2,256,256]{2,1,0:T(8,128)} %param.21), channel_id=1, source_target_pairs={{0,1},{1,0},{2,3},{3,2},{4,5},{5,4},{6,7},{7,6},{8,9},{9,8},{10,11... | collective-permute-start | bytes 1572872 | tf_op jit(solution)/shard_map/ppermute | solution.py:306
  2.0 17.2 %collective-permute-start.3 = (f32[1,2,256,256]{3,2,1,0:T(8,128)S(1)}, f32[1,2,256,256]{3,2,1,0:T(8,128)}, u32[]{:S(2)}, u32[]{:S(2)}) collective-permute-start(f32[1,2,256,256]{3,2,1,0:T(8,128)S(1)} %constant_dynamic-slice_fusion.1), channel_id=1, source_target_pairs={{4,0},{8,4},{12,8},{5,1},{9,5},{13,9},{6,2},{10,6},{14,10},{7,3},{... | collective-permute-start | bytes 1572872 | tf_op jit(solution)/shard_map/ppermute | solution.py:18
  8.4 13.4 %copy-start.5 = (s32[2,2]{1,0:T(2,128)S(1)}, s32[2,2]{1,0:T(2,128)}, u32[]{:S(2)}) copy-start(s32[2,2]{1,0:T(2,128)} %param.19) | copy-start | bytes 52
  9.5 17.6 %copy-start.1 = (bf16[2,256,256]{2,1,0:T(8,128)(2,1)S(1)}, bf16[2,256,256]{2,1,0:T(8,128)(2,1)}, u32[]{:S(2)}) copy-start(bf16[2,256,256]{2,1,0:T(8,128)(2,1)} %param.18) | copy-start | bytes 786436
  19.2 3.9 %collective-permute-start.4 = (f32[1,2,256,256]{3,2,1,0:T(8,128)}, f32[1,2,256,256]{3,2,1,0:T(8,128)S(1)}, u32[]{:S(2)}, u32[]{:S(2)}) collective-permute-start(f32[1,2,256,256]{3,2,1,0:T(8,128)} %collective-permute-done.3.mine_ref), channel_id=1, source_target_pairs={{0,1},{1,0},{2,3},{3,2},{4,5},{5,4},{6,7},{7,6},{8,9},{9,8},{10,11... | collective-permute-start | bytes 1572872 | tf_op jit(solution)/shard_map/ppermute | solution.py:300
  23.1 0.8 copy-start.4
  29.0 8.9 %collective-permute-start.5 = (bf16[1,2,256,256]{3,2,1,0:T(8,128)(2,1)}, bf16[1,2,256,256]{3,2,1,0:T(8,128)(2,1)S(1)}, u32[]{:S(2)}, u32[]{:S(2)}) collective-permute-start(bf16[1,2,256,256]{3,2,1,0:T(8,128)(2,1)} %get-tuple-element.189), channel_id=1, source_target_pairs={{0,2},{1,3},{4,6},{5,7},{8,10},{9,11},{12,14},{13,15},{16,18},{17,... | collective-permute-start | bytes 786440 | tf_op jit(solution)/shard_map/ppermute | solution.py:356
  37.9 0.7 copy-start.2
  38.6 0.7 copy-start
  41.9 16.5 %collective-permute-start.6 = (bf16[1,2,256,256]{3,2,1,0:T(8,128)(2,1)}, bf16[1,2,256,256]{3,2,1,0:T(8,128)(2,1)}, u32[]{:S(2)}, u32[]{:S(2)}) collective-permute-start(bf16[1,2,256,256]{3,2,1,0:T(8,128)(2,1)} %get-tuple-element.142), channel_id=1, source_target_pairs={{2,0},{3,1},{6,4},{7,5},{10,8},{11,9},{14,12},{15,13},{18,16},{19,... | collective-permute-start | bytes 786440 | tf_op jit(solution)/shard_map/ppermute | solution.py:372
  68.7 14.0 %collective-permute-start.7 = (bf16[2,256,512]{2,1,0:T(8,128)(2,1)S(1)}, bf16[2,256,512]{2,1,0:T(8,128)(2,1)S(1)}, u32[]{:S(2)}, u32[]{:S(2)}) collective-permute-start(bf16[2,256,512]{2,1,0:T(8,128)(2,1)S(1)} %slice.68), channel_id=1, source_target_pairs={{0,4},{4,8},{8,12},{1,5},{5,9},{9,13},{2,6},{6,10},{10,14},{3,7},{... | collective-permute-start | bytes 1572872 | tf_op jit(solution)/shard_map/ppermute | solution.py:380
  84.0 2.0 %collective-permute-start.8 = (bf16[2,256,512]{2,1,0:T(8,128)(2,1)S(1)}, bf16[2,256,512]{2,1,0:T(8,128)(2,1)S(1)}, u32[]{:S(2)}, u32[]{:S(2)}) collective-permute-start(bf16[2,256,512]{2,1,0:T(8,128)(2,1)S(1)} %fusion), channel_id=1, source_target_pairs={{0,1},{1,0},{2,3},{3,2},{4,5},{5,4},{6,7},{7,6},{8,9},{9,8},{10,11... | collective-permute-start | bytes 1572872 | tf_op jit(solution)/shard_map/ppermute | solution.py:383

commit v4 on v3

--- a/solution.py
+++ b/solution.py
@@ -312,18 +312,15 @@
     all_counts = jnp.where(
         first_core, jnp.concatenate([counts, both_counts]), jnp.concatenate([both_counts, counts])
     )
-    all_measured = jnp.where(
-        first_core,
-        jnp.concatenate([measured, both_measured]),
-        jnp.concatenate([both_measured, measured]),
-    )
     entry = batch_index * share + jnp.arange(share, dtype=jnp.int32)
     live = entry < all_counts[0] + all_counts[1]
     later = entry >= all_counts[0]
     slot = jnp.clip(jnp.where(later, entry - all_counts[0], entry), 0, capacity - 1)
     flat = jnp.where(later, capacity, 0) + slot
     chosen = all_positions[flat]
-    measured = all_measured[flat]
+    measured = jnp.where(
+        (later == first_core)[:, None, None], both_measured[slot], measured[slot]
+    )
     local_rows = chosen[:, 0] - tile_index * tile_rows
     local_columns = chosen[:, 1]
     order = jnp.reshape(batch_index, (1,)).astype(jnp.int32)
@@ -376,12 +373,20 @@
     gradient = scatter_terms(
         terms, local_rows, local_columns, live, tile_rows + width, columns_all
     )
-    spill = gradient[:, tile_rows:, :].astype(jnp.bfloat16)
-    arrived = lax.ppermute(spill, "tile", [(t, t + 1) for t in range(tile_count - 1)])
-    own = gradient[:, :tile_rows, :]
-    own = own.at[:, :width, :].add(arrived.astype(jnp.float32)).astype(jnp.bfloat16)
-    partner = lax.ppermute(own, "batch", pairs)
-    summed = own.astype(jnp.float32) + partner.astype(jnp.float32)
+    gradient = gradient.astype(jnp.bfloat16)
+    other = lax.ppermute(gradient, "batch", pairs)
+    total = gradient.astype(jnp.float32) + other.astype(jnp.float32)
+    spill = lax.dynamic_slice_in_dim(total[:, tile_rows:, :], batch_index * half, half, 2)
+    arrived = lax.ppermute(
+        spill.astype(jnp.bfloat16), "tile", [(t, t + 1) for t in range(tile_count - 1)]
+    )
+    arrived_other = lax.ppermute(arrived, "batch", pairs)
+    incoming = jnp.where(
+        first_core,
+        jnp.concatenate([arrived, arrived_other], axis=2),
+        jnp.concatenate([arrived_other, arrived], axis=2),
+    )
+    summed = total[:, :tile_rows, :].at[:, :width, :].add(incoming.astype(jnp.float32))
     return summed[None]
 
 

time: 87.8 us -> 84.5 us (0.962)
  other arithmetic: 16.1 us -> 13.9 us
  local copies, waits for them, and re-layouts: 7.4 us -> 6.18 us
    ppermute x1, waiting for transfers between devices: 3.48 us -> 6.5 us  [local(): carry = lax.ppermute(carry, 'depth', [(turn - 1, turn)])]
    concatenate x1 -> x0, other arithmetic: 3.02 us -> none  [local(): jnp.concatenate([both_measured, measured])]
    ppermute x2 -> x3, waiting for transfers between devices: 12.3 us -> 10 us  [the longest x1 5.83 us: local(): lax.ppermute(spill.astype(jnp.bfloat16), 'tile', [(t, t + 1) for t in ran...]
    slice x1, local copies, waits for them, and re-layouts: 1.29 us -> 0.07 us  [local(): total[:, tile_rows:, :]]
    ppermute x2 -> x3, starting transfers between devices: 3.59 us -> 3.57 us  [the longest x1 3.5 us: local(): lax.ppermute(spill.astype(jnp.bfloat16), 'tile', [(t, t + 1) for t in ran...]
    unnamed x10 -> x12, local copies, waits for them, and re-layouts: 2.19 us -> 2.19 us
  transfers between devices with their start and end apart: 9 -> 10, of which waited for: 5 -> 6; matrix products, arithmetic and copies ran while one was open for 15% -> 12% of each run, Pallas kernels for 6% -> 6%
where the time goes in v4:
time: 84.5 us; the launch traced here: 84 us
  waiting for transfers between devices  38.1 us (45%)
  other arithmetic  13.9 us (16%)
  Pallas kernels  12.1 us (14%)
  starting transfers between devices  9.52 us (11%)
  local copies, waits for them, and re-layouts  6.18 us (7%)
  between operations  4.09 us (5%)
    ppermute x1, waiting for transfers between devices, local(): carry = lax.ppermute(carry, 'depth', [(turn + 1, turn)])  13.9 us
    ppermute x1, waiting for transfers between devices, from_behind(): return lax.ppermute(block, axis, route)  7.69 us
    ppermute x1, waiting for transfers between devices, local(): carry = lax.ppermute(carry, 'depth', [(turn - 1, turn)])  6.5 us
    ppermute x1, waiting for transfers between devices, local(): lax.ppermute(spill.astype(jnp.bfloat16), 'tile', [(t, t + 1) for t in ran...  5.83 us
    pallas_call x2, Pallas kernels, run_waves(): pl.pallas_call(wave_kernel(transmit_first, residual_after, backward), gri...  5.03 us
    pallas_call x1, Pallas kernels, scatter_terms(): pl.pallas_call(scatter_kernel, grid_spec=grid_spec, out_shape=jax.ShapeDt...  3.96 us
    ppermute x1, starting transfers between devices, local(): lax.ppermute(spill.astype(jnp.bfloat16), 'tile', [(t, t + 1) for t in ran...  3.5 us
    pallas_call x1, Pallas kernels, cut_patches(): pl.pallas_call(cut_kernel, grid_spec=grid_spec, out_shape=jax.ShapeDtypeS...  3.08 us
  transfers between devices with their start and end apart: 10, of which 6 were waited for; matrix products, arithmetic and copies ran while one was open for 12% of the time, Pallas kernels for 6%

profile of v4, /device:TPU:0, one launch (start us, length us, event | category | flops | bytes accessed | tf_op | source)
XLA Modules:
  0.0 84.0 jit_solution(12433255220336380319)
XLA Ops:
  0.5 1.1 %constant_dynamic-slice_fusion.1 = f32[1,2,256,256]{3,2,1,0:T(8,128)S(1)} fusion(f32[1,2,256,512]{3,2,1,0:T(8,128)} %tile_ref.1, s32[]{:T(128)S(6)} %select_n.148), kind=kLoop, calls=%fused_computation.48 | loop fusion | bytes 1048580 | tf_op jit(solution)/shard_map/dynamic_slice | solution.py:297
  1.6 1.3 %collective-permute-start.3 = (f32[1,2,256,256]{3,2,1,0:T(8,128)S(1)}, f32[1,2,256,256]{3,2,1,0:T(8,128)}, u32[]{:S(2)}, u32[]{:S(2)}) collective-permute-start(f32[1,2,256,256]{3,2,1,0:T(8,128)S(1)} %constant_dynamic-slice_fusion.1), channel_id=1, source_target_pairs={{4,0},{8,4},{12,8},{5,1},{9,5},{13,9},{6,2},{10,6},{14,10},{7,3},{... | collective-permute-start | bytes 1572872 | tf_op jit(solution)/shard_map/ppermute | solution.py:18
  4.1 1.0 %multiply_convert_fusion.2 = bf16[256,256]{1,0:T(8,128)(2,1)S(1)} fusion(), kind=kLoop, calls=%fused_computation.28 | loop fusion | flops 1048576 | bytes 131072 | tf_op jit(solution)/shard_map/convert_element_type | solution.py:26
  5.1 1.7 %fusion.14 = (bf16[256,256]{1,0:T(8,128)(2,1)}, bf16[256,256]{1,0:T(8,128)(2,1)}) fusion(), kind=kLoop, calls=%fused_computation.37 | loop fusion | flops 1572864 | bytes 262144 | tf_op jit(solution)/shard_map/neg | solution.py:28
  6.8 1.7 %multiply_convert_fusion = (bf16[256,256]{1,0:T(8,128)(2,1)}, bf16[256,256]{1,0:T(8,128)(2,1)}) fusion(), kind=kLoop, calls=%fused_computation.26 | loop fusion | flops 1179648 | bytes 262144 | tf_op jit(solution)/shard_map/convert_element_type | solution.py:27
  8.5 1.0 %fusion.11 = (f32[1,256,256]{2,1,0:T(8,128)S(1)}, f32[1,256,256]{2,1,0:T(8,128)S(1)}) fusion(s32[256]{0:T(256)S(1)} %fusion.17, f32[]{:T(128)S(6)} %neg.15), kind=kLoop, calls=%fused_computation.33 | loop fusion | flops 196608 | bytes 525316 | tf_op jit(solution)/shard_map/cos | solution.py:51
  9.5 1.5 %fusion.4 = (bf16[512,512]{1,0:T(8,128)(2,1)S(1)}, bf16[512,512]{1,0:T(8,128)(2,1)S(1)}, bf16[512,512]{1,0:T(8,128)(2,1)S(1)}, bf16[512,512]{1,0:T(8,128)(2,1)S(1)}) fusion(bf16[256,256]{1,0:T(8,128)(2,1)S(1)} %multiply_convert_fusion.2, bf16[256,256]{1,0:T(8,128)(2,1)} %get-tuple-element.219, bf16[256,256]{1,0:T(8,128)(2,1)} %get-tuple-element.216, ...), kind=kLoop, calls=%fused_computation.15 | loop fusion | flops 6815744 | bytes 2752512 | tf_op jit(solution)/shard_map/concatenate | solution.py:42
  11.0 7.7 %collective-permute-done.3.mine_ref = f32[1,2,256,256]{3,2,1,0:T(8,128)} collective-permute-done((f32[1,2,256,256]{3,2,1,0:T(8,128)S(1)}, f32[1,2,256,256]{3,2,1,0:T(8,128)}, u32[]{:S(2)}, u32[]{:S(2)}) %collective-permute-start.3) | collective-permute-done | bytes 524320 | tf_op jit(solution)/shard_map/ppermute | solution.py:18
  18.7 0.7 broadcast_select_fusion.1
  22.7 0.8 copy-done.5
  23.5 3.1 %shard_map.60 = f32[1,2,256,256]{3,2,1,0:T(8,128)S(1)} custom-call(s32[1]{0:T(128)S(6)} %sub.14.rows_ref, s32[1]{0:T(128)} %bitcast.7.columns_ref, s32[1]{0:T(128)} %bitcast.3.order_ref, f32[1,2,256,512]{3,2,1,0:T(8,128)} %tile_ref.1, f32[1,2,256,256]{3,2,1,0:T(8,128)} %collective-permute-done.3.mine_ref, f32[1,2,256,256]{3,2,1,0:T(8,128)} %copy-done.5), custom_call_target="tpu_custom_call" | custom-call | tf_op jit(solution)/shard_map/pallas_call | solution.py:279
  26.6 1.9 %conditional.4 = (bf16[1,2,256,256]{3,2,1,0:T(8,128)(2,1)}) conditional(s32[]{:T(128)} %convert_element_type.121, () %tuple.42, (bf16[1,2,256,256]{3,2,1,0:T(8,128)(2,1)S(1)}, f32[1,2,256,256]{3,2,1,0:T(8,128)S(1)}, f32[2,256,256]{2,1,0:T(8,128)S(1)}, bf16[512,512]{1,0:T(8,128)(2,1)S(1)}, bf16[512,512]{1,0:T(8,128)(2,1)S(1)}, ...), branch_computations={%region_0.1_spmd, %region_1.2_spmd} | conditional | bytes 262154 | solution.py:356
  26.6 1.9 %branch_1_fun.5 = bf16[1,2,256,256]{3,2,1,0:T(8,128)(2,1)} custom-call(bf16[1,2,256,256]{3,2,1,0:T(8,128)(2,1)S(1)} %get-tuple-element.131.refs_0_, f32[1,2,256,256]{3,2,1,0:T(8,128)S(1)} %get-tuple-element.132.refs_1_, f32[2,256,256]{2,1,0:T(8,128)S(1)} %get-tuple-element.133.refs_2_, bf16[512,512]{1,0:T(8,128)(2,1)S(1)} %get-tuple-element.134.refs_3_, ...), custom_call_target="tpu_custom_call" | custom-call | tf_op jit(solution)/shard_map/cond/branch_1_fun/pallas_call | solution.py:197
  28.5 2.3 %collective-permute-start.5 = (bf16[1,2,256,256]{3,2,1,0:T(8,128)(2,1)}, bf16[1,2,256,256]{3,2,1,0:T(8,128)(2,1)S(1)}, u32[]{:S(2)}, u32[]{:S(2)}) collective-permute-start(bf16[1,2,256,256]{3,2,1,0:T(8,128)(2,1)} %get-tuple-element.224), channel_id=1, source_target_pairs={{0,2},{1,3},{4,6},{5,7},{8,10},{9,11},{12,14},{13,15},{16,18},{17,... | collective-permute-start | bytes 786440 | tf_op jit(solution)/shard_map/ppermute | solution.py:353
  30.9 6.5 %collective-permute-done.5 = bf16[1,2,256,256]{3,2,1,0:T(8,128)(2,1)S(1)} collective-permute-done((bf16[1,2,256,256]{3,2,1,0:T(8,128)(2,1)}, bf16[1,2,256,256]{3,2,1,0:T(8,128)(2,1)S(1)}, u32[]{:S(2)}, u32[]{:S(2)}) %collective-permute-start.5) | collective-permute-done | bytes 262176 | tf_op jit(solution)/shard_map/ppermute | solution.py:353
  37.4 0.7 copy-done.3
  38.8 1.0 %broadcast_select_fusion = bf16[1,2,256,256]{3,2,1,0:T(8,128)(2,1)S(1)} fusion(bf16[1,2,256,256]{3,2,1,0:T(8,128)(2,1)} %copy-done.3, pred[]{:T(512)S(6)} %eq.34, bf16[2,256,256]{2,1,0:T(8,128)(2,1)} %param.18), kind=kLoop, calls=%fused_computation.35 | loop fusion | flops 131072 | bytes 786433 | tf_op jit(solution)/shard_map/jit(_where)/select_n | solution.py:354
  39.8 1.6 %conditional.6 = ((bf16[1,2,256,256]{3,2,1,0:T(8,128)(2,1)}, f32[1,2,256,256]{3,2,1,0:T(8,128)})) conditional(s32[]{:T(128)} %convert_element_type.122, () %tuple.40, (bf16[1,2,256,256]{3,2,1,0:T(8,128)(2,1)}, f32[1,2,256,256]{3,2,1,0:T(8,128)S(1)}, f32[2,256,256]{2,1,0:T(8,128)S(1)}, bf16[512,512]{1,0:T(8,128)(2,1)S(1)}, ...), branch_computations={%region_4.5_spmd, %region_5.6_spmd} | conditional | bytes 786462 | solution.py:370
  39.8 0.7 broadcast.223
  40.5 0.8 broadcast.224
  41.4 1.3 %collective-permute-start.6 = (bf16[1,2,256,256]{3,2,1,0:T(8,128)(2,1)}, bf16[1,2,256,256]{3,2,1,0:T(8,128)(2,1)}, u32[]{:S(2)}, u32[]{:S(2)}) collective-permute-start(bf16[1,2,256,256]{3,2,1,0:T(8,128)(2,1)} %get-tuple-element.169), channel_id=1, source_target_pairs={{2,0},{3,1},{6,4},{7,5},{10,8},{11,9},{14,12},{15,13},{18,16},{19,... | collective-permute-start | bytes 786440 | tf_op jit(solution)/shard_map/ppermute | solution.py:369
  43.9 13.9 %collective-permute-done.6 = bf16[1,2,256,256]{3,2,1,0:T(8,128)(2,1)} collective-permute-done((bf16[1,2,256,256]{3,2,1,0:T(8,128)(2,1)}, bf16[1,2,256,256]{3,2,1,0:T(8,128)(2,1)}, u32[]{:S(2)}, u32[]{:S(2)}) %collective-permute-start.6) | collective-permute-done | bytes 262176 | tf_op jit(solution)/shard_map/ppermute | solution.py:369
  57.9 3.1 %conditional.7 = (f32[1,2,256,256]{3,2,1,0:T(8,128)}) conditional(s32[]{:T(128)} %convert_element_type.121, () %tuple.39, (bf16[1,2,256,256]{3,2,1,0:T(8,128)(2,1)}, f32[1,2,256,256]{3,2,1,0:T(8,128)S(1)}, f32[2,256,256]{2,1,0:T(8,128)S(1)}, bf16[512,512]{1,0:T(8,128)(2,1)S(1)}, bf16[512,512]{1,0:T(8,128)(2,1)S(1)}, ...), branch_computations={%region_6.7_spmd, %region_7.8_spmd} | conditional | bytes 524300 | solution.py:370
  57.9 3.1 %branch_1_fun.8 = (bf16[1,2,256,256]{3,2,1,0:T(8,128)(2,1)}, f32[1,2,256,256]{3,2,1,0:T(8,128)}) custom-call(bf16[1,2,256,256]{3,2,1,0:T(8,128)(2,1)} %get-tuple-element.158.refs_0_, f32[1,2,256,256]{3,2,1,0:T(8,128)S(1)} %get-tuple-element.159.refs_1_, f32[2,256,256]{2,1,0:T(8,128)S(1)} %get-tuple-element.160.refs_2_, ...), custom_call_target="tpu_custom_call" | custom-call | tf_op jit(solution)/shard_map/cond/branch_1_fun/pallas_call | solution.py:197
  61.0 1.9 %select_select_fusion.terms_ref = f32[1,2,256,256]{3,2,1,0:T(8,128)} fusion(f32[1,2,256,256]{3,2,1,0:T(8,128)} %get-tuple-element.227, f32[1,2,256,256]{3,2,1,0:T(8,128)} %get-tuple-element.170, pred[]{:T(512)S(6)} %eq.34, pred[]{:T(512)S(6)} %eq.33), kind=kLoop, calls=%fused_computation.19 | loop fusion | flops 262144 | bytes 1572866 | tf_op jit(solution)/shard_map/jit(_where)/select_n | solution.py:371
  62.9 4.0 %shard_map.61 = f32[2,512,512]{2,1,0:T(8,128)} custom-call(s32[1]{0:T(128)S(6)} %sub.14.rows_ref, s32[1]{0:T(128)} %bitcast.7.columns_ref, s32[1]{0:T(128)S(6)} %convert_element_type.120.live_ref, f32[1,2,256,256]{3,2,1,0:T(8,128)} %select_select_fusion.terms_ref), custom_call_target="tpu_custom_call" | custom-call | tf_op jit(solution)/shard_map/pallas_call | solution.py:240
  66.8 1.9 %convert_element_type.128 = bf16[2,512,512]{2,1,0:T(8,128)(2,1)S(1)} convert(f32[2,512,512]{2,1,0:T(8,128)} %shard_map.61) | non-fusion elementwise | flops 524288 | bytes 3145728 | tf_op jit(solution)/shard_map/convert_element_type | solution.py:376
  68.8 2.6 %collective-permute-done.7 = bf16[2,512,512]{2,1,0:T(8,128)(2,1)S(1)} collective-permute-done((bf16[2,512,512]{2,1,0:T(8,128)(2,1)S(1)}, bf16[2,512,512]{2,1,0:T(8,128)(2,1)S(1)}, u32[]{:S(2)}, u32[]{:S(2)}) %collective-permute-start.7) | collective-permute-done | bytes 1048608 | tf_op jit(solution)/shard_map/ppermute | solution.py:377
  71.9 3.5 %collective-permute-start.8 = (bf16[2,256,256]{2,1,0:T(8,128)(2,1)S(1)}, bf16[2,256,256]{2,1,0:T(8,128)(2,1)S(1)}, u32[]{:S(2)}, u32[]{:S(2)}) collective-permute-start(bf16[2,256,256]{2,1,0:T(8,128)(2,1)S(1)} %dynamic-slice_convert_fusion), channel_id=1, source_target_pairs={{0,4},{4,8},{8,12},{1,5},{5,9},{9,13},{2,6},{6,10},{10,14},{3,7},{... | collective-permute-start | bytes 786440 | tf_op jit(solution)/shard_map/ppermute | solution.py:380
  75.4 5.8 %collective-permute-done.8 = bf16[2,256,256]{2,1,0:T(8,128)(2,1)S(1)} collective-permute-done((bf16[2,256,256]{2,1,0:T(8,128)(2,1)S(1)}, bf16[2,256,256]{2,1,0:T(8,128)(2,1)S(1)}, u32[]{:S(2)}, u32[]{:S(2)}) %collective-permute-start.8) | collective-permute-done | bytes 262176 | tf_op jit(solution)/shard_map/ppermute | solution.py:380
  81.2 1.5 %collective-permute-done.9 = bf16[2,256,256]{2,1,0:T(8,128)(2,1)S(1)} collective-permute-done((bf16[2,256,256]{2,1,0:T(8,128)(2,1)S(1)}, bf16[2,256,256]{2,1,0:T(8,128)(2,1)S(1)}, u32[]{:S(2)}, u32[]{:S(2)}) %collective-permute-start.9) | collective-permute-done | bytes 262176 | tf_op jit(solution)/shard_map/ppermute | solution.py:383
  82.8 1.2 %fusion = f32[1,2,256,512]{3,2,1,0:T(8,128)} fusion(f32[2,512,512]{2,1,0:T(8,128)S(1)} %convert_add_fusion, bf16[2,256,256]{2,1,0:T(8,128)(2,1)S(1)} %collective-permute-done.9, bf16[2,256,256]{2,1,0:T(8,128)(2,1)S(1)} %collective-permute-done.8, pred[]{:T(512)} %eq.32), kind=kLoop, calls=%fused_computation.3 | loop fusion | flops 2883584 | bytes 2621441 | tf_op jit(solution)/shard_map/broadcast_in_dim | solution.py:390
  (31 shorter events, 3.6 us)
Async XLA Ops:
  0.0 18.7 %collective-permute-start.1 = (s32[1]{0:T(128)}, s32[1]{0:T(128)}, u32[]{:S(2)}, u32[]{:S(2)}) collective-permute-start(s32[1]{0:T(128)} %param.20), channel_id=1, source_target_pairs={{0,1},{1,0},{2,3},{3,2},{4,5},{5,4},{6,7},{7,6},{8,9},{9,8},{10,11... | collective-permute-start | bytes 20 | tf_op jit(solution)/shard_map/ppermute | solution.py:305
  0.5 20.9 %collective-permute-start = (s32[2,2]{1,0:T(2,128)}, s32[2,2]{1,0:T(2,128)S(1)}, u32[]{:S(2)}, u32[]{:S(2)}) collective-permute-start(s32[2,2]{1,0:T(2,128)} %param.19), channel_id=1, source_target_pairs={{0,1},{1,0},{2,3},{3,2},{4,5},{5,4},{6,7},{7,6},{8,9},{9,8},{10,11... | collective-permute-start | bytes 56 | tf_op jit(solution)/shard_map/ppermute | solution.py:304
  1.6 17.1 %collective-permute-start.3 = (f32[1,2,256,256]{3,2,1,0:T(8,128)S(1)}, f32[1,2,256,256]{3,2,1,0:T(8,128)}, u32[]{:S(2)}, u32[]{:S(2)}) collective-permute-start(f32[1,2,256,256]{3,2,1,0:T(8,128)S(1)} %constant_dynamic-slice_fusion.1), channel_id=1, source_target_pairs={{4,0},{8,4},{12,8},{5,1},{9,5},{13,9},{6,2},{10,6},{14,10},{7,3},{... | collective-permute-start | bytes 1572872 | tf_op jit(solution)/shard_map/ppermute | solution.py:18
  2.9 28.0 %collective-permute-start.2 = (f32[2,256,256]{2,1,0:T(8,128)}, f32[2,256,256]{2,1,0:T(8,128)}, u32[]{:S(2)}, u32[]{:S(2)}) collective-permute-start(f32[2,256,256]{2,1,0:T(8,128)} %param.21), channel_id=1, source_target_pairs={{0,1},{1,0},{2,3},{3,2},{4,5},{5,4},{6,7},{7,6},{8,9},{9,8},{10,11... | collective-permute-start | bytes 1572872 | tf_op jit(solution)/shard_map/ppermute | solution.py:306
  8.5 12.9 %copy-start.6 = (s32[2,2]{1,0:T(2,128)S(1)}, s32[2,2]{1,0:T(2,128)}, u32[]{:S(2)}) copy-start(s32[2,2]{1,0:T(2,128)} %param.19) | copy-start | bytes 52
  9.5 17.0 %copy-start.2 = (bf16[2,256,256]{2,1,0:T(8,128)(2,1)S(1)}, bf16[2,256,256]{2,1,0:T(8,128)(2,1)}, u32[]{:S(2)}) copy-start(bf16[2,256,256]{2,1,0:T(8,128)(2,1)} %param.18) | copy-start | bytes 786436
  18.7 4.0 %collective-permute-start.4 = (f32[1,2,256,256]{3,2,1,0:T(8,128)}, f32[1,2,256,256]{3,2,1,0:T(8,128)S(1)}, u32[]{:S(2)}, u32[]{:S(2)}) collective-permute-start(f32[1,2,256,256]{3,2,1,0:T(8,128)} %collective-permute-done.3.mine_ref), channel_id=1, source_target_pairs={{0,1},{1,0},{2,3},{3,2},{4,5},{5,4},{6,7},{7,6},{8,9},{9,8},{10,11... | collective-permute-start | bytes 1572872 | tf_op jit(solution)/shard_map/ppermute | solution.py:300
  22.7 0.8 copy-start.5
  28.5 8.9 %collective-permute-start.5 = (bf16[1,2,256,256]{3,2,1,0:T(8,128)(2,1)}, bf16[1,2,256,256]{3,2,1,0:T(8,128)(2,1)S(1)}, u32[]{:S(2)}, u32[]{:S(2)}) collective-permute-start(bf16[1,2,256,256]{3,2,1,0:T(8,128)(2,1)} %get-tuple-element.224), channel_id=1, source_target_pairs={{0,2},{1,3},{4,6},{5,7},{8,10},{9,11},{12,14},{13,15},{16,18},{17,... | collective-permute-start | bytes 786440 | tf_op jit(solution)/shard_map/ppermute | solution.py:353
  37.4 0.7 copy-start.3
  38.1 0.7 copy-start.1
  41.4 16.5 %collective-permute-start.6 = (bf16[1,2,256,256]{3,2,1,0:T(8,128)(2,1)}, bf16[1,2,256,256]{3,2,1,0:T(8,128)(2,1)}, u32[]{:S(2)}, u32[]{:S(2)}) collective-permute-start(bf16[1,2,256,256]{3,2,1,0:T(8,128)(2,1)} %get-tuple-element.169), channel_id=1, source_target_pairs={{2,0},{3,1},{6,4},{7,5},{10,8},{11,9},{14,12},{15,13},{18,16},{19,... | collective-permute-start | bytes 786440 | tf_op jit(solution)/shard_map/ppermute | solution.py:369
  66.8 4.6 %copy-start = (f32[2,512,512]{2,1,0:T(8,128)S(1)}, f32[2,512,512]{2,1,0:T(8,128)}, u32[]{:S(2)}) copy-start(f32[2,512,512]{2,1,0:T(8,128)} %shard_map.61) | copy-start | bytes 6291460
  68.7 2.7 %collective-permute-start.7 = (bf16[2,512,512]{2,1,0:T(8,128)(2,1)S(1)}, bf16[2,512,512]{2,1,0:T(8,128)(2,1)S(1)}, u32[]{:S(2)}, u32[]{:S(2)}) collective-permute-start(bf16[2,512,512]{2,1,0:T(8,128)(2,1)S(1)} %convert_element_type.128), channel_id=1, source_target_pairs={{0,1},{1,0},{2,3},{3,2},{4,5},{5,4},{6,7},{7,6},{8,9},{9,8},{10,11... | collective-permute-start | bytes 3145736 | tf_op jit(solution)/shard_map/ppermute | solution.py:377
  71.9 9.3 %collective-permute-start.8 = (bf16[2,256,256]{2,1,0:T(8,128)(2,1)S(1)}, bf16[2,256,256]{2,1,0:T(8,128)(2,1)S(1)}, u32[]{:S(2)}, u32[]{:S(2)}) collective-permute-start(bf16[2,256,256]{2,1,0:T(8,128)(2,1)S(1)} %dynamic-slice_convert_fusion), channel_id=1, source_target_pairs={{0,4},{4,8},{8,12},{1,5},{5,9},{9,13},{2,6},{6,10},{10,14},{3,7},{... | collective-permute-start | bytes 786440 | tf_op jit(solution)/shard_map/ppermute | solution.py:380
  81.2 1.5 %collective-permute-start.9 = (bf16[2,256,256]{2,1,0:T(8,128)(2,1)S(1)}, bf16[2,256,256]{2,1,0:T(8,128)(2,1)S(1)}, u32[]{:S(2)}, u32[]{:S(2)}) collective-permute-start(bf16[2,256,256]{2,1,0:T(8,128)(2,1)S(1)} %collective-permute-done.8), channel_id=1, source_target_pairs={{0,1},{1,0},{2,3},{3,2},{4,5},{5,4},{6,7},{7,6},{8,9},{9,8},{10,11... | collective-permute-start | bytes 786440 | tf_op jit(solution)/shard_map/ppermute | solution.py:383

commit v5 on v4

--- a/solution.py
+++ b/solution.py
@@ -283,6 +283,132 @@
     )(rows, columns, order, tile, mine, partner)
 
 
+def propagate_block(wave_re, wave_im, blocks, chirp_re, chirp_im):
+    fl_ref, fr_ref, gl_ref, gr_ref = blocks
+    width = wave_re.shape[0]
+    stacked = jnp.concatenate([wave_re, wave_im], axis=0).astype(jnp.bfloat16)
+    first = jnp.dot(fl_ref[...], stacked, preferred_element_type=jnp.float32).astype(jnp.bfloat16)
+    rowwise = jnp.concatenate([first[:width], first[width:]], axis=1)
+    spectrum = jnp.dot(rowwise, fr_ref[...], preferred_element_type=jnp.float32)
+    spec_re = spectrum[:, :width]
+    spec_im = spectrum[:, width:]
+    filtered = jnp.concatenate(
+        [spec_re * chirp_re - spec_im * chirp_im, spec_re * chirp_im + spec_im * chirp_re],
+        axis=1,
+    ).astype(jnp.bfloat16)
+    back = jnp.dot(filtered, gr_ref[...], preferred_element_type=jnp.float32).astype(jnp.bfloat16)
+    columnwise = jnp.concatenate([back[:, :width], back[:, width:]], axis=0)
+    out = jnp.dot(gl_ref[...], columnwise, preferred_element_type=jnp.float32).astype(jnp.bfloat16)
+    values = out.astype(jnp.float32)
+    return (values[:width], values[width:])
+
+
+def place_term(term_re, term_im, row, column, alive, total_ref):
+    width = term_re.shape[0]
+    height = total_ref.shape[1]
+    columns_all = total_ref.shape[2]
+    row_shift = row % height
+    column_shift = column % columns_all
+    for part, term in enumerate((term_re, term_im)):
+        term = jnp.where(alive, term, 0.0)
+        wide = jnp.concatenate(
+            [term, jnp.zeros((width, columns_all - width), jnp.float32)], axis=1
+        )
+        wide = pltpu.roll(wide, column_shift, 1)
+        tall = jnp.concatenate(
+            [wide, jnp.zeros((height - width, columns_all), jnp.float32)], axis=0
+        )
+        total_ref[part] = total_ref[part] + pltpu.roll(tall, row_shift, 0)
+
+
+def adjoint_kernel(last):
+    def kernel(rows_ref, columns_ref, live_ref, slot_ref, other_ref, *refs):
+        refs = list(refs)
+        wave_ref = refs.pop(0)
+        patch_ref = refs.pop(0)
+        chirp_ref = refs.pop(0)
+        blocks = refs[:4]
+        refs = refs[4:]
+        if last:
+            own_ref = refs.pop(0)
+            partner_ref = refs.pop(0)
+        else:
+            source_ref = refs.pop(0)
+        passed_ref, grad_ref, total_ref = refs
+        index = pl.program_id(0)
+
+        @pl.when(index == 0)
+        def _():
+            total_ref[...] = jnp.zeros(total_ref.shape, total_ref.dtype)
+
+        wave = wave_ref[0].astype(jnp.float32)
+        patch_re = patch_ref[0, 0]
+        patch_im = patch_ref[0, 1]
+        chirp_re = chirp_ref[0]
+        chirp_im = chirp_ref[1]
+        if last:
+            source_re = wave[0]
+            source_im = wave[1]
+            lit_re = patch_re * wave[0] - patch_im * wave[1]
+            lit_im = patch_re * wave[1] + patch_im * wave[0]
+            out_re, out_im = propagate_block(lit_re, lit_im, blocks, chirp_re, chirp_im)
+            measured = jnp.where(other_ref[index] > 0, partner_ref[0], own_ref[0])
+            weight = RESIDUAL_SCALE * (out_re * out_re + out_im * out_im - measured)
+            in_re = (weight * out_re).astype(jnp.bfloat16).astype(jnp.float32)
+            in_im = (weight * out_im).astype(jnp.bfloat16).astype(jnp.float32)
+        else:
+            source = source_ref[0].astype(jnp.float32)
+            source_re = source[0]
+            source_im = source[1]
+            in_re = wave[0]
+            in_im = wave[1]
+        spread_re, spread_im = propagate_block(in_re, in_im, blocks, chirp_re, -chirp_im)
+        passed_ref[0, 0] = (patch_re * spread_re + patch_im * spread_im).astype(jnp.bfloat16)
+        passed_ref[0, 1] = (patch_re * spread_im - patch_im * spread_re).astype(jnp.bfloat16)
+        term_re = source_re * spread_re + source_im * spread_im
+        term_im = source_re * spread_im - source_im * spread_re
+        place_term(
+            term_re, term_im, rows_ref[index], columns_ref[index], live_ref[index] > 0, total_ref
+        )
+
+        @pl.when(index == pl.num_programs(0) - 1)
+        def _():
+            grad_ref[...] = total_ref[...].astype(grad_ref.dtype)
+
+    return kernel
+
+
+def run_adjoint(waves, patches, chirps, blocks, scalars, extra, height, columns_all, last):
+    number, _, width, _ = waves.shape
+    wave_spec = pl.BlockSpec((1, 2, width, width), lambda i, *s: (i, 0, 0, 0))
+    chirp_spec = pl.BlockSpec((2, width, width), lambda i, *s: (0, 0, 0))
+    block_spec = pl.BlockSpec((2 * width, 2 * width), lambda i, *s: (0, 0))
+    in_specs = [wave_spec, wave_spec, chirp_spec] + [block_spec] * 4
+    if last:
+        slot_spec = pl.BlockSpec((1, width, width), lambda i, r, c, a, s, o: (s[i], 0, 0))
+        in_specs += [slot_spec, slot_spec]
+    else:
+        in_specs += [wave_spec]
+    grid_spec = pltpu.PrefetchScalarGridSpec(
+        num_scalar_prefetch=5,
+        grid=(number,),
+        in_specs=in_specs,
+        out_specs=(
+            wave_spec,
+            pl.BlockSpec((2, height, columns_all), lambda i, *s: (0, 0, 0)),
+        ),
+        scratch_shapes=[pltpu.VMEM((2, height, columns_all), jnp.float32)],
+    )
+    return pl.pallas_call(
+        adjoint_kernel(last),
+        grid_spec=grid_spec,
+        out_shape=(
+            jax.ShapeDtypeStruct(waves.shape, jnp.bfloat16),
+            jax.ShapeDtypeStruct((2, height, columns_all), jnp.bfloat16),
+        ),
+    )(*scalars, waves, patches, chirps, *blocks, *extra)
+
+
 def local(object_field, probe, positions, counts, measured):
     width = probe.shape[1]
     tile_rows = object_field.shape[2]
@@ -318,9 +444,7 @@
     slot = jnp.clip(jnp.where(later, entry - all_counts[0], entry), 0, capacity - 1)
     flat = jnp.where(later, capacity, 0) + slot
     chosen = all_positions[flat]
-    measured = jnp.where(
-        (later == first_core)[:, None, None], both_measured[slot], measured[slot]
-    )
+    other = (later == first_core).astype(jnp.int32)
     local_rows = chosen[:, 0] - tile_index * tile_rows
     local_columns = chosen[:, 1]
     order = jnp.reshape(batch_index, (1,)).astype(jnp.int32)
@@ -340,39 +464,45 @@
     def forward_all(waves):
         return run_waves(waves, patches, chirps, blocks)
 
-    def forward_last(waves):
-        return run_waves(waves, patches, chirps, blocks, measured, residual_after=True)
-
     def silent(waves):
         return jnp.zeros_like(waves)
 
     carry = start
     inputs = start
-    for turn in range(depth_count):
+    for turn in range(depth_count - 1):
         if turn > 0:
             carry = lax.ppermute(carry, "depth", [(turn - 1, turn)])
             inputs = jnp.where(segment == turn, carry, inputs)
-        step = forward_last if turn == depth_count - 1 else forward_all
-        carry = lax.cond(segment == turn, step, silent, carry)
-
-    def back_pass(incoming):
-        return run_waves(
-            incoming, patches, chirps, blocks, inputs, transmit_first=False, backward=True
-        )
-
-    def back_silent(incoming):
-        return (jnp.zeros_like(incoming), jnp.zeros(incoming.shape, jnp.float32))
-
-    terms = jnp.zeros(start.shape, jnp.float32)
-    for turn in reversed(range(depth_count)):
-        if turn < depth_count - 1:
-            carry = lax.ppermute(carry, "depth", [(turn + 1, turn)])
-        carry, got = lax.cond(segment == turn, back_pass, back_silent, carry)
-        terms = jnp.where(segment == turn, got, terms)
-
-    gradient = scatter_terms(
-        terms, local_rows, local_columns, live, tile_rows + width, columns_all
-    )
+        carry = lax.cond(segment == turn, forward_all, silent, carry)
+
+    height = tile_rows + width
+    scalars = (local_rows, local_columns, live.astype(jnp.int32), slot, other)
+
+    def last_pass(incoming):
+        return run_adjoint(
+            incoming, patches, chirps, blocks, scalars, (measured, both_measured),
+            height, columns_all, True,
+        )
+
+    def last_silent(incoming):
+        return (jnp.zeros_like(incoming), jnp.zeros((2, height, columns_all), jnp.bfloat16))
+
+    if depth_count > 1:
+        carry = lax.ppermute(carry, "depth", [(depth_count - 2, depth_count - 1)])
+    carry, gradient = lax.cond(segment == depth_count - 1, last_pass, last_silent, carry)
+
+    def back_pass(incoming, previous):
+        return run_adjoint(
+            incoming, patches, chirps, blocks, scalars, (inputs,), height, columns_all, False
+        )
+
+    def back_silent(incoming, previous):
+        return (jnp.zeros_like(incoming), previous)
+
+    for turn in reversed(range(depth_count - 1)):
+        carry = lax.ppermute(carry, "depth", [(turn + 1, turn)])
+        carry, gradient = lax.cond(segment == turn, back_pass, back_silent, carry, gradient)
+
     gradient = gradient.astype(jnp.bfloat16)
     other = lax.ppermute(gradient, "batch", pairs)
     total = gradient.astype(jnp.float32) + other.astype(jnp.float32)

time: 84.5 us -> 75.2 us (0.89)
  other arithmetic: 13.9 us -> 10.3 us
  Pallas kernels: 12.1 us -> 9.69 us
  waiting for transfers between devices: 38.1 us -> 35.8 us
  local copies, waits for them, and re-layouts: 6.18 us -> 4.97 us
    pallas_call x2 -> x1, Pallas kernels: 5.03 us -> 1.93 us  [run_waves(): pl.pallas_call(wave_kernel(transmit_first, residual_after, backward), gri...]
    select_n x2 -> x0, other arithmetic: 2.89 us -> none  [the longest x1 1.9 us: local(): terms = jnp.where(segment == turn, got, terms)]
    convert_element_type x1 -> x0, other arithmetic: 1.87 us -> none  [local(): gradient = gradient.astype(jnp.bfloat16)]
    ppermute x1, waiting for transfers between devices: 6.5 us -> 4.64 us  [local(): carry = lax.ppermute(carry, 'depth', [(depth_count - 2, depth_count - 1)])]
    unnamed x12 -> x6, local copies, waits for them, and re-layouts: 2.19 us -> 0.8 us
    add x1, other arithmetic: 0.35 us -> 1.53 us  [local(): total = gradient.astype(jnp.float32) + other.astype(jnp.float32)]
    another operation x3 -> x2, local copies, waits for them, and re-layouts: 1.57 us -> 1.76 us
  transfers between devices with their start and end apart: 10 -> 10, of which waited for: 6 -> 6; matrix products, arithmetic and copies ran while one was open for 12% -> 13% of each run, Pallas kernels for 6% -> 7%
where the time goes in v5:
time: 75.2 us; the launch traced here: 74.8 us
  waiting for transfers between devices  35.8 us (48%)
  other arithmetic  10.3 us (14%)
  starting transfers between devices  10.1 us (13%)
  Pallas kernels  9.69 us (13%)
  local copies, waits for them, and re-layouts  4.97 us (7%)
  between operations  3.91 us (5%)
    ppermute x1, waiting for transfers between devices, local(): carry = lax.ppermute(carry, 'depth', [(turn + 1, turn)])  13.2 us
    ppermute x1, waiting for transfers between devices, from_behind(): return lax.ppermute(block, axis, route)  7.7 us
    ppermute x1, waiting for transfers between devices, local(): lax.ppermute(spill.astype(jnp.bfloat16), 'tile', [(t, t + 1) for t in ran...  5.83 us
    ppermute x1, waiting for transfers between devices, local(): carry = lax.ppermute(carry, 'depth', [(depth_count - 2, depth_count - 1)])  4.64 us
    pallas_call x1, Pallas kernels, run_adjoint(): pl.pallas_call(adjoint_kernel(last), grid_spec=grid_spec, out_shape=(jax....  4.62 us
    ppermute x1, starting transfers between devices, local(): lax.ppermute(spill.astype(jnp.bfloat16), 'tile', [(t, t + 1) for t in ran...  3.5 us
    pallas_call x1, Pallas kernels, cut_patches(): pl.pallas_call(cut_kernel, grid_spec=grid_spec, out_shape=jax.ShapeDtypeS...  3.14 us
    ppermute x1, starting transfers between devices, local(): carry = lax.ppermute(carry, 'depth', [(depth_count - 2, depth_count - 1)])  3.03 us
  transfers between devices with their start and end apart: 10, of which 6 were waited for; matrix products, arithmetic and copies ran while one was open for 13% of the time, Pallas kernels for 7%

profile of v5, /device:TPU:0, one launch (start us, length us, event | category | flops | bytes accessed | tf_op | source)
XLA Modules:
  0.0 74.8 jit_solution(14397849448889233657)
XLA Ops:
  0.0 0.5 collective-permute-start.1
  0.5 1.1 %constant_dynamic-slice_fusion.1 = f32[1,2,256,256]{3,2,1,0:T(8,128)S(1)} fusion(f32[1,2,256,512]{3,2,1,0:T(8,128)} %tile_ref.1, s32[]{:T(128)S(6)} %select_n.111), kind=kLoop, calls=%fused_computation.45 | loop fusion | bytes 1048580 | tf_op jit(solution)/shard_map/dynamic_slice | solution.py:423
  1.6 1.3 %collective-permute-start.2 = (f32[1,2,256,256]{3,2,1,0:T(8,128)S(1)}, f32[1,2,256,256]{3,2,1,0:T(8,128)}, u32[]{:S(2)}, u32[]{:S(2)}) collective-permute-start(f32[1,2,256,256]{3,2,1,0:T(8,128)S(1)} %constant_dynamic-slice_fusion.1), channel_id=1, source_target_pairs={{4,0},{8,4},{12,8},{5,1},{9,5},{13,9},{6,2},{10,6},{14,10},{7,3},{... | collective-permute-start | bytes 1572872 | tf_op jit(solution)/shard_map/ppermute | solution.py:18
  2.9 0.5 collective-permute-start.5
  4.1 1.0 %multiply_convert_fusion.2 = bf16[256,256]{1,0:T(8,128)(2,1)S(1)} fusion(), kind=kLoop, calls=%fused_computation.26 | loop fusion | flops 1048576 | bytes 131072 | tf_op jit(solution)/shard_map/convert_element_type | solution.py:26
  5.1 1.7 %fusion.14 = (bf16[256,256]{1,0:T(8,128)(2,1)}, bf16[256,256]{1,0:T(8,128)(2,1)}) fusion(), kind=kLoop, calls=%fused_computation.34 | loop fusion | flops 1572864 | bytes 262144 | tf_op jit(solution)/shard_map/neg | solution.py:28
  6.7 1.7 %multiply_convert_fusion = (bf16[256,256]{1,0:T(8,128)(2,1)}, bf16[256,256]{1,0:T(8,128)(2,1)}) fusion(), kind=kLoop, calls=%fused_computation.24 | loop fusion | flops 1179648 | bytes 262144 | tf_op jit(solution)/shard_map/convert_element_type | solution.py:27
  8.5 1.0 %fusion.11 = (f32[1,256,256]{2,1,0:T(8,128)S(1)}, f32[1,256,256]{2,1,0:T(8,128)S(1)}) fusion(s32[256]{0:T(256)S(1)} %fusion.17, f32[]{:T(128)S(6)} %neg.15), kind=kLoop, calls=%fused_computation.31 | loop fusion | flops 196608 | bytes 525316 | tf_op jit(solution)/shard_map/cos | solution.py:51
  9.5 1.5 %fusion.4 = (bf16[512,512]{1,0:T(8,128)(2,1)S(1)}, bf16[512,512]{1,0:T(8,128)(2,1)S(1)}, bf16[512,512]{1,0:T(8,128)(2,1)S(1)}, bf16[512,512]{1,0:T(8,128)(2,1)S(1)}) fusion(bf16[256,256]{1,0:T(8,128)(2,1)S(1)} %multiply_convert_fusion.2, bf16[256,256]{1,0:T(8,128)(2,1)} %get-tuple-element.174, bf16[256,256]{1,0:T(8,128)(2,1)} %get-tuple-element.171, ...), kind=kLoop, calls=%fused_computation.14 | loop fusion | flops 6815744 | bytes 2752512 | tf_op jit(solution)/shard_map/concatenate | solution.py:42
  11.0 7.7 %collective-permute-done.2.mine_ref = f32[1,2,256,256]{3,2,1,0:T(8,128)} collective-permute-done((f32[1,2,256,256]{3,2,1,0:T(8,128)S(1)}, f32[1,2,256,256]{3,2,1,0:T(8,128)}, u32[]{:S(2)}, u32[]{:S(2)}) %collective-permute-start.2) | collective-permute-done | bytes 524320 | tf_op jit(solution)/shard_map/ppermute | solution.py:18
  18.7 0.7 broadcast_select_fusion
  19.4 0.6 fusion.19
  21.3 0.6 fusion.20
  22.6 0.8 %copy-done.1 = f32[1,2,256,256]{3,2,1,0:T(8,128)} copy-done((f32[1,2,256,256]{3,2,1,0:T(8,128)}, f32[1,2,256,256]{3,2,1,0:T(8,128)S(1)}, u32[]{:S(2)}) %copy-start.1) | copy-done | bytes 524312
  23.4 3.1 %shard_map.60 = f32[1,2,256,256]{3,2,1,0:T(8,128)S(1)} custom-call(s32[1]{0:T(128)} %sub.14.rows_ref, s32[1]{0:T(128)} %bitcast.4.columns_ref, s32[1]{0:T(128)} %bitcast.order_ref, f32[1,2,256,512]{3,2,1,0:T(8,128)} %tile_ref.1, f32[1,2,256,256]{3,2,1,0:T(8,128)} %collective-permute-done.2.mine_ref, f32[1,2,256,256]{3,2,1,0:T(8,128)} %copy-done.1), custom_call_target="tpu_custom_call" | custom-call | tf_op jit(solution)/shard_map/pallas_call | solution.py:279
  26.6 2.0 %conditional.3 = (bf16[1,2,256,256]{3,2,1,0:T(8,128)(2,1)}) conditional(s32[]{:T(128)} %convert_element_type.125, () %tuple.46, (bf16[1,2,256,256]{3,2,1,0:T(8,128)(2,1)S(1)}, f32[1,2,256,256]{3,2,1,0:T(8,128)S(1)}, f32[2,256,256]{2,1,0:T(8,128)S(1)}, bf16[512,512]{1,0:T(8,128)(2,1)S(1)}, bf16[512,512]{1,0:T(8,128)(2,1)S(1)}, ...), branch_computations={%region_0.1_spmd, %region_1.2_spmd} | conditional | bytes 262154 | solution.py:476
  26.6 1.9 %branch_1_fun.3 = bf16[1,2,256,256]{3,2,1,0:T(8,128)(2,1)} custom-call(bf16[1,2,256,256]{3,2,1,0:T(8,128)(2,1)S(1)} %get-tuple-element.109.refs_0_, f32[1,2,256,256]{3,2,1,0:T(8,128)S(1)} %get-tuple-element.110.refs_1_, f32[2,256,256]{2,1,0:T(8,128)S(1)} %get-tuple-element.111.refs_2_, bf16[512,512]{1,0:T(8,128)(2,1)S(1)} %get-tuple-element.112.refs_3_, ...), custom_call_target="tpu_custom_call" | custom-call | tf_op jit(solution)/shard_map/cond/branch_1_fun/pallas_call | solution.py:197
  28.5 3.0 %collective-permute-start.4 = (bf16[1,2,256,256]{3,2,1,0:T(8,128)(2,1)}, bf16[1,2,256,256]{3,2,1,0:T(8,128)(2,1)}, u32[]{:S(2)}, u32[]{:S(2)}) collective-permute-start(bf16[1,2,256,256]{3,2,1,0:T(8,128)(2,1)} %get-tuple-element.179), channel_id=1, source_target_pairs={{0,2},{1,3},{4,6},{5,7},{8,10},{9,11},{12,14},{13,15},{16,18},{17,... | collective-permute-start | bytes 786440 | tf_op jit(solution)/shard_map/ppermute | solution.py:491
  32.7 4.6 %collective-permute-done.4 = bf16[1,2,256,256]{3,2,1,0:T(8,128)(2,1)} collective-permute-done((bf16[1,2,256,256]{3,2,1,0:T(8,128)(2,1)}, bf16[1,2,256,256]{3,2,1,0:T(8,128)(2,1)}, u32[]{:S(2)}, u32[]{:S(2)}) %collective-permute-start.4) | collective-permute-done | bytes 262176 | tf_op jit(solution)/shard_map/ppermute | solution.py:491
  37.4 1.8 %conditional.4 = ((bf16[1,2,256,256]{3,2,1,0:T(8,128)(2,1)}, bf16[2,512,512]{2,1,0:T(8,128)(2,1)})) conditional(s32[]{:T(128)} %convert_element_type.126, () %tuple.45, (s32[1]{0:T(128)}, s32[1]{0:T(128)}, s32[1]{0:T(128)}, s32[1]{0:T(128)}, s32[1]{0:T(128)}, /*index=5*/bf16[1,2,256,256]{3,2,1,0:T(8,128)(2,1)}, f32[1,2,256,256]{3,2,1,0:T(8,128)S(1)}, ...), branch_computations={%region_2.3_spmd, %region_3.4_spmd} | conditional | bytes 1310748 | solution.py:492
  37.4 0.7 broadcast.204
  38.1 1.0 %broadcast.205 = bf16[2,512,512]{2,1,0:T(8,128)(2,1)} broadcast(bf16[]{:T(256)} %constant.95.clone), dimensions={} | broadcast | bytes 1048578 | tf_op jit(solution)/shard_map/broadcast.12
  39.1 1.3 %collective-permute-start.6 = (bf16[1,2,256,256]{3,2,1,0:T(8,128)(2,1)}, bf16[1,2,256,256]{3,2,1,0:T(8,128)(2,1)}, u32[]{:S(2)}, u32[]{:S(2)}) collective-permute-start(bf16[1,2,256,256]{3,2,1,0:T(8,128)(2,1)} %get-tuple-element.147), channel_id=1, source_target_pairs={{2,0},{3,1},{6,4},{7,5},{10,8},{11,9},{14,12},{15,13},{18,16},{19,... | collective-permute-start | bytes 786440 | tf_op jit(solution)/shard_map/ppermute | solution.py:503
  40.4 13.2 %collective-permute-done.6 = bf16[1,2,256,256]{3,2,1,0:T(8,128)(2,1)} collective-permute-done((bf16[1,2,256,256]{3,2,1,0:T(8,128)(2,1)}, bf16[1,2,256,256]{3,2,1,0:T(8,128)(2,1)}, u32[]{:S(2)}, u32[]{:S(2)}) %collective-permute-start.6) | collective-permute-done | bytes 262176 | tf_op jit(solution)/shard_map/ppermute | solution.py:503
  53.6 4.6 %conditional.5 = (bf16[2,512,512]{2,1,0:T(8,128)(2,1)}) conditional(s32[]{:T(128)} %convert_element_type.125, bf16[2,512,512]{2,1,0:T(8,128)(2,1)} %get-tuple-element.146, (s32[1]{0:T(128)}, s32[1]{0:T(128)}, s32[1]{0:T(128)}, s32[1]{0:T(128)}, s32[1]{0:T(128)}, /*index=5*/bf16[1,2,256,256]{3,2,1,0:T(8,128)(2,1)}, f32[1,2,256,256]{3,2,1,0:T(8,128)S(1)}, ...), branch_computations={%region_4.5_spmd, %region_5.6_spmd} | conditional | bytes 8 | solution.py:504
  53.6 4.6 %branch_1_fun.5 = (bf16[1,2,256,256]{3,2,1,0:T(8,128)(2,1)}, bf16[2,512,512]{2,1,0:T(8,128)(2,1)}) custom-call(s32[1]{0:T(128)} %get-tuple-element.130.rows_ref, s32[1]{0:T(128)} %get-tuple-element.131.columns_ref, s32[1]{0:T(128)} %get-tuple-element.132.live_ref, s32[1]{0:T(128)} %get-tuple-element.133.slot_ref, s32[1]{0:T(128)} %get-tuple-element.134.other_ref, ...), custom_call_target="tpu_custom_call" | custom-call | tf_op jit(solution)/shard_map/cond/branch_1_fun/pallas_call | solution.py:402
  58.2 2.9 %collective-permute-done.7 = bf16[2,512,512]{2,1,0:T(8,128)(2,1)S(1)} collective-permute-done((bf16[2,512,512]{2,1,0:T(8,128)(2,1)}, bf16[2,512,512]{2,1,0:T(8,128)(2,1)S(1)}, u32[]{:S(2)}, u32[]{:S(2)}) %collective-permute-start.7) | collective-permute-done | bytes 1048608 | tf_op jit(solution)/shard_map/ppermute | solution.py:507
  61.1 1.5 %convert_add_fusion = f32[2,512,512]{2,1,0:T(8,128)S(1)} fusion(bf16[2,512,512]{2,1,0:T(8,128)(2,1)S(1)} %collective-permute-done.7, bf16[2,512,512]{2,1,0:T(8,128)(2,1)} %get-tuple-element.181), kind=kLoop, calls=%fused_computation | loop fusion | flops 1572864 | bytes 4194304 | tf_op jit(solution)/shard_map/add | solution.py:508
  62.8 3.5 %collective-permute-start.8 = (bf16[2,256,256]{2,1,0:T(8,128)(2,1)S(1)}, bf16[2,256,256]{2,1,0:T(8,128)(2,1)S(1)}, u32[]{:S(2)}, u32[]{:S(2)}) collective-permute-start(bf16[2,256,256]{2,1,0:T(8,128)(2,1)S(1)} %dynamic-slice_convert_fusion), channel_id=1, source_target_pairs={{0,4},{4,8},{8,12},{1,5},{5,9},{9,13},{2,6},{6,10},{10,14},{3,7},{... | collective-permute-start | bytes 786440 | tf_op jit(solution)/shard_map/ppermute | solution.py:510
  66.3 5.8 %collective-permute-done.8 = bf16[2,256,256]{2,1,0:T(8,128)(2,1)S(1)} collective-permute-done((bf16[2,256,256]{2,1,0:T(8,128)(2,1)S(1)}, bf16[2,256,256]{2,1,0:T(8,128)(2,1)S(1)}, u32[]{:S(2)}, u32[]{:S(2)}) %collective-permute-start.8) | collective-permute-done | bytes 262176 | tf_op jit(solution)/shard_map/ppermute | solution.py:510
  72.1 1.5 %collective-permute-done.9 = bf16[2,256,256]{2,1,0:T(8,128)(2,1)S(1)} collective-permute-done((bf16[2,256,256]{2,1,0:T(8,128)(2,1)S(1)}, bf16[2,256,256]{2,1,0:T(8,128)(2,1)S(1)}, u32[]{:S(2)}, u32[]{:S(2)}) %collective-permute-start.9) | collective-permute-done | bytes 262176 | tf_op jit(solution)/shard_map/ppermute | solution.py:513
  73.6 1.2 %fusion = f32[1,2,256,512]{3,2,1,0:T(8,128)} fusion(f32[2,512,512]{2,1,0:T(8,128)S(1)} %convert_add_fusion, bf16[2,256,256]{2,1,0:T(8,128)(2,1)S(1)} %collective-permute-done.9, bf16[2,256,256]{2,1,0:T(8,128)(2,1)S(1)} %collective-permute-done.8, pred[]{:T(512)} %eq.26), kind=kLoop, calls=%fused_computation.2 | loop fusion | flops 2883584 | bytes 2621441 | tf_op jit(solution)/shard_map/broadcast_in_dim | solution.py:520
  (19 shorter events, 0.2 us)
Async XLA Ops:
  0.0 18.7 %collective-permute-start.1 = (s32[1]{0:T(128)}, s32[1]{0:T(128)}, u32[]{:S(2)}, u32[]{:S(2)}) collective-permute-start(s32[1]{0:T(128)} %param.18), channel_id=1, source_target_pairs={{0,1},{1,0},{2,3},{3,2},{4,5},{5,4},{6,7},{7,6},{8,9},{9,8},{10,11... | collective-permute-start | bytes 20 | tf_op jit(solution)/shard_map/ppermute | solution.py:431
  0.5 20.8 %collective-permute-start = (s32[2,2]{1,0:T(2,128)}, s32[2,2]{1,0:T(2,128)S(1)}, u32[]{:S(2)}, u32[]{:S(2)}) collective-permute-start(s32[2,2]{1,0:T(2,128)} %param.17), channel_id=1, source_target_pairs={{0,1},{1,0},{2,3},{3,2},{4,5},{5,4},{6,7},{7,6},{8,9},{9,8},{10,11... | collective-permute-start | bytes 56 | tf_op jit(solution)/shard_map/ppermute | solution.py:430
  1.6 17.1 %collective-permute-start.2 = (f32[1,2,256,256]{3,2,1,0:T(8,128)S(1)}, f32[1,2,256,256]{3,2,1,0:T(8,128)}, u32[]{:S(2)}, u32[]{:S(2)}) collective-permute-start(f32[1,2,256,256]{3,2,1,0:T(8,128)S(1)} %constant_dynamic-slice_fusion.1), channel_id=1, source_target_pairs={{4,0},{8,4},{12,8},{5,1},{9,5},{13,9},{6,2},{10,6},{14,10},{7,3},{... | collective-permute-start | bytes 1572872 | tf_op jit(solution)/shard_map/ppermute | solution.py:18
  2.9 29.8 %collective-permute-start.5 = (f32[2,256,256]{2,1,0:T(8,128)}, f32[2,256,256]{2,1,0:T(8,128)}, u32[]{:S(2)}, u32[]{:S(2)}) collective-permute-start(f32[2,256,256]{2,1,0:T(8,128)} %param.19), channel_id=1, source_target_pairs={{0,1},{1,0},{2,3},{3,2},{4,5},{5,4},{6,7},{7,6},{8,9},{9,8},{10,11... | collective-permute-start | bytes 1572872 | tf_op jit(solution)/shard_map/ppermute | solution.py:432
  8.5 12.8 %copy-start.2 = (s32[2,2]{1,0:T(2,128)S(1)}, s32[2,2]{1,0:T(2,128)}, u32[]{:S(2)}) copy-start(s32[2,2]{1,0:T(2,128)} %param.17) | copy-start | bytes 52
  9.5 17.0 %copy-start = (bf16[2,256,256]{2,1,0:T(8,128)(2,1)S(1)}, bf16[2,256,256]{2,1,0:T(8,128)(2,1)}, u32[]{:S(2)}) copy-start(bf16[2,256,256]{2,1,0:T(8,128)(2,1)} %param.16) | copy-start | bytes 786436
  18.7 3.9 %collective-permute-start.3 = (f32[1,2,256,256]{3,2,1,0:T(8,128)}, f32[1,2,256,256]{3,2,1,0:T(8,128)S(1)}, u32[]{:S(2)}, u32[]{:S(2)}) collective-permute-start(f32[1,2,256,256]{3,2,1,0:T(8,128)} %collective-permute-done.2.mine_ref), channel_id=1, source_target_pairs={{0,1},{1,0},{2,3},{3,2},{4,5},{5,4},{6,7},{7,6},{8,9},{9,8},{10,11... | collective-permute-start | bytes 1572872 | tf_op jit(solution)/shard_map/ppermute | solution.py:426
  22.6 0.8 %copy-start.1 = (f32[1,2,256,256]{3,2,1,0:T(8,128)}, f32[1,2,256,256]{3,2,1,0:T(8,128)S(1)}, u32[]{:S(2)}) copy-start(f32[1,2,256,256]{3,2,1,0:T(8,128)S(1)} %collective-permute-done.3.partner_ref) | copy-start | bytes 1572868
  28.5 8.9 %collective-permute-start.4 = (bf16[1,2,256,256]{3,2,1,0:T(8,128)(2,1)}, bf16[1,2,256,256]{3,2,1,0:T(8,128)(2,1)}, u32[]{:S(2)}, u32[]{:S(2)}) collective-permute-start(bf16[1,2,256,256]{3,2,1,0:T(8,128)(2,1)} %get-tuple-element.179), channel_id=1, source_target_pairs={{0,2},{1,3},{4,6},{5,7},{8,10},{9,11},{12,14},{13,15},{16,18},{17,... | collective-permute-start | bytes 786440 | tf_op jit(solution)/shard_map/ppermute | solution.py:491
  39.1 14.5 %collective-permute-start.6 = (bf16[1,2,256,256]{3,2,1,0:T(8,128)(2,1)}, bf16[1,2,256,256]{3,2,1,0:T(8,128)(2,1)}, u32[]{:S(2)}, u32[]{:S(2)}) collective-permute-start(bf16[1,2,256,256]{3,2,1,0:T(8,128)(2,1)} %get-tuple-element.147), channel_id=1, source_target_pairs={{2,0},{3,1},{6,4},{7,5},{10,8},{11,9},{14,12},{15,13},{18,16},{19,... | collective-permute-start | bytes 786440 | tf_op jit(solution)/shard_map/ppermute | solution.py:503
  58.2 2.9 %collective-permute-start.7 = (bf16[2,512,512]{2,1,0:T(8,128)(2,1)}, bf16[2,512,512]{2,1,0:T(8,128)(2,1)S(1)}, u32[]{:S(2)}, u32[]{:S(2)}) collective-permute-start(bf16[2,512,512]{2,1,0:T(8,128)(2,1)} %get-tuple-element.181), channel_id=1, source_target_pairs={{0,1},{1,0},{2,3},{3,2},{4,5},{5,4},{6,7},{7,6},{8,9},{9,8},{10,11... | collective-permute-start | bytes 3145736 | tf_op jit(solution)/shard_map/ppermute | solution.py:507
  62.8 9.3 %collective-permute-start.8 = (bf16[2,256,256]{2,1,0:T(8,128)(2,1)S(1)}, bf16[2,256,256]{2,1,0:T(8,128)(2,1)S(1)}, u32[]{:S(2)}, u32[]{:S(2)}) collective-permute-start(bf16[2,256,256]{2,1,0:T(8,128)(2,1)S(1)} %dynamic-slice_convert_fusion), channel_id=1, source_target_pairs={{0,4},{4,8},{8,12},{1,5},{5,9},{9,13},{2,6},{6,10},{10,14},{3,7},{... | collective-permute-start | bytes 786440 | tf_op jit(solution)/shard_map/ppermute | solution.py:510
  72.1 1.5 %collective-permute-start.9 = (bf16[2,256,256]{2,1,0:T(8,128)(2,1)S(1)}, bf16[2,256,256]{2,1,0:T(8,128)(2,1)S(1)}, u32[]{:S(2)}, u32[]{:S(2)}) collective-permute-start(bf16[2,256,256]{2,1,0:T(8,128)(2,1)S(1)} %collective-permute-done.8), channel_id=1, source_target_pairs={{0,1},{1,0},{2,3},{3,2},{4,5},{5,4},{6,7},{7,6},{8,9},{9,8},{10,11... | collective-permute-start | bytes 786440 | tf_op jit(solution)/shard_map/ppermute | solution.py:513

commit v6 on v5

--- a/solution.py
+++ b/solution.py
@@ -253,8 +253,8 @@
     column_shift = (columns_all - columns_ref[index]) % columns_all
     first = order_ref[0] == 0
     for part in range(2):
-        mine = mine_ref[0, part]
-        partner = partner_ref[0, part]
+        mine = mine_ref[0, part].astype(jnp.float32)
+        partner = partner_ref[0, part].astype(jnp.float32)
         rim = jnp.concatenate(
             [jnp.where(first, mine, partner), jnp.where(first, partner, mine)], axis=1
         )
@@ -421,7 +421,7 @@
     batch_count = lax.axis_size("batch")
     half = columns_all // batch_count
     wanted = lax.dynamic_slice_in_dim(object_field[:, :, :width, :], batch_index * half, half, 3)
-    mine = from_behind(wanted, "tile", -1)
+    mine = from_behind(wanted.astype(jnp.bfloat16), "tile", -1)
     pairs = [(b, (b + 1) % batch_count) for b in range(batch_count)]
     partner = lax.ppermute(mine, "batch", pairs)
     capacity = positions.shape[0]

time: 75.2 us -> 66.3 us (0.88)
  waiting for transfers between devices: 35.8 us -> 29.6 us
  other arithmetic: 10.3 us -> 7.66 us
    ppermute x1, waiting for transfers between devices: 7.7 us -> 2.02 us  [from_behind(): return lax.ppermute(block, axis, route)]
    concatenate x1, other arithmetic: 1.49 us -> 0.17 us  [dft_right(): return jnp.concatenate([upper, lower], axis=0)]
    dynamic_slice x1 -> x0, local copies, waits for them, and re-layouts: 1.08 us -> none  [local(): lax.dynamic_slice_in_dim(object_field[:, :, :width, :], batch_index * hal...]
    convert_element_type x0 -> x1, local copies, waits for them, and re-layouts: none -> 1.07 us  [local(): mine = from_behind(wanted.astype(jnp.bfloat16), 'tile', -1)]
  transfers between devices with their start and end apart: 10 -> 10, of which waited for: 6 -> 7; matrix products, arithmetic and copies ran while one was open for 13% -> 11% of each run, Pallas kernels for 7% -> 7%
where the time goes in v6:
time: 66.3 us; the launch traced here: 65.9 us
  waiting for transfers between devices  29.6 us (45%)
  starting transfers between devices  10.4 us (16%)
  Pallas kernels  9.34 us (14%)
  other arithmetic  7.66 us (12%)
  local copies, waits for them, and re-layouts  4.89 us (7%)
  between operations  3.93 us (6%)
    ppermute x1, waiting for transfers between devices, local(): carry = lax.ppermute(carry, 'depth', [(turn + 1, turn)])  12.8 us
    ppermute x1, waiting for transfers between devices, local(): lax.ppermute(spill.astype(jnp.bfloat16), 'tile', [(t, t + 1) for t in ran...  5.83 us
    pallas_call x1, Pallas kernels, run_adjoint(): pl.pallas_call(adjoint_kernel(last), grid_spec=grid_spec, out_shape=(jax....  4.56 us
    ppermute x1, waiting for transfers between devices, local(): carry = lax.ppermute(carry, 'depth', [(depth_count - 2, depth_count - 1)])  4.28 us
    ppermute x1, starting transfers between devices, local(): lax.ppermute(spill.astype(jnp.bfloat16), 'tile', [(t, t + 1) for t in ran...  3.79 us
    ppermute x1, starting transfers between devices, local(): carry = lax.ppermute(carry, 'depth', [(depth_count - 2, depth_count - 1)])  3.04 us
    ppermute x1, waiting for transfers between devices, local(): other = lax.ppermute(gradient, 'batch', pairs)  2.87 us
    pallas_call x1, Pallas kernels, cut_patches(): pl.pallas_call(cut_kernel, grid_spec=grid_spec, out_shape=jax.ShapeDtypeS...  2.86 us
  transfers between devices with their start and end apart: 10, of which 7 were waited for; matrix products, arithmetic and copies ran while one was open for 11% of the time, Pallas kernels for 7%

profile of v6, /device:TPU:0, one launch (start us, length us, event | category | flops | bytes accessed | tf_op | source)
XLA Modules:
  0.0 65.9 jit_solution(6043811005338434205)
XLA Ops:
  0.0 0.5 collective-permute-start.1
  0.5 1.1 %dynamic-slice_convert_fusion.1 = bf16[1,2,256,256]{3,2,1,0:T(8,128)(2,1)S(1)} fusion(f32[1,2,256,512]{3,2,1,0:T(8,128)} %tile_ref.1, s32[]{:T(128)S(6)} %select_n.111), kind=kLoop, calls=%fused_computation.18 | loop fusion | bytes 524292 | tf_op jit(solution)/shard_map/convert_element_type | solution.py:424
  1.6 1.3 %collective-permute-start.2 = (bf16[1,2,256,256]{3,2,1,0:T(8,128)(2,1)S(1)}, bf16[1,2,256,256]{3,2,1,0:T(8,128)(2,1)S(1)}, u32[]{:S(2)}, u32[]{:S(2)}) collective-permute-start(bf16[1,2,256,256]{3,2,1,0:T(8,128)(2,1)S(1)} %dynamic-slice_convert_fusion.1), channel_id=1, source_target_pairs={{4,0},{8,4},{12,8},{5,1},{9,5},{13,9},{6,2},{10,6},{14,10},{7,3},{... | collective-permute-start | bytes 786440 | tf_op jit(solution)/shard_map/ppermute | solution.py:18
  2.9 0.5 collective-permute-start.5
  3.4 1.0 %multiply_convert_fusion.2 = bf16[256,256]{1,0:T(8,128)(2,1)S(1)} fusion(), kind=kLoop, calls=%fused_computation.27 | loop fusion | flops 1048576 | bytes 131072 | tf_op jit(solution)/shard_map/convert_element_type | solution.py:26
  4.4 1.0 %fusion.14 = (bf16[256,256]{1,0:T(8,128)(2,1)S(1)}, bf16[256,256]{1,0:T(8,128)(2,1)S(1)}) fusion(), kind=kLoop, calls=%fused_computation.35 | loop fusion | flops 1572864 | bytes 262144 | tf_op jit(solution)/shard_map/neg | solution.py:28
  5.4 1.0 %multiply_convert_fusion = (bf16[256,256]{1,0:T(8,128)(2,1)S(1)}, bf16[256,256]{1,0:T(8,128)(2,1)S(1)}) fusion(), kind=kLoop, calls=%fused_computation.25 | loop fusion | flops 1179648 | bytes 262144 | tf_op jit(solution)/shard_map/convert_element_type | solution.py:27
  6.4 1.0 %fusion.11 = (f32[1,256,256]{2,1,0:T(8,128)S(1)}, f32[1,256,256]{2,1,0:T(8,128)S(1)}) fusion(s32[256]{0:T(256)S(1)} %fusion.17, f32[]{:T(128)S(6)} %neg.15), kind=kLoop, calls=%fused_computation.32 | loop fusion | flops 196608 | bytes 525316 | tf_op jit(solution)/shard_map/cos | solution.py:51
  8.4 0.8 %broadcast_select_fusion = s32[2]{0:T(128)S(1)} fusion(pred[]{:T(512)} %eq.26, s32[1]{0:T(128)} %collective-permute-done.1, s32[1]{0:T(128)S(6)} %copy.14), kind=kLoop, calls=%fused_computation.44 | loop fusion | flops 6 | bytes 17 | tf_op jit(solution)/shard_map/jit(_where)/select_n | solution.py:438
  9.1 0.7 %fusion.19 = (s32[1]{0:T(128)}, s32[1]{0:T(128)}) fusion(s32[2]{0:T(128)S(1)} %broadcast_select_fusion), kind=kLoop, calls=%fused_computation.46 | loop fusion | bytes 16 | tf_op jit(solution)/shard_map/slice | solution.py:442
  11.0 2.0 %collective-permute-done.2.mine_ref = bf16[1,2,256,256]{3,2,1,0:T(8,128)(2,1)S(1)} collective-permute-done((bf16[1,2,256,256]{3,2,1,0:T(8,128)(2,1)S(1)}, bf16[1,2,256,256]{3,2,1,0:T(8,128)(2,1)S(1)}, u32[]{:S(2)}, u32[]{:S(2)}) %collective-permute-start.2) | collective-permute-done | bytes 262176 | tf_op jit(solution)/shard_map/ppermute | solution.py:18
  13.0 0.6 fusion.20
  14.2 0.3 collective-permute-done.3.partner_ref
  14.5 0.7 %copy-done.2 = bf16[1,2,256,256]{3,2,1,0:T(8,128)(2,1)} copy-done((bf16[1,2,256,256]{3,2,1,0:T(8,128)(2,1)}, bf16[1,2,256,256]{3,2,1,0:T(8,128)(2,1)S(1)}, u32[]{:S(2)}) %copy-start.2) | copy-done | bytes 262168
  15.2 2.9 %shard_map.60 = f32[1,2,256,256]{3,2,1,0:T(8,128)S(1)} custom-call(s32[1]{0:T(128)} %sub.14.rows_ref, s32[1]{0:T(128)} %bitcast.4.columns_ref, s32[1]{0:T(128)} %bitcast.order_ref, f32[1,2,256,512]{3,2,1,0:T(8,128)} %tile_ref.1, bf16[1,2,256,256]{3,2,1,0:T(8,128)(2,1)} %copy-done.1, bf16[1,2,256,256]{3,2,1,0:T(8,128)(2,1)} %copy-done.2), custom_call_target="tpu_custom_call" | custom-call | tf_op jit(solution)/shard_map/pallas_call | solution.py:279
  18.1 2.0 %conditional.3 = (bf16[1,2,256,256]{3,2,1,0:T(8,128)(2,1)}) conditional(s32[]{:T(128)} %convert_element_type.128, () %tuple.46, (bf16[1,2,256,256]{3,2,1,0:T(8,128)(2,1)S(1)}, f32[1,2,256,256]{3,2,1,0:T(8,128)S(1)}, f32[2,256,256]{2,1,0:T(8,128)S(1)}, bf16[512,512]{1,0:T(8,128)(2,1)S(1)}, bf16[512,512]{1,0:T(8,128)(2,1)S(1)}, ...), branch_computations={%region_0.1_spmd, %region_1.2_spmd} | conditional | bytes 262154 | solution.py:476
  18.1 1.9 %branch_1_fun.3 = bf16[1,2,256,256]{3,2,1,0:T(8,128)(2,1)} custom-call(bf16[1,2,256,256]{3,2,1,0:T(8,128)(2,1)S(1)} %get-tuple-element.109.refs_0_, f32[1,2,256,256]{3,2,1,0:T(8,128)S(1)} %get-tuple-element.110.refs_1_, f32[2,256,256]{2,1,0:T(8,128)S(1)} %get-tuple-element.111.refs_2_, bf16[512,512]{1,0:T(8,128)(2,1)S(1)} %get-tuple-element.112.refs_3_, ...), custom_call_target="tpu_custom_call" | custom-call | tf_op jit(solution)/shard_map/cond/branch_1_fun/pallas_call | solution.py:197
  20.0 3.0 %collective-permute-start.4 = (bf16[1,2,256,256]{3,2,1,0:T(8,128)(2,1)}, bf16[1,2,256,256]{3,2,1,0:T(8,128)(2,1)}, u32[]{:S(2)}, u32[]{:S(2)}) collective-permute-start(bf16[1,2,256,256]{3,2,1,0:T(8,128)(2,1)} %get-tuple-element.179), channel_id=1, source_target_pairs={{0,2},{1,3},{4,6},{5,7},{8,10},{9,11},{12,14},{13,15},{16,18},{17,... | collective-permute-start | bytes 786440 | tf_op jit(solution)/shard_map/ppermute | solution.py:491
  24.4 4.3 %collective-permute-done.4 = bf16[1,2,256,256]{3,2,1,0:T(8,128)(2,1)} collective-permute-done((bf16[1,2,256,256]{3,2,1,0:T(8,128)(2,1)}, bf16[1,2,256,256]{3,2,1,0:T(8,128)(2,1)}, u32[]{:S(2)}, u32[]{:S(2)}) %collective-permute-start.4) | collective-permute-done | bytes 262176 | tf_op jit(solution)/shard_map/ppermute | solution.py:491
  28.6 1.8 %conditional.4 = ((bf16[1,2,256,256]{3,2,1,0:T(8,128)(2,1)}, bf16[2,512,512]{2,1,0:T(8,128)(2,1)})) conditional(s32[]{:T(128)} %convert_element_type.129, () %tuple.45, (s32[1]{0:T(128)}, s32[1]{0:T(128)}, s32[1]{0:T(128)}, s32[1]{0:T(128)}, s32[1]{0:T(128)}, /*index=5*/bf16[1,2,256,256]{3,2,1,0:T(8,128)(2,1)}, f32[1,2,256,256]{3,2,1,0:T(8,128)S(1)}, ...), branch_computations={%region_2.3_spmd, %region_3.4_spmd} | conditional | bytes 1310748 | solution.py:492
  28.6 0.7 %broadcast.204 = bf16[1,2,256,256]{3,2,1,0:T(8,128)(2,1)} broadcast(bf16[]{:T(256)} %constant.95.clone), dimensions={} | broadcast | bytes 262146 | tf_op jit(solution)/shard_map/broadcast.13
  29.4 1.0 %broadcast.205 = bf16[2,512,512]{2,1,0:T(8,128)(2,1)} broadcast(bf16[]{:T(256)} %constant.95.clone), dimensions={} | broadcast | bytes 1048578 | tf_op jit(solution)/shard_map/broadcast.12
  30.4 1.3 %collective-permute-start.6 = (bf16[1,2,256,256]{3,2,1,0:T(8,128)(2,1)}, bf16[1,2,256,256]{3,2,1,0:T(8,128)(2,1)}, u32[]{:S(2)}, u32[]{:S(2)}) collective-permute-start(bf16[1,2,256,256]{3,2,1,0:T(8,128)(2,1)} %get-tuple-element.147), channel_id=1, source_target_pairs={{2,0},{3,1},{6,4},{7,5},{10,8},{11,9},{14,12},{15,13},{18,16},{19,... | collective-permute-start | bytes 786440 | tf_op jit(solution)/shard_map/ppermute | solution.py:503
  31.7 12.8 %collective-permute-done.6 = bf16[1,2,256,256]{3,2,1,0:T(8,128)(2,1)} collective-permute-done((bf16[1,2,256,256]{3,2,1,0:T(8,128)(2,1)}, bf16[1,2,256,256]{3,2,1,0:T(8,128)(2,1)}, u32[]{:S(2)}, u32[]{:S(2)}) %collective-permute-start.6) | collective-permute-done | bytes 262176 | tf_op jit(solution)/shard_map/ppermute | solution.py:503
  44.5 4.6 %conditional.5 = (bf16[2,512,512]{2,1,0:T(8,128)(2,1)}) conditional(s32[]{:T(128)} %convert_element_type.128, bf16[2,512,512]{2,1,0:T(8,128)(2,1)} %get-tuple-element.146, (s32[1]{0:T(128)}, s32[1]{0:T(128)}, s32[1]{0:T(128)}, s32[1]{0:T(128)}, s32[1]{0:T(128)}, /*index=5*/bf16[1,2,256,256]{3,2,1,0:T(8,128)(2,1)}, f32[1,2,256,256]{3,2,1,0:T(8,128)S(1)}, ...), branch_computations={%region_4.5_spmd, %region_5.6_spmd} | conditional | bytes 8 | solution.py:504
  44.5 4.6 %branch_1_fun.5 = (bf16[1,2,256,256]{3,2,1,0:T(8,128)(2,1)}, bf16[2,512,512]{2,1,0:T(8,128)(2,1)}) custom-call(s32[1]{0:T(128)} %get-tuple-element.130.rows_ref, s32[1]{0:T(128)} %get-tuple-element.131.columns_ref, s32[1]{0:T(128)} %get-tuple-element.132.live_ref, s32[1]{0:T(128)} %get-tuple-element.133.slot_ref, s32[1]{0:T(128)} %get-tuple-element.134.other_ref, ...), custom_call_target="tpu_custom_call" | custom-call | tf_op jit(solution)/shard_map/cond/branch_1_fun/pallas_call | solution.py:402
  49.1 2.9 %collective-permute-done.7 = bf16[2,512,512]{2,1,0:T(8,128)(2,1)S(1)} collective-permute-done((bf16[2,512,512]{2,1,0:T(8,128)(2,1)}, bf16[2,512,512]{2,1,0:T(8,128)(2,1)S(1)}, u32[]{:S(2)}, u32[]{:S(2)}) %collective-permute-start.7) | collective-permute-done | bytes 1048608 | tf_op jit(solution)/shard_map/ppermute | solution.py:507
  51.9 1.5 %convert_add_fusion = f32[2,512,512]{2,1,0:T(8,128)S(1)} fusion(bf16[2,512,512]{2,1,0:T(8,128)(2,1)S(1)} %collective-permute-done.7, bf16[2,512,512]{2,1,0:T(8,128)(2,1)} %get-tuple-element.181), kind=kLoop, calls=%fused_computation | loop fusion | flops 1572864 | bytes 4194304 | tf_op jit(solution)/shard_map/add | solution.py:508
  53.6 3.8 %collective-permute-start.8 = (bf16[2,256,256]{2,1,0:T(8,128)(2,1)S(1)}, bf16[2,256,256]{2,1,0:T(8,128)(2,1)S(1)}, u32[]{:S(2)}, u32[]{:S(2)}) collective-permute-start(bf16[2,256,256]{2,1,0:T(8,128)(2,1)S(1)} %dynamic-slice_convert_fusion), channel_id=1, source_target_pairs={{0,4},{4,8},{8,12},{1,5},{5,9},{9,13},{2,6},{6,10},{10,14},{3,7},{... | collective-permute-start | bytes 786440 | tf_op jit(solution)/shard_map/ppermute | solution.py:510
  57.4 5.8 %collective-permute-done.8 = bf16[2,256,256]{2,1,0:T(8,128)(2,1)S(1)} collective-permute-done((bf16[2,256,256]{2,1,0:T(8,128)(2,1)S(1)}, bf16[2,256,256]{2,1,0:T(8,128)(2,1)S(1)}, u32[]{:S(2)}, u32[]{:S(2)}) %collective-permute-start.8) | collective-permute-done | bytes 262176 | tf_op jit(solution)/shard_map/ppermute | solution.py:510
  63.2 1.5 %collective-permute-done.9 = bf16[2,256,256]{2,1,0:T(8,128)(2,1)S(1)} collective-permute-done((bf16[2,256,256]{2,1,0:T(8,128)(2,1)S(1)}, bf16[2,256,256]{2,1,0:T(8,128)(2,1)S(1)}, u32[]{:S(2)}, u32[]{:S(2)}) %collective-permute-start.9) | collective-permute-done | bytes 262176 | tf_op jit(solution)/shard_map/ppermute | solution.py:513
  64.8 1.2 %fusion = f32[1,2,256,512]{3,2,1,0:T(8,128)} fusion(f32[2,512,512]{2,1,0:T(8,128)S(1)} %convert_add_fusion, bf16[2,256,256]{2,1,0:T(8,128)(2,1)S(1)} %collective-permute-done.9, bf16[2,256,256]{2,1,0:T(8,128)(2,1)S(1)} %collective-permute-done.8, pred[]{:T(512)} %eq.26), kind=kLoop, calls=%fused_computation.2 | loop fusion | flops 2883584 | bytes 2621441 | tf_op jit(solution)/shard_map/broadcast_in_dim | solution.py:520
  (21 shorter events, 0.4 us)
Async XLA Ops:
  0.0 8.4 %collective-permute-start.1 = (s32[1]{0:T(128)}, s32[1]{0:T(128)}, u32[]{:S(2)}, u32[]{:S(2)}) collective-permute-start(s32[1]{0:T(128)} %param.18), channel_id=1, source_target_pairs={{0,1},{1,0},{2,3},{3,2},{4,5},{5,4},{6,7},{7,6},{8,9},{9,8},{10,11... | collective-permute-start | bytes 20 | tf_op jit(solution)/shard_map/ppermute | solution.py:431
  0.5 12.5 %collective-permute-start = (s32[2,2]{1,0:T(2,128)}, s32[2,2]{1,0:T(2,128)S(1)}, u32[]{:S(2)}, u32[]{:S(2)}) collective-permute-start(s32[2,2]{1,0:T(2,128)} %param.17), channel_id=1, source_target_pairs={{0,1},{1,0},{2,3},{3,2},{4,5},{5,4},{6,7},{7,6},{8,9},{9,8},{10,11... | collective-permute-start | bytes 56 | tf_op jit(solution)/shard_map/ppermute | solution.py:430
  1.6 11.4 %collective-permute-start.2 = (bf16[1,2,256,256]{3,2,1,0:T(8,128)(2,1)S(1)}, bf16[1,2,256,256]{3,2,1,0:T(8,128)(2,1)S(1)}, u32[]{:S(2)}, u32[]{:S(2)}) collective-permute-start(bf16[1,2,256,256]{3,2,1,0:T(8,128)(2,1)S(1)} %dynamic-slice_convert_fusion.1), channel_id=1, source_target_pairs={{4,0},{8,4},{12,8},{5,1},{9,5},{13,9},{6,2},{10,6},{14,10},{7,3},{... | collective-permute-start | bytes 786440 | tf_op jit(solution)/shard_map/ppermute | solution.py:18
  2.9 21.5 %collective-permute-start.5 = (f32[2,256,256]{2,1,0:T(8,128)}, f32[2,256,256]{2,1,0:T(8,128)}, u32[]{:S(2)}, u32[]{:S(2)}) collective-permute-start(f32[2,256,256]{2,1,0:T(8,128)} %param.19), channel_id=1, source_target_pairs={{0,1},{1,0},{2,3},{3,2},{4,5},{5,4},{6,7},{7,6},{8,9},{9,8},{10,11... | collective-permute-start | bytes 1572872 | tf_op jit(solution)/shard_map/ppermute | solution.py:432
  6.4 6.6 %copy-start.3 = (s32[2,2]{1,0:T(2,128)S(1)}, s32[2,2]{1,0:T(2,128)}, u32[]{:S(2)}) copy-start(s32[2,2]{1,0:T(2,128)} %param.17) | copy-start | bytes 52
  7.6 10.5 %copy-start = (bf16[2,256,256]{2,1,0:T(8,128)(2,1)S(1)}, bf16[2,256,256]{2,1,0:T(8,128)(2,1)}, u32[]{:S(2)}) copy-start(bf16[2,256,256]{2,1,0:T(8,128)(2,1)} %param.16) | copy-start | bytes 786436
  13.0 1.5 %copy-start.1 = (bf16[1,2,256,256]{3,2,1,0:T(8,128)(2,1)}, bf16[1,2,256,256]{3,2,1,0:T(8,128)(2,1)S(1)}, u32[]{:S(2)}) copy-start(bf16[1,2,256,256]{3,2,1,0:T(8,128)(2,1)S(1)} %collective-permute-done.2.mine_ref) | copy-start | bytes 786436
  13.0 1.5 %collective-permute-start.3 = (bf16[1,2,256,256]{3,2,1,0:T(8,128)(2,1)S(1)}, bf16[1,2,256,256]{3,2,1,0:T(8,128)(2,1)S(1)}, u32[]{:S(2)}, u32[]{:S(2)}) collective-permute-start(bf16[1,2,256,256]{3,2,1,0:T(8,128)(2,1)S(1)} %collective-permute-done.2.mine_ref), channel_id=1, source_target_pairs={{0,1},{1,0},{2,3},{3,2},{4,5},{5,4},{6,7},{7,6},{8,9},{9,8},{10,11... | collective-permute-start | bytes 786440 | tf_op jit(solution)/shard_map/ppermute | solution.py:426
  14.5 0.7 %copy-start.2 = (bf16[1,2,256,256]{3,2,1,0:T(8,128)(2,1)}, bf16[1,2,256,256]{3,2,1,0:T(8,128)(2,1)S(1)}, u32[]{:S(2)}) copy-start(bf16[1,2,256,256]{3,2,1,0:T(8,128)(2,1)S(1)} %collective-permute-done.3.partner_ref) | copy-start | bytes 786436
  20.0 8.6 %collective-permute-start.4 = (bf16[1,2,256,256]{3,2,1,0:T(8,128)(2,1)}, bf16[1,2,256,256]{3,2,1,0:T(8,128)(2,1)}, u32[]{:S(2)}, u32[]{:S(2)}) collective-permute-start(bf16[1,2,256,256]{3,2,1,0:T(8,128)(2,1)} %get-tuple-element.179), channel_id=1, source_target_pairs={{0,2},{1,3},{4,6},{5,7},{8,10},{9,11},{12,14},{13,15},{16,18},{17,... | collective-permute-start | bytes 786440 | tf_op jit(solution)/shard_map/ppermute | solution.py:491
  30.4 14.1 %collective-permute-start.6 = (bf16[1,2,256,256]{3,2,1,0:T(8,128)(2,1)}, bf16[1,2,256,256]{3,2,1,0:T(8,128)(2,1)}, u32[]{:S(2)}, u32[]{:S(2)}) collective-permute-start(bf16[1,2,256,256]{3,2,1,0:T(8,128)(2,1)} %get-tuple-element.147), channel_id=1, source_target_pairs={{2,0},{3,1},{6,4},{7,5},{10,8},{11,9},{14,12},{15,13},{18,16},{19,... | collective-permute-start | bytes 786440 | tf_op jit(solution)/shard_map/ppermute | solution.py:503
  49.1 2.9 %collective-permute-start.7 = (bf16[2,512,512]{2,1,0:T(8,128)(2,1)}, bf16[2,512,512]{2,1,0:T(8,128)(2,1)S(1)}, u32[]{:S(2)}, u32[]{:S(2)}) collective-permute-start(bf16[2,512,512]{2,1,0:T(8,128)(2,1)} %get-tuple-element.181), channel_id=1, source_target_pairs={{0,1},{1,0},{2,3},{3,2},{4,5},{5,4},{6,7},{7,6},{8,9},{9,8},{10,11... | collective-permute-start | bytes 3145736 | tf_op jit(solution)/shard_map/ppermute | solution.py:507
  53.6 9.6 %collective-permute-start.8 = (bf16[2,256,256]{2,1,0:T(8,128)(2,1)S(1)}, bf16[2,256,256]{2,1,0:T(8,128)(2,1)S(1)}, u32[]{:S(2)}, u32[]{:S(2)}) collective-permute-start(bf16[2,256,256]{2,1,0:T(8,128)(2,1)S(1)} %dynamic-slice_convert_fusion), channel_id=1, source_target_pairs={{0,4},{4,8},{8,12},{1,5},{5,9},{9,13},{2,6},{6,10},{10,14},{3,7},{... | collective-permute-start | bytes 786440 | tf_op jit(solution)/shard_map/ppermute | solution.py:510
  63.2 1.5 %collective-permute-start.9 = (bf16[2,256,256]{2,1,0:T(8,128)(2,1)S(1)}, bf16[2,256,256]{2,1,0:T(8,128)(2,1)S(1)}, u32[]{:S(2)}, u32[]{:S(2)}) collective-permute-start(bf16[2,256,256]{2,1,0:T(8,128)(2,1)S(1)} %collective-permute-done.8), channel_id=1, source_target_pairs={{0,1},{1,0},{2,3},{3,2},{4,5},{5,4},{6,7},{7,6},{8,9},{9,8},{10,11... | collective-permute-start | bytes 786440 | tf_op jit(solution)/shard_map/ppermute | solution.py:513

commit v7 on v6

--- a/solution.py
+++ b/solution.py
@@ -504,19 +504,22 @@
         carry, gradient = lax.cond(segment == turn, back_pass, back_silent, carry, gradient)
 
     gradient = gradient.astype(jnp.bfloat16)
-    other = lax.ppermute(gradient, "batch", pairs)
-    total = gradient.astype(jnp.float32) + other.astype(jnp.float32)
-    spill = lax.dynamic_slice_in_dim(total[:, tile_rows:, :], batch_index * half, half, 2)
-    arrived = lax.ppermute(
-        spill.astype(jnp.bfloat16), "tile", [(t, t + 1) for t in range(tile_count - 1)]
-    )
+    spill = gradient[:, tile_rows:, :]
+    keep = lax.dynamic_slice_in_dim(spill, batch_index * half, half, 2)
+    give = lax.dynamic_slice_in_dim(spill, (1 - batch_index) * half, half, 2)
+    got = lax.ppermute(give, "batch", pairs)
+    spill_sum = (keep.astype(jnp.float32) + got.astype(jnp.float32)).astype(jnp.bfloat16)
+    arrived = lax.ppermute(spill_sum, "tile", [(t, t + 1) for t in range(tile_count - 1)])
+    own = gradient[:, :tile_rows, :]
+    other = lax.ppermute(own, "batch", pairs)
     arrived_other = lax.ppermute(arrived, "batch", pairs)
     incoming = jnp.where(
         first_core,
         jnp.concatenate([arrived, arrived_other], axis=2),
         jnp.concatenate([arrived_other, arrived], axis=2),
     )
-    summed = total[:, :tile_rows, :].at[:, :width, :].add(incoming.astype(jnp.float32))
+    summed = own.astype(jnp.float32) + other.astype(jnp.float32)
+    summed = summed.at[:, :width, :].add(incoming.astype(jnp.float32))
     return summed[None]
 
 

time: 66.3 us -> 65.9 us (level)
  other arithmetic: 7.66 us -> 6.25 us
  waiting for transfers between devices: 29.6 us -> 28.2 us
  local copies, waits for them, and re-layouts: 4.89 us -> 6.21 us
  starting transfers between devices: 10.4 us -> 11.1 us
    add x1 -> x0, other arithmetic: 1.53 us -> none  [local(): total = gradient.astype(jnp.float32) + other.astype(jnp.float32)]
    ppermute x2 -> x3, waiting for transfers between devices: 8.7 us -> 7.28 us  [the longest x1 5.75 us: local(): lax.ppermute(spill_sum, 'tile', [(t, t + 1) for t in range(tile_count - 1)])]
    slice x1, local copies, waits for them, and re-layouts: 0.07 us -> 1.27 us  [local(): spill = gradient[:, tile_rows:, :]]
    ppermute x2 -> x3, starting transfers between devices: 3.79 us -> 4.4 us  [the longest x1 4.25 us: local(): lax.ppermute(spill_sum, 'tile', [(t, t + 1) for t in range(tile_count - 1)])]
  transfers between devices with their start and end apart: 10 -> 11, of which waited for: 7 -> 7; matrix products, arithmetic and copies ran while one was open for 11% -> 11% of each run, Pallas kernels for 7% -> 7%
where the time goes in v7:
time: 65.9 us; the launch traced here: 65.5 us
  waiting for transfers between devices  28.2 us (43%)
  starting transfers between devices  11.1 us (17%)
  Pallas kernels  9.53 us (14%)
  other arithmetic  6.25 us (9%)
  local copies, waits for them, and re-layouts  6.21 us (9%)
  between operations  4.14 us (6%)
    ppermute x1, waiting for transfers between devices, local(): carry = lax.ppermute(carry, 'depth', [(turn + 1, turn)])  13 us
    ppermute x1, waiting for transfers between devices, local(): lax.ppermute(spill_sum, 'tile', [(t, t + 1) for t in range(tile_count - 1)])  5.75 us
    pallas_call x1, Pallas kernels, run_adjoint(): pl.pallas_call(adjoint_kernel(last), grid_spec=grid_spec, out_shape=(jax....  4.63 us
    ppermute x1, waiting for transfers between devices, local(): carry = lax.ppermute(carry, 'depth', [(depth_count - 2, depth_count - 1)])  4.32 us
    ppermute x1, starting transfers between devices, local(): lax.ppermute(spill_sum, 'tile', [(t, t + 1) for t in range(tile_count - 1)])  4.25 us
    ppermute x1, starting transfers between devices, local(): carry = lax.ppermute(carry, 'depth', [(depth_count - 2, depth_count - 1)])  3.06 us
    pallas_call x1, Pallas kernels, cut_patches(): pl.pallas_call(cut_kernel, grid_spec=grid_spec, out_shape=jax.ShapeDtypeS...  2.97 us
    ppermute x1, waiting for transfers between devices, from_behind(): return lax.ppermute(block, axis, route)  1.95 us
  transfers between devices with their start and end apart: 11, of which 7 were waited for; matrix products, arithmetic and copies ran while one was open for 11% of the time, Pallas kernels for 7%

profile of v7, /device:TPU:0, one launch (start us, length us, event | category | flops | bytes accessed | tf_op | source)
XLA Modules:
  0.0 65.5 jit_solution(12844190665607144278)
XLA Ops:
  0.0 0.5 collective-permute-start.1
  0.5 1.1 %dynamic-slice_convert_fusion = bf16[1,2,256,256]{3,2,1,0:T(8,128)(2,1)S(1)} fusion(f32[1,2,256,512]{3,2,1,0:T(8,128)} %tile_ref.1, s32[]{:T(128)S(6)} %select_n.114), kind=kLoop, calls=%fused_computation.16 | loop fusion | bytes 524292 | tf_op jit(solution)/shard_map/convert_element_type | solution.py:424
  1.6 1.3 %collective-permute-start.2 = (bf16[1,2,256,256]{3,2,1,0:T(8,128)(2,1)S(1)}, bf16[1,2,256,256]{3,2,1,0:T(8,128)(2,1)S(1)}, u32[]{:S(2)}, u32[]{:S(2)}) collective-permute-start(bf16[1,2,256,256]{3,2,1,0:T(8,128)(2,1)S(1)} %dynamic-slice_convert_fusion), channel_id=1, source_target_pairs={{4,0},{8,4},{12,8},{5,1},{9,5},{13,9},{6,2},{10,6},{14,10},{7,3},{... | collective-permute-start | bytes 786440 | tf_op jit(solution)/shard_map/ppermute | solution.py:18
  2.9 0.5 collective-permute-start.5
  3.4 1.0 %multiply_convert_fusion.2 = bf16[256,256]{1,0:T(8,128)(2,1)S(1)} fusion(), kind=kLoop, calls=%fused_computation.25 | loop fusion | flops 1048576 | bytes 131072 | tf_op jit(solution)/shard_map/convert_element_type | solution.py:26
  4.4 1.0 %fusion.13 = (bf16[256,256]{1,0:T(8,128)(2,1)S(1)}, bf16[256,256]{1,0:T(8,128)(2,1)S(1)}) fusion(), kind=kLoop, calls=%fused_computation.33 | loop fusion | flops 1572864 | bytes 262144 | tf_op jit(solution)/shard_map/neg | solution.py:28
  5.4 1.0 %multiply_convert_fusion = (bf16[256,256]{1,0:T(8,128)(2,1)S(1)}, bf16[256,256]{1,0:T(8,128)(2,1)S(1)}) fusion(), kind=kLoop, calls=%fused_computation.23 | loop fusion | flops 1179648 | bytes 262144 | tf_op jit(solution)/shard_map/convert_element_type | solution.py:27
  6.4 1.0 %fusion.10 = (f32[1,256,256]{2,1,0:T(8,128)S(1)}, f32[1,256,256]{2,1,0:T(8,128)S(1)}) fusion(s32[256]{0:T(256)S(1)} %fusion.16, f32[]{:T(128)S(6)} %neg.15), kind=kLoop, calls=%fused_computation.30 | loop fusion | flops 196608 | bytes 525316 | tf_op jit(solution)/shard_map/cos | solution.py:51
  7.4 0.2 fusion.3
  8.3 0.8 %broadcast_select_fusion = s32[2]{0:T(128)S(1)} fusion(pred[]{:T(512)} %eq.26, s32[1]{0:T(128)} %collective-permute-done.1, s32[1]{0:T(128)S(6)} %copy.14), kind=kLoop, calls=%fused_computation.44 | loop fusion | flops 6 | bytes 17 | tf_op jit(solution)/shard_map/jit(_where)/select_n | solution.py:438
  9.1 0.7 %fusion.19 = (s32[1]{0:T(128)}, s32[1]{0:T(128)}) fusion(s32[2]{0:T(128)S(1)} %broadcast_select_fusion), kind=kLoop, calls=%fused_computation.46 | loop fusion | bytes 16 | tf_op jit(solution)/shard_map/slice | solution.py:442
  11.0 1.9 %collective-permute-done.2.mine_ref = bf16[1,2,256,256]{3,2,1,0:T(8,128)(2,1)S(1)} collective-permute-done((bf16[1,2,256,256]{3,2,1,0:T(8,128)(2,1)S(1)}, bf16[1,2,256,256]{3,2,1,0:T(8,128)(2,1)S(1)}, u32[]{:S(2)}, u32[]{:S(2)}) %collective-permute-start.2) | collective-permute-done | bytes 262176 | tf_op jit(solution)/shard_map/ppermute | solution.py:18
  13.0 0.6 fusion.20
  14.5 0.7 %copy-done.3 = bf16[1,2,256,256]{3,2,1,0:T(8,128)(2,1)} copy-done((bf16[1,2,256,256]{3,2,1,0:T(8,128)(2,1)}, bf16[1,2,256,256]{3,2,1,0:T(8,128)(2,1)S(1)}, u32[]{:S(2)}) %copy-start.3) | copy-done | bytes 262168
  15.2 3.0 %shard_map.60 = f32[1,2,256,256]{3,2,1,0:T(8,128)S(1)} custom-call(s32[1]{0:T(128)} %sub.17.rows_ref, s32[1]{0:T(128)} %bitcast.4.columns_ref, s32[1]{0:T(128)} %bitcast.order_ref, f32[1,2,256,512]{3,2,1,0:T(8,128)} %tile_ref.1, bf16[1,2,256,256]{3,2,1,0:T(8,128)(2,1)} %copy-done.2, bf16[1,2,256,256]{3,2,1,0:T(8,128)(2,1)} %copy-done.3), custom_call_target="tpu_custom_call" | custom-call | tf_op jit(solution)/shard_map/pallas_call | solution.py:279
  18.2 1.9 %conditional.3 = (bf16[1,2,256,256]{3,2,1,0:T(8,128)(2,1)}) conditional(s32[]{:T(128)} %convert_element_type.128, () %tuple.54, (bf16[1,2,256,256]{3,2,1,0:T(8,128)(2,1)S(1)}, f32[1,2,256,256]{3,2,1,0:T(8,128)S(1)}, f32[2,256,256]{2,1,0:T(8,128)S(1)}, bf16[512,512]{1,0:T(8,128)(2,1)S(1)}, bf16[512,512]{1,0:T(8,128)(2,1)S(1)}, ...), branch_computations={%region_0.1_spmd, %region_1.2_spmd} | conditional | bytes 262154 | solution.py:476
  18.3 1.9 %branch_1_fun.5 = bf16[1,2,256,256]{3,2,1,0:T(8,128)(2,1)} custom-call(bf16[1,2,256,256]{3,2,1,0:T(8,128)(2,1)S(1)} %get-tuple-element.121.refs_0_, f32[1,2,256,256]{3,2,1,0:T(8,128)S(1)} %get-tuple-element.122.refs_1_, f32[2,256,256]{2,1,0:T(8,128)S(1)} %get-tuple-element.123.refs_2_, bf16[512,512]{1,0:T(8,128)(2,1)S(1)} %get-tuple-element.124.refs_3_, ...), custom_call_target="tpu_custom_call" | custom-call | tf_op jit(solution)/shard_map/cond/branch_1_fun/pallas_call | solution.py:197
  20.2 3.1 %collective-permute-start.4 = (bf16[1,2,256,256]{3,2,1,0:T(8,128)(2,1)}, bf16[1,2,256,256]{3,2,1,0:T(8,128)(2,1)}, u32[]{:S(2)}, u32[]{:S(2)}) collective-permute-start(bf16[1,2,256,256]{3,2,1,0:T(8,128)(2,1)} %get-tuple-element.193), channel_id=1, source_target_pairs={{0,2},{1,3},{4,6},{5,7},{8,10},{9,11},{12,14},{13,15},{16,18},{17,... | collective-permute-start | bytes 786440 | tf_op jit(solution)/shard_map/ppermute | solution.py:491
  24.6 4.3 %collective-permute-done.4 = bf16[1,2,256,256]{3,2,1,0:T(8,128)(2,1)} collective-permute-done((bf16[1,2,256,256]{3,2,1,0:T(8,128)(2,1)}, bf16[1,2,256,256]{3,2,1,0:T(8,128)(2,1)}, u32[]{:S(2)}, u32[]{:S(2)}) %collective-permute-start.4) | collective-permute-done | bytes 262176 | tf_op jit(solution)/shard_map/ppermute | solution.py:491
  28.9 1.8 %conditional.4 = ((bf16[1,2,256,256]{3,2,1,0:T(8,128)(2,1)}, bf16[2,512,512]{2,1,0:T(8,128)(2,1)})) conditional(s32[]{:T(128)} %convert_element_type.129, () %tuple.53, (s32[1]{0:T(128)}, s32[1]{0:T(128)}, s32[1]{0:T(128)}, s32[1]{0:T(128)}, s32[1]{0:T(128)}, /*index=5*/bf16[1,2,256,256]{3,2,1,0:T(8,128)(2,1)}, f32[1,2,256,256]{3,2,1,0:T(8,128)S(1)}, ...), branch_computations={%region_2.3_spmd, %region_3.4_spmd} | conditional | bytes 1310748 | solution.py:492
  28.9 0.7 %broadcast.204 = bf16[1,2,256,256]{3,2,1,0:T(8,128)(2,1)} broadcast(bf16[]{:T(256)} %constant.95.clone), dimensions={} | broadcast | bytes 262146 | tf_op jit(solution)/shard_map/broadcast.13
  29.6 1.0 %broadcast.205 = bf16[2,512,512]{2,1,0:T(8,128)(2,1)} broadcast(bf16[]{:T(256)} %constant.95.clone), dimensions={} | broadcast | bytes 1048578 | tf_op jit(solution)/shard_map/broadcast.12
  30.7 1.3 %collective-permute-start.6 = (bf16[1,2,256,256]{3,2,1,0:T(8,128)(2,1)}, bf16[1,2,256,256]{3,2,1,0:T(8,128)(2,1)}, u32[]{:S(2)}, u32[]{:S(2)}) collective-permute-start(bf16[1,2,256,256]{3,2,1,0:T(8,128)(2,1)} %get-tuple-element.159), channel_id=1, source_target_pairs={{2,0},{3,1},{6,4},{7,5},{10,8},{11,9},{14,12},{15,13},{18,16},{19,... | collective-permute-start | bytes 786440 | tf_op jit(solution)/shard_map/ppermute | solution.py:503
  32.0 13.0 %collective-permute-done.6 = bf16[1,2,256,256]{3,2,1,0:T(8,128)(2,1)} collective-permute-done((bf16[1,2,256,256]{3,2,1,0:T(8,128)(2,1)}, bf16[1,2,256,256]{3,2,1,0:T(8,128)(2,1)}, u32[]{:S(2)}, u32[]{:S(2)}) %collective-permute-start.6) | collective-permute-done | bytes 262176 | tf_op jit(solution)/shard_map/ppermute | solution.py:503
  45.0 4.6 %conditional.5 = (bf16[2,512,512]{2,1,0:T(8,128)(2,1)}) conditional(s32[]{:T(128)} %convert_element_type.128, bf16[2,512,512]{2,1,0:T(8,128)(2,1)} %get-tuple-element.158, (s32[1]{0:T(128)}, s32[1]{0:T(128)}, s32[1]{0:T(128)}, s32[1]{0:T(128)}, s32[1]{0:T(128)}, /*index=5*/bf16[1,2,256,256]{3,2,1,0:T(8,128)(2,1)}, f32[1,2,256,256]{3,2,1,0:T(8,128)S(1)}, ...), branch_computations={%region_4.5_spmd, %region_5.6_spmd} | conditional | bytes 8 | solution.py:504
  45.0 4.6 %branch_1_fun.7 = (bf16[1,2,256,256]{3,2,1,0:T(8,128)(2,1)}, bf16[2,512,512]{2,1,0:T(8,128)(2,1)}) custom-call(s32[1]{0:T(128)} %get-tuple-element.142.rows_ref, s32[1]{0:T(128)} %get-tuple-element.143.columns_ref, s32[1]{0:T(128)} %get-tuple-element.144.live_ref, s32[1]{0:T(128)} %get-tuple-element.145.slot_ref, s32[1]{0:T(128)} %get-tuple-element.146.other_ref, ...), custom_call_target="tpu_custom_call" | custom-call | tf_op jit(solution)/shard_map/cond/branch_1_fun/pallas_call | solution.py:402
  49.6 1.3 %fusion.18 = (bf16[2,256,512]{2,1,0:T(8,128)(2,1)S(1)}, bf16[2,256,512]{2,1,0:T(8,128)(2,1)S(1)}) fusion(bf16[2,512,512]{2,1,0:T(8,128)(2,1)} %get-tuple-element.195), kind=kLoop, calls=%fused_computation.45 | loop fusion | bytes 2097152 | tf_op jit(solution)/shard_map/slice | solution.py:507
  51.0 1.5 %collective-permute-done.8 = bf16[2,256,256]{2,1,0:T(8,128)(2,1)S(1)} collective-permute-done((bf16[2,256,256]{2,1,0:T(8,128)(2,1)S(1)}, bf16[2,256,256]{2,1,0:T(8,128)(2,1)S(1)}, u32[]{:S(2)}, u32[]{:S(2)}) %collective-permute-start.8) | collective-permute-done | bytes 262176 | tf_op jit(solution)/shard_map/ppermute | solution.py:510
  52.6 4.3 %collective-permute-start.9 = (bf16[2,256,256]{2,1,0:T(8,128)(2,1)S(1)}, bf16[2,256,256]{2,1,0:T(8,128)(2,1)S(1)}, u32[]{:S(2)}, u32[]{:S(2)}) collective-permute-start(bf16[2,256,256]{2,1,0:T(8,128)(2,1)S(1)} %add_convert_fusion), channel_id=1, source_target_pairs={{0,4},{4,8},{8,12},{1,5},{5,9},{9,13},{2,6},{6,10},{10,14},{3,7},{... | collective-permute-start | bytes 786440 | tf_op jit(solution)/shard_map/ppermute | solution.py:512
  56.9 5.8 %collective-permute-done.9 = bf16[2,256,256]{2,1,0:T(8,128)(2,1)S(1)} collective-permute-done((bf16[2,256,256]{2,1,0:T(8,128)(2,1)S(1)}, bf16[2,256,256]{2,1,0:T(8,128)(2,1)S(1)}, u32[]{:S(2)}, u32[]{:S(2)}) %collective-permute-start.9) | collective-permute-done | bytes 262176 | tf_op jit(solution)/shard_map/ppermute | solution.py:512
  62.7 1.5 %collective-permute-done.10 = bf16[2,256,256]{2,1,0:T(8,128)(2,1)S(1)} collective-permute-done((bf16[2,256,256]{2,1,0:T(8,128)(2,1)S(1)}, bf16[2,256,256]{2,1,0:T(8,128)(2,1)S(1)}, u32[]{:S(2)}, u32[]{:S(2)}) %collective-permute-start.10) | collective-permute-done | bytes 262176 | tf_op jit(solution)/shard_map/ppermute | solution.py:515
  64.2 1.2 %add_bitcast_fusion = f32[1,2,256,512]{3,2,1,0:T(8,128)} fusion(bf16[2,256,512]{2,1,0:T(8,128)(2,1)S(1)} %collective-permute-done.7, bf16[2,256,256]{2,1,0:T(8,128)(2,1)S(1)} %collective-permute-done.10, bf16[2,256,256]{2,1,0:T(8,128)(2,1)S(1)} %collective-permute-done.9, pred[]{:T(512)} %eq.26, bf16[2,512,512]{2,1,0:T(8,128)(2,1)S(1)} %copy-done), kind=kLoop, calls=%fused_computation | loop fusion | flops 3670016 | bytes 2621441 | tf_op jit(solution)/shard_map/broadcast_in_dim | solution.py:523
  (25 shorter events, 0.5 us)
Async XLA Ops:
  0.0 8.3 %collective-permute-start.1 = (s32[1]{0:T(128)}, s32[1]{0:T(128)}, u32[]{:S(2)}, u32[]{:S(2)}) collective-permute-start(s32[1]{0:T(128)} %param.18), channel_id=1, source_target_pairs={{0,1},{1,0},{2,3},{3,2},{4,5},{5,4},{6,7},{7,6},{8,9},{9,8},{10,11... | collective-permute-start | bytes 20 | tf_op jit(solution)/shard_map/ppermute | solution.py:431
  0.5 12.5 %collective-permute-start = (s32[2,2]{1,0:T(2,128)}, s32[2,2]{1,0:T(2,128)S(1)}, u32[]{:S(2)}, u32[]{:S(2)}) collective-permute-start(s32[2,2]{1,0:T(2,128)} %param.17), channel_id=1, source_target_pairs={{0,1},{1,0},{2,3},{3,2},{4,5},{5,4},{6,7},{7,6},{8,9},{9,8},{10,11... | collective-permute-start | bytes 56 | tf_op jit(solution)/shard_map/ppermute | solution.py:430
  1.6 11.4 %collective-permute-start.2 = (bf16[1,2,256,256]{3,2,1,0:T(8,128)(2,1)S(1)}, bf16[1,2,256,256]{3,2,1,0:T(8,128)(2,1)S(1)}, u32[]{:S(2)}, u32[]{:S(2)}) collective-permute-start(bf16[1,2,256,256]{3,2,1,0:T(8,128)(2,1)S(1)} %dynamic-slice_convert_fusion), channel_id=1, source_target_pairs={{4,0},{8,4},{12,8},{5,1},{9,5},{13,9},{6,2},{10,6},{14,10},{7,3},{... | collective-permute-start | bytes 786440 | tf_op jit(solution)/shard_map/ppermute | solution.py:18
  2.9 21.7 %collective-permute-start.5 = (f32[2,256,256]{2,1,0:T(8,128)}, f32[2,256,256]{2,1,0:T(8,128)}, u32[]{:S(2)}, u32[]{:S(2)}) collective-permute-start(f32[2,256,256]{2,1,0:T(8,128)} %param.19), channel_id=1, source_target_pairs={{0,1},{1,0},{2,3},{3,2},{4,5},{5,4},{6,7},{7,6},{8,9},{9,8},{10,11... | collective-permute-start | bytes 1572872 | tf_op jit(solution)/shard_map/ppermute | solution.py:432
  11.0 2.0 %copy-start.4 = (s32[2,2]{1,0:T(2,128)S(1)}, s32[2,2]{1,0:T(2,128)}, u32[]{:S(2)}) copy-start(s32[2,2]{1,0:T(2,128)} %param.17) | copy-start | bytes 52
  13.0 1.5 %copy-start.2 = (bf16[1,2,256,256]{3,2,1,0:T(8,128)(2,1)}, bf16[1,2,256,256]{3,2,1,0:T(8,128)(2,1)S(1)}, u32[]{:S(2)}) copy-start(bf16[1,2,256,256]{3,2,1,0:T(8,128)(2,1)S(1)} %collective-permute-done.2.mine_ref) | copy-start | bytes 786436
  13.0 1.5 %collective-permute-start.3 = (bf16[1,2,256,256]{3,2,1,0:T(8,128)(2,1)S(1)}, bf16[1,2,256,256]{3,2,1,0:T(8,128)(2,1)S(1)}, u32[]{:S(2)}, u32[]{:S(2)}) collective-permute-start(bf16[1,2,256,256]{3,2,1,0:T(8,128)(2,1)S(1)} %collective-permute-done.2.mine_ref), channel_id=1, source_target_pairs={{0,1},{1,0},{2,3},{3,2},{4,5},{5,4},{6,7},{7,6},{8,9},{9,8},{10,11... | collective-permute-start | bytes 786440 | tf_op jit(solution)/shard_map/ppermute | solution.py:426
  14.5 0.7 %copy-start.3 = (bf16[1,2,256,256]{3,2,1,0:T(8,128)(2,1)}, bf16[1,2,256,256]{3,2,1,0:T(8,128)(2,1)S(1)}, u32[]{:S(2)}) copy-start(bf16[1,2,256,256]{3,2,1,0:T(8,128)(2,1)S(1)} %collective-permute-done.3.partner_ref) | copy-start | bytes 786436
  15.2 3.0 %copy-start.1 = (bf16[2,256,256]{2,1,0:T(8,128)(2,1)S(1)}, bf16[2,256,256]{2,1,0:T(8,128)(2,1)}, u32[]{:S(2)}) copy-start(bf16[2,256,256]{2,1,0:T(8,128)(2,1)} %param.16) | copy-start | bytes 786436
  20.2 8.7 %collective-permute-start.4 = (bf16[1,2,256,256]{3,2,1,0:T(8,128)(2,1)}, bf16[1,2,256,256]{3,2,1,0:T(8,128)(2,1)}, u32[]{:S(2)}, u32[]{:S(2)}) collective-permute-start(bf16[1,2,256,256]{3,2,1,0:T(8,128)(2,1)} %get-tuple-element.193), channel_id=1, source_target_pairs={{0,2},{1,3},{4,6},{5,7},{8,10},{9,11},{12,14},{13,15},{16,18},{17,... | collective-permute-start | bytes 786440 | tf_op jit(solution)/shard_map/ppermute | solution.py:491
  30.7 14.3 %collective-permute-start.6 = (bf16[1,2,256,256]{3,2,1,0:T(8,128)(2,1)}, bf16[1,2,256,256]{3,2,1,0:T(8,128)(2,1)}, u32[]{:S(2)}, u32[]{:S(2)}) collective-permute-start(bf16[1,2,256,256]{3,2,1,0:T(8,128)(2,1)} %get-tuple-element.159), channel_id=1, source_target_pairs={{2,0},{3,1},{6,4},{7,5},{10,8},{11,9},{14,12},{15,13},{18,16},{19,... | collective-permute-start | bytes 786440 | tf_op jit(solution)/shard_map/ppermute | solution.py:503
  50.9 13.4 %copy-start = (bf16[2,512,512]{2,1,0:T(8,128)(2,1)S(1)}, bf16[2,512,512]{2,1,0:T(8,128)(2,1)}, u32[]{:S(2)}) copy-start(bf16[2,512,512]{2,1,0:T(8,128)(2,1)} %get-tuple-element.195) | copy-start | bytes 3145732
  50.9 1.6 %collective-permute-start.8 = (bf16[2,256,256]{2,1,0:T(8,128)(2,1)S(1)}, bf16[2,256,256]{2,1,0:T(8,128)(2,1)S(1)}, u32[]{:S(2)}, u32[]{:S(2)}) collective-permute-start(bf16[2,256,256]{2,1,0:T(8,128)(2,1)S(1)} %constant_dynamic-slice_fusion.1), channel_id=1, source_target_pairs={{0,1},{1,0},{2,3},{3,2},{4,5},{5,4},{6,7},{7,6},{8,9},{9,8},{10,11... | collective-permute-start | bytes 786440 | tf_op jit(solution)/shard_map/ppermute | solution.py:510
  52.6 10.1 %collective-permute-start.9 = (bf16[2,256,256]{2,1,0:T(8,128)(2,1)S(1)}, bf16[2,256,256]{2,1,0:T(8,128)(2,1)S(1)}, u32[]{:S(2)}, u32[]{:S(2)}) collective-permute-start(bf16[2,256,256]{2,1,0:T(8,128)(2,1)S(1)} %add_convert_fusion), channel_id=1, source_target_pairs={{0,4},{4,8},{8,12},{1,5},{5,9},{9,13},{2,6},{6,10},{10,14},{3,7},{... | collective-permute-start | bytes 786440 | tf_op jit(solution)/shard_map/ppermute | solution.py:512
  56.9 5.8 %collective-permute-start.7 = (bf16[2,256,512]{2,1,0:T(8,128)(2,1)S(1)}, bf16[2,256,512]{2,1,0:T(8,128)(2,1)S(1)}, u32[]{:S(2)}, u32[]{:S(2)}) collective-permute-start(bf16[2,256,512]{2,1,0:T(8,128)(2,1)S(1)} %get-tuple-element.172), channel_id=1, source_target_pairs={{0,1},{1,0},{2,3},{3,2},{4,5},{5,4},{6,7},{7,6},{8,9},{9,8},{10,11... | collective-permute-start | bytes 1572872 | tf_op jit(solution)/shard_map/ppermute | solution.py:514
  62.7 1.5 %collective-permute-start.10 = (bf16[2,256,256]{2,1,0:T(8,128)(2,1)S(1)}, bf16[2,256,256]{2,1,0:T(8,128)(2,1)S(1)}, u32[]{:S(2)}, u32[]{:S(2)}) collective-permute-start(bf16[2,256,256]{2,1,0:T(8,128)(2,1)S(1)} %collective-permute-done.9), channel_id=1, source_target_pairs={{0,1},{1,0},{2,3},{3,2},{4,5},{5,4},{6,7},{7,6},{8,9},{9,8},{10,11... | collective-permute-start | bytes 786440 | tf_op jit(solution)/shard_map/ppermute | solution.py:515

commit v8 on v7

--- a/solution.py
+++ b/solution.py
@@ -449,6 +449,23 @@
     local_columns = chosen[:, 1]
     order = jnp.reshape(batch_index, (1,)).astype(jnp.int32)
     patches = cut_patches(object_field, mine, partner, local_rows, local_columns, order, width)
+    columns_half = lax.dynamic_slice_in_dim(object_field, batch_index * half, half, 3)
+    prior_tile = lax.ppermute(columns_half.astype(jnp.bfloat16), "depth", [(0, 1)])
+    prior_rim = lax.ppermute(
+        wanted.astype(jnp.bfloat16),
+        ("tile", "depth"),
+        [((t + 1) * depth_count, t * depth_count + 1) for t in range(tile_count - 1)],
+    )
+    prior_tile_other = lax.ppermute(prior_tile, "batch", pairs)
+    prior_rim_other = lax.ppermute(prior_rim, "batch", pairs)
+    prior_full = jnp.where(
+        first_core,
+        jnp.concatenate([prior_tile, prior_tile_other], axis=3),
+        jnp.concatenate([prior_tile_other, prior_tile], axis=3),
+    ).astype(jnp.float32)
+    prior_patches = cut_patches(
+        prior_full, prior_rim, prior_rim_other, local_rows, local_columns, order, width
+    )
     number = patches.shape[0]
     forward_block = dft_block(width, -1.0)
     inverse_block = dft_block(width, 1.0)
@@ -467,10 +484,16 @@
     def silent(waves):
         return jnp.zeros_like(waves)
 
-    carry = start
-    inputs = start
-    for turn in range(depth_count - 1):
-        if turn > 0:
+    first_re, first_im = chirp_parts(width, jnp.float32(SLICE_COEF))
+    first_chirps = jnp.stack([first_re, first_im])
+
+    def forward_first(waves):
+        return run_waves(waves, prior_patches, first_chirps, blocks)
+
+    carry = lax.cond(segment == 1, forward_first, silent, start)
+    inputs = jnp.where(segment == 1, carry, start)
+    for turn in range(1, depth_count - 1):
+        if turn > 1:
             carry = lax.ppermute(carry, "depth", [(turn - 1, turn)])
             inputs = jnp.where(segment == turn, carry, inputs)
         carry = lax.cond(segment == turn, forward_all, silent, carry)
@@ -487,7 +510,7 @@
     def last_silent(incoming):
         return (jnp.zeros_like(incoming), jnp.zeros((2, height, columns_all), jnp.bfloat16))
 
-    if depth_count > 1:
+    if depth_count > 2:
         carry = lax.ppermute(carry, "depth", [(depth_count - 2, depth_count - 1)])
     carry, gradient = lax.cond(segment == depth_count - 1, last_pass, last_silent, carry)
 

time: 65.9 us -> 72.4 us (1.099)
  other arithmetic: 6.25 us -> 12.6 us
  waiting for transfers between devices: 28.2 us -> 23.1 us
  starting transfers between devices: 11.1 us -> 15.8 us
  Pallas kernels: 9.53 us -> 10.9 us
  local copies, waits for them, and re-layouts: 6.21 us -> 5.01 us
    ppermute x1 -> x4, starting transfers between devices: 3.06 us -> 7.93 us  [the longest x1 5.52 us: local(): lax.ppermute(columns_half.astype(jnp.bfloat16), 'depth', [(0, 1)])]
    ppermute x1 -> x4, waiting for transfers between devices: 4.32 us -> 0.01 us  [the longest x1 0.01 us: local(): prior_rim_other = lax.ppermute(prior_rim, 'batch', pairs)]
    pallas_call x1 -> x2, Pallas kernels: 2.97 us -> 6.77 us  [cut_patches(): pl.pallas_call(cut_kernel, grid_spec=grid_spec, out_shape=jax.ShapeDtypeS...]
    convert_element_type x0 -> x1, other arithmetic: none -> 2.17 us  [local(): prior_full = jnp.where(first_core, jnp.concatenate([prior_tile, prior_til...]
    ppermute x1, waiting for transfers between devices: 1.95 us -> 0.01 us  [from_behind(): return lax.ppermute(block, axis, route)]
    pallas_call x1 -> x0, Pallas kernels: 1.93 us -> none  [run_waves(): pl.pallas_call(wave_kernel(transmit_first, residual_after, backward), gri...]
    select_n x0 -> x1, other arithmetic: none -> 1.7 us  [local(): inputs = jnp.where(segment == 1, carry, start)]
    ppermute x1, waiting for transfers between devices: 13 us -> 14.2 us  [local(): carry = lax.ppermute(carry, 'depth', [(turn + 1, turn)])]
  transfers between devices with their start and end apart: 11 -> 14, of which waited for: 7 -> 4; matrix products, arithmetic and copies ran while one was open for 11% -> 15% of each run, Pallas kernels for 7% -> 9%
where the time goes in v8:
time: 72.4 us; the launch traced here: 71.6 us
  waiting for transfers between devices  23.1 us (32%)
  starting transfers between devices  15.8 us (22%)
  other arithmetic  12.6 us (17%)
  Pallas kernels  10.9 us (15%)
  local copies, waits for them, and re-layouts  5.01 us (7%)
  between operations  4.26 us (6%)
    ppermute x1, waiting for transfers between devices, local(): carry = lax.ppermute(carry, 'depth', [(turn + 1, turn)])  14.2 us
    pallas_call x2, Pallas kernels, cut_patches(): pl.pallas_call(cut_kernel, grid_spec=grid_spec, out_shape=jax.ShapeDtypeS...  6.77 us
    ppermute x1, waiting for transfers between devices, local(): lax.ppermute(spill_sum, 'tile', [(t, t + 1) for t in range(tile_count - 1)])  5.75 us
    ppermute x1, starting transfers between devices, local(): lax.ppermute(columns_half.astype(jnp.bfloat16), 'depth', [(0, 1)])  5.52 us
    ppermute x1, starting transfers between devices, local(): lax.ppermute(spill_sum, 'tile', [(t, t + 1) for t in range(tile_count - 1)])  4.29 us
    pallas_call x1, Pallas kernels, run_adjoint(): pl.pallas_call(adjoint_kernel(last), grid_spec=grid_spec, out_shape=(jax....  4.11 us
    convert_element_type x1, other arithmetic, local(): prior_full = jnp.where(first_core, jnp.concatenate([prior_tile, prior_til...  2.17 us
    cos x1, other arithmetic, chirp_parts(): return (jnp.cos(phase), jnp.sin(phase))  1.9 us
  transfers between devices with their start and end apart: 14, of which 4 were waited for; matrix products, arithmetic and copies ran while one was open for 15% of the time, Pallas kernels for 9%

profile of v8, /device:TPU:0, one launch (start us, length us, event | category | flops | bytes accessed | tf_op | source)
XLA Modules:
  0.0 71.6 jit_solution(2559118779429546651)
XLA Ops:
  0.0 1.8 %dynamic-slice_convert_fusion = bf16[1,2,256,256]{3,2,1,0:T(8,128)(2,1)} fusion(f32[1,2,256,512]{3,2,1,0:T(8,128)} %tile_ref.1, s32[]{:T(128)S(6)} %select_n.152), kind=kLoop, calls=%fused_computation.20 | loop fusion | bytes 524292 | tf_op jit(solution)/shard_map/convert_element_type | solution.py:453
  1.8 1.3 %collective-permute-start.6 = (bf16[1,2,256,256]{3,2,1,0:T(8,128)(2,1)}, bf16[1,2,256,256]{3,2,1,0:T(8,128)(2,1)}, u32[]{:S(2)}, u32[]{:S(2)}) collective-permute-start(bf16[1,2,256,256]{3,2,1,0:T(8,128)(2,1)} %dynamic-slice_convert_fusion), channel_id=1, source_target_pairs={{4,0},{8,4},{12,8},{5,1},{9,5},{13,9},{6,2},{10,6},{14,10},{7,3},{... | collective-permute-start | bytes 786440 | tf_op jit(solution)/shard_map/ppermute | solution.py:18
  3.1 1.4 %collective-permute-start.4 = (bf16[1,2,256,256]{3,2,1,0:T(8,128)(2,1)}, bf16[1,2,256,256]{3,2,1,0:T(8,128)(2,1)}, u32[]{:S(2)}, u32[]{:S(2)}) collective-permute-start(bf16[1,2,256,256]{3,2,1,0:T(8,128)(2,1)} %dynamic-slice_convert_fusion), channel_id=1, source_target_pairs={{4,2},{8,6},{12,10},{5,3},{9,7},{13,11},{20,18},{24,22},{28,26},{2... | collective-permute-start | bytes 786440 | tf_op jit(solution)/shard_map/ppermute | solution.py:454
  4.5 5.5 %collective-permute-start.2 = (bf16[1,2,256,256]{3,2,1,0:T(8,128)(2,1)}, bf16[1,2,256,256]{3,2,1,0:T(8,128)(2,1)}, u32[]{:S(2)}, u32[]{:S(2)}) collective-permute-start(bf16[1,2,256,256]{3,2,1,0:T(8,128)(2,1)} %dynamic-slice_convert_fusion), channel_id=1, source_target_pairs={{0,2},{1,3},{4,6},{5,7},{8,10},{9,11},{12,14},{13,15},{16,18},{17,... | collective-permute-start | bytes 786440 | tf_op jit(solution)/shard_map/ppermute | solution.py:453
  10.0 0.5 collective-permute-start
  10.5 1.0 %multiply_convert_fusion.2 = bf16[256,256]{1,0:T(8,128)(2,1)S(1)} fusion(), kind=kLoop, calls=%fused_computation.29 | loop fusion | flops 1048576 | bytes 131072 | tf_op jit(solution)/shard_map/convert_element_type | solution.py:26
  11.5 1.0 %fusion.16 = (bf16[256,256]{1,0:T(8,128)(2,1)S(1)}, bf16[256,256]{1,0:T(8,128)(2,1)S(1)}) fusion(), kind=kLoop, calls=%fused_computation.40 | loop fusion | flops 1572864 | bytes 262144 | tf_op jit(solution)/shard_map/neg | solution.py:28
  12.5 1.7 %multiply_convert_fusion = (bf16[256,256]{1,0:T(8,128)(2,1)}, bf16[256,256]{1,0:T(8,128)(2,1)}) fusion(), kind=kLoop, calls=%fused_computation.27 | loop fusion | flops 1179648 | bytes 262144 | tf_op jit(solution)/shard_map/convert_element_type | solution.py:27
  14.2 1.9 %fusion.13 = (f32[1,256,256]{2,1,0:T(8,128)S(1)}, f32[1,256,256]{2,1,0:T(8,128)S(1)}, f32[1,256,256]{2,1,0:T(8,128)S(1)}, f32[1,256,256]{2,1,0:T(8,128)S(1)}) fusion(f32[]{:T(128)S(6)} %neg.17, s32[256]{0:T(256)S(1)} %fusion.19), kind=kLoop, calls=%fused_computation.37 | loop fusion | flops 262144 | bytes 1049604 | tf_op jit(solution)/shard_map/cos | solution.py:51
  16.1 0.8 %pad_maximum_fusion.9 = f32[2,256,256]{2,1,0:T(8,128)} fusion(f32[1,256,256]{2,1,0:T(8,128)S(1)} %get-tuple-element.196, f32[1,256,256]{2,1,0:T(8,128)S(1)} %get-tuple-element.193), kind=kLoop, calls=%fused_computation.17 | loop fusion | flops 131072 | bytes 1048576 | tf_op jit(solution)/shard_map/stack | solution.py:478
  17.0 0.2 copy-done.1
  18.2 0.8 %broadcast_select_fusion.1 = s32[2]{0:T(128)S(1)} fusion(pred[]{:T(512)} %eq.28, s32[1]{0:T(128)} %collective-permute-done.1, s32[1]{0:T(128)S(6)} %copy.14), kind=kLoop, calls=%fused_computation.51 | loop fusion | flops 6 | bytes 17 | tf_op jit(solution)/shard_map/jit(_where)/select_n | solution.py:438
  19.0 0.7 fusion.22
  22.3 0.6 collective-permute-start.3
  23.0 0.5 collective-permute-start.5
  23.5 0.7 fusion.23
  24.8 2.2 %fusion.4.tile_ref = f32[1,2,256,512]{3,2,1,0:T(8,128)} fusion(bf16[1,2,256,256]{3,2,1,0:T(8,128)(2,1)S(1)} %collective-permute-done.3, bf16[1,2,256,256]{3,2,1,0:T(8,128)(2,1)} %collective-permute-done.2, pred[]{:T(512)} %eq.28), kind=kLoop, calls=%fused_computation.15 | loop fusion | flops 2621440 | bytes 1572865 | tf_op jit(solution)/shard_map/convert_element_type | solution.py:465
  27.0 0.7 %copy-done.2 = bf16[1,2,256,256]{3,2,1,0:T(8,128)(2,1)} copy-done((bf16[1,2,256,256]{3,2,1,0:T(8,128)(2,1)}, bf16[1,2,256,256]{3,2,1,0:T(8,128)(2,1)S(1)}, u32[]{:S(2)}) %copy-start.2) | copy-done | bytes 262168
  27.7 3.0 %shard_map.60 = f32[1,2,256,256]{3,2,1,0:T(8,128)S(1)} custom-call(s32[1]{0:T(128)} %sub.22.rows_ref, s32[1]{0:T(128)} %bitcast.4.columns_ref, s32[1]{0:T(128)} %bitcast.order_ref, f32[1,2,256,512]{3,2,1,0:T(8,128)} %fusion.4.tile_ref, bf16[1,2,256,256]{3,2,1,0:T(8,128)(2,1)} %collective-permute-done.4.mine_ref, bf16[1,2,256,256]{3,2,1,0:T(8,128)(2,1)} %copy-done.2), custom_call_target="tpu_custom_call" | custom-call | tf_op jit(solution)/shard_map/pallas_call | solution.py:279
  30.8 3.8 %shard_map.61 = f32[1,2,256,256]{3,2,1,0:T(8,128)} custom-call(s32[1]{0:T(128)} %sub.22.rows_ref, s32[1]{0:T(128)} %bitcast.4.columns_ref, s32[1]{0:T(128)} %bitcast.order_ref, f32[1,2,256,512]{3,2,1,0:T(8,128)} %tile_ref.1, bf16[1,2,256,256]{3,2,1,0:T(8,128)(2,1)} %collective-permute-done.6.mine_ref, bf16[1,2,256,256]{3,2,1,0:T(8,128)(2,1)} %collective-permute-done.7.partner_ref), custom_call_target="tpu_custom_call" | custom-call | tf_op jit(solution)/shard_map/pallas_call | solution.py:279
  34.6 0.8 %conditional.4 = ((bf16[1,2,256,256]{3,2,1,0:T(8,128)(2,1)}, bf16[2,512,512]{2,1,0:T(8,128)(2,1)S(1)})) conditional(s32[]{:T(128)} %convert_element_type.147, () %tuple.53, (s32[1]{0:T(128)}, s32[1]{0:T(128)}, s32[1]{0:T(128)}, s32[1]{0:T(128)}, s32[1]{0:T(128)}, /*index=5*/bf16[1,2,256,256]{3,2,1,0:T(8,128)(2,1)S(1)}, f32[1,2,256,256]{3,2,1,0:T(8,128)}, ...), branch_computations={%region_2.3_spmd, %region_3.4_spmd} | conditional | bytes 1310748 | solution.py:515
  34.6 0.7 %broadcast.286 = bf16[1,2,256,256]{3,2,1,0:T(8,128)(2,1)} broadcast(bf16[]{:T(256)} %constant.99.clone), dimensions={} | broadcast | bytes 262146 | tf_op jit(solution)/shard_map/broadcast.13
  35.4 1.5 %collective-permute-start.9 = (bf16[1,2,256,256]{3,2,1,0:T(8,128)(2,1)}, bf16[1,2,256,256]{3,2,1,0:T(8,128)(2,1)}, u32[]{:S(2)}, u32[]{:S(2)}) collective-permute-start(bf16[1,2,256,256]{3,2,1,0:T(8,128)(2,1)} %get-tuple-element.173), channel_id=1, source_target_pairs={{2,0},{3,1},{6,4},{7,5},{10,8},{11,9},{14,12},{15,13},{18,16},{19,... | collective-permute-start | bytes 786440 | tf_op jit(solution)/shard_map/ppermute | solution.py:526
  36.9 14.2 %collective-permute-done.9 = bf16[1,2,256,256]{3,2,1,0:T(8,128)(2,1)} collective-permute-done((bf16[1,2,256,256]{3,2,1,0:T(8,128)(2,1)}, bf16[1,2,256,256]{3,2,1,0:T(8,128)(2,1)}, u32[]{:S(2)}, u32[]{:S(2)}) %collective-permute-start.9) | collective-permute-done | bytes 262176 | tf_op jit(solution)/shard_map/ppermute | solution.py:526
  51.1 5.8 %conditional.5 = (bf16[2,512,512]{2,1,0:T(8,128)(2,1)S(1)}) conditional(s32[]{:T(128)} %convert_element_type.146, bf16[2,512,512]{2,1,0:T(8,128)(2,1)S(1)} %get-tuple-element.172, (pred[]{:T(512)}, bf16[1,2,256,256]{3,2,1,0:T(8,128)(2,1)S(1)}, bf16[1,2,256,256]{3,2,1,0:T(8,128)(2,1)}, s32[1]{0:T(128)}, s32[1]{0:T(128)}, /*index=5*/s32[1]{0:T(128)}, ...), branch_computations={%region_4.5_spmd, %region_5.6_spmd} | conditional | flops 131072 | bytes 786441 | solution.py:527
  51.1 1.7 %broadcast_select_fusion.refs_7_ = bf16[1,2,256,256]{3,2,1,0:T(8,128)(2,1)} fusion(bf16[1,2,256,256]{3,2,1,0:T(8,128)(2,1)S(1)} %get-tuple-element.167, bf16[1,2,256,256]{3,2,1,0:T(8,128)(2,1)} %get-tuple-element.168, pred[]{:T(512)} %get-tuple-element.166), kind=kLoop, calls=%fused_computation | loop fusion | flops 131072 | bytes 786433 | tf_op jit(solution)/shard_map/jit(_where)/select_n | solution.py:494
  52.8 4.1 %branch_1_fun.7 = (bf16[1,2,256,256]{3,2,1,0:T(8,128)(2,1)}, bf16[2,512,512]{2,1,0:T(8,128)(2,1)S(1)}) custom-call(s32[1]{0:T(128)} %get-tuple-element.154.rows_ref, s32[1]{0:T(128)} %get-tuple-element.155.columns_ref, s32[1]{0:T(128)} %get-tuple-element.156.live_ref, s32[1]{0:T(128)} %get-tuple-element.157.slot_ref, s32[1]{0:T(128)} %get-tuple-element.158.other_ref, ...), custom_call_target="tpu_custom_call" | custom-call | tf_op jit(solution)/shard_map/cond/branch_1_fun/pallas_call | solution.py:402
  57.1 1.5 %collective-permute-done.11 = bf16[2,256,256]{2,1,0:T(8,128)(2,1)S(1)} collective-permute-done((bf16[2,256,256]{2,1,0:T(8,128)(2,1)S(1)}, bf16[2,256,256]{2,1,0:T(8,128)(2,1)S(1)}, u32[]{:S(2)}, u32[]{:S(2)}) %collective-permute-start.11) | collective-permute-done | bytes 262176 | tf_op jit(solution)/shard_map/ppermute | solution.py:533
  58.7 4.3 %collective-permute-start.12 = (bf16[2,256,256]{2,1,0:T(8,128)(2,1)S(1)}, bf16[2,256,256]{2,1,0:T(8,128)(2,1)S(1)}, u32[]{:S(2)}, u32[]{:S(2)}) collective-permute-start(bf16[2,256,256]{2,1,0:T(8,128)(2,1)S(1)} %add_convert_fusion), channel_id=1, source_target_pairs={{0,4},{4,8},{8,12},{1,5},{5,9},{9,13},{2,6},{6,10},{10,14},{3,7},{... | collective-permute-start | bytes 786440 | tf_op jit(solution)/shard_map/ppermute | solution.py:535
  63.1 5.8 %collective-permute-done.12 = bf16[2,256,256]{2,1,0:T(8,128)(2,1)S(1)} collective-permute-done((bf16[2,256,256]{2,1,0:T(8,128)(2,1)S(1)}, bf16[2,256,256]{2,1,0:T(8,128)(2,1)S(1)}, u32[]{:S(2)}, u32[]{:S(2)}) %collective-permute-start.12) | collective-permute-done | bytes 262176 | tf_op jit(solution)/shard_map/ppermute | solution.py:535
  68.9 1.5 %collective-permute-done.13 = bf16[2,256,256]{2,1,0:T(8,128)(2,1)S(1)} collective-permute-done((bf16[2,256,256]{2,1,0:T(8,128)(2,1)S(1)}, bf16[2,256,256]{2,1,0:T(8,128)(2,1)S(1)}, u32[]{:S(2)}, u32[]{:S(2)}) %collective-permute-start.13) | collective-permute-done | bytes 262176 | tf_op jit(solution)/shard_map/ppermute | solution.py:538
  70.4 1.2 %add_bitcast_fusion = f32[1,2,256,512]{3,2,1,0:T(8,128)} fusion(bf16[2,256,512]{2,1,0:T(8,128)(2,1)S(1)} %collective-permute-done.10, bf16[2,256,256]{2,1,0:T(8,128)(2,1)S(1)} %collective-permute-done.13, bf16[2,256,256]{2,1,0:T(8,128)(2,1)S(1)} %collective-permute-done.12, pred[]{:T(512)} %eq.28, bf16[2,512,512]{2,1,0:T(8,128)(2,1)S(1)} %get-tuple-element.211), kind=kLoop, calls=%fused_computation.1 | loop fusion | flops 3670016 | bytes 2621441 | tf_op jit(solution)/shard_map/broadcast_in_dim | solution.py:546
  (33 shorter events, 0.9 us)
Async XLA Ops:
  0.0 10.0 %copy-start.3 = (s32[2,2]{1,0:T(2,128)S(1)}, s32[2,2]{1,0:T(2,128)}, u32[]{:S(2)}) copy-start(s32[2,2]{1,0:T(2,128)} %param.17) | copy-start | bytes 52
  1.8 21.1 %collective-permute-start.6 = (bf16[1,2,256,256]{3,2,1,0:T(8,128)(2,1)}, bf16[1,2,256,256]{3,2,1,0:T(8,128)(2,1)}, u32[]{:S(2)}, u32[]{:S(2)}) collective-permute-start(bf16[1,2,256,256]{3,2,1,0:T(8,128)(2,1)} %dynamic-slice_convert_fusion), channel_id=1, source_target_pairs={{4,0},{8,4},{12,8},{5,1},{9,5},{13,9},{6,2},{10,6},{14,10},{7,3},{... | collective-permute-start | bytes 786440 | tf_op jit(solution)/shard_map/ppermute | solution.py:18
  3.1 19.9 %collective-permute-start.4 = (bf16[1,2,256,256]{3,2,1,0:T(8,128)(2,1)}, bf16[1,2,256,256]{3,2,1,0:T(8,128)(2,1)}, u32[]{:S(2)}, u32[]{:S(2)}) collective-permute-start(bf16[1,2,256,256]{3,2,1,0:T(8,128)(2,1)} %dynamic-slice_convert_fusion), channel_id=1, source_target_pairs={{4,2},{8,6},{12,10},{5,3},{9,7},{13,11},{20,18},{24,22},{28,26},{2... | collective-permute-start | bytes 786440 | tf_op jit(solution)/shard_map/ppermute | solution.py:454
  4.5 17.9 %collective-permute-start.2 = (bf16[1,2,256,256]{3,2,1,0:T(8,128)(2,1)}, bf16[1,2,256,256]{3,2,1,0:T(8,128)(2,1)}, u32[]{:S(2)}, u32[]{:S(2)}) collective-permute-start(bf16[1,2,256,256]{3,2,1,0:T(8,128)(2,1)} %dynamic-slice_convert_fusion), channel_id=1, source_target_pairs={{0,2},{1,3},{4,6},{5,7},{8,10},{9,11},{12,14},{13,15},{16,18},{17,... | collective-permute-start | bytes 786440 | tf_op jit(solution)/shard_map/ppermute | solution.py:453
  10.0 8.1 %collective-permute-start.1 = (s32[1]{0:T(128)}, s32[1]{0:T(128)}, u32[]{:S(2)}, u32[]{:S(2)}) collective-permute-start(s32[1]{0:T(128)} %param.18), channel_id=1, source_target_pairs={{0,1},{1,0},{2,3},{3,2},{4,5},{5,4},{6,7},{7,6},{8,9},{9,8},{10,11... | collective-permute-start | bytes 20 | tf_op jit(solution)/shard_map/ppermute | solution.py:431
  10.0 12.9 %collective-permute-start = (s32[2,2]{1,0:T(2,128)S(1)}, s32[2,2]{1,0:T(2,128)S(1)}, u32[]{:S(2)}, u32[]{:S(2)}) collective-permute-start(s32[2,2]{1,0:T(2,128)S(1)} %copy-done.3), channel_id=1, source_target_pairs={{0,1},{1,0},{2,3},{3,2},{4,5},{5,4},{6,7},{7,6},{8,9},{9,8},{10,11... | collective-permute-start | bytes 56 | tf_op jit(solution)/shard_map/ppermute | solution.py:430
  16.1 0.9 %copy-start = (bf16[256,256]{1,0:T(8,128)(2,1)S(1)}, bf16[256,256]{1,0:T(8,128)(2,1)}, u32[]{:S(2)}) copy-start(bf16[256,256]{1,0:T(8,128)(2,1)} %get-tuple-element.201) | copy-start | bytes 393220
  16.1 1.1 %copy-start.1 = (bf16[256,256]{1,0:T(8,128)(2,1)S(1)}, bf16[256,256]{1,0:T(8,128)(2,1)}, u32[]{:S(2)}) copy-start(bf16[256,256]{1,0:T(8,128)(2,1)} %get-tuple-element.202) | copy-start | bytes 393220
  18.1 16.5 %collective-permute-start.8 = (f32[2,256,256]{2,1,0:T(8,128)}, f32[2,256,256]{2,1,0:T(8,128)}, u32[]{:S(2)}, u32[]{:S(2)}) collective-permute-start(f32[2,256,256]{2,1,0:T(8,128)} %param.19), channel_id=1, source_target_pairs={{0,1},{1,0},{2,3},{3,2},{4,5},{5,4},{6,7},{7,6},{8,9},{9,8},{10,11... | collective-permute-start | bytes 1572872 | tf_op jit(solution)/shard_map/ppermute | solution.py:432
  22.3 2.5 %collective-permute-start.3 = (bf16[1,2,256,256]{3,2,1,0:T(8,128)(2,1)}, bf16[1,2,256,256]{3,2,1,0:T(8,128)(2,1)S(1)}, u32[]{:S(2)}, u32[]{:S(2)}) collective-permute-start(bf16[1,2,256,256]{3,2,1,0:T(8,128)(2,1)} %collective-permute-done.2), channel_id=1, source_target_pairs={{0,1},{1,0},{2,3},{3,2},{4,5},{5,4},{6,7},{7,6},{8,9},{9,8},{10,11... | collective-permute-start | bytes 786440 | tf_op jit(solution)/shard_map/ppermute | solution.py:459
  22.9 7.9 %collective-permute-start.7 = (bf16[1,2,256,256]{3,2,1,0:T(8,128)(2,1)}, bf16[1,2,256,256]{3,2,1,0:T(8,128)(2,1)}, u32[]{:S(2)}, u32[]{:S(2)}) collective-permute-start(bf16[1,2,256,256]{3,2,1,0:T(8,128)(2,1)} %collective-permute-done.6.mine_ref), channel_id=1, source_target_pairs={{0,1},{1,0},{2,3},{3,2},{4,5},{5,4},{6,7},{7,6},{8,9},{9,8},{10,11... | collective-permute-start | bytes 786440 | tf_op jit(solution)/shard_map/ppermute | solution.py:426
  23.0 4.0 %collective-permute-start.5 = (bf16[1,2,256,256]{3,2,1,0:T(8,128)(2,1)}, bf16[1,2,256,256]{3,2,1,0:T(8,128)(2,1)S(1)}, u32[]{:S(2)}, u32[]{:S(2)}) collective-permute-start(bf16[1,2,256,256]{3,2,1,0:T(8,128)(2,1)} %collective-permute-done.4.mine_ref), channel_id=1, source_target_pairs={{0,1},{1,0},{2,3},{3,2},{4,5},{5,4},{6,7},{7,6},{8,9},{9,8},{10,11... | collective-permute-start | bytes 786440 | tf_op jit(solution)/shard_map/ppermute | solution.py:460
  27.0 0.7 %copy-start.2 = (bf16[1,2,256,256]{3,2,1,0:T(8,128)(2,1)}, bf16[1,2,256,256]{3,2,1,0:T(8,128)(2,1)S(1)}, u32[]{:S(2)}) copy-start(bf16[1,2,256,256]{3,2,1,0:T(8,128)(2,1)S(1)} %collective-permute-done.5.partner_ref) | copy-start | bytes 786436
  35.4 15.7 %collective-permute-start.9 = (bf16[1,2,256,256]{3,2,1,0:T(8,128)(2,1)}, bf16[1,2,256,256]{3,2,1,0:T(8,128)(2,1)}, u32[]{:S(2)}, u32[]{:S(2)}) collective-permute-start(bf16[1,2,256,256]{3,2,1,0:T(8,128)(2,1)} %get-tuple-element.173), channel_id=1, source_target_pairs={{2,0},{3,1},{6,4},{7,5},{10,8},{11,9},{14,12},{15,13},{18,16},{19,... | collective-permute-start | bytes 786440 | tf_op jit(solution)/shard_map/ppermute | solution.py:526
  57.1 1.6 %collective-permute-start.11 = (bf16[2,256,256]{2,1,0:T(8,128)(2,1)S(1)}, bf16[2,256,256]{2,1,0:T(8,128)(2,1)S(1)}, u32[]{:S(2)}, u32[]{:S(2)}) collective-permute-start(bf16[2,256,256]{2,1,0:T(8,128)(2,1)S(1)} %constant_dynamic-slice_fusion.1), channel_id=1, source_target_pairs={{0,1},{1,0},{2,3},{3,2},{4,5},{5,4},{6,7},{7,6},{8,9},{9,8},{10,11... | collective-permute-start | bytes 786440 | tf_op jit(solution)/shard_map/ppermute | solution.py:533
  58.7 10.1 %collective-permute-start.12 = (bf16[2,256,256]{2,1,0:T(8,128)(2,1)S(1)}, bf16[2,256,256]{2,1,0:T(8,128)(2,1)S(1)}, u32[]{:S(2)}, u32[]{:S(2)}) collective-permute-start(bf16[2,256,256]{2,1,0:T(8,128)(2,1)S(1)} %add_convert_fusion), channel_id=1, source_target_pairs={{0,4},{4,8},{8,12},{1,5},{5,9},{9,13},{2,6},{6,10},{10,14},{3,7},{... | collective-permute-start | bytes 786440 | tf_op jit(solution)/shard_map/ppermute | solution.py:535
  63.0 5.8 %collective-permute-start.10 = (bf16[2,256,512]{2,1,0:T(8,128)(2,1)S(1)}, bf16[2,256,512]{2,1,0:T(8,128)(2,1)S(1)}, u32[]{:S(2)}, u32[]{:S(2)}) collective-permute-start(bf16[2,256,512]{2,1,0:T(8,128)(2,1)S(1)} %get-tuple-element.186), channel_id=1, source_target_pairs={{0,1},{1,0},{2,3},{3,2},{4,5},{5,4},{6,7},{7,6},{8,9},{9,8},{10,11... | collective-permute-start | bytes 1572872 | tf_op jit(solution)/shard_map/ppermute | solution.py:537
  68.9 1.5 %collective-permute-start.13 = (bf16[2,256,256]{2,1,0:T(8,128)(2,1)S(1)}, bf16[2,256,256]{2,1,0:T(8,128)(2,1)S(1)}, u32[]{:S(2)}, u32[]{:S(2)}) collective-permute-start(bf16[2,256,256]{2,1,0:T(8,128)(2,1)S(1)} %collective-permute-done.12), channel_id=1, source_target_pairs={{0,1},{1,0},{2,3},{3,2},{4,5},{5,4},{6,7},{7,6},{8,9},{9,8},{10,11... | collective-permute-start | bytes 786440 | tf_op jit(solution)/shard_map/ppermute | solution.py:538

commit v9 on v7

--- a/solution.py
+++ b/solution.py
@@ -303,7 +303,7 @@
     return (values[:width], values[width:])
 
 
-def place_term(term_re, term_im, row, column, alive, total_ref):
+def place_term(term_re, term_im, row, column, alive, total_ref, direct_ref=None):
     width = term_re.shape[0]
     height = total_ref.shape[1]
     columns_all = total_ref.shape[2]
@@ -318,10 +318,13 @@
         tall = jnp.concatenate(
             [wide, jnp.zeros((height - width, columns_all), jnp.float32)], axis=0
         )
-        total_ref[part] = total_ref[part] + pltpu.roll(tall, row_shift, 0)
-
-
-def adjoint_kernel(last):
+        if direct_ref is None:
+            total_ref[part] = total_ref[part] + pltpu.roll(tall, row_shift, 0)
+        else:
+            direct_ref[part] = pltpu.roll(tall, row_shift, 0).astype(direct_ref.dtype)
+
+
+def adjoint_kernel(last, single):
     def kernel(rows_ref, columns_ref, live_ref, slot_ref, other_ref, *refs):
         refs = list(refs)
         wave_ref = refs.pop(0)
@@ -337,9 +340,10 @@
         passed_ref, grad_ref, total_ref = refs
         index = pl.program_id(0)
 
-        @pl.when(index == 0)
-        def _():
-            total_ref[...] = jnp.zeros(total_ref.shape, total_ref.dtype)
+        if not single:
+            @pl.when(index == 0)
+            def _():
+                total_ref[...] = jnp.zeros(total_ref.shape, total_ref.dtype)
 
         wave = wave_ref[0].astype(jnp.float32)
         patch_re = patch_ref[0, 0]
@@ -368,12 +372,14 @@
         term_re = source_re * spread_re + source_im * spread_im
         term_im = source_re * spread_im - source_im * spread_re
         place_term(
-            term_re, term_im, rows_ref[index], columns_ref[index], live_ref[index] > 0, total_ref
-        )
-
-        @pl.when(index == pl.num_programs(0) - 1)
-        def _():
-            grad_ref[...] = total_ref[...].astype(grad_ref.dtype)
+            term_re, term_im, rows_ref[index], columns_ref[index], live_ref[index] > 0,
+            total_ref, grad_ref if single else None,
+        )
+
+        if not single:
+            @pl.when(index == pl.num_programs(0) - 1)
+            def _():
+                grad_ref[...] = total_ref[...].astype(grad_ref.dtype)
 
     return kernel
 
@@ -400,7 +406,7 @@
         scratch_shapes=[pltpu.VMEM((2, height, columns_all), jnp.float32)],
     )
     return pl.pallas_call(
-        adjoint_kernel(last),
+        adjoint_kernel(last, number == 1),
         grid_spec=grid_spec,
         out_shape=(
             jax.ShapeDtypeStruct(waves.shape, jnp.bfloat16),

time: 65.9 us -> 65.9 us (level)
  no operation moved by 1% of the time
where the time goes in v9:
time: 65.9 us; the launch traced here: 65.5 us
  waiting for transfers between devices  28.2 us (43%)
  starting transfers between devices  11.1 us (17%)
  Pallas kernels  9.53 us (14%)
  other arithmetic  6.25 us (9%)
  local copies, waits for them, and re-layouts  6.21 us (9%)
  between operations  4.14 us (6%)
    ppermute x1, waiting for transfers between devices, local(): carry = lax.ppermute(carry, 'depth', [(turn + 1, turn)])  13 us
    ppermute x1, waiting for transfers between devices, local(): lax.ppermute(spill_sum, 'tile', [(t, t + 1) for t in range(tile_count - 1)])  5.75 us
    pallas_call x1, Pallas kernels, run_adjoint(): pl.pallas_call(adjoint_kernel(last, number == 1), grid_spec=grid_spec, ou...  4.63 us
    ppermute x1, waiting for transfers between devices, local(): carry = lax.ppermute(carry, 'depth', [(depth_count - 2, depth_count - 1)])  4.32 us
    ppermute x1, starting transfers between devices, local(): lax.ppermute(spill_sum, 'tile', [(t, t + 1) for t in range(tile_count - 1)])  4.25 us
    ppermute x1, starting transfers between devices, local(): carry = lax.ppermute(carry, 'depth', [(depth_count - 2, depth_count - 1)])  3.06 us
    pallas_call x1, Pallas kernels, cut_patches(): pl.pallas_call(cut_kernel, grid_spec=grid_spec, out_shape=jax.ShapeDtypeS...  2.97 us
    ppermute x1, waiting for transfers between devices, from_behind(): return lax.ppermute(block, axis, route)  1.95 us
  transfers between devices with their start and end apart: 11, of which 7 were waited for; matrix products, arithmetic and copies ran while one was open for 11% of the time, Pallas kernels for 7%

profile of v9, /device:TPU:0, one launch (start us, length us, event | category | flops | bytes accessed | tf_op | source)
XLA Modules:
  0.0 65.5 jit_solution(12844190665607144278)
XLA Ops:
  0.0 0.5 collective-permute-start.1
  0.5 1.1 %dynamic-slice_convert_fusion = bf16[1,2,256,256]{3,2,1,0:T(8,128)(2,1)S(1)} fusion(f32[1,2,256,512]{3,2,1,0:T(8,128)} %tile_ref.1, s32[]{:T(128)S(6)} %select_n.114), kind=kLoop, calls=%fused_computation.16 | loop fusion | bytes 524292 | tf_op jit(solution)/shard_map/convert_element_type | solution.py:430
  1.6 1.3 %collective-permute-start.2 = (bf16[1,2,256,256]{3,2,1,0:T(8,128)(2,1)S(1)}, bf16[1,2,256,256]{3,2,1,0:T(8,128)(2,1)S(1)}, u32[]{:S(2)}, u32[]{:S(2)}) collective-permute-start(bf16[1,2,256,256]{3,2,1,0:T(8,128)(2,1)S(1)} %dynamic-slice_convert_fusion), channel_id=1, source_target_pairs={{4,0},{8,4},{12,8},{5,1},{9,5},{13,9},{6,2},{10,6},{14,10},{7,3},{... | collective-permute-start | bytes 786440 | tf_op jit(solution)/shard_map/ppermute | solution.py:18
  2.9 0.5 collective-permute-start.5
  3.4 1.0 %multiply_convert_fusion.2 = bf16[256,256]{1,0:T(8,128)(2,1)S(1)} fusion(), kind=kLoop, calls=%fused_computation.25 | loop fusion | flops 1048576 | bytes 131072 | tf_op jit(solution)/shard_map/convert_element_type | solution.py:26
  4.4 1.0 %fusion.13 = (bf16[256,256]{1,0:T(8,128)(2,1)S(1)}, bf16[256,256]{1,0:T(8,128)(2,1)S(1)}) fusion(), kind=kLoop, calls=%fused_computation.33 | loop fusion | flops 1572864 | bytes 262144 | tf_op jit(solution)/shard_map/neg | solution.py:28
  5.4 1.0 %multiply_convert_fusion = (bf16[256,256]{1,0:T(8,128)(2,1)S(1)}, bf16[256,256]{1,0:T(8,128)(2,1)S(1)}) fusion(), kind=kLoop, calls=%fused_computation.23 | loop fusion | flops 1179648 | bytes 262144 | tf_op jit(solution)/shard_map/convert_element_type | solution.py:27
  6.4 1.0 %fusion.10 = (f32[1,256,256]{2,1,0:T(8,128)S(1)}, f32[1,256,256]{2,1,0:T(8,128)S(1)}) fusion(s32[256]{0:T(256)S(1)} %fusion.16, f32[]{:T(128)S(6)} %neg.15), kind=kLoop, calls=%fused_computation.30 | loop fusion | flops 196608 | bytes 525316 | tf_op jit(solution)/shard_map/cos | solution.py:51
  7.4 0.2 fusion.3
  8.3 0.8 %broadcast_select_fusion = s32[2]{0:T(128)S(1)} fusion(pred[]{:T(512)} %eq.26, s32[1]{0:T(128)} %collective-permute-done.1, s32[1]{0:T(128)S(6)} %copy.14), kind=kLoop, calls=%fused_computation.44 | loop fusion | flops 6 | bytes 17 | tf_op jit(solution)/shard_map/jit(_where)/select_n | solution.py:444
  9.1 0.7 %fusion.19 = (s32[1]{0:T(128)}, s32[1]{0:T(128)}) fusion(s32[2]{0:T(128)S(1)} %broadcast_select_fusion), kind=kLoop, calls=%fused_computation.46 | loop fusion | bytes 16 | tf_op jit(solution)/shard_map/slice | solution.py:448
  11.0 1.9 %collective-permute-done.2.mine_ref = bf16[1,2,256,256]{3,2,1,0:T(8,128)(2,1)S(1)} collective-permute-done((bf16[1,2,256,256]{3,2,1,0:T(8,128)(2,1)S(1)}, bf16[1,2,256,256]{3,2,1,0:T(8,128)(2,1)S(1)}, u32[]{:S(2)}, u32[]{:S(2)}) %collective-permute-start.2) | collective-permute-done | bytes 262176 | tf_op jit(solution)/shard_map/ppermute | solution.py:18
  13.0 0.6 fusion.20
  14.5 0.7 %copy-done.3 = bf16[1,2,256,256]{3,2,1,0:T(8,128)(2,1)} copy-done((bf16[1,2,256,256]{3,2,1,0:T(8,128)(2,1)}, bf16[1,2,256,256]{3,2,1,0:T(8,128)(2,1)S(1)}, u32[]{:S(2)}) %copy-start.3) | copy-done | bytes 262168
  15.2 3.0 %shard_map.60 = f32[1,2,256,256]{3,2,1,0:T(8,128)S(1)} custom-call(s32[1]{0:T(128)} %sub.17.rows_ref, s32[1]{0:T(128)} %bitcast.4.columns_ref, s32[1]{0:T(128)} %bitcast.order_ref, f32[1,2,256,512]{3,2,1,0:T(8,128)} %tile_ref.1, bf16[1,2,256,256]{3,2,1,0:T(8,128)(2,1)} %copy-done.2, bf16[1,2,256,256]{3,2,1,0:T(8,128)(2,1)} %copy-done.3), custom_call_target="tpu_custom_call" | custom-call | tf_op jit(solution)/shard_map/pallas_call | solution.py:279
  18.2 1.9 %conditional.3 = (bf16[1,2,256,256]{3,2,1,0:T(8,128)(2,1)}) conditional(s32[]{:T(128)} %convert_element_type.128, () %tuple.54, (bf16[1,2,256,256]{3,2,1,0:T(8,128)(2,1)S(1)}, f32[1,2,256,256]{3,2,1,0:T(8,128)S(1)}, f32[2,256,256]{2,1,0:T(8,128)S(1)}, bf16[512,512]{1,0:T(8,128)(2,1)S(1)}, bf16[512,512]{1,0:T(8,128)(2,1)S(1)}, ...), branch_computations={%region_0.1_spmd, %region_1.2_spmd} | conditional | bytes 262154 | solution.py:482
  18.3 1.9 %branch_1_fun.5 = bf16[1,2,256,256]{3,2,1,0:T(8,128)(2,1)} custom-call(bf16[1,2,256,256]{3,2,1,0:T(8,128)(2,1)S(1)} %get-tuple-element.121.refs_0_, f32[1,2,256,256]{3,2,1,0:T(8,128)S(1)} %get-tuple-element.122.refs_1_, f32[2,256,256]{2,1,0:T(8,128)S(1)} %get-tuple-element.123.refs_2_, bf16[512,512]{1,0:T(8,128)(2,1)S(1)} %get-tuple-element.124.refs_3_, ...), custom_call_target="tpu_custom_call" | custom-call | tf_op jit(solution)/shard_map/cond/branch_1_fun/pallas_call | solution.py:197
  20.2 3.1 %collective-permute-start.4 = (bf16[1,2,256,256]{3,2,1,0:T(8,128)(2,1)}, bf16[1,2,256,256]{3,2,1,0:T(8,128)(2,1)}, u32[]{:S(2)}, u32[]{:S(2)}) collective-permute-start(bf16[1,2,256,256]{3,2,1,0:T(8,128)(2,1)} %get-tuple-element.193), channel_id=1, source_target_pairs={{0,2},{1,3},{4,6},{5,7},{8,10},{9,11},{12,14},{13,15},{16,18},{17,... | collective-permute-start | bytes 786440 | tf_op jit(solution)/shard_map/ppermute | solution.py:497
  24.6 4.3 %collective-permute-done.4 = bf16[1,2,256,256]{3,2,1,0:T(8,128)(2,1)} collective-permute-done((bf16[1,2,256,256]{3,2,1,0:T(8,128)(2,1)}, bf16[1,2,256,256]{3,2,1,0:T(8,128)(2,1)}, u32[]{:S(2)}, u32[]{:S(2)}) %collective-permute-start.4) | collective-permute-done | bytes 262176 | tf_op jit(solution)/shard_map/ppermute | solution.py:497
  28.9 1.8 %conditional.4 = ((bf16[1,2,256,256]{3,2,1,0:T(8,128)(2,1)}, bf16[2,512,512]{2,1,0:T(8,128)(2,1)})) conditional(s32[]{:T(128)} %convert_element_type.129, () %tuple.53, (s32[1]{0:T(128)}, s32[1]{0:T(128)}, s32[1]{0:T(128)}, s32[1]{0:T(128)}, s32[1]{0:T(128)}, /*index=5*/bf16[1,2,256,256]{3,2,1,0:T(8,128)(2,1)}, f32[1,2,256,256]{3,2,1,0:T(8,128)S(1)}, ...), branch_computations={%region_2.3_spmd, %region_3.4_spmd} | conditional | bytes 1310748 | solution.py:498
  28.9 0.7 %broadcast.204 = bf16[1,2,256,256]{3,2,1,0:T(8,128)(2,1)} broadcast(bf16[]{:T(256)} %constant.95.clone), dimensions={} | broadcast | bytes 262146 | tf_op jit(solution)/shard_map/broadcast.13
  29.6 1.0 %broadcast.205 = bf16[2,512,512]{2,1,0:T(8,128)(2,1)} broadcast(bf16[]{:T(256)} %constant.95.clone), dimensions={} | broadcast | bytes 1048578 | tf_op jit(solution)/shard_map/broadcast.12
  30.7 1.3 %collective-permute-start.6 = (bf16[1,2,256,256]{3,2,1,0:T(8,128)(2,1)}, bf16[1,2,256,256]{3,2,1,0:T(8,128)(2,1)}, u32[]{:S(2)}, u32[]{:S(2)}) collective-permute-start(bf16[1,2,256,256]{3,2,1,0:T(8,128)(2,1)} %get-tuple-element.159), channel_id=1, source_target_pairs={{2,0},{3,1},{6,4},{7,5},{10,8},{11,9},{14,12},{15,13},{18,16},{19,... | collective-permute-start | bytes 786440 | tf_op jit(solution)/shard_map/ppermute | solution.py:509
  32.0 13.0 %collective-permute-done.6 = bf16[1,2,256,256]{3,2,1,0:T(8,128)(2,1)} collective-permute-done((bf16[1,2,256,256]{3,2,1,0:T(8,128)(2,1)}, bf16[1,2,256,256]{3,2,1,0:T(8,128)(2,1)}, u32[]{:S(2)}, u32[]{:S(2)}) %collective-permute-start.6) | collective-permute-done | bytes 262176 | tf_op jit(solution)/shard_map/ppermute | solution.py:509
  45.0 4.6 %conditional.5 = (bf16[2,512,512]{2,1,0:T(8,128)(2,1)}) conditional(s32[]{:T(128)} %convert_element_type.128, bf16[2,512,512]{2,1,0:T(8,128)(2,1)} %get-tuple-element.158, (s32[1]{0:T(128)}, s32[1]{0:T(128)}, s32[1]{0:T(128)}, s32[1]{0:T(128)}, s32[1]{0:T(128)}, /*index=5*/bf16[1,2,256,256]{3,2,1,0:T(8,128)(2,1)}, f32[1,2,256,256]{3,2,1,0:T(8,128)S(1)}, ...), branch_computations={%region_4.5_spmd, %region_5.6_spmd} | conditional | bytes 8 | solution.py:510
  45.0 4.6 %branch_1_fun.7 = (bf16[1,2,256,256]{3,2,1,0:T(8,128)(2,1)}, bf16[2,512,512]{2,1,0:T(8,128)(2,1)}) custom-call(s32[1]{0:T(128)} %get-tuple-element.142.rows_ref, s32[1]{0:T(128)} %get-tuple-element.143.columns_ref, s32[1]{0:T(128)} %get-tuple-element.144.live_ref, s32[1]{0:T(128)} %get-tuple-element.145.slot_ref, s32[1]{0:T(128)} %get-tuple-element.146.other_ref, ...), custom_call_target="tpu_custom_call" | custom-call | tf_op jit(solution)/shard_map/cond/branch_1_fun/pallas_call | solution.py:408
  49.6 1.3 %fusion.18 = (bf16[2,256,512]{2,1,0:T(8,128)(2,1)S(1)}, bf16[2,256,512]{2,1,0:T(8,128)(2,1)S(1)}) fusion(bf16[2,512,512]{2,1,0:T(8,128)(2,1)} %get-tuple-element.195), kind=kLoop, calls=%fused_computation.45 | loop fusion | bytes 2097152 | tf_op jit(solution)/shard_map/slice | solution.py:513
  51.0 1.5 %collective-permute-done.8 = bf16[2,256,256]{2,1,0:T(8,128)(2,1)S(1)} collective-permute-done((bf16[2,256,256]{2,1,0:T(8,128)(2,1)S(1)}, bf16[2,256,256]{2,1,0:T(8,128)(2,1)S(1)}, u32[]{:S(2)}, u32[]{:S(2)}) %collective-permute-start.8) | collective-permute-done | bytes 262176 | tf_op jit(solution)/shard_map/ppermute | solution.py:516
  52.6 4.3 %collective-permute-start.9 = (bf16[2,256,256]{2,1,0:T(8,128)(2,1)S(1)}, bf16[2,256,256]{2,1,0:T(8,128)(2,1)S(1)}, u32[]{:S(2)}, u32[]{:S(2)}) collective-permute-start(bf16[2,256,256]{2,1,0:T(8,128)(2,1)S(1)} %add_convert_fusion), channel_id=1, source_target_pairs={{0,4},{4,8},{8,12},{1,5},{5,9},{9,13},{2,6},{6,10},{10,14},{3,7},{... | collective-permute-start | bytes 786440 | tf_op jit(solution)/shard_map/ppermute | solution.py:518
  56.9 5.8 %collective-permute-done.9 = bf16[2,256,256]{2,1,0:T(8,128)(2,1)S(1)} collective-permute-done((bf16[2,256,256]{2,1,0:T(8,128)(2,1)S(1)}, bf16[2,256,256]{2,1,0:T(8,128)(2,1)S(1)}, u32[]{:S(2)}, u32[]{:S(2)}) %collective-permute-start.9) | collective-permute-done | bytes 262176 | tf_op jit(solution)/shard_map/ppermute | solution.py:518
  62.7 1.5 %collective-permute-done.10 = bf16[2,256,256]{2,1,0:T(8,128)(2,1)S(1)} collective-permute-done((bf16[2,256,256]{2,1,0:T(8,128)(2,1)S(1)}, bf16[2,256,256]{2,1,0:T(8,128)(2,1)S(1)}, u32[]{:S(2)}, u32[]{:S(2)}) %collective-permute-start.10) | collective-permute-done | bytes 262176 | tf_op jit(solution)/shard_map/ppermute | solution.py:521
  64.2 1.2 %add_bitcast_fusion = f32[1,2,256,512]{3,2,1,0:T(8,128)} fusion(bf16[2,256,512]{2,1,0:T(8,128)(2,1)S(1)} %collective-permute-done.7, bf16[2,256,256]{2,1,0:T(8,128)(2,1)S(1)} %collective-permute-done.10, bf16[2,256,256]{2,1,0:T(8,128)(2,1)S(1)} %collective-permute-done.9, pred[]{:T(512)} %eq.26, bf16[2,512,512]{2,1,0:T(8,128)(2,1)S(1)} %copy-done), kind=kLoop, calls=%fused_computation | loop fusion | flops 3670016 | bytes 2621441 | tf_op jit(solution)/shard_map/broadcast_in_dim | solution.py:529
  (25 shorter events, 0.5 us)
Async XLA Ops:
  0.0 8.3 %collective-permute-start.1 = (s32[1]{0:T(128)}, s32[1]{0:T(128)}, u32[]{:S(2)}, u32[]{:S(2)}) collective-permute-start(s32[1]{0:T(128)} %param.18), channel_id=1, source_target_pairs={{0,1},{1,0},{2,3},{3,2},{4,5},{5,4},{6,7},{7,6},{8,9},{9,8},{10,11... | collective-permute-start | bytes 20 | tf_op jit(solution)/shard_map/ppermute | solution.py:437
  0.5 12.5 %collective-permute-start = (s32[2,2]{1,0:T(2,128)}, s32[2,2]{1,0:T(2,128)S(1)}, u32[]{:S(2)}, u32[]{:S(2)}) collective-permute-start(s32[2,2]{1,0:T(2,128)} %param.17), channel_id=1, source_target_pairs={{0,1},{1,0},{2,3},{3,2},{4,5},{5,4},{6,7},{7,6},{8,9},{9,8},{10,11... | collective-permute-start | bytes 56 | tf_op jit(solution)/shard_map/ppermute | solution.py:436
  1.6 11.4 %collective-permute-start.2 = (bf16[1,2,256,256]{3,2,1,0:T(8,128)(2,1)S(1)}, bf16[1,2,256,256]{3,2,1,0:T(8,128)(2,1)S(1)}, u32[]{:S(2)}, u32[]{:S(2)}) collective-permute-start(bf16[1,2,256,256]{3,2,1,0:T(8,128)(2,1)S(1)} %dynamic-slice_convert_fusion), channel_id=1, source_target_pairs={{4,0},{8,4},{12,8},{5,1},{9,5},{13,9},{6,2},{10,6},{14,10},{7,3},{... | collective-permute-start | bytes 786440 | tf_op jit(solution)/shard_map/ppermute | solution.py:18
  2.9 21.7 %collective-permute-start.5 = (f32[2,256,256]{2,1,0:T(8,128)}, f32[2,256,256]{2,1,0:T(8,128)}, u32[]{:S(2)}, u32[]{:S(2)}) collective-permute-start(f32[2,256,256]{2,1,0:T(8,128)} %param.19), channel_id=1, source_target_pairs={{0,1},{1,0},{2,3},{3,2},{4,5},{5,4},{6,7},{7,6},{8,9},{9,8},{10,11... | collective-permute-start | bytes 1572872 | tf_op jit(solution)/shard_map/ppermute | solution.py:438
  11.0 2.0 %copy-start.4 = (s32[2,2]{1,0:T(2,128)S(1)}, s32[2,2]{1,0:T(2,128)}, u32[]{:S(2)}) copy-start(s32[2,2]{1,0:T(2,128)} %param.17) | copy-start | bytes 52
  13.0 1.5 %copy-start.2 = (bf16[1,2,256,256]{3,2,1,0:T(8,128)(2,1)}, bf16[1,2,256,256]{3,2,1,0:T(8,128)(2,1)S(1)}, u32[]{:S(2)}) copy-start(bf16[1,2,256,256]{3,2,1,0:T(8,128)(2,1)S(1)} %collective-permute-done.2.mine_ref) | copy-start | bytes 786436
  13.0 1.5 %collective-permute-start.3 = (bf16[1,2,256,256]{3,2,1,0:T(8,128)(2,1)S(1)}, bf16[1,2,256,256]{3,2,1,0:T(8,128)(2,1)S(1)}, u32[]{:S(2)}, u32[]{:S(2)}) collective-permute-start(bf16[1,2,256,256]{3,2,1,0:T(8,128)(2,1)S(1)} %collective-permute-done.2.mine_ref), channel_id=1, source_target_pairs={{0,1},{1,0},{2,3},{3,2},{4,5},{5,4},{6,7},{7,6},{8,9},{9,8},{10,11... | collective-permute-start | bytes 786440 | tf_op jit(solution)/shard_map/ppermute | solution.py:432
  14.5 0.7 %copy-start.3 = (bf16[1,2,256,256]{3,2,1,0:T(8,128)(2,1)}, bf16[1,2,256,256]{3,2,1,0:T(8,128)(2,1)S(1)}, u32[]{:S(2)}) copy-start(bf16[1,2,256,256]{3,2,1,0:T(8,128)(2,1)S(1)} %collective-permute-done.3.partner_ref) | copy-start | bytes 786436
  15.2 3.0 %copy-start.1 = (bf16[2,256,256]{2,1,0:T(8,128)(2,1)S(1)}, bf16[2,256,256]{2,1,0:T(8,128)(2,1)}, u32[]{:S(2)}) copy-start(bf16[2,256,256]{2,1,0:T(8,128)(2,1)} %param.16) | copy-start | bytes 786436
  20.2 8.7 %collective-permute-start.4 = (bf16[1,2,256,256]{3,2,1,0:T(8,128)(2,1)}, bf16[1,2,256,256]{3,2,1,0:T(8,128)(2,1)}, u32[]{:S(2)}, u32[]{:S(2)}) collective-permute-start(bf16[1,2,256,256]{3,2,1,0:T(8,128)(2,1)} %get-tuple-element.193), channel_id=1, source_target_pairs={{0,2},{1,3},{4,6},{5,7},{8,10},{9,11},{12,14},{13,15},{16,18},{17,... | collective-permute-start | bytes 786440 | tf_op jit(solution)/shard_map/ppermute | solution.py:497
  30.7 14.3 %collective-permute-start.6 = (bf16[1,2,256,256]{3,2,1,0:T(8,128)(2,1)}, bf16[1,2,256,256]{3,2,1,0:T(8,128)(2,1)}, u32[]{:S(2)}, u32[]{:S(2)}) collective-permute-start(bf16[1,2,256,256]{3,2,1,0:T(8,128)(2,1)} %get-tuple-element.159), channel_id=1, source_target_pairs={{2,0},{3,1},{6,4},{7,5},{10,8},{11,9},{14,12},{15,13},{18,16},{19,... | collective-permute-start | bytes 786440 | tf_op jit(solution)/shard_map/ppermute | solution.py:509
  50.9 13.4 %copy-start = (bf16[2,512,512]{2,1,0:T(8,128)(2,1)S(1)}, bf16[2,512,512]{2,1,0:T(8,128)(2,1)}, u32[]{:S(2)}) copy-start(bf16[2,512,512]{2,1,0:T(8,128)(2,1)} %get-tuple-element.195) | copy-start | bytes 3145732
  50.9 1.6 %collective-permute-start.8 = (bf16[2,256,256]{2,1,0:T(8,128)(2,1)S(1)}, bf16[2,256,256]{2,1,0:T(8,128)(2,1)S(1)}, u32[]{:S(2)}, u32[]{:S(2)}) collective-permute-start(bf16[2,256,256]{2,1,0:T(8,128)(2,1)S(1)} %constant_dynamic-slice_fusion.1), channel_id=1, source_target_pairs={{0,1},{1,0},{2,3},{3,2},{4,5},{5,4},{6,7},{7,6},{8,9},{9,8},{10,11... | collective-permute-start | bytes 786440 | tf_op jit(solution)/shard_map/ppermute | solution.py:516
  52.6 10.1 %collective-permute-start.9 = (bf16[2,256,256]{2,1,0:T(8,128)(2,1)S(1)}, bf16[2,256,256]{2,1,0:T(8,128)(2,1)S(1)}, u32[]{:S(2)}, u32[]{:S(2)}) collective-permute-start(bf16[2,256,256]{2,1,0:T(8,128)(2,1)S(1)} %add_convert_fusion), channel_id=1, source_target_pairs={{0,4},{4,8},{8,12},{1,5},{5,9},{9,13},{2,6},{6,10},{10,14},{3,7},{... | collective-permute-start | bytes 786440 | tf_op jit(solution)/shard_map/ppermute | solution.py:518
  56.9 5.8 %collective-permute-start.7 = (bf16[2,256,512]{2,1,0:T(8,128)(2,1)S(1)}, bf16[2,256,512]{2,1,0:T(8,128)(2,1)S(1)}, u32[]{:S(2)}, u32[]{:S(2)}) collective-permute-start(bf16[2,256,512]{2,1,0:T(8,128)(2,1)S(1)} %get-tuple-element.172), channel_id=1, source_target_pairs={{0,1},{1,0},{2,3},{3,2},{4,5},{5,4},{6,7},{7,6},{8,9},{9,8},{10,11... | collective-permute-start | bytes 1572872 | tf_op jit(solution)/shard_map/ppermute | solution.py:520
  62.7 1.5 %collective-permute-start.10 = (bf16[2,256,256]{2,1,0:T(8,128)(2,1)S(1)}, bf16[2,256,256]{2,1,0:T(8,128)(2,1)S(1)}, u32[]{:S(2)}, u32[]{:S(2)}) collective-permute-start(bf16[2,256,256]{2,1,0:T(8,128)(2,1)S(1)} %collective-permute-done.9), channel_id=1, source_target_pairs={{0,1},{1,0},{2,3},{3,2},{4,5},{5,4},{6,7},{7,6},{8,9},{9,8},{10,11... | collective-permute-start | bytes 786440 | tf_op jit(solution)/shard_map/ppermute | solution.py:521

commit v10 on v9

--- a/solution.py
+++ b/solution.py
@@ -40,6 +40,16 @@
     upper = jnp.concatenate([real_part, imag_part], axis=1)
     lower = jnp.concatenate([-imag_part, real_part], axis=1)
     return jnp.concatenate([upper, lower], axis=0)
+
+
+def dft_parts(width):
+    freq = jnp.arange(width, dtype=jnp.int32)
+    product = freq[:, None] * freq[None, :] % width
+    angle = 2.0 * math.pi / width * product.astype(jnp.float32)
+    scale = 1.0 / math.sqrt(width)
+    real_part = (jnp.cos(angle) * scale).astype(jnp.bfloat16)
+    imag_part = (-jnp.sin(angle) * scale).astype(jnp.bfloat16)
+    return (real_part, imag_part)
 
 
 def chirp_parts(width, coef):
@@ -119,10 +129,9 @@
         wave_ref = refs.pop(0)
         patch_ref = refs.pop(0)
         chirp_ref = refs.pop(0)
-        fl_ref, fr_ref, gl_ref, gr_ref = refs[:4]
-        refs = refs[4:]
+        blocks = refs[:2]
+        refs = refs[2:]
         extra_ref = refs.pop(0) if (residual_after or backward) else None
-        width = wave_ref.shape[2]
         wave = wave_ref[0].astype(jnp.float32)
         patch_re = patch_ref[0, 0]
         patch_im = patch_ref[0, 1]
@@ -132,26 +141,11 @@
         else:
             wave_re = wave[0]
             wave_im = wave[1]
-        stacked = jnp.concatenate([wave_re, wave_im], axis=0).astype(jnp.bfloat16)
-        first = jnp.dot(fl_ref[...], stacked, preferred_element_type=jnp.float32).astype(jnp.bfloat16)
-        rowwise = jnp.concatenate([first[:width], first[width:]], axis=1)
-        spectrum = jnp.dot(rowwise, fr_ref[...], preferred_element_type=jnp.float32)
-        spec_re = spectrum[:, :width]
-        spec_im = spectrum[:, width:]
         chirp_re = chirp_ref[0]
         chirp_im = chirp_ref[1]
         if backward:
             chirp_im = -chirp_im
-        filtered = jnp.concatenate(
-            [spec_re * chirp_re - spec_im * chirp_im, spec_re * chirp_im + spec_im * chirp_re],
-            axis=1,
-        ).astype(jnp.bfloat16)
-        back = jnp.dot(filtered, gr_ref[...], preferred_element_type=jnp.float32).astype(jnp.bfloat16)
-        columnwise = jnp.concatenate([back[:, :width], back[:, width:]], axis=0)
-        out = jnp.dot(gl_ref[...], columnwise, preferred_element_type=jnp.float32).astype(jnp.bfloat16)
-        values = out.astype(jnp.float32)
-        out_re = values[:width]
-        out_im = values[width:]
+        out_re, out_im = propagate_block(wave_re, wave_im, blocks, chirp_re, chirp_im)
         if residual_after:
             measured = extra_ref[0]
             weight = RESIDUAL_SCALE * (out_re * out_re + out_im * out_im - measured)
@@ -167,8 +161,8 @@
             term_ref[0, 1] = source[0] * out_im - source[1] * out_re
         else:
             result_ref = refs[0]
-            result_ref[0, 0] = out[:width]
-            result_ref[0, 1] = out[width:]
+            result_ref[0, 0] = out_re.astype(jnp.bfloat16)
+            result_ref[0, 1] = out_im.astype(jnp.bfloat16)
 
     return kernel
 
@@ -177,8 +171,10 @@
     number, _, width, _ = waves.shape
     wave_spec = pl.BlockSpec((1, 2, width, width), lambda i: (i, 0, 0, 0))
     chirp_spec = pl.BlockSpec((2, width, width), lambda i: (0, 0, 0))
-    block_spec = pl.BlockSpec((2 * width, 2 * width), lambda i: (0, 0))
-    in_specs = [wave_spec, wave_spec, chirp_spec] + [block_spec] * 4
+    in_specs = [wave_spec, wave_spec, chirp_spec] + [
+        pl.BlockSpec((2 * width, width), lambda i: (0, 0)),
+        pl.BlockSpec((width, 2 * width), lambda i: (0, 0)),
+    ]
     args = [waves, patches, chirps] + list(blocks)
     if residual_after:
         in_specs.append(pl.BlockSpec((1, width, width), lambda i: (i, 0, 0)))
@@ -284,23 +280,34 @@
 
 
 def propagate_block(wave_re, wave_im, blocks, chirp_re, chirp_im):
-    fl_ref, fr_ref, gl_ref, gr_ref = blocks
+    rows_ref, cols_ref = blocks
     width = wave_re.shape[0]
-    stacked = jnp.concatenate([wave_re, wave_im], axis=0).astype(jnp.bfloat16)
-    first = jnp.dot(fl_ref[...], stacked, preferred_element_type=jnp.float32).astype(jnp.bfloat16)
-    rowwise = jnp.concatenate([first[:width], first[width:]], axis=1)
-    spectrum = jnp.dot(rowwise, fr_ref[...], preferred_element_type=jnp.float32)
-    spec_re = spectrum[:, :width]
-    spec_im = spectrum[:, width:]
-    filtered = jnp.concatenate(
-        [spec_re * chirp_re - spec_im * chirp_im, spec_re * chirp_im + spec_im * chirp_re],
-        axis=1,
-    ).astype(jnp.bfloat16)
-    back = jnp.dot(filtered, gr_ref[...], preferred_element_type=jnp.float32).astype(jnp.bfloat16)
-    columnwise = jnp.concatenate([back[:, :width], back[:, width:]], axis=0)
-    out = jnp.dot(gl_ref[...], columnwise, preferred_element_type=jnp.float32).astype(jnp.bfloat16)
-    values = out.astype(jnp.float32)
-    return (values[:width], values[width:])
+    dft_rows = rows_ref[...]
+    dft_cols = cols_ref[...]
+
+    def left(part_re, part_im):
+        lanes = jnp.concatenate([part_re, part_im], axis=1).astype(jnp.bfloat16)
+        return jnp.dot(dft_rows, lanes, preferred_element_type=jnp.float32)
+
+    def right(part_re, part_im):
+        rows = jnp.concatenate([part_re, part_im], axis=0).astype(jnp.bfloat16)
+        return jnp.dot(rows, dft_cols, preferred_element_type=jnp.float32)
+
+    first = left(wave_re, wave_im)
+    z_re = (first[:width, :width] - first[width:, width:]).astype(jnp.bfloat16)
+    z_im = (first[:width, width:] + first[width:, :width]).astype(jnp.bfloat16)
+    second = right(z_re, z_im)
+    spec_re = second[:width, :width] - second[width:, width:]
+    spec_im = second[:width, width:] + second[width:, :width]
+    w_re = spec_re * chirp_re - spec_im * chirp_im
+    w_im = spec_re * chirp_im + spec_im * chirp_re
+    third = right(w_re.astype(jnp.bfloat16), w_im.astype(jnp.bfloat16))
+    v_re = (third[:width, :width] + third[width:, width:]).astype(jnp.bfloat16)
+    v_im = (third[width:, :width] - third[:width, width:]).astype(jnp.bfloat16)
+    fourth = left(v_re, v_im)
+    out_re = (fourth[:width, :width] + fourth[width:, width:]).astype(jnp.bfloat16)
+    out_im = (fourth[:width, width:] - fourth[width:, :width]).astype(jnp.bfloat16)
+    return (out_re.astype(jnp.float32), out_im.astype(jnp.float32))
 
 
 def place_term(term_re, term_im, row, column, alive, total_ref, direct_ref=None):
@@ -330,8 +337,8 @@
         wave_ref = refs.pop(0)
         patch_ref = refs.pop(0)
         chirp_ref = refs.pop(0)
-        blocks = refs[:4]
-        refs = refs[4:]
+        blocks = refs[:2]
+        refs = refs[2:]
         if last:
             own_ref = refs.pop(0)
             partner_ref = refs.pop(0)
@@ -388,8 +395,10 @@
     number, _, width, _ = waves.shape
     wave_spec = pl.BlockSpec((1, 2, width, width), lambda i, *s: (i, 0, 0, 0))
     chirp_spec = pl.BlockSpec((2, width, width), lambda i, *s: (0, 0, 0))
-    block_spec = pl.BlockSpec((2 * width, 2 * width), lambda i, *s: (0, 0))
-    in_specs = [wave_spec, wave_spec, chirp_spec] + [block_spec] * 4
+    in_specs = [wave_spec, wave_spec, chirp_spec] + [
+        pl.BlockSpec((2 * width, width), lambda i, *s: (0, 0)),
+        pl.BlockSpec((width, 2 * width), lambda i, *s: (0, 0)),
+    ]
     if last:
         slot_spec = pl.BlockSpec((1, width, width), lambda i, r, c, a, s, o: (s[i], 0, 0))
         in_specs += [slot_spec, slot_spec]
@@ -456,8 +465,6 @@
     order = jnp.reshape(batch_index, (1,)).astype(jnp.int32)
     patches = cut_patches(object_field, mine, partner, local_rows, local_columns, order, width)
     number = patches.shape[0]
-    forward_block = dft_block(width, -1.0)
-    inverse_block = dft_block(width, 1.0)
     coef = jnp.where(
         segment == depth_count - 1, jnp.float32(DETECTOR_COEF), jnp.float32(SLICE_COEF)
     )
@@ -465,7 +472,11 @@
     start = jnp.broadcast_to(probe[None], (number, 2, width, width))
 
     chirps = jnp.stack([chirp_re, chirp_im])
-    blocks = (forward_block, dft_right(width, -1.0), inverse_block, dft_right(width, 1.0))
+    dft_re, dft_im = dft_parts(width)
+    blocks = (
+        jnp.concatenate([dft_re, dft_im], axis=0),
+        jnp.concatenate([dft_re, dft_im], axis=1),
+    )
 
     def forward_all(waves):
         return run_waves(waves, patches, chirps, blocks)

time: 65.9 us -> 61.2 us (0.929)
  waiting for transfers between devices: 28.2 us -> 31.5 us
  local copies, waits for them, and re-layouts: 6.21 us -> 3.94 us
  other arithmetic: 6.25 us -> 4.1 us
  Pallas kernels: 9.53 us -> 7.47 us
  starting transfers between devices: 11.1 us -> 10 us
    ppermute x1, waiting for transfers between devices: 1.95 us -> 4.32 us  [from_behind(): return lax.ppermute(block, axis, route)]
    pallas_call x1, Pallas kernels: 4.63 us -> 3.01 us  [run_adjoint(): pl.pallas_call(adjoint_kernel(last, number == 1), grid_spec=grid_spec, ou...]
    slice x1, local copies, waits for them, and re-layouts: 1.27 us -> 0.07 us  [local(): spill = gradient[:, tile_rows:, :]]
    ppermute x1, waiting for transfers between devices: 13 us -> 14.1 us  [local(): carry = lax.ppermute(carry, 'depth', [(turn + 1, turn)])]
    neg x1 -> x0, other arithmetic: 1 us -> none  [dft_block(): upper = jnp.concatenate([real_part, -imag_part], axis=1)]
    another operation x2, local copies, waits for them, and re-layouts: 1.78 us -> 0.79 us
    convert_element_type x2 -> x1, other arithmetic: 1.99 us -> 1.1 us  [dft_parts(): imag_part = (-jnp.sin(angle) * scale).astype(jnp.bfloat16)]
    ppermute x1, starting transfers between devices: 4.25 us -> 3.5 us  [local(): lax.ppermute(spill_sum, 'tile', [(t, t + 1) for t in range(tile_count - 1)])]
  transfers between devices with their start and end apart: 11 -> 11, of which waited for: 7 -> 7; matrix products, arithmetic and copies ran while one was open for 11% -> 8% of each run, Pallas kernels for 7% -> 7%
where the time goes in v10:
time: 61.2 us; the launch traced here: 60.9 us
  waiting for transfers between devices  31.5 us (51%)
  starting transfers between devices  10 us (16%)
  Pallas kernels  7.47 us (12%)
  other arithmetic  4.1 us (7%)
  local copies, waits for them, and re-layouts  3.94 us (6%)
  between operations  3.78 us (6%)
    ppermute x1, waiting for transfers between devices, local(): carry = lax.ppermute(carry, 'depth', [(turn + 1, turn)])  14.1 us
    ppermute x1, waiting for transfers between devices, local(): lax.ppermute(spill_sum, 'tile', [(t, t + 1) for t in range(tile_count - 1)])  5.75 us
    ppermute x1, waiting for transfers between devices, from_behind(): return lax.ppermute(block, axis, route)  4.32 us
    ppermute x1, waiting for transfers between devices, local(): carry = lax.ppermute(carry, 'depth', [(depth_count - 2, depth_count - 1)])  3.96 us
    ppermute x1, starting transfers between devices, local(): lax.ppermute(spill_sum, 'tile', [(t, t + 1) for t in range(tile_count - 1)])  3.5 us
    pallas_call x1, Pallas kernels, run_adjoint(): pl.pallas_call(adjoint_kernel(last, number == 1), grid_spec=grid_spec, ou...  3.01 us
    pallas_call x1, Pallas kernels, cut_patches(): pl.pallas_call(cut_kernel, grid_spec=grid_spec, out_shape=jax.ShapeDtypeS...  2.98 us
    ppermute x1, starting transfers between devices, local(): carry = lax.ppermute(carry, 'depth', [(depth_count - 2, depth_count - 1)])  2.79 us
  transfers between devices with their start and end apart: 11, of which 7 were waited for; matrix products, arithmetic and copies ran while one was open for 8% of the time, Pallas kernels for 7%

profile of v10, /device:TPU:0, one launch (start us, length us, event | category | flops | bytes accessed | tf_op | source)
XLA Modules:
  0.0 60.9 jit_solution(17425425787479848271)
XLA Ops:
  0.0 0.5 collective-permute-start.1
  0.5 1.1 %dynamic-slice_convert_fusion = bf16[1,2,256,256]{3,2,1,0:T(8,128)(2,1)S(1)} fusion(f32[1,2,256,512]{3,2,1,0:T(8,128)} %tile_ref.1, s32[]{:T(128)S(6)} %select_n.84), kind=kLoop, calls=%fused_computation.4 | loop fusion | bytes 524292 | tf_op jit(solution)/shard_map/convert_element_type | solution.py:439
  1.6 1.3 %collective-permute-start.2 = (bf16[1,2,256,256]{3,2,1,0:T(8,128)(2,1)S(1)}, bf16[1,2,256,256]{3,2,1,0:T(8,128)(2,1)S(1)}, u32[]{:S(2)}, u32[]{:S(2)}) collective-permute-start(bf16[1,2,256,256]{3,2,1,0:T(8,128)(2,1)S(1)} %dynamic-slice_convert_fusion), channel_id=1, source_target_pairs={{4,0},{8,4},{12,8},{5,1},{9,5},{13,9},{6,2},{10,6},{14,10},{7,3},{... | collective-permute-start | bytes 786440 | tf_op jit(solution)/shard_map/ppermute | solution.py:18
  2.9 0.5 collective-permute-start.5
  3.4 1.1 %multiply_convert_fusion = (bf16[256,256]{1,0:T(8,128)(2,1)S(1)}, bf16[256,256]{1,0:T(8,128)(2,1)S(1)}) fusion(), kind=kLoop, calls=%fused_computation.13 | loop fusion | flops 1245184 | bytes 262144 | tf_op jit(solution)/shard_map/convert_element_type | solution.py:51
  4.6 1.0 %fusion.6 = (f32[1,256,256]{2,1,0:T(8,128)S(1)}, f32[1,256,256]{2,1,0:T(8,128)S(1)}) fusion(s32[256]{0:T(256)S(1)} %fusion.9, f32[]{:T(128)S(6)} %neg.8), kind=kLoop, calls=%fused_computation.19 | loop fusion | flops 196608 | bytes 525316 | tf_op jit(solution)/shard_map/cos | solution.py:61
  6.3 0.6 %broadcast_select_fusion = s32[2]{0:T(128)S(1)} fusion(pred[]{:T(512)} %eq.23, s32[1]{0:T(128)} %collective-permute-done.1, s32[1]{0:T(128)S(6)} %copy.14), kind=kLoop, calls=%fused_computation.30 | loop fusion | flops 6 | bytes 17 | tf_op jit(solution)/shard_map/jit(_where)/select_n | solution.py:453
  6.9 0.7 %fusion.12 = (s32[1]{0:T(128)}, s32[1]{0:T(128)}) fusion(s32[2]{0:T(128)S(1)} %broadcast_select_fusion), kind=kLoop, calls=%fused_computation.32 | loop fusion | bytes 16 | tf_op jit(solution)/shard_map/slice | solution.py:457
  8.7 4.3 %collective-permute-done.2.mine_ref = bf16[1,2,256,256]{3,2,1,0:T(8,128)(2,1)S(1)} collective-permute-done((bf16[1,2,256,256]{3,2,1,0:T(8,128)(2,1)S(1)}, bf16[1,2,256,256]{3,2,1,0:T(8,128)(2,1)S(1)}, u32[]{:S(2)}, u32[]{:S(2)}) %collective-permute-start.2) | collective-permute-done | bytes 262176 | tf_op jit(solution)/shard_map/ppermute | solution.py:18
  13.1 0.6 %fusion.13 = (s32[1,1]{1,0:T(1,128)}, s32[1,1]{1,0:T(1,128)}) fusion(s32[1,2]{1,0:T(1,128)S(1)} %constant_dynamic-slice_fusion), kind=kLoop, calls=%fused_computation.33 | loop fusion | bytes 16 | tf_op jit(solution)/shard_map/slice | solution.py:464
  14.3 0.3 collective-permute-done.3.partner_ref
  14.6 0.7 %copy-done.4 = bf16[1,2,256,256]{3,2,1,0:T(8,128)(2,1)} copy-done((bf16[1,2,256,256]{3,2,1,0:T(8,128)(2,1)}, bf16[1,2,256,256]{3,2,1,0:T(8,128)(2,1)S(1)}, u32[]{:S(2)}) %copy-start.4) | copy-done | bytes 262168
  15.3 3.0 %shard_map.60 = f32[1,2,256,256]{3,2,1,0:T(8,128)S(1)} custom-call(s32[1]{0:T(128)} %sub.17.rows_ref, s32[1]{0:T(128)} %bitcast.4.columns_ref, s32[1]{0:T(128)} %bitcast.order_ref, f32[1,2,256,512]{3,2,1,0:T(8,128)} %tile_ref.1, bf16[1,2,256,256]{3,2,1,0:T(8,128)(2,1)} %copy-done.3, bf16[1,2,256,256]{3,2,1,0:T(8,128)(2,1)} %copy-done.4), custom_call_target="tpu_custom_call" | custom-call | tf_op jit(solution)/shard_map/pallas_call | solution.py:275
  18.3 1.5 %conditional.3 = (bf16[1,2,256,256]{3,2,1,0:T(8,128)(2,1)S(1)}) conditional(s32[]{:T(128)} %convert_element_type.71, () %tuple.54, (bf16[1,2,256,256]{3,2,1,0:T(8,128)(2,1)S(1)}, f32[1,2,256,256]{3,2,1,0:T(8,128)S(1)}, f32[2,256,256]{2,1,0:T(8,128)S(1)}, bf16[512,256]{1,0:T(8,128)(2,1)S(1)}, bf16[256,512]{1,0:T(8,128)(2,1)S(1)}) %tuple.76), branch_computations={%region_0.1_spmd, %region_1.2_spmd} | conditional | bytes 262154 | solution.py:493
  18.3 1.5 %branch_1_fun.5 = bf16[1,2,256,256]{3,2,1,0:T(8,128)(2,1)S(1)} custom-call(bf16[1,2,256,256]{3,2,1,0:T(8,128)(2,1)S(1)} %get-tuple-element.109.refs_0_, f32[1,2,256,256]{3,2,1,0:T(8,128)S(1)} %get-tuple-element.110.refs_1_, f32[2,256,256]{2,1,0:T(8,128)S(1)} %get-tuple-element.111.refs_2_, bf16[512,256]{1,0:T(8,128)(2,1)S(1)} %get-tuple-element.112.refs_3_, ...), custom_call_target="tpu_custom_call" | custom-call | tf_op jit(solution)/shard_map/cond/branch_1_fun/pallas_call | solution.py:193
  19.8 2.8 %collective-permute-start.4 = (bf16[1,2,256,256]{3,2,1,0:T(8,128)(2,1)S(1)}, bf16[1,2,256,256]{3,2,1,0:T(8,128)(2,1)}, u32[]{:S(2)}, u32[]{:S(2)}) collective-permute-start(bf16[1,2,256,256]{3,2,1,0:T(8,128)(2,1)S(1)} %get-tuple-element.167), channel_id=1, source_target_pairs={{0,2},{1,3},{4,6},{5,7},{8,10},{9,11},{12,14},{13,15},{16,18},{17,... | collective-permute-start | bytes 786440 | tf_op jit(solution)/shard_map/ppermute | solution.py:508
  23.8 4.0 %collective-permute-done.4 = bf16[1,2,256,256]{3,2,1,0:T(8,128)(2,1)} collective-permute-done((bf16[1,2,256,256]{3,2,1,0:T(8,128)(2,1)S(1)}, bf16[1,2,256,256]{3,2,1,0:T(8,128)(2,1)}, u32[]{:S(2)}, u32[]{:S(2)}) %collective-permute-start.4) | collective-permute-done | bytes 262176 | tf_op jit(solution)/shard_map/ppermute | solution.py:508
  27.8 0.8 %conditional.4 = ((bf16[1,2,256,256]{3,2,1,0:T(8,128)(2,1)}, bf16[2,512,512]{2,1,0:T(8,128)(2,1)S(1)})) conditional(s32[]{:T(128)} %convert_element_type.72, () %tuple.53, (s32[1]{0:T(128)}, s32[1]{0:T(128)}, s32[1]{0:T(128)}, s32[1]{0:T(128)}, s32[1]{0:T(128)}, /*index=5*/bf16[1,2,256,256]{3,2,1,0:T(8,128)(2,1)}, f32[1,2,256,256]{3,2,1,0:T(8,128)S(1)}, ...), branch_computations={%region_2.3_spmd, %region_3.4_spmd} | conditional | bytes 2097188 | solution.py:509
  27.8 0.7 %broadcast.197 = bf16[1,2,256,256]{3,2,1,0:T(8,128)(2,1)} broadcast(bf16[]{:T(256)} %constant.84.clone), dimensions={} | broadcast | bytes 262146 | tf_op jit(solution)/shard_map/broadcast.11
  28.5 0.1 broadcast.198
  28.6 1.3 %collective-permute-start.6 = (bf16[1,2,256,256]{3,2,1,0:T(8,128)(2,1)}, bf16[1,2,256,256]{3,2,1,0:T(8,128)(2,1)S(1)}, u32[]{:S(2)}, u32[]{:S(2)}) collective-permute-start(bf16[1,2,256,256]{3,2,1,0:T(8,128)(2,1)} %get-tuple-element.141), channel_id=1, source_target_pairs={{2,0},{3,1},{6,4},{7,5},{10,8},{11,9},{14,12},{15,13},{18,16},{19,... | collective-permute-start | bytes 786440 | tf_op jit(solution)/shard_map/ppermute | solution.py:520
  29.9 14.1 %collective-permute-done.6 = bf16[1,2,256,256]{3,2,1,0:T(8,128)(2,1)S(1)} collective-permute-done((bf16[1,2,256,256]{3,2,1,0:T(8,128)(2,1)}, bf16[1,2,256,256]{3,2,1,0:T(8,128)(2,1)S(1)}, u32[]{:S(2)}, u32[]{:S(2)}) %collective-permute-start.6) | collective-permute-done | bytes 262176 | tf_op jit(solution)/shard_map/ppermute | solution.py:520
  44.0 3.0 %conditional.5 = (bf16[2,512,512]{2,1,0:T(8,128)(2,1)S(1)}) conditional(s32[]{:T(128)} %convert_element_type.71, bf16[2,512,512]{2,1,0:T(8,128)(2,1)S(1)} %get-tuple-element.140, (s32[1]{0:T(128)}, s32[1]{0:T(128)}, s32[1]{0:T(128)}, s32[1]{0:T(128)}, s32[1]{0:T(128)}, /*index=5*/bf16[1,2,256,256]{3,2,1,0:T(8,128)(2,1)S(1)}, ...), branch_computations={%region_4.5_spmd, %region_5.6_spmd} | conditional | bytes 8 | solution.py:521
  44.0 3.0 %branch_1_fun.7 = (bf16[1,2,256,256]{3,2,1,0:T(8,128)(2,1)}, bf16[2,512,512]{2,1,0:T(8,128)(2,1)S(1)}) custom-call(s32[1]{0:T(128)} %get-tuple-element.126.rows_ref, s32[1]{0:T(128)} %get-tuple-element.127.columns_ref, s32[1]{0:T(128)} %get-tuple-element.128.live_ref, s32[1]{0:T(128)} %get-tuple-element.129.slot_ref, s32[1]{0:T(128)} %get-tuple-element.130.other_ref, ...), custom_call_target="tpu_custom_call" | custom-call | tf_op jit(solution)/shard_map/cond/branch_1_fun/pallas_call | solution.py:417
  47.0 0.1 fusion.11
  47.1 0.1 collective-permute-start.8
  47.2 1.5 %collective-permute-done.8 = bf16[2,256,256]{2,1,0:T(8,128)(2,1)S(1)} collective-permute-done((bf16[2,256,256]{2,1,0:T(8,128)(2,1)S(1)}, bf16[2,256,256]{2,1,0:T(8,128)(2,1)S(1)}, u32[]{:S(2)}, u32[]{:S(2)}) %collective-permute-start.8) | collective-permute-done | bytes 262176 | tf_op jit(solution)/shard_map/ppermute | solution.py:527
  48.8 3.5 %collective-permute-start.9 = (bf16[2,256,256]{2,1,0:T(8,128)(2,1)S(1)}, bf16[2,256,256]{2,1,0:T(8,128)(2,1)S(1)}, u32[]{:S(2)}, u32[]{:S(2)}) collective-permute-start(bf16[2,256,256]{2,1,0:T(8,128)(2,1)S(1)} %add_convert_fusion), channel_id=1, source_target_pairs={{0,4},{4,8},{8,12},{1,5},{5,9},{9,13},{2,6},{6,10},{10,14},{3,7},{... | collective-permute-start | bytes 786440 | tf_op jit(solution)/shard_map/ppermute | solution.py:529
  52.3 0.1 collective-permute-start.7
  52.4 5.8 %collective-permute-done.9 = bf16[2,256,256]{2,1,0:T(8,128)(2,1)S(1)} collective-permute-done((bf16[2,256,256]{2,1,0:T(8,128)(2,1)S(1)}, bf16[2,256,256]{2,1,0:T(8,128)(2,1)S(1)}, u32[]{:S(2)}, u32[]{:S(2)}) %collective-permute-start.9) | collective-permute-done | bytes 262176 | tf_op jit(solution)/shard_map/ppermute | solution.py:529
  58.1 1.5 %collective-permute-done.10 = bf16[2,256,256]{2,1,0:T(8,128)(2,1)S(1)} collective-permute-done((bf16[2,256,256]{2,1,0:T(8,128)(2,1)S(1)}, bf16[2,256,256]{2,1,0:T(8,128)(2,1)S(1)}, u32[]{:S(2)}, u32[]{:S(2)}) %collective-permute-start.10) | collective-permute-done | bytes 262176 | tf_op jit(solution)/shard_map/ppermute | solution.py:532
  59.7 1.2 %add_bitcast_fusion = f32[1,2,256,512]{3,2,1,0:T(8,128)} fusion(bf16[2,256,512]{2,1,0:T(8,128)(2,1)S(1)} %collective-permute-done.7, bf16[2,256,256]{2,1,0:T(8,128)(2,1)S(1)} %collective-permute-done.10, bf16[2,256,256]{2,1,0:T(8,128)(2,1)S(1)} %collective-permute-done.9, pred[]{:T(512)} %eq.23, bf16[2,512,512]{2,1,0:T(8,128)(2,1)S(1)} %get-tuple-element.169), kind=kLoop, calls=%fused_computation | loop fusion | flops 3670016 | bytes 2621441 | tf_op jit(solution)/shard_map/broadcast_in_dim | solution.py:540
  (24 shorter events, 0.3 us)
Async XLA Ops:
  0.0 2.9 %copy-start.1 = (f32[2,256,256]{2,1,0:T(8,128)S(1)}, f32[2,256,256]{2,1,0:T(8,128)}, u32[]{:S(2)}) copy-start(f32[2,256,256]{2,1,0:T(8,128)} %param.19) | copy-start | bytes 1572868
  0.0 6.3 %collective-permute-start.1 = (s32[1]{0:T(128)}, s32[1]{0:T(128)}, u32[]{:S(2)}, u32[]{:S(2)}) collective-permute-start(s32[1]{0:T(128)} %param.18), channel_id=1, source_target_pairs={{0,1},{1,0},{2,3},{3,2},{4,5},{5,4},{6,7},{7,6},{8,9},{9,8},{10,11... | collective-permute-start | bytes 20 | tf_op jit(solution)/shard_map/ppermute | solution.py:446
  0.5 12.6 %collective-permute-start = (s32[2,2]{1,0:T(2,128)}, s32[2,2]{1,0:T(2,128)S(1)}, u32[]{:S(2)}, u32[]{:S(2)}) collective-permute-start(s32[2,2]{1,0:T(2,128)} %param.17), channel_id=1, source_target_pairs={{0,1},{1,0},{2,3},{3,2},{4,5},{5,4},{6,7},{7,6},{8,9},{9,8},{10,11... | collective-permute-start | bytes 56 | tf_op jit(solution)/shard_map/ppermute | solution.py:445
  1.6 11.5 %collective-permute-start.2 = (bf16[1,2,256,256]{3,2,1,0:T(8,128)(2,1)S(1)}, bf16[1,2,256,256]{3,2,1,0:T(8,128)(2,1)S(1)}, u32[]{:S(2)}, u32[]{:S(2)}) collective-permute-start(bf16[1,2,256,256]{3,2,1,0:T(8,128)(2,1)S(1)} %dynamic-slice_convert_fusion), channel_id=1, source_target_pairs={{4,0},{8,4},{12,8},{5,1},{9,5},{13,9},{6,2},{10,6},{14,10},{7,3},{... | collective-permute-start | bytes 786440 | tf_op jit(solution)/shard_map/ppermute | solution.py:18
  2.9 20.9 %collective-permute-start.5 = (f32[2,256,256]{2,1,0:T(8,128)S(1)}, f32[2,256,256]{2,1,0:T(8,128)S(1)}, u32[]{:S(2)}, u32[]{:S(2)}) collective-permute-start(f32[2,256,256]{2,1,0:T(8,128)S(1)} %copy-done.1), channel_id=1, source_target_pairs={{0,1},{1,0},{2,3},{3,2},{4,5},{5,4},{6,7},{7,6},{8,9},{9,8},{10,11... | collective-permute-start | bytes 1572872 | tf_op jit(solution)/shard_map/ppermute | solution.py:447
  8.7 4.3 %copy-start.5 = (s32[2,2]{1,0:T(2,128)S(1)}, s32[2,2]{1,0:T(2,128)}, u32[]{:S(2)}) copy-start(s32[2,2]{1,0:T(2,128)} %param.17) | copy-start | bytes 52
  13.0 1.5 %copy-start.3 = (bf16[1,2,256,256]{3,2,1,0:T(8,128)(2,1)}, bf16[1,2,256,256]{3,2,1,0:T(8,128)(2,1)S(1)}, u32[]{:S(2)}) copy-start(bf16[1,2,256,256]{3,2,1,0:T(8,128)(2,1)S(1)} %collective-permute-done.2.mine_ref) | copy-start | bytes 786436
  13.0 1.5 %collective-permute-start.3 = (bf16[1,2,256,256]{3,2,1,0:T(8,128)(2,1)S(1)}, bf16[1,2,256,256]{3,2,1,0:T(8,128)(2,1)S(1)}, u32[]{:S(2)}, u32[]{:S(2)}) collective-permute-start(bf16[1,2,256,256]{3,2,1,0:T(8,128)(2,1)S(1)} %collective-permute-done.2.mine_ref), channel_id=1, source_target_pairs={{0,1},{1,0},{2,3},{3,2},{4,5},{5,4},{6,7},{7,6},{8,9},{9,8},{10,11... | collective-permute-start | bytes 786440 | tf_op jit(solution)/shard_map/ppermute | solution.py:441
  14.6 0.7 %copy-start.4 = (bf16[1,2,256,256]{3,2,1,0:T(8,128)(2,1)}, bf16[1,2,256,256]{3,2,1,0:T(8,128)(2,1)S(1)}, u32[]{:S(2)}) copy-start(bf16[1,2,256,256]{3,2,1,0:T(8,128)(2,1)S(1)} %collective-permute-done.3.partner_ref) | copy-start | bytes 786436
  15.3 3.0 %copy-start = (bf16[2,256,256]{2,1,0:T(8,128)(2,1)S(1)}, bf16[2,256,256]{2,1,0:T(8,128)(2,1)}, u32[]{:S(2)}) copy-start(bf16[2,256,256]{2,1,0:T(8,128)(2,1)} %param.16) | copy-start | bytes 786436
  19.8 8.0 %collective-permute-start.4 = (bf16[1,2,256,256]{3,2,1,0:T(8,128)(2,1)S(1)}, bf16[1,2,256,256]{3,2,1,0:T(8,128)(2,1)}, u32[]{:S(2)}, u32[]{:S(2)}) collective-permute-start(bf16[1,2,256,256]{3,2,1,0:T(8,128)(2,1)S(1)} %get-tuple-element.167), channel_id=1, source_target_pairs={{0,2},{1,3},{4,6},{5,7},{8,10},{9,11},{12,14},{13,15},{16,18},{17,... | collective-permute-start | bytes 786440 | tf_op jit(solution)/shard_map/ppermute | solution.py:508
  28.6 15.4 %collective-permute-start.6 = (bf16[1,2,256,256]{3,2,1,0:T(8,128)(2,1)}, bf16[1,2,256,256]{3,2,1,0:T(8,128)(2,1)S(1)}, u32[]{:S(2)}, u32[]{:S(2)}) collective-permute-start(bf16[1,2,256,256]{3,2,1,0:T(8,128)(2,1)} %get-tuple-element.141), channel_id=1, source_target_pairs={{2,0},{3,1},{6,4},{7,5},{10,8},{11,9},{14,12},{15,13},{18,16},{19,... | collective-permute-start | bytes 786440 | tf_op jit(solution)/shard_map/ppermute | solution.py:520
  47.1 1.6 %collective-permute-start.8 = (bf16[2,256,256]{2,1,0:T(8,128)(2,1)S(1)}, bf16[2,256,256]{2,1,0:T(8,128)(2,1)S(1)}, u32[]{:S(2)}, u32[]{:S(2)}) collective-permute-start(bf16[2,256,256]{2,1,0:T(8,128)(2,1)S(1)} %constant_dynamic-slice_fusion.1), channel_id=1, source_target_pairs={{0,1},{1,0},{2,3},{3,2},{4,5},{5,4},{6,7},{7,6},{8,9},{9,8},{10,11... | collective-permute-start | bytes 786440 | tf_op jit(solution)/shard_map/ppermute | solution.py:527
  48.8 9.3 %collective-permute-start.9 = (bf16[2,256,256]{2,1,0:T(8,128)(2,1)S(1)}, bf16[2,256,256]{2,1,0:T(8,128)(2,1)S(1)}, u32[]{:S(2)}, u32[]{:S(2)}) collective-permute-start(bf16[2,256,256]{2,1,0:T(8,128)(2,1)S(1)} %add_convert_fusion), channel_id=1, source_target_pairs={{0,4},{4,8},{8,12},{1,5},{5,9},{9,13},{2,6},{6,10},{10,14},{3,7},{... | collective-permute-start | bytes 786440 | tf_op jit(solution)/shard_map/ppermute | solution.py:529
  52.3 5.8 %collective-permute-start.7 = (bf16[2,256,512]{2,1,0:T(8,128)(2,1)S(1)}, bf16[2,256,512]{2,1,0:T(8,128)(2,1)S(1)}, u32[]{:S(2)}, u32[]{:S(2)}) collective-permute-start(bf16[2,256,512]{2,1,0:T(8,128)(2,1)S(1)} %get-tuple-element.154), channel_id=1, source_target_pairs={{0,1},{1,0},{2,3},{3,2},{4,5},{5,4},{6,7},{7,6},{8,9},{9,8},{10,11... | collective-permute-start | bytes 1572872 | tf_op jit(solution)/shard_map/ppermute | solution.py:531
  58.1 1.5 %collective-permute-start.10 = (bf16[2,256,256]{2,1,0:T(8,128)(2,1)S(1)}, bf16[2,256,256]{2,1,0:T(8,128)(2,1)S(1)}, u32[]{:S(2)}, u32[]{:S(2)}) collective-permute-start(bf16[2,256,256]{2,1,0:T(8,128)(2,1)S(1)} %collective-permute-done.9), channel_id=1, source_target_pairs={{0,1},{1,0},{2,3},{3,2},{4,5},{5,4},{6,7},{7,6},{8,9},{9,8},{10,11... | collective-permute-start | bytes 786440 | tf_op jit(solution)/shard_map/ppermute | solution.py:532

commit v11 on v10

--- a/solution.py
+++ b/solution.py
@@ -424,6 +424,60 @@
     )(*scalars, waves, patches, chirps, *blocks, *extra)
 
 
+def first_kernel(rows_ref, columns_ref, order_ref, wave_ref, tile_ref, mine_ref, partner_ref,
+                 chirp_ref, dft_rows_ref, dft_cols_ref, result_ref):
+    index = pl.program_id(0)
+    width = wave_ref.shape[2]
+    height = tile_ref.shape[2] + mine_ref.shape[2]
+    columns_all = tile_ref.shape[3]
+    row_shift = (height - rows_ref[index]) % height
+    column_shift = (columns_all - columns_ref[index]) % columns_all
+    first = order_ref[0] == 0
+    patch = []
+    for part in range(2):
+        mine = mine_ref[0, part].astype(jnp.float32)
+        partner = partner_ref[0, part].astype(jnp.float32)
+        rim = jnp.concatenate(
+            [jnp.where(first, mine, partner), jnp.where(first, partner, mine)], axis=1
+        )
+        full = jnp.concatenate([tile_ref[0, part], rim], axis=0)
+        full = pltpu.roll(full, row_shift, 0)[:width]
+        patch.append(pltpu.roll(full, column_shift, 1)[:, :width])
+    wave = wave_ref[0].astype(jnp.float32)
+    wave_re = patch[0] * wave[0] - patch[1] * wave[1]
+    wave_im = patch[0] * wave[1] + patch[1] * wave[0]
+    out_re, out_im = propagate_block(
+        wave_re, wave_im, (dft_rows_ref, dft_cols_ref), chirp_ref[0], chirp_ref[1]
+    )
+    result_ref[0, 0] = out_re.astype(jnp.bfloat16)
+    result_ref[0, 1] = out_im.astype(jnp.bfloat16)
+
+
+def run_first(waves, tile, mine, partner, rows, columns, order, chirps, blocks):
+    number, _, width, _ = waves.shape
+    wave_spec = pl.BlockSpec((1, 2, width, width), lambda i, r, c, o: (i, 0, 0, 0))
+    whole = lambda shape: pl.BlockSpec(shape, lambda i, r, c, o: (0,) * len(shape))
+    grid_spec = pltpu.PrefetchScalarGridSpec(
+        num_scalar_prefetch=3,
+        grid=(number,),
+        in_specs=[
+            wave_spec,
+            whole(tile.shape),
+            whole(mine.shape),
+            whole(partner.shape),
+            whole(chirps.shape),
+            whole(blocks[0].shape),
+            whole(blocks[1].shape),
+        ],
+        out_specs=wave_spec,
+    )
+    return pl.pallas_call(
+        first_kernel,
+        grid_spec=grid_spec,
+        out_shape=jax.ShapeDtypeStruct(waves.shape, jnp.bfloat16),
+    )(rows, columns, order, waves, tile, mine, partner, chirps, *blocks)
+
+
 def local(object_field, probe, positions, counts, measured):
     width = probe.shape[1]
     tile_rows = object_field.shape[2]
@@ -479,7 +533,9 @@
     )
 
     def forward_all(waves):
-        return run_waves(waves, patches, chirps, blocks)
+        return run_first(
+            waves, object_field, mine, partner, local_rows, local_columns, order, chirps, blocks
+        )
 
     def silent(waves):
         return jnp.zeros_like(waves)

time: 61.2 us -> 59.6 us (0.974)
  local copies, waits for them, and re-layouts: 3.94 us -> 2.6 us
  Pallas kernels: 7.47 us -> 8.69 us
  waiting for transfers between devices: 31.5 us -> 30.4 us
    pallas_call x1, Pallas kernels: 1.49 us -> 3.98 us  [run_first(): pl.pallas_call(first_kernel, grid_spec=grid_spec, out_shape=jax.ShapeDtyp...]
    pallas_call x1, Pallas kernels: 2.98 us -> 1.65 us  [cut_patches(): pl.pallas_call(cut_kernel, grid_spec=grid_spec, out_shape=jax.ShapeDtypeS...]
    ppermute x1, waiting for transfers between devices: 3.96 us -> 3.06 us  [local(): carry = lax.ppermute(carry, 'depth', [(depth_count - 2, depth_count - 1)])]
    ppermute x1, starting transfers between devices: 2.79 us -> 1.98 us  [local(): carry = lax.ppermute(carry, 'depth', [(depth_count - 2, depth_count - 1)])]
    another operation x2, local copies, waits for them, and re-layouts: 0.79 us -> 0.09 us
    unnamed x10 -> x6, local copies, waits for them, and re-layouts: 0.71 us -> 0.02 us
  transfers between devices with their start and end apart: 11 -> 11, of which waited for: 7 -> 7; matrix products, arithmetic and copies ran while one was open for 8% -> 9% of each run, Pallas kernels for 7% -> 10%
where the time goes in v11:
time: 59.6 us; the launch traced here: 59.2 us
  waiting for transfers between devices  30.4 us (51%)
  starting transfers between devices  9.39 us (16%)
  Pallas kernels  8.69 us (15%)
  other arithmetic  4.12 us (7%)
  between operations  3.98 us (7%)
  local copies, waits for them, and re-layouts  2.6 us (4%)
    ppermute x1, waiting for transfers between devices, local(): carry = lax.ppermute(carry, 'depth', [(turn + 1, turn)])  14.3 us
    ppermute x1, waiting for transfers between devices, local(): lax.ppermute(spill_sum, 'tile', [(t, t + 1) for t in range(tile_count - 1)])  5.75 us
    ppermute x1, waiting for transfers between devices, from_behind(): return lax.ppermute(block, axis, route)  4.13 us
    pallas_call x1, Pallas kernels, run_first(): pl.pallas_call(first_kernel, grid_spec=grid_spec, out_shape=jax.ShapeDtyp...  3.98 us
    ppermute x1, starting transfers between devices, local(): lax.ppermute(spill_sum, 'tile', [(t, t + 1) for t in range(tile_count - 1)])  3.65 us
    pallas_call x1, Pallas kernels, run_adjoint(): pl.pallas_call(adjoint_kernel(last, number == 1), grid_spec=grid_spec, ou...  3.06 us
    ppermute x1, waiting for transfers between devices, local(): carry = lax.ppermute(carry, 'depth', [(depth_count - 2, depth_count - 1)])  3.06 us
    ppermute x1, starting transfers between devices, local(): carry = lax.ppermute(carry, 'depth', [(depth_count - 2, depth_count - 1)])  1.98 us
  transfers between devices with their start and end apart: 11, of which 7 were waited for; matrix products, arithmetic and copies ran while one was open for 9% of the time, Pallas kernels for 10%

profile of v11, /device:TPU:0, one launch (start us, length us, event | category | flops | bytes accessed | tf_op | source)
XLA Modules:
  0.0 59.2 jit_solution(6723327630772550093)
XLA Ops:
  0.0 0.5 collective-permute-start.1
  0.5 0.1 collective-permute-start
  0.5 1.1 %dynamic-slice_convert_fusion = bf16[1,2,256,256]{3,2,1,0:T(8,128)(2,1)S(1)} fusion(f32[1,2,256,512]{3,2,1,0:T(8,128)} %tile_ref.1, s32[]{:T(128)S(6)} %select_n.84), kind=kLoop, calls=%fused_computation.4 | loop fusion | bytes 524292 | tf_op jit(solution)/shard_map/convert_element_type | solution.py:493
  1.6 1.3 %collective-permute-start.2 = (bf16[1,2,256,256]{3,2,1,0:T(8,128)(2,1)S(1)}, bf16[1,2,256,256]{3,2,1,0:T(8,128)(2,1)S(1)}, u32[]{:S(2)}, u32[]{:S(2)}) collective-permute-start(bf16[1,2,256,256]{3,2,1,0:T(8,128)(2,1)S(1)} %dynamic-slice_convert_fusion), channel_id=1, source_target_pairs={{4,0},{8,4},{12,8},{5,1},{9,5},{13,9},{6,2},{10,6},{14,10},{7,3},{... | collective-permute-start | bytes 786440 | tf_op jit(solution)/shard_map/ppermute | solution.py:18
  2.9 0.5 collective-permute-start.5
  3.4 1.1 %multiply_convert_fusion = (bf16[256,256]{1,0:T(8,128)(2,1)S(1)}, bf16[256,256]{1,0:T(8,128)(2,1)S(1)}) fusion(), kind=kLoop, calls=%fused_computation.13 | loop fusion | flops 1245184 | bytes 262144 | tf_op jit(solution)/shard_map/convert_element_type | solution.py:51
  4.6 1.0 %fusion.6 = (f32[1,256,256]{2,1,0:T(8,128)S(1)}, f32[1,256,256]{2,1,0:T(8,128)S(1)}) fusion(s32[256]{0:T(256)S(1)} %fusion.9, f32[]{:T(128)S(6)} %neg.8), kind=kLoop, calls=%fused_computation.19 | loop fusion | flops 196608 | bytes 525316 | tf_op jit(solution)/shard_map/cos | solution.py:61
  6.4 0.6 %broadcast_select_fusion = s32[2]{0:T(128)S(1)} fusion(pred[]{:T(512)} %eq.23, s32[1]{0:T(128)} %collective-permute-done.1, s32[1]{0:T(128)S(6)} %copy.14), kind=kLoop, calls=%fused_computation.30 | loop fusion | flops 6 | bytes 17 | tf_op jit(solution)/shard_map/jit(_where)/select_n | solution.py:507
  7.0 0.7 %fusion.12 = (s32[1]{0:T(128)}, s32[1]{0:T(128)}) fusion(s32[2]{0:T(128)S(1)} %broadcast_select_fusion), kind=kLoop, calls=%fused_computation.32 | loop fusion | bytes 16 | tf_op jit(solution)/shard_map/slice | solution.py:511
  8.8 4.1 %collective-permute-done.2.mine_ref = bf16[1,2,256,256]{3,2,1,0:T(8,128)(2,1)S(1)} collective-permute-done((bf16[1,2,256,256]{3,2,1,0:T(8,128)(2,1)S(1)}, bf16[1,2,256,256]{3,2,1,0:T(8,128)(2,1)S(1)}, u32[]{:S(2)}, u32[]{:S(2)}) %collective-permute-start.2) | collective-permute-done | bytes 262176 | tf_op jit(solution)/shard_map/ppermute | solution.py:18
  13.0 0.7 %fusion.13 = (s32[1,1]{1,0:T(1,128)}, s32[1,1]{1,0:T(1,128)}) fusion(s32[1,2]{1,0:T(1,128)S(1)} %constant_dynamic-slice_fusion), kind=kLoop, calls=%fused_computation.33 | loop fusion | bytes 16 | tf_op jit(solution)/shard_map/slice | solution.py:518
  14.3 0.2 collective-permute-done.3.partner_ref
  14.5 4.0 %conditional.3 = (bf16[1,2,256,256]{3,2,1,0:T(8,128)(2,1)}) conditional(s32[]{:T(128)} %convert_element_type.71, () %tuple.54, (s32[1]{0:T(128)}, s32[1]{0:T(128)}, s32[1]{0:T(128)}, bf16[1,2,256,256]{3,2,1,0:T(8,128)(2,1)S(1)}, f32[1,2,256,512]{3,2,1,0:T(8,128)S(1)}, /*index=5*/bf16[1,2,256,256]{3,2,1,0:T(8,128)(2,1)S(1)}, ...), branch_computations={%region_0.1_spmd, %region_1.2_spmd} | conditional | bytes 262154 | solution.py:549
  14.5 4.0 %branch_1_fun.5 = bf16[1,2,256,256]{3,2,1,0:T(8,128)(2,1)} custom-call(s32[1]{0:T(128)} %get-tuple-element.119.rows_ref, s32[1]{0:T(128)} %get-tuple-element.120.columns_ref, s32[1]{0:T(128)} %get-tuple-element.121.order_ref, bf16[1,2,256,256]{3,2,1,0:T(8,128)(2,1)S(1)} %get-tuple-element.122.wave_ref, f32[1,2,256,512]{3,2,1,0:T(8,128)S(1)} %get-tuple-element.123.tile_ref, ...), custom_call_target="tpu_custom_call" | custom-call | tf_op jit(solution)/shard_map/cond/branch_1_fun/pallas_call | solution.py:474
  18.5 2.0 %collective-permute-start.4 = (bf16[1,2,256,256]{3,2,1,0:T(8,128)(2,1)}, bf16[1,2,256,256]{3,2,1,0:T(8,128)(2,1)}, u32[]{:S(2)}, u32[]{:S(2)}) collective-permute-start(bf16[1,2,256,256]{3,2,1,0:T(8,128)(2,1)} %get-tuple-element.182), channel_id=1, source_target_pairs={{0,2},{1,3},{4,6},{5,7},{8,10},{9,11},{12,14},{13,15},{16,18},{17,... | collective-permute-start | bytes 786440 | tf_op jit(solution)/shard_map/ppermute | solution.py:564
  21.7 1.7 %shard_map.60 = f32[1,2,256,256]{3,2,1,0:T(8,128)S(1)} custom-call(s32[1]{0:T(128)} %sub.17.rows_ref, s32[1]{0:T(128)} %bitcast.4.columns_ref, s32[1]{0:T(128)} %bitcast.order_ref, f32[1,2,256,512]{3,2,1,0:T(8,128)S(1)} %copy-done, bf16[1,2,256,256]{3,2,1,0:T(8,128)(2,1)S(1)} %collective-permute-done.2.mine_ref, ...), custom_call_target="tpu_custom_call" | custom-call | tf_op jit(solution)/shard_map/pallas_call | solution.py:275
  23.4 3.1 %collective-permute-done.4 = bf16[1,2,256,256]{3,2,1,0:T(8,128)(2,1)} collective-permute-done((bf16[1,2,256,256]{3,2,1,0:T(8,128)(2,1)}, bf16[1,2,256,256]{3,2,1,0:T(8,128)(2,1)}, u32[]{:S(2)}, u32[]{:S(2)}) %collective-permute-start.4) | collective-permute-done | bytes 262176 | tf_op jit(solution)/shard_map/ppermute | solution.py:564
  26.5 0.1 conditional.4
  26.5 0.1 broadcast.198
  26.6 1.3 %collective-permute-start.6 = (bf16[1,2,256,256]{3,2,1,0:T(8,128)(2,1)S(1)}, bf16[1,2,256,256]{3,2,1,0:T(8,128)(2,1)S(1)}, u32[]{:S(2)}, u32[]{:S(2)}) collective-permute-start(bf16[1,2,256,256]{3,2,1,0:T(8,128)(2,1)S(1)} %get-tuple-element.156), channel_id=1, source_target_pairs={{2,0},{3,1},{6,4},{7,5},{10,8},{11,9},{14,12},{15,13},{18,16},{19,... | collective-permute-start | bytes 786440 | tf_op jit(solution)/shard_map/ppermute | solution.py:576
  27.9 14.3 %collective-permute-done.6 = bf16[1,2,256,256]{3,2,1,0:T(8,128)(2,1)S(1)} collective-permute-done((bf16[1,2,256,256]{3,2,1,0:T(8,128)(2,1)S(1)}, bf16[1,2,256,256]{3,2,1,0:T(8,128)(2,1)S(1)}, u32[]{:S(2)}, u32[]{:S(2)}) %collective-permute-start.6) | collective-permute-done | bytes 262176 | tf_op jit(solution)/shard_map/ppermute | solution.py:576
  42.1 3.1 %conditional.5 = (bf16[2,512,512]{2,1,0:T(8,128)(2,1)S(1)}) conditional(s32[]{:T(128)} %convert_element_type.71, bf16[2,512,512]{2,1,0:T(8,128)(2,1)S(1)} %get-tuple-element.155, (s32[1]{0:T(128)}, s32[1]{0:T(128)}, s32[1]{0:T(128)}, s32[1]{0:T(128)}, s32[1]{0:T(128)}, /*index=5*/bf16[1,2,256,256]{3,2,1,0:T(8,128)(2,1)S(1)}, ...), branch_computations={%region_4.5_spmd, %region_5.6_spmd} | conditional | bytes 8 | solution.py:577
  42.1 3.1 %branch_1_fun.7 = (bf16[1,2,256,256]{3,2,1,0:T(8,128)(2,1)}, bf16[2,512,512]{2,1,0:T(8,128)(2,1)S(1)}) custom-call(s32[1]{0:T(128)} %get-tuple-element.141.rows_ref, s32[1]{0:T(128)} %get-tuple-element.142.columns_ref, s32[1]{0:T(128)} %get-tuple-element.143.live_ref, s32[1]{0:T(128)} %get-tuple-element.144.slot_ref, s32[1]{0:T(128)} %get-tuple-element.145.other_ref, ...), custom_call_target="tpu_custom_call" | custom-call | tf_op jit(solution)/shard_map/cond/branch_1_fun/pallas_call | solution.py:417
  45.2 0.1 fusion.11
  45.3 0.1 collective-permute-start.8
  45.4 1.5 %collective-permute-done.8 = bf16[2,256,256]{2,1,0:T(8,128)(2,1)S(1)} collective-permute-done((bf16[2,256,256]{2,1,0:T(8,128)(2,1)S(1)}, bf16[2,256,256]{2,1,0:T(8,128)(2,1)S(1)}, u32[]{:S(2)}, u32[]{:S(2)}) %collective-permute-start.8) | collective-permute-done | bytes 262176 | tf_op jit(solution)/shard_map/ppermute | solution.py:583
  46.9 0.1 add_convert_fusion
  47.0 3.7 %collective-permute-start.9 = (bf16[2,256,256]{2,1,0:T(8,128)(2,1)S(1)}, bf16[2,256,256]{2,1,0:T(8,128)(2,1)S(1)}, u32[]{:S(2)}, u32[]{:S(2)}) collective-permute-start(bf16[2,256,256]{2,1,0:T(8,128)(2,1)S(1)} %add_convert_fusion), channel_id=1, source_target_pairs={{0,4},{4,8},{8,12},{1,5},{5,9},{9,13},{2,6},{6,10},{10,14},{3,7},{... | collective-permute-start | bytes 786440 | tf_op jit(solution)/shard_map/ppermute | solution.py:585
  50.7 0.1 collective-permute-start.7
  50.7 5.8 %collective-permute-done.9 = bf16[2,256,256]{2,1,0:T(8,128)(2,1)S(1)} collective-permute-done((bf16[2,256,256]{2,1,0:T(8,128)(2,1)S(1)}, bf16[2,256,256]{2,1,0:T(8,128)(2,1)S(1)}, u32[]{:S(2)}, u32[]{:S(2)}) %collective-permute-start.9) | collective-permute-done | bytes 262176 | tf_op jit(solution)/shard_map/ppermute | solution.py:585
  56.5 1.5 %collective-permute-done.10 = bf16[2,256,256]{2,1,0:T(8,128)(2,1)S(1)} collective-permute-done((bf16[2,256,256]{2,1,0:T(8,128)(2,1)S(1)}, bf16[2,256,256]{2,1,0:T(8,128)(2,1)S(1)}, u32[]{:S(2)}, u32[]{:S(2)}) %collective-permute-start.10) | collective-permute-done | bytes 262176 | tf_op jit(solution)/shard_map/ppermute | solution.py:588
  58.0 1.2 %add_bitcast_fusion = f32[1,2,256,512]{3,2,1,0:T(8,128)} fusion(bf16[2,256,512]{2,1,0:T(8,128)(2,1)S(1)} %collective-permute-done.7, bf16[2,256,256]{2,1,0:T(8,128)(2,1)S(1)} %collective-permute-done.10, bf16[2,256,256]{2,1,0:T(8,128)(2,1)S(1)} %collective-permute-done.9, pred[]{:T(512)} %eq.23, bf16[2,512,512]{2,1,0:T(8,128)(2,1)S(1)} %get-tuple-element.184), kind=kLoop, calls=%fused_computation | loop fusion | flops 3670016 | bytes 2621441 | tf_op jit(solution)/shard_map/broadcast_in_dim | solution.py:596
  (20 shorter events, 0.2 us)
Async XLA Ops:
  0.0 6.4 %collective-permute-start.1 = (s32[1]{0:T(128)}, s32[1]{0:T(128)}, u32[]{:S(2)}, u32[]{:S(2)}) collective-permute-start(s32[1]{0:T(128)} %param.18), channel_id=1, source_target_pairs={{0,1},{1,0},{2,3},{3,2},{4,5},{5,4},{6,7},{7,6},{8,9},{9,8},{10,11... | collective-permute-start | bytes 20 | tf_op jit(solution)/shard_map/ppermute | solution.py:500
  0.5 12.5 %collective-permute-start = (s32[2,2]{1,0:T(2,128)}, s32[2,2]{1,0:T(2,128)S(1)}, u32[]{:S(2)}, u32[]{:S(2)}) collective-permute-start(s32[2,2]{1,0:T(2,128)} %param.17), channel_id=1, source_target_pairs={{0,1},{1,0},{2,3},{3,2},{4,5},{5,4},{6,7},{7,6},{8,9},{9,8},{10,11... | collective-permute-start | bytes 56 | tf_op jit(solution)/shard_map/ppermute | solution.py:499
  1.6 11.4 %collective-permute-start.2 = (bf16[1,2,256,256]{3,2,1,0:T(8,128)(2,1)S(1)}, bf16[1,2,256,256]{3,2,1,0:T(8,128)(2,1)S(1)}, u32[]{:S(2)}, u32[]{:S(2)}) collective-permute-start(bf16[1,2,256,256]{3,2,1,0:T(8,128)(2,1)S(1)} %dynamic-slice_convert_fusion), channel_id=1, source_target_pairs={{4,0},{8,4},{12,8},{5,1},{9,5},{13,9},{6,2},{10,6},{14,10},{7,3},{... | collective-permute-start | bytes 786440 | tf_op jit(solution)/shard_map/ppermute | solution.py:18
  2.9 20.5 %collective-permute-start.5 = (f32[2,256,256]{2,1,0:T(8,128)}, f32[2,256,256]{2,1,0:T(8,128)}, u32[]{:S(2)}, u32[]{:S(2)}) collective-permute-start(f32[2,256,256]{2,1,0:T(8,128)} %param.19), channel_id=1, source_target_pairs={{0,1},{1,0},{2,3},{3,2},{4,5},{5,4},{6,7},{7,6},{8,9},{9,8},{10,11... | collective-permute-start | bytes 1572872 | tf_op jit(solution)/shard_map/ppermute | solution.py:501
  4.6 10.0 %copy-start = (f32[1,2,256,512]{3,2,1,0:T(8,128)S(1)}, f32[1,2,256,512]{3,2,1,0:T(8,128)}, u32[]{:S(2)}) copy-start(f32[1,2,256,512]{3,2,1,0:T(8,128)} %tile_ref.1) | copy-start | bytes 3145732
  5.6 8.9 %copy-start.1 = (bf16[2,256,256]{2,1,0:T(8,128)(2,1)S(1)}, bf16[2,256,256]{2,1,0:T(8,128)(2,1)}, u32[]{:S(2)}) copy-start(bf16[2,256,256]{2,1,0:T(8,128)(2,1)} %param.16) | copy-start | bytes 786436
  8.8 4.2 %copy-start.2 = (s32[2,2]{1,0:T(2,128)S(1)}, s32[2,2]{1,0:T(2,128)}, u32[]{:S(2)}) copy-start(s32[2,2]{1,0:T(2,128)} %param.17) | copy-start | bytes 52
  13.0 1.5 %collective-permute-start.3 = (bf16[1,2,256,256]{3,2,1,0:T(8,128)(2,1)S(1)}, bf16[1,2,256,256]{3,2,1,0:T(8,128)(2,1)S(1)}, u32[]{:S(2)}, u32[]{:S(2)}) collective-permute-start(bf16[1,2,256,256]{3,2,1,0:T(8,128)(2,1)S(1)} %collective-permute-done.2.mine_ref), channel_id=1, source_target_pairs={{0,1},{1,0},{2,3},{3,2},{4,5},{5,4},{6,7},{7,6},{8,9},{9,8},{10,11... | collective-permute-start | bytes 786440 | tf_op jit(solution)/shard_map/ppermute | solution.py:495
  18.5 8.0 %collective-permute-start.4 = (bf16[1,2,256,256]{3,2,1,0:T(8,128)(2,1)}, bf16[1,2,256,256]{3,2,1,0:T(8,128)(2,1)}, u32[]{:S(2)}, u32[]{:S(2)}) collective-permute-start(bf16[1,2,256,256]{3,2,1,0:T(8,128)(2,1)} %get-tuple-element.182), channel_id=1, source_target_pairs={{0,2},{1,3},{4,6},{5,7},{8,10},{9,11},{12,14},{13,15},{16,18},{17,... | collective-permute-start | bytes 786440 | tf_op jit(solution)/shard_map/ppermute | solution.py:564
  26.6 15.6 %collective-permute-start.6 = (bf16[1,2,256,256]{3,2,1,0:T(8,128)(2,1)S(1)}, bf16[1,2,256,256]{3,2,1,0:T(8,128)(2,1)S(1)}, u32[]{:S(2)}, u32[]{:S(2)}) collective-permute-start(bf16[1,2,256,256]{3,2,1,0:T(8,128)(2,1)S(1)} %get-tuple-element.156), channel_id=1, source_target_pairs={{2,0},{3,1},{6,4},{7,5},{10,8},{11,9},{14,12},{15,13},{18,16},{19,... | collective-permute-start | bytes 786440 | tf_op jit(solution)/shard_map/ppermute | solution.py:576
  45.3 1.6 %collective-permute-start.8 = (bf16[2,256,256]{2,1,0:T(8,128)(2,1)S(1)}, bf16[2,256,256]{2,1,0:T(8,128)(2,1)S(1)}, u32[]{:S(2)}, u32[]{:S(2)}) collective-permute-start(bf16[2,256,256]{2,1,0:T(8,128)(2,1)S(1)} %constant_dynamic-slice_fusion.1), channel_id=1, source_target_pairs={{0,1},{1,0},{2,3},{3,2},{4,5},{5,4},{6,7},{7,6},{8,9},{9,8},{10,11... | collective-permute-start | bytes 786440 | tf_op jit(solution)/shard_map/ppermute | solution.py:583
  47.0 9.5 %collective-permute-start.9 = (bf16[2,256,256]{2,1,0:T(8,128)(2,1)S(1)}, bf16[2,256,256]{2,1,0:T(8,128)(2,1)S(1)}, u32[]{:S(2)}, u32[]{:S(2)}) collective-permute-start(bf16[2,256,256]{2,1,0:T(8,128)(2,1)S(1)} %add_convert_fusion), channel_id=1, source_target_pairs={{0,4},{4,8},{8,12},{1,5},{5,9},{9,13},{2,6},{6,10},{10,14},{3,7},{... | collective-permute-start | bytes 786440 | tf_op jit(solution)/shard_map/ppermute | solution.py:585
  50.7 5.8 %collective-permute-start.7 = (bf16[2,256,512]{2,1,0:T(8,128)(2,1)S(1)}, bf16[2,256,512]{2,1,0:T(8,128)(2,1)S(1)}, u32[]{:S(2)}, u32[]{:S(2)}) collective-permute-start(bf16[2,256,512]{2,1,0:T(8,128)(2,1)S(1)} %get-tuple-element.169), channel_id=1, source_target_pairs={{0,1},{1,0},{2,3},{3,2},{4,5},{5,4},{6,7},{7,6},{8,9},{9,8},{10,11... | collective-permute-start | bytes 1572872 | tf_op jit(solution)/shard_map/ppermute | solution.py:587
  56.5 1.5 %collective-permute-start.10 = (bf16[2,256,256]{2,1,0:T(8,128)(2,1)S(1)}, bf16[2,256,256]{2,1,0:T(8,128)(2,1)S(1)}, u32[]{:S(2)}, u32[]{:S(2)}) collective-permute-start(bf16[2,256,256]{2,1,0:T(8,128)(2,1)S(1)} %collective-permute-done.9), channel_id=1, source_target_pairs={{0,1},{1,0},{2,3},{3,2},{4,5},{5,4},{6,7},{7,6},{8,9},{9,8},{10,11... | collective-permute-start | bytes 786440 | tf_op jit(solution)/shard_map/ppermute | solution.py:588

commit v12 on v11

--- a/solution.py
+++ b/solution.py
@@ -322,6 +322,18 @@
             [term, jnp.zeros((width, columns_all - width), jnp.float32)], axis=1
         )
         wide = pltpu.roll(wide, column_shift, 1)
+        if height == 2 * width:
+            rolled = pltpu.roll(wide, row % width, 0)
+            below = lax.broadcasted_iota(jnp.int32, rolled.shape, 0) < row
+            upper = jnp.where(below, 0.0, rolled)
+            lower = jnp.where(below, rolled, 0.0)
+            if direct_ref is None:
+                total_ref[part, :width] = total_ref[part, :width] + upper
+                total_ref[part, width:] = total_ref[part, width:] + lower
+            else:
+                direct_ref[part, :width] = upper.astype(direct_ref.dtype)
+                direct_ref[part, width:] = lower.astype(direct_ref.dtype)
+            continue
         tall = jnp.concatenate(
             [wide, jnp.zeros((height - width, columns_all), jnp.float32)], axis=0
         )

time: 59.6 us -> 59.5 us (level)
  no operation moved by 1% of the time
where the time goes in v12:
time: 59.5 us; the launch traced here: 59.1 us
  waiting for transfers between devices  30.3 us (51%)
  starting transfers between devices  9.39 us (16%)
  Pallas kernels  8.71 us (15%)
  other arithmetic  4.12 us (7%)
  between operations  3.97 us (7%)
  local copies, waits for them, and re-layouts  2.6 us (4%)
    ppermute x1, waiting for transfers between devices, local(): carry = lax.ppermute(carry, 'depth', [(turn + 1, turn)])  14.1 us
    ppermute x1, waiting for transfers between devices, local(): lax.ppermute(spill_sum, 'tile', [(t, t + 1) for t in range(tile_count - 1)])  5.75 us
    ppermute x1, waiting for transfers between devices, from_behind(): return lax.ppermute(block, axis, route)  4.13 us
    pallas_call x1, Pallas kernels, run_first(): pl.pallas_call(first_kernel, grid_spec=grid_spec, out_shape=jax.ShapeDtyp...  3.98 us
    ppermute x1, starting transfers between devices, local(): lax.ppermute(spill_sum, 'tile', [(t, t + 1) for t in range(tile_count - 1)])  3.65 us
    pallas_call x1, Pallas kernels, run_adjoint(): pl.pallas_call(adjoint_kernel(last, number == 1), grid_spec=grid_spec, ou...  3.08 us
    ppermute x1, waiting for transfers between devices, local(): carry = lax.ppermute(carry, 'depth', [(depth_count - 2, depth_count - 1)])  3.06 us
    ppermute x1, starting transfers between devices, local(): carry = lax.ppermute(carry, 'depth', [(depth_count - 2, depth_count - 1)])  1.98 us
  transfers between devices with their start and end apart: 11, of which 7 were waited for; matrix products, arithmetic and copies ran while one was open for 9% of the time, Pallas kernels for 10%

profile of v12, /device:TPU:0, one launch (start us, length us, event | category | flops | bytes accessed | tf_op | source)
XLA Modules:
  0.0 59.1 jit_solution(5658195261143010873)
XLA Ops:
  0.0 0.5 collective-permute-start.1
  0.5 0.1 collective-permute-start
  0.5 1.1 %dynamic-slice_convert_fusion = bf16[1,2,256,256]{3,2,1,0:T(8,128)(2,1)S(1)} fusion(f32[1,2,256,512]{3,2,1,0:T(8,128)} %tile_ref.1, s32[]{:T(128)S(6)} %select_n.84), kind=kLoop, calls=%fused_computation.4 | loop fusion | bytes 524292 | tf_op jit(solution)/shard_map/convert_element_type | solution.py:505
  1.6 1.3 %collective-permute-start.2 = (bf16[1,2,256,256]{3,2,1,0:T(8,128)(2,1)S(1)}, bf16[1,2,256,256]{3,2,1,0:T(8,128)(2,1)S(1)}, u32[]{:S(2)}, u32[]{:S(2)}) collective-permute-start(bf16[1,2,256,256]{3,2,1,0:T(8,128)(2,1)S(1)} %dynamic-slice_convert_fusion), channel_id=1, source_target_pairs={{4,0},{8,4},{12,8},{5,1},{9,5},{13,9},{6,2},{10,6},{14,10},{7,3},{... | collective-permute-start | bytes 786440 | tf_op jit(solution)/shard_map/ppermute | solution.py:18
  2.9 0.5 collective-permute-start.5
  3.4 1.1 %multiply_convert_fusion = (bf16[256,256]{1,0:T(8,128)(2,1)S(1)}, bf16[256,256]{1,0:T(8,128)(2,1)S(1)}) fusion(), kind=kLoop, calls=%fused_computation.13 | loop fusion | flops 1245184 | bytes 262144 | tf_op jit(solution)/shard_map/convert_element_type | solution.py:51
  4.6 1.0 %fusion.6 = (f32[1,256,256]{2,1,0:T(8,128)S(1)}, f32[1,256,256]{2,1,0:T(8,128)S(1)}) fusion(s32[256]{0:T(256)S(1)} %fusion.9, f32[]{:T(128)S(6)} %neg.8), kind=kLoop, calls=%fused_computation.19 | loop fusion | flops 196608 | bytes 525316 | tf_op jit(solution)/shard_map/cos | solution.py:61
  6.4 0.6 %broadcast_select_fusion = s32[2]{0:T(128)S(1)} fusion(pred[]{:T(512)} %eq.23, s32[1]{0:T(128)} %collective-permute-done.1, s32[1]{0:T(128)S(6)} %copy.14), kind=kLoop, calls=%fused_computation.30 | loop fusion | flops 6 | bytes 17 | tf_op jit(solution)/shard_map/jit(_where)/select_n | solution.py:519
  7.0 0.7 %fusion.12 = (s32[1]{0:T(128)}, s32[1]{0:T(128)}) fusion(s32[2]{0:T(128)S(1)} %broadcast_select_fusion), kind=kLoop, calls=%fused_computation.32 | loop fusion | bytes 16 | tf_op jit(solution)/shard_map/slice | solution.py:523
  8.8 4.1 %collective-permute-done.2.mine_ref = bf16[1,2,256,256]{3,2,1,0:T(8,128)(2,1)S(1)} collective-permute-done((bf16[1,2,256,256]{3,2,1,0:T(8,128)(2,1)S(1)}, bf16[1,2,256,256]{3,2,1,0:T(8,128)(2,1)S(1)}, u32[]{:S(2)}, u32[]{:S(2)}) %collective-permute-start.2) | collective-permute-done | bytes 262176 | tf_op jit(solution)/shard_map/ppermute | solution.py:18
  13.0 0.7 %fusion.13 = (s32[1,1]{1,0:T(1,128)}, s32[1,1]{1,0:T(1,128)}) fusion(s32[1,2]{1,0:T(1,128)S(1)} %constant_dynamic-slice_fusion), kind=kLoop, calls=%fused_computation.33 | loop fusion | bytes 16 | tf_op jit(solution)/shard_map/slice | solution.py:530
  14.3 0.2 collective-permute-done.3.partner_ref
  14.5 4.0 %conditional.3 = (bf16[1,2,256,256]{3,2,1,0:T(8,128)(2,1)}) conditional(s32[]{:T(128)} %convert_element_type.71, () %tuple.54, (s32[1]{0:T(128)}, s32[1]{0:T(128)}, s32[1]{0:T(128)}, bf16[1,2,256,256]{3,2,1,0:T(8,128)(2,1)S(1)}, f32[1,2,256,512]{3,2,1,0:T(8,128)S(1)}, /*index=5*/bf16[1,2,256,256]{3,2,1,0:T(8,128)(2,1)S(1)}, ...), branch_computations={%region_0.1_spmd, %region_1.2_spmd} | conditional | bytes 262154 | solution.py:561
  14.5 4.0 %branch_1_fun.5 = bf16[1,2,256,256]{3,2,1,0:T(8,128)(2,1)} custom-call(s32[1]{0:T(128)} %get-tuple-element.119.rows_ref, s32[1]{0:T(128)} %get-tuple-element.120.columns_ref, s32[1]{0:T(128)} %get-tuple-element.121.order_ref, bf16[1,2,256,256]{3,2,1,0:T(8,128)(2,1)S(1)} %get-tuple-element.122.wave_ref, f32[1,2,256,512]{3,2,1,0:T(8,128)S(1)} %get-tuple-element.123.tile_ref, ...), custom_call_target="tpu_custom_call" | custom-call | tf_op jit(solution)/shard_map/cond/branch_1_fun/pallas_call | solution.py:486
  18.5 2.0 %collective-permute-start.4 = (bf16[1,2,256,256]{3,2,1,0:T(8,128)(2,1)}, bf16[1,2,256,256]{3,2,1,0:T(8,128)(2,1)}, u32[]{:S(2)}, u32[]{:S(2)}) collective-permute-start(bf16[1,2,256,256]{3,2,1,0:T(8,128)(2,1)} %get-tuple-element.182), channel_id=1, source_target_pairs={{0,2},{1,3},{4,6},{5,7},{8,10},{9,11},{12,14},{13,15},{16,18},{17,... | collective-permute-start | bytes 786440 | tf_op jit(solution)/shard_map/ppermute | solution.py:576
  21.7 1.7 %shard_map.60 = f32[1,2,256,256]{3,2,1,0:T(8,128)S(1)} custom-call(s32[1]{0:T(128)} %sub.17.rows_ref, s32[1]{0:T(128)} %bitcast.4.columns_ref, s32[1]{0:T(128)} %bitcast.order_ref, f32[1,2,256,512]{3,2,1,0:T(8,128)S(1)} %copy-done, bf16[1,2,256,256]{3,2,1,0:T(8,128)(2,1)S(1)} %collective-permute-done.2.mine_ref, ...), custom_call_target="tpu_custom_call" | custom-call | tf_op jit(solution)/shard_map/pallas_call | solution.py:275
  23.4 3.1 %collective-permute-done.4 = bf16[1,2,256,256]{3,2,1,0:T(8,128)(2,1)} collective-permute-done((bf16[1,2,256,256]{3,2,1,0:T(8,128)(2,1)}, bf16[1,2,256,256]{3,2,1,0:T(8,128)(2,1)}, u32[]{:S(2)}, u32[]{:S(2)}) %collective-permute-start.4) | collective-permute-done | bytes 262176 | tf_op jit(solution)/shard_map/ppermute | solution.py:576
  26.5 0.1 conditional.4
  26.5 0.1 broadcast.198
  26.6 1.3 %collective-permute-start.6 = (bf16[1,2,256,256]{3,2,1,0:T(8,128)(2,1)S(1)}, bf16[1,2,256,256]{3,2,1,0:T(8,128)(2,1)S(1)}, u32[]{:S(2)}, u32[]{:S(2)}) collective-permute-start(bf16[1,2,256,256]{3,2,1,0:T(8,128)(2,1)S(1)} %get-tuple-element.156), channel_id=1, source_target_pairs={{2,0},{3,1},{6,4},{7,5},{10,8},{11,9},{14,12},{15,13},{18,16},{19,... | collective-permute-start | bytes 786440 | tf_op jit(solution)/shard_map/ppermute | solution.py:588
  27.9 14.1 %collective-permute-done.6 = bf16[1,2,256,256]{3,2,1,0:T(8,128)(2,1)S(1)} collective-permute-done((bf16[1,2,256,256]{3,2,1,0:T(8,128)(2,1)S(1)}, bf16[1,2,256,256]{3,2,1,0:T(8,128)(2,1)S(1)}, u32[]{:S(2)}, u32[]{:S(2)}) %collective-permute-start.6) | collective-permute-done | bytes 262176 | tf_op jit(solution)/shard_map/ppermute | solution.py:588
  42.0 3.1 %conditional.5 = (bf16[2,512,512]{2,1,0:T(8,128)(2,1)S(1)}) conditional(s32[]{:T(128)} %convert_element_type.71, bf16[2,512,512]{2,1,0:T(8,128)(2,1)S(1)} %get-tuple-element.155, (s32[1]{0:T(128)}, s32[1]{0:T(128)}, s32[1]{0:T(128)}, s32[1]{0:T(128)}, s32[1]{0:T(128)}, /*index=5*/bf16[1,2,256,256]{3,2,1,0:T(8,128)(2,1)S(1)}, ...), branch_computations={%region_4.5_spmd, %region_5.6_spmd} | conditional | bytes 8 | solution.py:589
  42.0 3.1 %branch_1_fun.7 = (bf16[1,2,256,256]{3,2,1,0:T(8,128)(2,1)}, bf16[2,512,512]{2,1,0:T(8,128)(2,1)S(1)}) custom-call(s32[1]{0:T(128)} %get-tuple-element.141.rows_ref, s32[1]{0:T(128)} %get-tuple-element.142.columns_ref, s32[1]{0:T(128)} %get-tuple-element.143.live_ref, s32[1]{0:T(128)} %get-tuple-element.144.slot_ref, s32[1]{0:T(128)} %get-tuple-element.145.other_ref, ...), custom_call_target="tpu_custom_call" | custom-call | tf_op jit(solution)/shard_map/cond/branch_1_fun/pallas_call | solution.py:429
  45.1 0.1 fusion.11
  45.2 0.1 collective-permute-start.8
  45.3 1.5 %collective-permute-done.8 = bf16[2,256,256]{2,1,0:T(8,128)(2,1)S(1)} collective-permute-done((bf16[2,256,256]{2,1,0:T(8,128)(2,1)S(1)}, bf16[2,256,256]{2,1,0:T(8,128)(2,1)S(1)}, u32[]{:S(2)}, u32[]{:S(2)}) %collective-permute-start.8) | collective-permute-done | bytes 262176 | tf_op jit(solution)/shard_map/ppermute | solution.py:595
  46.8 0.1 add_convert_fusion
  46.9 3.7 %collective-permute-start.9 = (bf16[2,256,256]{2,1,0:T(8,128)(2,1)S(1)}, bf16[2,256,256]{2,1,0:T(8,128)(2,1)S(1)}, u32[]{:S(2)}, u32[]{:S(2)}) collective-permute-start(bf16[2,256,256]{2,1,0:T(8,128)(2,1)S(1)} %add_convert_fusion), channel_id=1, source_target_pairs={{0,4},{4,8},{8,12},{1,5},{5,9},{9,13},{2,6},{6,10},{10,14},{3,7},{... | collective-permute-start | bytes 786440 | tf_op jit(solution)/shard_map/ppermute | solution.py:597
  50.5 0.1 collective-permute-start.7
  50.6 5.8 %collective-permute-done.9 = bf16[2,256,256]{2,1,0:T(8,128)(2,1)S(1)} collective-permute-done((bf16[2,256,256]{2,1,0:T(8,128)(2,1)S(1)}, bf16[2,256,256]{2,1,0:T(8,128)(2,1)S(1)}, u32[]{:S(2)}, u32[]{:S(2)}) %collective-permute-start.9) | collective-permute-done | bytes 262176 | tf_op jit(solution)/shard_map/ppermute | solution.py:597
  56.4 1.5 %collective-permute-done.10 = bf16[2,256,256]{2,1,0:T(8,128)(2,1)S(1)} collective-permute-done((bf16[2,256,256]{2,1,0:T(8,128)(2,1)S(1)}, bf16[2,256,256]{2,1,0:T(8,128)(2,1)S(1)}, u32[]{:S(2)}, u32[]{:S(2)}) %collective-permute-start.10) | collective-permute-done | bytes 262176 | tf_op jit(solution)/shard_map/ppermute | solution.py:600
  57.9 1.2 %add_bitcast_fusion = f32[1,2,256,512]{3,2,1,0:T(8,128)} fusion(bf16[2,256,512]{2,1,0:T(8,128)(2,1)S(1)} %collective-permute-done.7, bf16[2,256,256]{2,1,0:T(8,128)(2,1)S(1)} %collective-permute-done.10, bf16[2,256,256]{2,1,0:T(8,128)(2,1)S(1)} %collective-permute-done.9, pred[]{:T(512)} %eq.23, bf16[2,512,512]{2,1,0:T(8,128)(2,1)S(1)} %get-tuple-element.184), kind=kLoop, calls=%fused_computation | loop fusion | flops 3670016 | bytes 2621441 | tf_op jit(solution)/shard_map/broadcast_in_dim | solution.py:608
  (20 shorter events, 0.2 us)
Async XLA Ops:
  0.0 6.4 %collective-permute-start.1 = (s32[1]{0:T(128)}, s32[1]{0:T(128)}, u32[]{:S(2)}, u32[]{:S(2)}) collective-permute-start(s32[1]{0:T(128)} %param.18), channel_id=1, source_target_pairs={{0,1},{1,0},{2,3},{3,2},{4,5},{5,4},{6,7},{7,6},{8,9},{9,8},{10,11... | collective-permute-start | bytes 20 | tf_op jit(solution)/shard_map/ppermute | solution.py:512
  0.5 12.5 %collective-permute-start = (s32[2,2]{1,0:T(2,128)}, s32[2,2]{1,0:T(2,128)S(1)}, u32[]{:S(2)}, u32[]{:S(2)}) collective-permute-start(s32[2,2]{1,0:T(2,128)} %param.17), channel_id=1, source_target_pairs={{0,1},{1,0},{2,3},{3,2},{4,5},{5,4},{6,7},{7,6},{8,9},{9,8},{10,11... | collective-permute-start | bytes 56 | tf_op jit(solution)/shard_map/ppermute | solution.py:511
  1.6 11.4 %collective-permute-start.2 = (bf16[1,2,256,256]{3,2,1,0:T(8,128)(2,1)S(1)}, bf16[1,2,256,256]{3,2,1,0:T(8,128)(2,1)S(1)}, u32[]{:S(2)}, u32[]{:S(2)}) collective-permute-start(bf16[1,2,256,256]{3,2,1,0:T(8,128)(2,1)S(1)} %dynamic-slice_convert_fusion), channel_id=1, source_target_pairs={{4,0},{8,4},{12,8},{5,1},{9,5},{13,9},{6,2},{10,6},{14,10},{7,3},{... | collective-permute-start | bytes 786440 | tf_op jit(solution)/shard_map/ppermute | solution.py:18
  2.9 20.5 %collective-permute-start.5 = (f32[2,256,256]{2,1,0:T(8,128)}, f32[2,256,256]{2,1,0:T(8,128)}, u32[]{:S(2)}, u32[]{:S(2)}) collective-permute-start(f32[2,256,256]{2,1,0:T(8,128)} %param.19), channel_id=1, source_target_pairs={{0,1},{1,0},{2,3},{3,2},{4,5},{5,4},{6,7},{7,6},{8,9},{9,8},{10,11... | collective-permute-start | bytes 1572872 | tf_op jit(solution)/shard_map/ppermute | solution.py:513
  4.6 10.0 %copy-start = (f32[1,2,256,512]{3,2,1,0:T(8,128)S(1)}, f32[1,2,256,512]{3,2,1,0:T(8,128)}, u32[]{:S(2)}) copy-start(f32[1,2,256,512]{3,2,1,0:T(8,128)} %tile_ref.1) | copy-start | bytes 3145732
  5.6 8.9 %copy-start.1 = (bf16[2,256,256]{2,1,0:T(8,128)(2,1)S(1)}, bf16[2,256,256]{2,1,0:T(8,128)(2,1)}, u32[]{:S(2)}) copy-start(bf16[2,256,256]{2,1,0:T(8,128)(2,1)} %param.16) | copy-start | bytes 786436
  8.8 4.2 %copy-start.2 = (s32[2,2]{1,0:T(2,128)S(1)}, s32[2,2]{1,0:T(2,128)}, u32[]{:S(2)}) copy-start(s32[2,2]{1,0:T(2,128)} %param.17) | copy-start | bytes 52
  13.0 1.5 %collective-permute-start.3 = (bf16[1,2,256,256]{3,2,1,0:T(8,128)(2,1)S(1)}, bf16[1,2,256,256]{3,2,1,0:T(8,128)(2,1)S(1)}, u32[]{:S(2)}, u32[]{:S(2)}) collective-permute-start(bf16[1,2,256,256]{3,2,1,0:T(8,128)(2,1)S(1)} %collective-permute-done.2.mine_ref), channel_id=1, source_target_pairs={{0,1},{1,0},{2,3},{3,2},{4,5},{5,4},{6,7},{7,6},{8,9},{9,8},{10,11... | collective-permute-start | bytes 786440 | tf_op jit(solution)/shard_map/ppermute | solution.py:507
  18.5 8.0 %collective-permute-start.4 = (bf16[1,2,256,256]{3,2,1,0:T(8,128)(2,1)}, bf16[1,2,256,256]{3,2,1,0:T(8,128)(2,1)}, u32[]{:S(2)}, u32[]{:S(2)}) collective-permute-start(bf16[1,2,256,256]{3,2,1,0:T(8,128)(2,1)} %get-tuple-element.182), channel_id=1, source_target_pairs={{0,2},{1,3},{4,6},{5,7},{8,10},{9,11},{12,14},{13,15},{16,18},{17,... | collective-permute-start | bytes 786440 | tf_op jit(solution)/shard_map/ppermute | solution.py:576
  26.6 15.4 %collective-permute-start.6 = (bf16[1,2,256,256]{3,2,1,0:T(8,128)(2,1)S(1)}, bf16[1,2,256,256]{3,2,1,0:T(8,128)(2,1)S(1)}, u32[]{:S(2)}, u32[]{:S(2)}) collective-permute-start(bf16[1,2,256,256]{3,2,1,0:T(8,128)(2,1)S(1)} %get-tuple-element.156), channel_id=1, source_target_pairs={{2,0},{3,1},{6,4},{7,5},{10,8},{11,9},{14,12},{15,13},{18,16},{19,... | collective-permute-start | bytes 786440 | tf_op jit(solution)/shard_map/ppermute | solution.py:588
  45.2 1.6 %collective-permute-start.8 = (bf16[2,256,256]{2,1,0:T(8,128)(2,1)S(1)}, bf16[2,256,256]{2,1,0:T(8,128)(2,1)S(1)}, u32[]{:S(2)}, u32[]{:S(2)}) collective-permute-start(bf16[2,256,256]{2,1,0:T(8,128)(2,1)S(1)} %constant_dynamic-slice_fusion.1), channel_id=1, source_target_pairs={{0,1},{1,0},{2,3},{3,2},{4,5},{5,4},{6,7},{7,6},{8,9},{9,8},{10,11... | collective-permute-start | bytes 786440 | tf_op jit(solution)/shard_map/ppermute | solution.py:595
  46.9 9.5 %collective-permute-start.9 = (bf16[2,256,256]{2,1,0:T(8,128)(2,1)S(1)}, bf16[2,256,256]{2,1,0:T(8,128)(2,1)S(1)}, u32[]{:S(2)}, u32[]{:S(2)}) collective-permute-start(bf16[2,256,256]{2,1,0:T(8,128)(2,1)S(1)} %add_convert_fusion), channel_id=1, source_target_pairs={{0,4},{4,8},{8,12},{1,5},{5,9},{9,13},{2,6},{6,10},{10,14},{3,7},{... | collective-permute-start | bytes 786440 | tf_op jit(solution)/shard_map/ppermute | solution.py:597
  50.5 5.8 %collective-permute-start.7 = (bf16[2,256,512]{2,1,0:T(8,128)(2,1)S(1)}, bf16[2,256,512]{2,1,0:T(8,128)(2,1)S(1)}, u32[]{:S(2)}, u32[]{:S(2)}) collective-permute-start(bf16[2,256,512]{2,1,0:T(8,128)(2,1)S(1)} %get-tuple-element.169), channel_id=1, source_target_pairs={{0,1},{1,0},{2,3},{3,2},{4,5},{5,4},{6,7},{7,6},{8,9},{9,8},{10,11... | collective-permute-start | bytes 1572872 | tf_op jit(solution)/shard_map/ppermute | solution.py:599
  56.4 1.5 %collective-permute-start.10 = (bf16[2,256,256]{2,1,0:T(8,128)(2,1)S(1)}, bf16[2,256,256]{2,1,0:T(8,128)(2,1)S(1)}, u32[]{:S(2)}, u32[]{:S(2)}) collective-permute-start(bf16[2,256,256]{2,1,0:T(8,128)(2,1)S(1)} %collective-permute-done.9), channel_id=1, source_target_pairs={{0,1},{1,0},{2,3},{3,2},{4,5},{5,4},{6,7},{7,6},{8,9},{9,8},{10,11... | collective-permute-start | bytes 786440 | tf_op jit(solution)/shard_map/ppermute | solution.py:600

commit v13 on v12

--- a/solution.py
+++ b/solution.py
@@ -388,6 +388,10 @@
         spread_re, spread_im = propagate_block(in_re, in_im, blocks, chirp_re, -chirp_im)
         passed_ref[0, 0] = (patch_re * spread_re + patch_im * spread_im).astype(jnp.bfloat16)
         passed_ref[0, 1] = (patch_re * spread_im - patch_im * spread_re).astype(jnp.bfloat16)
+        if last:
+            grad_ref[0, 0] = spread_re.astype(jnp.bfloat16)
+            grad_ref[0, 1] = spread_im.astype(jnp.bfloat16)
+            return
         term_re = source_re * spread_re + source_im * spread_im
         term_im = source_re * spread_im - source_im * spread_re
         place_term(
@@ -416,24 +420,61 @@
         in_specs += [slot_spec, slot_spec]
     else:
         in_specs += [wave_spec]
+    if last:
+        second_spec = wave_spec
+        second_shape = jax.ShapeDtypeStruct(waves.shape, jnp.bfloat16)
+    else:
+        second_spec = pl.BlockSpec((2, height, columns_all), lambda i, *s: (0, 0, 0))
+        second_shape = jax.ShapeDtypeStruct((2, height, columns_all), jnp.bfloat16)
     grid_spec = pltpu.PrefetchScalarGridSpec(
         num_scalar_prefetch=5,
         grid=(number,),
         in_specs=in_specs,
-        out_specs=(
-            wave_spec,
-            pl.BlockSpec((2, height, columns_all), lambda i, *s: (0, 0, 0)),
-        ),
+        out_specs=(wave_spec, second_spec),
         scratch_shapes=[pltpu.VMEM((2, height, columns_all), jnp.float32)],
     )
     return pl.pallas_call(
         adjoint_kernel(last, number == 1),
         grid_spec=grid_spec,
-        out_shape=(
-            jax.ShapeDtypeStruct(waves.shape, jnp.bfloat16),
-            jax.ShapeDtypeStruct((2, height, columns_all), jnp.bfloat16),
-        ),
+        out_shape=(jax.ShapeDtypeStruct(waves.shape, jnp.bfloat16), second_shape),
     )(*scalars, waves, patches, chirps, *blocks, *extra)
+
+
+def place_kernel(rows_ref, columns_ref, live_ref, spread_ref, source_ref, grad_ref, total_ref):
+    index = pl.program_id(0)
+
+    @pl.when(index == 0)
+    def _():
+        total_ref[...] = jnp.zeros(total_ref.shape, total_ref.dtype)
+
+    spread = spread_ref[0].astype(jnp.float32)
+    source = source_ref[0].astype(jnp.float32)
+    term_re = source[0] * spread[0] + source[1] * spread[1]
+    term_im = source[0] * spread[1] - source[1] * spread[0]
+    place_term(
+        term_re, term_im, rows_ref[index], columns_ref[index], live_ref[index] > 0, total_ref
+    )
+
+    @pl.when(index == pl.num_programs(0) - 1)
+    def _():
+        grad_ref[...] = total_ref[...].astype(grad_ref.dtype)
+
+
+def run_place(spread, source, scalars, height, columns_all):
+    number, _, width, _ = spread.shape
+    wave_spec = pl.BlockSpec((1, 2, width, width), lambda i, *s: (i, 0, 0, 0))
+    grid_spec = pltpu.PrefetchScalarGridSpec(
+        num_scalar_prefetch=3,
+        grid=(number,),
+        in_specs=[wave_spec, wave_spec],
+        out_specs=pl.BlockSpec((2, height, columns_all), lambda i, *s: (0, 0, 0)),
+        scratch_shapes=[pltpu.VMEM((2, height, columns_all), jnp.float32)],
+    )
+    return pl.pallas_call(
+        place_kernel,
+        grid_spec=grid_spec,
+        out_shape=jax.ShapeDtypeStruct((2, height, columns_all), jnp.bfloat16),
+    )(*scalars[:3], spread, source)
 
 
 def first_kernel(rows_ref, columns_ref, order_ref, wave_ref, tile_ref, mine_ref, partner_ref,
@@ -570,11 +611,13 @@
         )
 
     def last_silent(incoming):
-        return (jnp.zeros_like(incoming), jnp.zeros((2, height, columns_all), jnp.bfloat16))
+        return (jnp.zeros_like(incoming), jnp.zeros_like(incoming))
 
     if depth_count > 1:
         carry = lax.ppermute(carry, "depth", [(depth_count - 2, depth_count - 1)])
-    carry, gradient = lax.cond(segment == depth_count - 1, last_pass, last_silent, carry)
+    arrived_last = carry
+    carry, spread_last = lax.cond(segment == depth_count - 1, last_pass, last_silent, carry)
+    gradient = run_place(spread_last, arrived_last, scalars, height, columns_all)
 
     def back_pass(incoming, previous):
         return run_adjoint(

time: 59.5 us -> 59.7 us (level)
  Pallas kernels: 8.71 us -> 12.1 us
  waiting for transfers between devices: 30.3 us -> 27.2 us
    ppermute x1, waiting for transfers between devices: 14.1 us -> 11 us  [local(): carry = lax.ppermute(carry, 'depth', [(turn + 1, turn)])]
    pallas_call x0 -> x1, Pallas kernels: none -> 2.58 us  [run_place(): pl.pallas_call(place_kernel, grid_spec=grid_spec, out_shape=jax.ShapeDtyp...]
    pallas_call x1, Pallas kernels: 3.08 us -> 3.9 us  [run_adjoint(): pl.pallas_call(adjoint_kernel(last, number == 1), grid_spec=grid_spec, ou...]
  transfers between devices with their start and end apart: 11 -> 11, of which waited for: 7 -> 7; matrix products, arithmetic and copies ran while one was open for 9% -> 9% of each run, Pallas kernels for 10% -> 14%
where the time goes in v13:
time: 59.7 us; the launch traced here: 59.3 us
  waiting for transfers between devices  27.2 us (46%)
  Pallas kernels  12.1 us (20%)
  starting transfers between devices  9.39 us (16%)
  other arithmetic  4.12 us (7%)
  between operations  3.99 us (7%)
  local copies, waits for them, and re-layouts  2.55 us (4%)
    ppermute x1, waiting for transfers between devices, local(): carry = lax.ppermute(carry, 'depth', [(turn + 1, turn)])  11 us
    ppermute x1, waiting for transfers between devices, local(): lax.ppermute(spill_sum, 'tile', [(t, t + 1) for t in range(tile_count - 1)])  5.75 us
    ppermute x1, waiting for transfers between devices, from_behind(): return lax.ppermute(block, axis, route)  4.13 us
    pallas_call x1, Pallas kernels, run_first(): pl.pallas_call(first_kernel, grid_spec=grid_spec, out_shape=jax.ShapeDtyp...  3.98 us
    pallas_call x1, Pallas kernels, run_adjoint(): pl.pallas_call(adjoint_kernel(last, number == 1), grid_spec=grid_spec, ou...  3.9 us
    ppermute x1, starting transfers between devices, local(): lax.ppermute(spill_sum, 'tile', [(t, t + 1) for t in range(tile_count - 1)])  3.65 us
    ppermute x1, waiting for transfers between devices, local(): carry = lax.ppermute(carry, 'depth', [(depth_count - 2, depth_count - 1)])  3.06 us
    pallas_call x1, Pallas kernels, run_place(): pl.pallas_call(place_kernel, grid_spec=grid_spec, out_shape=jax.ShapeDtyp...  2.58 us
  transfers between devices with their start and end apart: 11, of which 7 were waited for; matrix products, arithmetic and copies ran while one was open for 9% of the time, Pallas kernels for 14%

profile of v13, /device:TPU:0, one launch (start us, length us, event | category | flops | bytes accessed | tf_op | source)
XLA Modules:
  0.0 59.3 jit_solution(12959773763567281997)
XLA Ops:
  0.0 0.5 collective-permute-start.1
  0.5 0.1 collective-permute-start
  0.5 1.1 %dynamic-slice_convert_fusion = bf16[1,2,256,256]{3,2,1,0:T(8,128)(2,1)S(1)} fusion(f32[1,2,256,512]{3,2,1,0:T(8,128)} %tile_ref.1, s32[]{:T(128)S(6)} %select_n.84), kind=kLoop, calls=%fused_computation.4 | loop fusion | bytes 524292 | tf_op jit(solution)/shard_map/convert_element_type | solution.py:546
  1.6 1.3 %collective-permute-start.2 = (bf16[1,2,256,256]{3,2,1,0:T(8,128)(2,1)S(1)}, bf16[1,2,256,256]{3,2,1,0:T(8,128)(2,1)S(1)}, u32[]{:S(2)}, u32[]{:S(2)}) collective-permute-start(bf16[1,2,256,256]{3,2,1,0:T(8,128)(2,1)S(1)} %dynamic-slice_convert_fusion), channel_id=1, source_target_pairs={{4,0},{8,4},{12,8},{5,1},{9,5},{13,9},{6,2},{10,6},{14,10},{7,3},{... | collective-permute-start | bytes 786440 | tf_op jit(solution)/shard_map/ppermute | solution.py:18
  2.9 0.5 collective-permute-start.5
  3.4 1.1 %multiply_convert_fusion = (bf16[256,256]{1,0:T(8,128)(2,1)S(1)}, bf16[256,256]{1,0:T(8,128)(2,1)S(1)}) fusion(), kind=kLoop, calls=%fused_computation.13 | loop fusion | flops 1245184 | bytes 262144 | tf_op jit(solution)/shard_map/convert_element_type | solution.py:51
  4.6 1.0 %fusion.6 = (f32[1,256,256]{2,1,0:T(8,128)S(1)}, f32[1,256,256]{2,1,0:T(8,128)S(1)}) fusion(s32[256]{0:T(256)S(1)} %fusion.9, f32[]{:T(128)S(6)} %neg.8), kind=kLoop, calls=%fused_computation.19 | loop fusion | flops 196608 | bytes 525316 | tf_op jit(solution)/shard_map/cos | solution.py:61
  6.4 0.6 %broadcast_select_fusion = s32[2]{0:T(128)S(1)} fusion(pred[]{:T(512)} %eq.22, s32[1]{0:T(128)} %collective-permute-done.1, s32[1]{0:T(128)S(6)} %copy.14), kind=kLoop, calls=%fused_computation.30 | loop fusion | flops 6 | bytes 17 | tf_op jit(solution)/shard_map/jit(_where)/select_n | solution.py:560
  7.0 0.7 %fusion.12 = (s32[1]{0:T(128)}, s32[1]{0:T(128)}) fusion(s32[2]{0:T(128)S(1)} %broadcast_select_fusion), kind=kLoop, calls=%fused_computation.32 | loop fusion | bytes 16 | tf_op jit(solution)/shard_map/slice | solution.py:564
  8.8 4.1 %collective-permute-done.2.mine_ref = bf16[1,2,256,256]{3,2,1,0:T(8,128)(2,1)S(1)} collective-permute-done((bf16[1,2,256,256]{3,2,1,0:T(8,128)(2,1)S(1)}, bf16[1,2,256,256]{3,2,1,0:T(8,128)(2,1)S(1)}, u32[]{:S(2)}, u32[]{:S(2)}) %collective-permute-start.2) | collective-permute-done | bytes 262176 | tf_op jit(solution)/shard_map/ppermute | solution.py:18
  13.0 0.7 %fusion.13 = (s32[1,1]{1,0:T(1,128)}, s32[1,1]{1,0:T(1,128)}) fusion(s32[1,2]{1,0:T(1,128)S(1)} %constant_dynamic-slice_fusion), kind=kLoop, calls=%fused_computation.33 | loop fusion | bytes 16 | tf_op jit(solution)/shard_map/slice | solution.py:571
  14.3 0.2 collective-permute-done.3.partner_ref
  14.5 4.0 %conditional.3 = (bf16[1,2,256,256]{3,2,1,0:T(8,128)(2,1)}) conditional(s32[]{:T(128)} %convert_element_type.71, () %tuple.50, (s32[1]{0:T(128)}, s32[1]{0:T(128)}, s32[1]{0:T(128)}, bf16[1,2,256,256]{3,2,1,0:T(8,128)(2,1)S(1)}, f32[1,2,256,512]{3,2,1,0:T(8,128)S(1)}, /*index=5*/bf16[1,2,256,256]{3,2,1,0:T(8,128)(2,1)S(1)}, ...), branch_computations={%region_0.1_spmd, %region_1.2_spmd} | conditional | bytes 262154 | solution.py:602
  14.5 4.0 %branch_1_fun.5 = bf16[1,2,256,256]{3,2,1,0:T(8,128)(2,1)} custom-call(s32[1]{0:T(128)} %get-tuple-element.116.rows_ref, s32[1]{0:T(128)} %get-tuple-element.117.columns_ref, s32[1]{0:T(128)} %get-tuple-element.118.order_ref, bf16[1,2,256,256]{3,2,1,0:T(8,128)(2,1)S(1)} %get-tuple-element.119.wave_ref, f32[1,2,256,512]{3,2,1,0:T(8,128)S(1)} %get-tuple-element.120.tile_ref, ...), custom_call_target="tpu_custom_call" | custom-call | tf_op jit(solution)/shard_map/cond/branch_1_fun/pallas_call | solution.py:527
  18.5 2.0 %collective-permute-start.4 = (bf16[1,2,256,256]{3,2,1,0:T(8,128)(2,1)}, bf16[1,2,256,256]{3,2,1,0:T(8,128)(2,1)}, u32[]{:S(2)}, u32[]{:S(2)}) collective-permute-start(bf16[1,2,256,256]{3,2,1,0:T(8,128)(2,1)} %get-tuple-element.179), channel_id=1, source_target_pairs={{0,2},{1,3},{4,6},{5,7},{8,10},{9,11},{12,14},{13,15},{16,18},{17,... | collective-permute-start | bytes 786440 | tf_op jit(solution)/shard_map/ppermute | solution.py:617
  21.7 1.7 %shard_map.60 = f32[1,2,256,256]{3,2,1,0:T(8,128)S(1)} custom-call(s32[1]{0:T(128)} %sub.17.rows_ref, s32[1]{0:T(128)} %bitcast.4.columns_ref, s32[1]{0:T(128)} %bitcast.order_ref, f32[1,2,256,512]{3,2,1,0:T(8,128)S(1)} %copy-done, bf16[1,2,256,256]{3,2,1,0:T(8,128)(2,1)S(1)} %collective-permute-done.2.mine_ref, ...), custom_call_target="tpu_custom_call" | custom-call | tf_op jit(solution)/shard_map/pallas_call | solution.py:275
  23.4 3.1 %collective-permute-done.4.source_ref = bf16[1,2,256,256]{3,2,1,0:T(8,128)(2,1)} collective-permute-done((bf16[1,2,256,256]{3,2,1,0:T(8,128)(2,1)}, bf16[1,2,256,256]{3,2,1,0:T(8,128)(2,1)}, u32[]{:S(2)}, u32[]{:S(2)}) %collective-permute-start.4) | collective-permute-done | bytes 262176 | tf_op jit(solution)/shard_map/ppermute | solution.py:617
  26.5 0.1 conditional.4
  26.5 1.3 %collective-permute-start.6 = (bf16[1,2,256,256]{3,2,1,0:T(8,128)(2,1)S(1)}, bf16[1,2,256,256]{3,2,1,0:T(8,128)(2,1)}, u32[]{:S(2)}, u32[]{:S(2)}) collective-permute-start(bf16[1,2,256,256]{3,2,1,0:T(8,128)(2,1)S(1)} %get-tuple-element.153), channel_id=1, source_target_pairs={{2,0},{3,1},{6,4},{7,5},{10,8},{11,9},{14,12},{15,13},{18,16},{19,... | collective-permute-start | bytes 786440 | tf_op jit(solution)/shard_map/ppermute | solution.py:631
  27.8 2.6 %shard_map.61 = bf16[2,512,512]{2,1,0:T(8,128)(2,1)S(1)} custom-call(s32[1]{0:T(128)} %sub.17.rows_ref, s32[1]{0:T(128)} %bitcast.4.columns_ref, s32[1]{0:T(128)} %convert_element_type.72.live_ref, bf16[1,2,256,256]{3,2,1,0:T(8,128)(2,1)S(1)} %get-tuple-element.152.spread_ref, bf16[1,2,256,256]{3,2,1,0:T(8,128)(2,1)} %collective-permute-done.4.source_ref), custom_call_target="tpu_custom_call" | custom-call | tf_op jit(solution)/shard_map/pallas_call | solution.py:473
  30.4 11.0 %collective-permute-done.6 = bf16[1,2,256,256]{3,2,1,0:T(8,128)(2,1)} collective-permute-done((bf16[1,2,256,256]{3,2,1,0:T(8,128)(2,1)S(1)}, bf16[1,2,256,256]{3,2,1,0:T(8,128)(2,1)}, u32[]{:S(2)}, u32[]{:S(2)}) %collective-permute-start.6) | collective-permute-done | bytes 262176 | tf_op jit(solution)/shard_map/ppermute | solution.py:631
  41.4 3.9 %conditional.5 = (bf16[2,512,512]{2,1,0:T(8,128)(2,1)S(1)}) conditional(s32[]{:T(128)} %convert_element_type.71, bf16[2,512,512]{2,1,0:T(8,128)(2,1)S(1)} %shard_map.61, (s32[1]{0:T(128)}, s32[1]{0:T(128)}, s32[1]{0:T(128)}, s32[1]{0:T(128)}, s32[1]{0:T(128)}, /*index=5*/bf16[1,2,256,256]{3,2,1,0:T(8,128)(2,1)}, f32[1,2,256,256]{3,2,1,0:T(8,128)S(1)}, ...), branch_computations={%region_4.5_spmd, %region_5.6_spmd} | conditional | bytes 8 | solution.py:632
  41.4 3.9 %branch_1_fun.7 = (bf16[1,2,256,256]{3,2,1,0:T(8,128)(2,1)}, bf16[2,512,512]{2,1,0:T(8,128)(2,1)S(1)}) custom-call(s32[1]{0:T(128)} %get-tuple-element.138.rows_ref, s32[1]{0:T(128)} %get-tuple-element.139.columns_ref, s32[1]{0:T(128)} %get-tuple-element.140.live_ref, s32[1]{0:T(128)} %get-tuple-element.141.slot_ref, s32[1]{0:T(128)} %get-tuple-element.142.other_ref, ...), custom_call_target="tpu_custom_call" | custom-call | tf_op jit(solution)/shard_map/cond/branch_1_fun/pallas_call | solution.py:436
  45.3 0.1 fusion.11
  45.4 0.1 collective-permute-start.8
  45.5 1.5 %collective-permute-done.8 = bf16[2,256,256]{2,1,0:T(8,128)(2,1)S(1)} collective-permute-done((bf16[2,256,256]{2,1,0:T(8,128)(2,1)S(1)}, bf16[2,256,256]{2,1,0:T(8,128)(2,1)S(1)}, u32[]{:S(2)}, u32[]{:S(2)}) %collective-permute-start.8) | collective-permute-done | bytes 262176 | tf_op jit(solution)/shard_map/ppermute | solution.py:638
  47.0 0.1 add_convert_fusion
  47.1 3.7 %collective-permute-start.9 = (bf16[2,256,256]{2,1,0:T(8,128)(2,1)S(1)}, bf16[2,256,256]{2,1,0:T(8,128)(2,1)S(1)}, u32[]{:S(2)}, u32[]{:S(2)}) collective-permute-start(bf16[2,256,256]{2,1,0:T(8,128)(2,1)S(1)} %add_convert_fusion), channel_id=1, source_target_pairs={{0,4},{4,8},{8,12},{1,5},{5,9},{9,13},{2,6},{6,10},{10,14},{3,7},{... | collective-permute-start | bytes 786440 | tf_op jit(solution)/shard_map/ppermute | solution.py:640
  50.7 0.1 collective-permute-start.7
  50.8 5.8 %collective-permute-done.9 = bf16[2,256,256]{2,1,0:T(8,128)(2,1)S(1)} collective-permute-done((bf16[2,256,256]{2,1,0:T(8,128)(2,1)S(1)}, bf16[2,256,256]{2,1,0:T(8,128)(2,1)S(1)}, u32[]{:S(2)}, u32[]{:S(2)}) %collective-permute-start.9) | collective-permute-done | bytes 262176 | tf_op jit(solution)/shard_map/ppermute | solution.py:640
  56.6 1.5 %collective-permute-done.10 = bf16[2,256,256]{2,1,0:T(8,128)(2,1)S(1)} collective-permute-done((bf16[2,256,256]{2,1,0:T(8,128)(2,1)S(1)}, bf16[2,256,256]{2,1,0:T(8,128)(2,1)S(1)}, u32[]{:S(2)}, u32[]{:S(2)}) %collective-permute-start.10) | collective-permute-done | bytes 262176 | tf_op jit(solution)/shard_map/ppermute | solution.py:643
  58.1 1.2 %add_bitcast_fusion = f32[1,2,256,512]{3,2,1,0:T(8,128)} fusion(bf16[2,256,512]{2,1,0:T(8,128)(2,1)S(1)} %collective-permute-done.7, bf16[2,256,256]{2,1,0:T(8,128)(2,1)S(1)} %collective-permute-done.10, bf16[2,256,256]{2,1,0:T(8,128)(2,1)S(1)} %collective-permute-done.9, pred[]{:T(512)} %eq.22, bf16[2,512,512]{2,1,0:T(8,128)(2,1)S(1)} %get-tuple-element.181), kind=kLoop, calls=%fused_computation | loop fusion | flops 3670016 | bytes 2621441 | tf_op jit(solution)/shard_map/broadcast_in_dim | solution.py:651
  (21 shorter events, 0.2 us)
Async XLA Ops:
  0.0 6.4 %collective-permute-start.1 = (s32[1]{0:T(128)}, s32[1]{0:T(128)}, u32[]{:S(2)}, u32[]{:S(2)}) collective-permute-start(s32[1]{0:T(128)} %param.18), channel_id=1, source_target_pairs={{0,1},{1,0},{2,3},{3,2},{4,5},{5,4},{6,7},{7,6},{8,9},{9,8},{10,11... | collective-permute-start | bytes 20 | tf_op jit(solution)/shard_map/ppermute | solution.py:553
  0.5 12.5 %collective-permute-start = (s32[2,2]{1,0:T(2,128)}, s32[2,2]{1,0:T(2,128)S(1)}, u32[]{:S(2)}, u32[]{:S(2)}) collective-permute-start(s32[2,2]{1,0:T(2,128)} %param.17), channel_id=1, source_target_pairs={{0,1},{1,0},{2,3},{3,2},{4,5},{5,4},{6,7},{7,6},{8,9},{9,8},{10,11... | collective-permute-start | bytes 56 | tf_op jit(solution)/shard_map/ppermute | solution.py:552
  1.6 11.4 %collective-permute-start.2 = (bf16[1,2,256,256]{3,2,1,0:T(8,128)(2,1)S(1)}, bf16[1,2,256,256]{3,2,1,0:T(8,128)(2,1)S(1)}, u32[]{:S(2)}, u32[]{:S(2)}) collective-permute-start(bf16[1,2,256,256]{3,2,1,0:T(8,128)(2,1)S(1)} %dynamic-slice_convert_fusion), channel_id=1, source_target_pairs={{4,0},{8,4},{12,8},{5,1},{9,5},{13,9},{6,2},{10,6},{14,10},{7,3},{... | collective-permute-start | bytes 786440 | tf_op jit(solution)/shard_map/ppermute | solution.py:18
  2.9 20.5 %collective-permute-start.5 = (f32[2,256,256]{2,1,0:T(8,128)}, f32[2,256,256]{2,1,0:T(8,128)}, u32[]{:S(2)}, u32[]{:S(2)}) collective-permute-start(f32[2,256,256]{2,1,0:T(8,128)} %param.19), channel_id=1, source_target_pairs={{0,1},{1,0},{2,3},{3,2},{4,5},{5,4},{6,7},{7,6},{8,9},{9,8},{10,11... | collective-permute-start | bytes 1572872 | tf_op jit(solution)/shard_map/ppermute | solution.py:554
  4.6 10.0 %copy-start = (f32[1,2,256,512]{3,2,1,0:T(8,128)S(1)}, f32[1,2,256,512]{3,2,1,0:T(8,128)}, u32[]{:S(2)}) copy-start(f32[1,2,256,512]{3,2,1,0:T(8,128)} %tile_ref.1) | copy-start | bytes 3145732
  5.6 8.9 %copy-start.1 = (bf16[2,256,256]{2,1,0:T(8,128)(2,1)S(1)}, bf16[2,256,256]{2,1,0:T(8,128)(2,1)}, u32[]{:S(2)}) copy-start(bf16[2,256,256]{2,1,0:T(8,128)(2,1)} %param.16) | copy-start | bytes 786436
  8.8 4.2 %copy-start.2 = (s32[2,2]{1,0:T(2,128)S(1)}, s32[2,2]{1,0:T(2,128)}, u32[]{:S(2)}) copy-start(s32[2,2]{1,0:T(2,128)} %param.17) | copy-start | bytes 52
  13.0 1.5 %collective-permute-start.3 = (bf16[1,2,256,256]{3,2,1,0:T(8,128)(2,1)S(1)}, bf16[1,2,256,256]{3,2,1,0:T(8,128)(2,1)S(1)}, u32[]{:S(2)}, u32[]{:S(2)}) collective-permute-start(bf16[1,2,256,256]{3,2,1,0:T(8,128)(2,1)S(1)} %collective-permute-done.2.mine_ref), channel_id=1, source_target_pairs={{0,1},{1,0},{2,3},{3,2},{4,5},{5,4},{6,7},{7,6},{8,9},{9,8},{10,11... | collective-permute-start | bytes 786440 | tf_op jit(solution)/shard_map/ppermute | solution.py:548
  18.5 8.0 %collective-permute-start.4 = (bf16[1,2,256,256]{3,2,1,0:T(8,128)(2,1)}, bf16[1,2,256,256]{3,2,1,0:T(8,128)(2,1)}, u32[]{:S(2)}, u32[]{:S(2)}) collective-permute-start(bf16[1,2,256,256]{3,2,1,0:T(8,128)(2,1)} %get-tuple-element.179), channel_id=1, source_target_pairs={{0,2},{1,3},{4,6},{5,7},{8,10},{9,11},{12,14},{13,15},{16,18},{17,... | collective-permute-start | bytes 786440 | tf_op jit(solution)/shard_map/ppermute | solution.py:617
  26.5 14.9 %collective-permute-start.6 = (bf16[1,2,256,256]{3,2,1,0:T(8,128)(2,1)S(1)}, bf16[1,2,256,256]{3,2,1,0:T(8,128)(2,1)}, u32[]{:S(2)}, u32[]{:S(2)}) collective-permute-start(bf16[1,2,256,256]{3,2,1,0:T(8,128)(2,1)S(1)} %get-tuple-element.153), channel_id=1, source_target_pairs={{2,0},{3,1},{6,4},{7,5},{10,8},{11,9},{14,12},{15,13},{18,16},{19,... | collective-permute-start | bytes 786440 | tf_op jit(solution)/shard_map/ppermute | solution.py:631
  45.4 1.6 %collective-permute-start.8 = (bf16[2,256,256]{2,1,0:T(8,128)(2,1)S(1)}, bf16[2,256,256]{2,1,0:T(8,128)(2,1)S(1)}, u32[]{:S(2)}, u32[]{:S(2)}) collective-permute-start(bf16[2,256,256]{2,1,0:T(8,128)(2,1)S(1)} %constant_dynamic-slice_fusion.1), channel_id=1, source_target_pairs={{0,1},{1,0},{2,3},{3,2},{4,5},{5,4},{6,7},{7,6},{8,9},{9,8},{10,11... | collective-permute-start | bytes 786440 | tf_op jit(solution)/shard_map/ppermute | solution.py:638
  47.1 9.5 %collective-permute-start.9 = (bf16[2,256,256]{2,1,0:T(8,128)(2,1)S(1)}, bf16[2,256,256]{2,1,0:T(8,128)(2,1)S(1)}, u32[]{:S(2)}, u32[]{:S(2)}) collective-permute-start(bf16[2,256,256]{2,1,0:T(8,128)(2,1)S(1)} %add_convert_fusion), channel_id=1, source_target_pairs={{0,4},{4,8},{8,12},{1,5},{5,9},{9,13},{2,6},{6,10},{10,14},{3,7},{... | collective-permute-start | bytes 786440 | tf_op jit(solution)/shard_map/ppermute | solution.py:640
  50.7 5.8 %collective-permute-start.7 = (bf16[2,256,512]{2,1,0:T(8,128)(2,1)S(1)}, bf16[2,256,512]{2,1,0:T(8,128)(2,1)S(1)}, u32[]{:S(2)}, u32[]{:S(2)}) collective-permute-start(bf16[2,256,512]{2,1,0:T(8,128)(2,1)S(1)} %get-tuple-element.166), channel_id=1, source_target_pairs={{0,1},{1,0},{2,3},{3,2},{4,5},{5,4},{6,7},{7,6},{8,9},{9,8},{10,11... | collective-permute-start | bytes 1572872 | tf_op jit(solution)/shard_map/ppermute | solution.py:642
  56.6 1.5 %collective-permute-start.10 = (bf16[2,256,256]{2,1,0:T(8,128)(2,1)S(1)}, bf16[2,256,256]{2,1,0:T(8,128)(2,1)S(1)}, u32[]{:S(2)}, u32[]{:S(2)}) collective-permute-start(bf16[2,256,256]{2,1,0:T(8,128)(2,1)S(1)} %collective-permute-done.9), channel_id=1, source_target_pairs={{0,1},{1,0},{2,3},{3,2},{4,5},{5,4},{6,7},{7,6},{8,9},{9,8},{10,11... | collective-permute-start | bytes 786440 | tf_op jit(solution)/shard_map/ppermute | solution.py:643

commit v14 on v12

--- a/solution.py
+++ b/solution.py
@@ -510,7 +510,6 @@
     first_core = batch_index == 0
     both_positions = lax.ppermute(positions, "batch", pairs)
     both_counts = lax.ppermute(counts, "batch", pairs)
-    both_measured = lax.ppermute(measured, "batch", pairs)
     all_positions = jnp.where(
         first_core,
         jnp.concatenate([positions, both_positions]),
@@ -560,6 +559,8 @@
             inputs = jnp.where(segment == turn, carry, inputs)
         carry = lax.cond(segment == turn, forward_all, silent, carry)
 
+    measured, carry = lax.optimization_barrier((measured, carry))
+    both_measured = lax.ppermute(measured, "batch", pairs)
     height = tile_rows + width
     scalars = (local_rows, local_columns, live.astype(jnp.int32), slot, other)
 

time: 59.5 us -> 59.4 us (level)
  transfers between devices with their start and end apart: 11 -> 11, of which waited for: 7 -> 7; matrix products, arithmetic and copies ran while one was open for 9% -> 9% of each run, Pallas kernels for 10% -> 3%
where the time goes in v14:
time: 59.4 us; the launch traced here: 59.1 us
  waiting for transfers between devices  30.4 us (51%)
  starting transfers between devices  9.25 us (16%)
  Pallas kernels  8.71 us (15%)
  other arithmetic  4.13 us (7%)
  between operations  3.97 us (7%)
  local copies, waits for them, and re-layouts  2.6 us (4%)
    ppermute x1, waiting for transfers between devices, local(): carry = lax.ppermute(carry, 'depth', [(turn + 1, turn)])  14 us
    ppermute x1, waiting for transfers between devices, local(): lax.ppermute(spill_sum, 'tile', [(t, t + 1) for t in range(tile_count - 1)])  5.75 us
    ppermute x1, waiting for transfers between devices, from_behind(): return lax.ppermute(block, axis, route)  4.64 us
    pallas_call x1, Pallas kernels, run_first(): pl.pallas_call(first_kernel, grid_spec=grid_spec, out_shape=jax.ShapeDtyp...  3.98 us
    ppermute x1, starting transfers between devices, local(): lax.ppermute(spill_sum, 'tile', [(t, t + 1) for t in range(tile_count - 1)])  3.66 us
    pallas_call x1, Pallas kernels, run_adjoint(): pl.pallas_call(adjoint_kernel(last, number == 1), grid_spec=grid_spec, ou...  3.08 us
    ppermute x1, waiting for transfers between devices, local(): carry = lax.ppermute(carry, 'depth', [(depth_count - 2, depth_count - 1)])  2.83 us
    ppermute x1, starting transfers between devices, local(): carry = lax.ppermute(carry, 'depth', [(depth_count - 2, depth_count - 1)])  1.98 us
  transfers between devices with their start and end apart: 11, of which 7 were waited for; matrix products, arithmetic and copies ran while one was open for 9% of the time, Pallas kernels for 3%

profile of v14, /device:TPU:0, one launch (start us, length us, event | category | flops | bytes accessed | tf_op | source)
XLA Modules:
  0.0 59.1 jit_solution(14186971042492728945)
XLA Ops:
  0.0 0.5 collective-permute-start.1
  0.5 0.1 collective-permute-start
  0.5 1.1 %dynamic-slice_convert_fusion = bf16[1,2,256,256]{3,2,1,0:T(8,128)(2,1)S(1)} fusion(f32[1,2,256,512]{3,2,1,0:T(8,128)} %tile_ref.1, s32[]{:T(128)S(6)} %select_n.84), kind=kLoop, calls=%fused_computation.4 | loop fusion | bytes 524292 | tf_op jit(solution)/shard_map/convert_element_type | solution.py:505
  1.6 1.3 %collective-permute-start.2 = (bf16[1,2,256,256]{3,2,1,0:T(8,128)(2,1)S(1)}, bf16[1,2,256,256]{3,2,1,0:T(8,128)(2,1)S(1)}, u32[]{:S(2)}, u32[]{:S(2)}) collective-permute-start(bf16[1,2,256,256]{3,2,1,0:T(8,128)(2,1)S(1)} %dynamic-slice_convert_fusion), channel_id=1, source_target_pairs={{4,0},{8,4},{12,8},{5,1},{9,5},{13,9},{6,2},{10,6},{14,10},{7,3},{... | collective-permute-start | bytes 786440 | tf_op jit(solution)/shard_map/ppermute | solution.py:18
  2.9 1.1 %multiply_convert_fusion = (bf16[256,256]{1,0:T(8,128)(2,1)S(1)}, bf16[256,256]{1,0:T(8,128)(2,1)S(1)}) fusion(), kind=kLoop, calls=%fused_computation.13 | loop fusion | flops 1245184 | bytes 262144 | tf_op jit(solution)/shard_map/convert_element_type | solution.py:51
  4.1 1.0 %fusion.6 = (f32[1,256,256]{2,1,0:T(8,128)S(1)}, f32[1,256,256]{2,1,0:T(8,128)S(1)}) fusion(s32[256]{0:T(256)S(1)} %fusion.9, f32[]{:T(128)S(6)} %neg.8), kind=kLoop, calls=%fused_computation.19 | loop fusion | flops 196608 | bytes 525316 | tf_op jit(solution)/shard_map/cos | solution.py:61
  5.9 0.6 %broadcast_select_fusion = s32[2]{0:T(128)S(1)} fusion(pred[]{:T(512)} %eq.23, s32[1]{0:T(128)} %collective-permute-done.1, s32[1]{0:T(128)S(6)} %copy.14), kind=kLoop, calls=%fused_computation.30 | loop fusion | flops 6 | bytes 17 | tf_op jit(solution)/shard_map/jit(_where)/select_n | solution.py:518
  6.5 0.7 %fusion.12 = (s32[1]{0:T(128)}, s32[1]{0:T(128)}) fusion(s32[2]{0:T(128)S(1)} %broadcast_select_fusion), kind=kLoop, calls=%fused_computation.32 | loop fusion | bytes 16 | tf_op jit(solution)/shard_map/slice | solution.py:522
  8.3 4.6 %collective-permute-done.2.mine_ref = bf16[1,2,256,256]{3,2,1,0:T(8,128)(2,1)S(1)} collective-permute-done((bf16[1,2,256,256]{3,2,1,0:T(8,128)(2,1)S(1)}, bf16[1,2,256,256]{3,2,1,0:T(8,128)(2,1)S(1)}, u32[]{:S(2)}, u32[]{:S(2)}) %collective-permute-start.2) | collective-permute-done | bytes 262176 | tf_op jit(solution)/shard_map/ppermute | solution.py:18
  13.0 0.7 %fusion.13 = (s32[1,1]{1,0:T(1,128)}, s32[1,1]{1,0:T(1,128)}) fusion(s32[1,2]{1,0:T(1,128)S(1)} %constant_dynamic-slice_fusion), kind=kLoop, calls=%fused_computation.33 | loop fusion | bytes 16 | tf_op jit(solution)/shard_map/slice | solution.py:529
  14.3 0.2 collective-permute-done.3.partner_ref
  14.5 4.0 %conditional.3 = (bf16[1,2,256,256]{3,2,1,0:T(8,128)(2,1)}) conditional(s32[]{:T(128)} %convert_element_type.71, () %tuple.55, (s32[1]{0:T(128)}, s32[1]{0:T(128)}, s32[1]{0:T(128)}, bf16[1,2,256,256]{3,2,1,0:T(8,128)(2,1)S(1)}, f32[1,2,256,512]{3,2,1,0:T(8,128)S(1)}, /*index=5*/bf16[1,2,256,256]{3,2,1,0:T(8,128)(2,1)S(1)}, ...), branch_computations={%region_0.1_spmd, %region_1.2_spmd} | conditional | bytes 262154 | solution.py:560
  14.5 4.0 %branch_1_fun.5 = bf16[1,2,256,256]{3,2,1,0:T(8,128)(2,1)} custom-call(s32[1]{0:T(128)} %get-tuple-element.119.rows_ref, s32[1]{0:T(128)} %get-tuple-element.120.columns_ref, s32[1]{0:T(128)} %get-tuple-element.121.order_ref, bf16[1,2,256,256]{3,2,1,0:T(8,128)(2,1)S(1)} %get-tuple-element.122.wave_ref, f32[1,2,256,512]{3,2,1,0:T(8,128)S(1)} %get-tuple-element.123.tile_ref, ...), custom_call_target="tpu_custom_call" | custom-call | tf_op jit(solution)/shard_map/cond/branch_1_fun/pallas_call | solution.py:486
  18.5 0.4 collective-permute-start.5
  18.9 2.0 %collective-permute-start.4 = (bf16[1,2,256,256]{3,2,1,0:T(8,128)(2,1)}, bf16[1,2,256,256]{3,2,1,0:T(8,128)(2,1)}, u32[]{:S(2)}, u32[]{:S(2)}) collective-permute-start(bf16[1,2,256,256]{3,2,1,0:T(8,128)(2,1)} %get-tuple-element.186), channel_id=1, source_target_pairs={{0,2},{1,3},{4,6},{5,7},{8,10},{9,11},{12,14},{13,15},{16,18},{17,... | collective-permute-start | bytes 786440 | tf_op jit(solution)/shard_map/ppermute | solution.py:577
  22.1 1.7 %shard_map.60 = f32[1,2,256,256]{3,2,1,0:T(8,128)S(1)} custom-call(s32[1]{0:T(128)} %sub.17.rows_ref, s32[1]{0:T(128)} %bitcast.4.columns_ref, s32[1]{0:T(128)} %bitcast.order_ref, f32[1,2,256,512]{3,2,1,0:T(8,128)S(1)} %copy-done, bf16[1,2,256,256]{3,2,1,0:T(8,128)(2,1)S(1)} %collective-permute-done.2.mine_ref, ...), custom_call_target="tpu_custom_call" | custom-call | tf_op jit(solution)/shard_map/pallas_call | solution.py:275
  23.8 2.8 %collective-permute-done.4 = bf16[1,2,256,256]{3,2,1,0:T(8,128)(2,1)} collective-permute-done((bf16[1,2,256,256]{3,2,1,0:T(8,128)(2,1)}, bf16[1,2,256,256]{3,2,1,0:T(8,128)(2,1)}, u32[]{:S(2)}, u32[]{:S(2)}) %collective-permute-start.4) | collective-permute-done | bytes 262176 | tf_op jit(solution)/shard_map/ppermute | solution.py:577
  26.6 0.1 conditional.4
  26.6 0.1 broadcast.198
  26.7 1.3 %collective-permute-start.6 = (bf16[1,2,256,256]{3,2,1,0:T(8,128)(2,1)S(1)}, bf16[1,2,256,256]{3,2,1,0:T(8,128)(2,1)S(1)}, u32[]{:S(2)}, u32[]{:S(2)}) collective-permute-start(bf16[1,2,256,256]{3,2,1,0:T(8,128)(2,1)S(1)} %get-tuple-element.160), channel_id=1, source_target_pairs={{2,0},{3,1},{6,4},{7,5},{10,8},{11,9},{14,12},{15,13},{18,16},{19,... | collective-permute-start | bytes 786440 | tf_op jit(solution)/shard_map/ppermute | solution.py:589
  28.0 14.0 %collective-permute-done.6 = bf16[1,2,256,256]{3,2,1,0:T(8,128)(2,1)S(1)} collective-permute-done((bf16[1,2,256,256]{3,2,1,0:T(8,128)(2,1)S(1)}, bf16[1,2,256,256]{3,2,1,0:T(8,128)(2,1)S(1)}, u32[]{:S(2)}, u32[]{:S(2)}) %collective-permute-start.6) | collective-permute-done | bytes 262176 | tf_op jit(solution)/shard_map/ppermute | solution.py:589
  42.0 3.1 %conditional.5 = (bf16[2,512,512]{2,1,0:T(8,128)(2,1)S(1)}) conditional(s32[]{:T(128)} %convert_element_type.71, bf16[2,512,512]{2,1,0:T(8,128)(2,1)S(1)} %get-tuple-element.159, (s32[1]{0:T(128)}, s32[1]{0:T(128)}, s32[1]{0:T(128)}, s32[1]{0:T(128)}, s32[1]{0:T(128)}, /*index=5*/bf16[1,2,256,256]{3,2,1,0:T(8,128)(2,1)S(1)}, ...), branch_computations={%region_4.5_spmd, %region_5.6_spmd} | conditional | bytes 8 | solution.py:590
  42.0 3.1 %branch_1_fun.7 = (bf16[1,2,256,256]{3,2,1,0:T(8,128)(2,1)}, bf16[2,512,512]{2,1,0:T(8,128)(2,1)S(1)}) custom-call(s32[1]{0:T(128)} %get-tuple-element.141.rows_ref, s32[1]{0:T(128)} %get-tuple-element.142.columns_ref, s32[1]{0:T(128)} %get-tuple-element.143.live_ref, s32[1]{0:T(128)} %get-tuple-element.144.slot_ref, s32[1]{0:T(128)} %get-tuple-element.145.other_ref, ...), custom_call_target="tpu_custom_call" | custom-call | tf_op jit(solution)/shard_map/cond/branch_1_fun/pallas_call | solution.py:429
  45.1 0.1 fusion.11
  45.2 0.1 collective-permute-start.8
  45.3 1.5 %collective-permute-done.8 = bf16[2,256,256]{2,1,0:T(8,128)(2,1)S(1)} collective-permute-done((bf16[2,256,256]{2,1,0:T(8,128)(2,1)S(1)}, bf16[2,256,256]{2,1,0:T(8,128)(2,1)S(1)}, u32[]{:S(2)}, u32[]{:S(2)}) %collective-permute-start.8) | collective-permute-done | bytes 262176 | tf_op jit(solution)/shard_map/ppermute | solution.py:596
  46.8 0.1 add_convert_fusion
  46.9 3.7 %collective-permute-start.9 = (bf16[2,256,256]{2,1,0:T(8,128)(2,1)S(1)}, bf16[2,256,256]{2,1,0:T(8,128)(2,1)S(1)}, u32[]{:S(2)}, u32[]{:S(2)}) collective-permute-start(bf16[2,256,256]{2,1,0:T(8,128)(2,1)S(1)} %add_convert_fusion), channel_id=1, source_target_pairs={{0,4},{4,8},{8,12},{1,5},{5,9},{9,13},{2,6},{6,10},{10,14},{3,7},{... | collective-permute-start | bytes 786440 | tf_op jit(solution)/shard_map/ppermute | solution.py:598
  50.5 0.1 collective-permute-start.7
  50.6 5.8 %collective-permute-done.9 = bf16[2,256,256]{2,1,0:T(8,128)(2,1)S(1)} collective-permute-done((bf16[2,256,256]{2,1,0:T(8,128)(2,1)S(1)}, bf16[2,256,256]{2,1,0:T(8,128)(2,1)S(1)}, u32[]{:S(2)}, u32[]{:S(2)}) %collective-permute-start.9) | collective-permute-done | bytes 262176 | tf_op jit(solution)/shard_map/ppermute | solution.py:598
  56.4 1.5 %collective-permute-done.10 = bf16[2,256,256]{2,1,0:T(8,128)(2,1)S(1)} collective-permute-done((bf16[2,256,256]{2,1,0:T(8,128)(2,1)S(1)}, bf16[2,256,256]{2,1,0:T(8,128)(2,1)S(1)}, u32[]{:S(2)}, u32[]{:S(2)}) %collective-permute-start.10) | collective-permute-done | bytes 262176 | tf_op jit(solution)/shard_map/ppermute | solution.py:601
  57.9 1.2 %add_bitcast_fusion = f32[1,2,256,512]{3,2,1,0:T(8,128)} fusion(bf16[2,256,512]{2,1,0:T(8,128)(2,1)S(1)} %collective-permute-done.7, bf16[2,256,256]{2,1,0:T(8,128)(2,1)S(1)} %collective-permute-done.10, bf16[2,256,256]{2,1,0:T(8,128)(2,1)S(1)} %collective-permute-done.9, pred[]{:T(512)} %eq.23, bf16[2,512,512]{2,1,0:T(8,128)(2,1)S(1)} %get-tuple-element.188), kind=kLoop, calls=%fused_computation | loop fusion | flops 3670016 | bytes 2621441 | tf_op jit(solution)/shard_map/broadcast_in_dim | solution.py:609
  (20 shorter events, 0.2 us)
Async XLA Ops:
  0.0 5.9 %collective-permute-start.1 = (s32[1]{0:T(128)}, s32[1]{0:T(128)}, u32[]{:S(2)}, u32[]{:S(2)}) collective-permute-start(s32[1]{0:T(128)} %param.18), channel_id=1, source_target_pairs={{0,1},{1,0},{2,3},{3,2},{4,5},{5,4},{6,7},{7,6},{8,9},{9,8},{10,11... | collective-permute-start | bytes 20 | tf_op jit(solution)/shard_map/ppermute | solution.py:512
  0.5 12.5 %collective-permute-start = (s32[2,2]{1,0:T(2,128)}, s32[2,2]{1,0:T(2,128)S(1)}, u32[]{:S(2)}, u32[]{:S(2)}) collective-permute-start(s32[2,2]{1,0:T(2,128)} %param.17), channel_id=1, source_target_pairs={{0,1},{1,0},{2,3},{3,2},{4,5},{5,4},{6,7},{7,6},{8,9},{9,8},{10,11... | collective-permute-start | bytes 56 | tf_op jit(solution)/shard_map/ppermute | solution.py:511
  1.6 11.4 %collective-permute-start.2 = (bf16[1,2,256,256]{3,2,1,0:T(8,128)(2,1)S(1)}, bf16[1,2,256,256]{3,2,1,0:T(8,128)(2,1)S(1)}, u32[]{:S(2)}, u32[]{:S(2)}) collective-permute-start(bf16[1,2,256,256]{3,2,1,0:T(8,128)(2,1)S(1)} %dynamic-slice_convert_fusion), channel_id=1, source_target_pairs={{4,0},{8,4},{12,8},{5,1},{9,5},{13,9},{6,2},{10,6},{14,10},{7,3},{... | collective-permute-start | bytes 786440 | tf_op jit(solution)/shard_map/ppermute | solution.py:18
  4.0 10.5 %copy-start = (f32[1,2,256,512]{3,2,1,0:T(8,128)S(1)}, f32[1,2,256,512]{3,2,1,0:T(8,128)}, u32[]{:S(2)}) copy-start(f32[1,2,256,512]{3,2,1,0:T(8,128)} %tile_ref.1) | copy-start | bytes 3145732
  5.1 9.4 %copy-start.1 = (bf16[2,256,256]{2,1,0:T(8,128)(2,1)S(1)}, bf16[2,256,256]{2,1,0:T(8,128)(2,1)}, u32[]{:S(2)}) copy-start(bf16[2,256,256]{2,1,0:T(8,128)(2,1)} %param.16) | copy-start | bytes 786436
  8.3 4.7 %copy-start.2 = (s32[2,2]{1,0:T(2,128)S(1)}, s32[2,2]{1,0:T(2,128)}, u32[]{:S(2)}) copy-start(s32[2,2]{1,0:T(2,128)} %param.17) | copy-start | bytes 52
  13.0 1.5 %collective-permute-start.3 = (bf16[1,2,256,256]{3,2,1,0:T(8,128)(2,1)S(1)}, bf16[1,2,256,256]{3,2,1,0:T(8,128)(2,1)S(1)}, u32[]{:S(2)}, u32[]{:S(2)}) collective-permute-start(bf16[1,2,256,256]{3,2,1,0:T(8,128)(2,1)S(1)} %collective-permute-done.2.mine_ref), channel_id=1, source_target_pairs={{0,1},{1,0},{2,3},{3,2},{4,5},{5,4},{6,7},{7,6},{8,9},{9,8},{10,11... | collective-permute-start | bytes 786440 | tf_op jit(solution)/shard_map/ppermute | solution.py:507
  18.5 8.1 %collective-permute-start.5 = (f32[2,256,256]{2,1,0:T(8,128)}, f32[2,256,256]{2,1,0:T(8,128)}, u32[]{:S(2)}, u32[]{:S(2)}) collective-permute-start(f32[2,256,256]{2,1,0:T(8,128)} %param.19), channel_id=1, source_target_pairs={{0,1},{1,0},{2,3},{3,2},{4,5},{5,4},{6,7},{7,6},{8,9},{9,8},{10,11... | collective-permute-start | bytes 1572872 | tf_op jit(solution)/shard_map/ppermute | solution.py:563
  18.9 7.7 %collective-permute-start.4 = (bf16[1,2,256,256]{3,2,1,0:T(8,128)(2,1)}, bf16[1,2,256,256]{3,2,1,0:T(8,128)(2,1)}, u32[]{:S(2)}, u32[]{:S(2)}) collective-permute-start(bf16[1,2,256,256]{3,2,1,0:T(8,128)(2,1)} %get-tuple-element.186), channel_id=1, source_target_pairs={{0,2},{1,3},{4,6},{5,7},{8,10},{9,11},{12,14},{13,15},{16,18},{17,... | collective-permute-start | bytes 786440 | tf_op jit(solution)/shard_map/ppermute | solution.py:577
  26.7 15.3 %collective-permute-start.6 = (bf16[1,2,256,256]{3,2,1,0:T(8,128)(2,1)S(1)}, bf16[1,2,256,256]{3,2,1,0:T(8,128)(2,1)S(1)}, u32[]{:S(2)}, u32[]{:S(2)}) collective-permute-start(bf16[1,2,256,256]{3,2,1,0:T(8,128)(2,1)S(1)} %get-tuple-element.160), channel_id=1, source_target_pairs={{2,0},{3,1},{6,4},{7,5},{10,8},{11,9},{14,12},{15,13},{18,16},{19,... | collective-permute-start | bytes 786440 | tf_op jit(solution)/shard_map/ppermute | solution.py:589
  45.2 1.6 %collective-permute-start.8 = (bf16[2,256,256]{2,1,0:T(8,128)(2,1)S(1)}, bf16[2,256,256]{2,1,0:T(8,128)(2,1)S(1)}, u32[]{:S(2)}, u32[]{:S(2)}) collective-permute-start(bf16[2,256,256]{2,1,0:T(8,128)(2,1)S(1)} %constant_dynamic-slice_fusion.1), channel_id=1, source_target_pairs={{0,1},{1,0},{2,3},{3,2},{4,5},{5,4},{6,7},{7,6},{8,9},{9,8},{10,11... | collective-permute-start | bytes 786440 | tf_op jit(solution)/shard_map/ppermute | solution.py:596
  46.9 9.5 %collective-permute-start.9 = (bf16[2,256,256]{2,1,0:T(8,128)(2,1)S(1)}, bf16[2,256,256]{2,1,0:T(8,128)(2,1)S(1)}, u32[]{:S(2)}, u32[]{:S(2)}) collective-permute-start(bf16[2,256,256]{2,1,0:T(8,128)(2,1)S(1)} %add_convert_fusion), channel_id=1, source_target_pairs={{0,4},{4,8},{8,12},{1,5},{5,9},{9,13},{2,6},{6,10},{10,14},{3,7},{... | collective-permute-start | bytes 786440 | tf_op jit(solution)/shard_map/ppermute | solution.py:598
  50.5 5.8 %collective-permute-start.7 = (bf16[2,256,512]{2,1,0:T(8,128)(2,1)S(1)}, bf16[2,256,512]{2,1,0:T(8,128)(2,1)S(1)}, u32[]{:S(2)}, u32[]{:S(2)}) collective-permute-start(bf16[2,256,512]{2,1,0:T(8,128)(2,1)S(1)} %get-tuple-element.173), channel_id=1, source_target_pairs={{0,1},{1,0},{2,3},{3,2},{4,5},{5,4},{6,7},{7,6},{8,9},{9,8},{10,11... | collective-permute-start | bytes 1572872 | tf_op jit(solution)/shard_map/ppermute | solution.py:600
  56.3 1.5 %collective-permute-start.10 = (bf16[2,256,256]{2,1,0:T(8,128)(2,1)S(1)}, bf16[2,256,256]{2,1,0:T(8,128)(2,1)S(1)}, u32[]{:S(2)}, u32[]{:S(2)}) collective-permute-start(bf16[2,256,256]{2,1,0:T(8,128)(2,1)S(1)} %collective-permute-done.9), channel_id=1, source_target_pairs={{0,1},{1,0},{2,3},{3,2},{4,5},{5,4},{6,7},{7,6},{8,9},{9,8},{10,11... | collective-permute-start | bytes 786440 | tf_op jit(solution)/shard_map/ppermute | solution.py:601

commit v15 on v14

--- a/solution.py
+++ b/solution.py
@@ -436,15 +436,44 @@
     )(*scalars, waves, patches, chirps, *blocks, *extra)
 
 
-def first_kernel(rows_ref, columns_ref, order_ref, wave_ref, tile_ref, mine_ref, partner_ref,
+def tile_cut_kernel(rows_ref, columns_ref, tile_ref, out_ref):
+    index = pl.program_id(0)
+    width = out_ref.shape[2]
+    rows_all = tile_ref.shape[2]
+    columns_all = tile_ref.shape[3]
+    row_shift = (rows_all - rows_ref[index]) % rows_all
+    column_shift = (columns_all - columns_ref[index]) % columns_all
+    for part in range(2):
+        rolled = pltpu.roll(tile_ref[0, part], row_shift, 0)
+        out_ref[0, part] = pltpu.roll(rolled, column_shift, 1)[:, :width]
+
+
+def cut_tile(tile, rows, columns, width):
+    number = rows.shape[0]
+    grid_spec = pltpu.PrefetchScalarGridSpec(
+        num_scalar_prefetch=2,
+        grid=(number,),
+        in_specs=[pl.BlockSpec(tile.shape, lambda i, r, c: (0, 0, 0, 0))],
+        out_specs=pl.BlockSpec((1, 2, width, width), lambda i, r, c: (i, 0, 0, 0)),
+    )
+    return pl.pallas_call(
+        tile_cut_kernel,
+        grid_spec=grid_spec,
+        out_shape=jax.ShapeDtypeStruct((number, 2, width, width), jnp.float32),
+    )(rows, columns, tile)
+
+
+def first_kernel(rows_ref, columns_ref, order_ref, wave_ref, top_ref, mine_ref, partner_ref,
                  chirp_ref, dft_rows_ref, dft_cols_ref, result_ref):
     index = pl.program_id(0)
     width = wave_ref.shape[2]
-    height = tile_ref.shape[2] + mine_ref.shape[2]
-    columns_all = tile_ref.shape[3]
-    row_shift = (height - rows_ref[index]) % height
+    rim_rows = mine_ref.shape[2]
+    columns_all = 2 * mine_ref.shape[3]
+    row = rows_ref[index]
+    row_shift = (rim_rows - row) % rim_rows
     column_shift = (columns_all - columns_ref[index]) % columns_all
     first = order_ref[0] == 0
+    from_tile = lax.broadcasted_iota(jnp.int32, (width, width), 0) < width - row
     patch = []
     for part in range(2):
         mine = mine_ref[0, part].astype(jnp.float32)
@@ -452,9 +481,8 @@
         rim = jnp.concatenate(
             [jnp.where(first, mine, partner), jnp.where(first, partner, mine)], axis=1
         )
-        full = jnp.concatenate([tile_ref[0, part], rim], axis=0)
-        full = pltpu.roll(full, row_shift, 0)[:width]
-        patch.append(pltpu.roll(full, column_shift, 1)[:, :width])
+        rim = pltpu.roll(pltpu.roll(rim, row_shift, 0), column_shift, 1)[:width, :width]
+        patch.append(jnp.where(from_tile, top_ref[0, part], rim))
     wave = wave_ref[0].astype(jnp.float32)
     wave_re = patch[0] * wave[0] - patch[1] * wave[1]
     wave_im = patch[0] * wave[1] + patch[1] * wave[0]
@@ -465,7 +493,7 @@
     result_ref[0, 1] = out_im.astype(jnp.bfloat16)
 
 
-def run_first(waves, tile, mine, partner, rows, columns, order, chirps, blocks):
+def run_first(waves, top, mine, partner, rows, columns, order, chirps, blocks):
     number, _, width, _ = waves.shape
     wave_spec = pl.BlockSpec((1, 2, width, width), lambda i, r, c, o: (i, 0, 0, 0))
     whole = lambda shape: pl.BlockSpec(shape, lambda i, r, c, o: (0,) * len(shape))
@@ -474,7 +502,7 @@
         grid=(number,),
         in_specs=[
             wave_spec,
-            whole(tile.shape),
+            wave_spec,
             whole(mine.shape),
             whole(partner.shape),
             whole(chirps.shape),
@@ -487,7 +515,7 @@
         first_kernel,
         grid_spec=grid_spec,
         out_shape=jax.ShapeDtypeStruct(waves.shape, jnp.bfloat16),
-    )(rows, columns, order, waves, tile, mine, partner, chirps, *blocks)
+    )(rows, columns, order, waves, top, mine, partner, chirps, *blocks)
 
 
 def local(object_field, probe, positions, counts, measured):
@@ -528,6 +556,7 @@
     local_rows = chosen[:, 0] - tile_index * tile_rows
     local_columns = chosen[:, 1]
     order = jnp.reshape(batch_index, (1,)).astype(jnp.int32)
+    top = cut_tile(object_field, local_rows, local_columns, width)
     patches = cut_patches(object_field, mine, partner, local_rows, local_columns, order, width)
     number = patches.shape[0]
     coef = jnp.where(
@@ -545,7 +574,7 @@
 
     def forward_all(waves):
         return run_first(
-            waves, object_field, mine, partner, local_rows, local_columns, order, chirps, blocks
+            waves, top, mine, partner, local_rows, local_columns, order, chirps, blocks
         )
 
     def silent(waves):

time: 59.4 us -> 61.4 us (1.034)
  Pallas kernels: 8.71 us -> 11.9 us
  waiting for transfers between devices: 30.4 us -> 28.3 us
  local copies, waits for them, and re-layouts: 2.6 us -> 3.3 us
    pallas_call x0 -> x1, Pallas kernels: none -> 2.41 us  [cut_tile(): pl.pallas_call(tile_cut_kernel, grid_spec=grid_spec, out_shape=jax.ShapeD...]
    ppermute x1, waiting for transfers between devices: 2.83 us -> 1.48 us  [local(): carry = lax.ppermute(carry, 'depth', [(depth_count - 2, depth_count - 1)])]
    pallas_call x1, Pallas kernels: 1.65 us -> 2.87 us  [cut_patches(): pl.pallas_call(cut_kernel, grid_spec=grid_spec, out_shape=jax.ShapeDtypeS...]
    another operation x2, local copies, waits for them, and re-layouts: 0.09 us -> 0.79 us
    ppermute x1, waiting for transfers between devices: 14 us -> 13.3 us  [local(): carry = lax.ppermute(carry, 'depth', [(turn + 1, turn)])]
  transfers between devices with their start and end apart: 11 -> 11, of which waited for: 7 -> 6; matrix products, arithmetic and copies ran while one was open for 9% -> 9% of each run, Pallas kernels for 3% -> 9%
where the time goes in v15:
time: 61.4 us; the launch traced here: 61 us
  waiting for transfers between devices  28.3 us (46%)
  Pallas kernels  11.9 us (19%)
  starting transfers between devices  9.38 us (15%)
  other arithmetic  4.13 us (7%)
  between operations  3.96 us (6%)
  local copies, waits for them, and re-layouts  3.3 us (5%)
    ppermute x1, waiting for transfers between devices, local(): carry = lax.ppermute(carry, 'depth', [(turn + 1, turn)])  13.3 us
    ppermute x1, waiting for transfers between devices, local(): lax.ppermute(spill_sum, 'tile', [(t, t + 1) for t in range(tile_count - 1)])  5.75 us
    ppermute x1, waiting for transfers between devices, from_behind(): return lax.ppermute(block, axis, route)  4.7 us
    ppermute x1, starting transfers between devices, local(): lax.ppermute(spill_sum, 'tile', [(t, t + 1) for t in range(tile_count - 1)])  3.65 us
    pallas_call x1, Pallas kernels, run_first(): pl.pallas_call(first_kernel, grid_spec=grid_spec, out_shape=jax.ShapeDtyp...  3.58 us
    pallas_call x1, Pallas kernels, run_adjoint(): pl.pallas_call(adjoint_kernel(last, number == 1), grid_spec=grid_spec, ou...  3.08 us
    pallas_call x1, Pallas kernels, cut_patches(): pl.pallas_call(cut_kernel, grid_spec=grid_spec, out_shape=jax.ShapeDtypeS...  2.87 us
    pallas_call x1, Pallas kernels, cut_tile(): pl.pallas_call(tile_cut_kernel, grid_spec=grid_spec, out_shape=jax.ShapeD...  2.41 us
  transfers between devices with their start and end apart: 11, of which 6 were waited for; matrix products, arithmetic and copies ran while one was open for 9% of the time, Pallas kernels for 9%

profile of v15, /device:TPU:0, one launch (start us, length us, event | category | flops | bytes accessed | tf_op | source)
XLA Modules:
  0.0 61.0 jit_solution(15341965662063769509)
XLA Ops:
  0.0 0.5 collective-permute-start.1
  0.5 1.1 %dynamic-slice_convert_fusion = bf16[1,2,256,256]{3,2,1,0:T(8,128)(2,1)S(1)} fusion(f32[1,2,256,512]{3,2,1,0:T(8,128)} %tile_ref.3, s32[]{:T(128)S(6)} %select_n.84), kind=kLoop, calls=%fused_computation.4 | loop fusion | bytes 524292 | tf_op jit(solution)/shard_map/convert_element_type | solution.py:533
  1.6 1.3 %collective-permute-start.2 = (bf16[1,2,256,256]{3,2,1,0:T(8,128)(2,1)S(1)}, bf16[1,2,256,256]{3,2,1,0:T(8,128)(2,1)S(1)}, u32[]{:S(2)}, u32[]{:S(2)}) collective-permute-start(bf16[1,2,256,256]{3,2,1,0:T(8,128)(2,1)S(1)} %dynamic-slice_convert_fusion), channel_id=1, source_target_pairs={{4,0},{8,4},{12,8},{5,1},{9,5},{13,9},{6,2},{10,6},{14,10},{7,3},{... | collective-permute-start | bytes 786440 | tf_op jit(solution)/shard_map/ppermute | solution.py:18
  2.9 1.1 %multiply_convert_fusion = (bf16[256,256]{1,0:T(8,128)(2,1)S(1)}, bf16[256,256]{1,0:T(8,128)(2,1)S(1)}) fusion(), kind=kLoop, calls=%fused_computation.13 | loop fusion | flops 1245184 | bytes 262144 | tf_op jit(solution)/shard_map/convert_element_type | solution.py:51
  4.0 1.0 %fusion.6 = (f32[1,256,256]{2,1,0:T(8,128)S(1)}, f32[1,256,256]{2,1,0:T(8,128)S(1)}) fusion(s32[256]{0:T(256)S(1)} %fusion.9, f32[]{:T(128)S(6)} %neg.8), kind=kLoop, calls=%fused_computation.19 | loop fusion | flops 196608 | bytes 525316 | tf_op jit(solution)/shard_map/cos | solution.py:61
  5.8 0.6 %broadcast_select_fusion = s32[2]{0:T(128)S(1)} fusion(pred[]{:T(512)} %eq.23, s32[1]{0:T(128)} %collective-permute-done.1, s32[1]{0:T(128)S(6)} %copy.14), kind=kLoop, calls=%fused_computation.30 | loop fusion | flops 6 | bytes 17 | tf_op jit(solution)/shard_map/jit(_where)/select_n | solution.py:546
  6.4 0.7 %fusion.12 = (s32[1]{0:T(128)}, s32[1]{0:T(128)}) fusion(s32[2]{0:T(128)S(1)} %broadcast_select_fusion), kind=kLoop, calls=%fused_computation.32 | loop fusion | bytes 16 | tf_op jit(solution)/shard_map/slice | solution.py:550
  8.3 4.7 %collective-permute-done.2.mine_ref = bf16[1,2,256,256]{3,2,1,0:T(8,128)(2,1)S(1)} collective-permute-done((bf16[1,2,256,256]{3,2,1,0:T(8,128)(2,1)S(1)}, bf16[1,2,256,256]{3,2,1,0:T(8,128)(2,1)S(1)}, u32[]{:S(2)}, u32[]{:S(2)}) %collective-permute-start.2) | collective-permute-done | bytes 262176 | tf_op jit(solution)/shard_map/ppermute | solution.py:18
  13.0 0.7 %fusion.13 = (s32[1,1]{1,0:T(1,128)}, s32[1,1]{1,0:T(1,128)}) fusion(s32[1,2]{1,0:T(1,128)S(1)} %constant_dynamic-slice_fusion), kind=kLoop, calls=%fused_computation.33 | loop fusion | bytes 16 | tf_op jit(solution)/shard_map/slice | solution.py:557
  14.4 2.4 %shard_map.60 = f32[1,2,256,256]{3,2,1,0:T(8,128)S(1)} custom-call(s32[1]{0:T(128)} %sub.17.rows_ref, s32[1]{0:T(128)} %bitcast.4.columns_ref, f32[1,2,256,512]{3,2,1,0:T(8,128)} %tile_ref.3), custom_call_target="tpu_custom_call" | custom-call | tf_op jit(solution)/shard_map/pallas_call | solution.py:459
  16.8 3.6 %conditional.3 = (bf16[1,2,256,256]{3,2,1,0:T(8,128)(2,1)}) conditional(s32[]{:T(128)} %convert_element_type.71, () %tuple.55, (s32[1]{0:T(128)}, s32[1]{0:T(128)}, s32[1]{0:T(128)}, bf16[1,2,256,256]{3,2,1,0:T(8,128)(2,1)S(1)}, f32[1,2,256,256]{3,2,1,0:T(8,128)S(1)}, /*index=5*/bf16[1,2,256,256]{3,2,1,0:T(8,128)(2,1)S(1)}, ...), branch_computations={%region_0.1_spmd, %region_1.2_spmd} | conditional | bytes 262154 | solution.py:589
  16.8 3.6 %branch_1_fun.5 = bf16[1,2,256,256]{3,2,1,0:T(8,128)(2,1)} custom-call(s32[1]{0:T(128)} %get-tuple-element.119.rows_ref, s32[1]{0:T(128)} %get-tuple-element.120.columns_ref, s32[1]{0:T(128)} %get-tuple-element.121.order_ref, bf16[1,2,256,256]{3,2,1,0:T(8,128)(2,1)S(1)} %get-tuple-element.122.wave_ref, f32[1,2,256,256]{3,2,1,0:T(8,128)S(1)} %get-tuple-element.123.top_ref, ...), custom_call_target="tpu_custom_call" | custom-call | tf_op jit(solution)/shard_map/cond/branch_1_fun/pallas_call | solution.py:514
  20.4 0.5 collective-permute-start.5
  20.9 2.0 %collective-permute-start.4 = (bf16[1,2,256,256]{3,2,1,0:T(8,128)(2,1)}, bf16[1,2,256,256]{3,2,1,0:T(8,128)(2,1)}, u32[]{:S(2)}, u32[]{:S(2)}) collective-permute-start(bf16[1,2,256,256]{3,2,1,0:T(8,128)(2,1)} %get-tuple-element.186), channel_id=1, source_target_pairs={{0,2},{1,3},{4,6},{5,7},{8,10},{9,11},{12,14},{13,15},{16,18},{17,... | collective-permute-start | bytes 786440 | tf_op jit(solution)/shard_map/ppermute | solution.py:606
  24.2 2.9 %shard_map.61 = f32[1,2,256,256]{3,2,1,0:T(8,128)S(1)} custom-call(s32[1]{0:T(128)} %sub.17.rows_ref, s32[1]{0:T(128)} %bitcast.4.columns_ref, s32[1]{0:T(128)} %bitcast.order_ref, f32[1,2,256,512]{3,2,1,0:T(8,128)} %tile_ref.3, bf16[1,2,256,256]{3,2,1,0:T(8,128)(2,1)S(1)} %collective-permute-done.2.mine_ref, ...), custom_call_target="tpu_custom_call" | custom-call | tf_op jit(solution)/shard_map/pallas_call | solution.py:275
  27.0 1.5 %collective-permute-done.4 = bf16[1,2,256,256]{3,2,1,0:T(8,128)(2,1)} collective-permute-done((bf16[1,2,256,256]{3,2,1,0:T(8,128)(2,1)}, bf16[1,2,256,256]{3,2,1,0:T(8,128)(2,1)}, u32[]{:S(2)}, u32[]{:S(2)}) %collective-permute-start.4) | collective-permute-done | bytes 262176 | tf_op jit(solution)/shard_map/ppermute | solution.py:606
  28.5 0.8 %conditional.4 = ((bf16[1,2,256,256]{3,2,1,0:T(8,128)(2,1)}, bf16[2,512,512]{2,1,0:T(8,128)(2,1)S(1)})) conditional(s32[]{:T(128)} %convert_element_type.72, () %tuple.54, (s32[1]{0:T(128)}, s32[1]{0:T(128)}, s32[1]{0:T(128)}, s32[1]{0:T(128)}, s32[1]{0:T(128)}, /*index=5*/bf16[1,2,256,256]{3,2,1,0:T(8,128)(2,1)}, f32[1,2,256,256]{3,2,1,0:T(8,128)S(1)}, ...), branch_computations={%region_2.3_spmd, %region_3.4_spmd} | conditional | bytes 1310748 | solution.py:607
  28.5 0.7 %broadcast.197 = bf16[1,2,256,256]{3,2,1,0:T(8,128)(2,1)} broadcast(bf16[]{:T(256)} %constant.84.clone), dimensions={} | broadcast | bytes 262146 | tf_op jit(solution)/shard_map/broadcast.11
  29.2 0.1 broadcast.198
  29.3 1.3 %collective-permute-start.6 = (bf16[1,2,256,256]{3,2,1,0:T(8,128)(2,1)}, bf16[1,2,256,256]{3,2,1,0:T(8,128)(2,1)S(1)}, u32[]{:S(2)}, u32[]{:S(2)}) collective-permute-start(bf16[1,2,256,256]{3,2,1,0:T(8,128)(2,1)} %get-tuple-element.160), channel_id=1, source_target_pairs={{2,0},{3,1},{6,4},{7,5},{10,8},{11,9},{14,12},{15,13},{18,16},{19,... | collective-permute-start | bytes 786440 | tf_op jit(solution)/shard_map/ppermute | solution.py:618
  30.6 13.3 %collective-permute-done.6 = bf16[1,2,256,256]{3,2,1,0:T(8,128)(2,1)S(1)} collective-permute-done((bf16[1,2,256,256]{3,2,1,0:T(8,128)(2,1)}, bf16[1,2,256,256]{3,2,1,0:T(8,128)(2,1)S(1)}, u32[]{:S(2)}, u32[]{:S(2)}) %collective-permute-start.6) | collective-permute-done | bytes 262176 | tf_op jit(solution)/shard_map/ppermute | solution.py:618
  43.9 3.1 %conditional.5 = (bf16[2,512,512]{2,1,0:T(8,128)(2,1)S(1)}) conditional(s32[]{:T(128)} %convert_element_type.71, bf16[2,512,512]{2,1,0:T(8,128)(2,1)S(1)} %get-tuple-element.159, (s32[1]{0:T(128)}, s32[1]{0:T(128)}, s32[1]{0:T(128)}, s32[1]{0:T(128)}, s32[1]{0:T(128)}, /*index=5*/bf16[1,2,256,256]{3,2,1,0:T(8,128)(2,1)S(1)}, ...), branch_computations={%region_4.5_spmd, %region_5.6_spmd} | conditional | bytes 8 | solution.py:619
  43.9 3.1 %branch_1_fun.7 = (bf16[1,2,256,256]{3,2,1,0:T(8,128)(2,1)}, bf16[2,512,512]{2,1,0:T(8,128)(2,1)S(1)}) custom-call(s32[1]{0:T(128)} %get-tuple-element.141.rows_ref, s32[1]{0:T(128)} %get-tuple-element.142.columns_ref, s32[1]{0:T(128)} %get-tuple-element.143.live_ref, s32[1]{0:T(128)} %get-tuple-element.144.slot_ref, s32[1]{0:T(128)} %get-tuple-element.145.other_ref, ...), custom_call_target="tpu_custom_call" | custom-call | tf_op jit(solution)/shard_map/cond/branch_1_fun/pallas_call | solution.py:429
  47.0 0.1 fusion.11
  47.1 0.1 collective-permute-start.8
  47.2 1.5 %collective-permute-done.8 = bf16[2,256,256]{2,1,0:T(8,128)(2,1)S(1)} collective-permute-done((bf16[2,256,256]{2,1,0:T(8,128)(2,1)S(1)}, bf16[2,256,256]{2,1,0:T(8,128)(2,1)S(1)}, u32[]{:S(2)}, u32[]{:S(2)}) %collective-permute-start.8) | collective-permute-done | bytes 262176 | tf_op jit(solution)/shard_map/ppermute | solution.py:625
  48.7 0.1 add_convert_fusion
  48.8 3.7 %collective-permute-start.9 = (bf16[2,256,256]{2,1,0:T(8,128)(2,1)S(1)}, bf16[2,256,256]{2,1,0:T(8,128)(2,1)S(1)}, u32[]{:S(2)}, u32[]{:S(2)}) collective-permute-start(bf16[2,256,256]{2,1,0:T(8,128)(2,1)S(1)} %add_convert_fusion), channel_id=1, source_target_pairs={{0,4},{4,8},{8,12},{1,5},{5,9},{9,13},{2,6},{6,10},{10,14},{3,7},{... | collective-permute-start | bytes 786440 | tf_op jit(solution)/shard_map/ppermute | solution.py:627
  52.4 0.1 collective-permute-start.7
  52.5 5.8 %collective-permute-done.9 = bf16[2,256,256]{2,1,0:T(8,128)(2,1)S(1)} collective-permute-done((bf16[2,256,256]{2,1,0:T(8,128)(2,1)S(1)}, bf16[2,256,256]{2,1,0:T(8,128)(2,1)S(1)}, u32[]{:S(2)}, u32[]{:S(2)}) %collective-permute-start.9) | collective-permute-done | bytes 262176 | tf_op jit(solution)/shard_map/ppermute | solution.py:627
  58.3 1.5 %collective-permute-done.10 = bf16[2,256,256]{2,1,0:T(8,128)(2,1)S(1)} collective-permute-done((bf16[2,256,256]{2,1,0:T(8,128)(2,1)S(1)}, bf16[2,256,256]{2,1,0:T(8,128)(2,1)S(1)}, u32[]{:S(2)}, u32[]{:S(2)}) %collective-permute-start.10) | collective-permute-done | bytes 262176 | tf_op jit(solution)/shard_map/ppermute | solution.py:630
  59.8 1.2 %add_bitcast_fusion = f32[1,2,256,512]{3,2,1,0:T(8,128)} fusion(bf16[2,256,512]{2,1,0:T(8,128)(2,1)S(1)} %collective-permute-done.7, bf16[2,256,256]{2,1,0:T(8,128)(2,1)S(1)} %collective-permute-done.10, bf16[2,256,256]{2,1,0:T(8,128)(2,1)S(1)} %collective-permute-done.9, pred[]{:T(512)} %eq.23, bf16[2,512,512]{2,1,0:T(8,128)(2,1)S(1)} %get-tuple-element.188), kind=kLoop, calls=%fused_computation | loop fusion | flops 3670016 | bytes 2621441 | tf_op jit(solution)/shard_map/broadcast_in_dim | solution.py:638
  (21 shorter events, 0.2 us)
Async XLA Ops:
  0.0 5.8 %collective-permute-start.1 = (s32[1]{0:T(128)}, s32[1]{0:T(128)}, u32[]{:S(2)}, u32[]{:S(2)}) collective-permute-start(s32[1]{0:T(128)} %param.18), channel_id=1, source_target_pairs={{0,1},{1,0},{2,3},{3,2},{4,5},{5,4},{6,7},{7,6},{8,9},{9,8},{10,11... | collective-permute-start | bytes 20 | tf_op jit(solution)/shard_map/ppermute | solution.py:540
  0.5 12.5 %collective-permute-start = (s32[2,2]{1,0:T(2,128)}, s32[2,2]{1,0:T(2,128)S(1)}, u32[]{:S(2)}, u32[]{:S(2)}) collective-permute-start(s32[2,2]{1,0:T(2,128)} %param.17), channel_id=1, source_target_pairs={{0,1},{1,0},{2,3},{3,2},{4,5},{5,4},{6,7},{7,6},{8,9},{9,8},{10,11... | collective-permute-start | bytes 56 | tf_op jit(solution)/shard_map/ppermute | solution.py:539
  1.6 11.4 %collective-permute-start.2 = (bf16[1,2,256,256]{3,2,1,0:T(8,128)(2,1)S(1)}, bf16[1,2,256,256]{3,2,1,0:T(8,128)(2,1)S(1)}, u32[]{:S(2)}, u32[]{:S(2)}) collective-permute-start(bf16[1,2,256,256]{3,2,1,0:T(8,128)(2,1)S(1)} %dynamic-slice_convert_fusion), channel_id=1, source_target_pairs={{4,0},{8,4},{12,8},{5,1},{9,5},{13,9},{6,2},{10,6},{14,10},{7,3},{... | collective-permute-start | bytes 786440 | tf_op jit(solution)/shard_map/ppermute | solution.py:18
  8.3 4.7 %copy-start.2 = (s32[2,2]{1,0:T(2,128)S(1)}, s32[2,2]{1,0:T(2,128)}, u32[]{:S(2)}) copy-start(s32[2,2]{1,0:T(2,128)} %param.17) | copy-start | bytes 52
  13.0 3.8 %collective-permute-start.3 = (bf16[1,2,256,256]{3,2,1,0:T(8,128)(2,1)S(1)}, bf16[1,2,256,256]{3,2,1,0:T(8,128)(2,1)S(1)}, u32[]{:S(2)}, u32[]{:S(2)}) collective-permute-start(bf16[1,2,256,256]{3,2,1,0:T(8,128)(2,1)S(1)} %collective-permute-done.2.mine_ref), channel_id=1, source_target_pairs={{0,1},{1,0},{2,3},{3,2},{4,5},{5,4},{6,7},{7,6},{8,9},{9,8},{10,11... | collective-permute-start | bytes 786440 | tf_op jit(solution)/shard_map/ppermute | solution.py:535
  14.3 2.4 %copy-start = (bf16[2,256,256]{2,1,0:T(8,128)(2,1)S(1)}, bf16[2,256,256]{2,1,0:T(8,128)(2,1)}, u32[]{:S(2)}) copy-start(bf16[2,256,256]{2,1,0:T(8,128)(2,1)} %param.16) | copy-start | bytes 786436
  16.8 3.6 %copy-start.1 = (f32[2,256,256]{2,1,0:T(8,128)S(1)}, f32[2,256,256]{2,1,0:T(8,128)}, u32[]{:S(2)}) copy-start(f32[2,256,256]{2,1,0:T(8,128)} %param.19) | copy-start | bytes 1572868
  20.4 8.1 %collective-permute-start.5 = (f32[2,256,256]{2,1,0:T(8,128)S(1)}, f32[2,256,256]{2,1,0:T(8,128)}, u32[]{:S(2)}, u32[]{:S(2)}) collective-permute-start(f32[2,256,256]{2,1,0:T(8,128)S(1)} %copy-done.1), channel_id=1, source_target_pairs={{0,1},{1,0},{2,3},{3,2},{4,5},{5,4},{6,7},{7,6},{8,9},{9,8},{10,11... | collective-permute-start | bytes 1572872 | tf_op jit(solution)/shard_map/ppermute | solution.py:592
  20.9 7.6 %collective-permute-start.4 = (bf16[1,2,256,256]{3,2,1,0:T(8,128)(2,1)}, bf16[1,2,256,256]{3,2,1,0:T(8,128)(2,1)}, u32[]{:S(2)}, u32[]{:S(2)}) collective-permute-start(bf16[1,2,256,256]{3,2,1,0:T(8,128)(2,1)} %get-tuple-element.186), channel_id=1, source_target_pairs={{0,2},{1,3},{4,6},{5,7},{8,10},{9,11},{12,14},{13,15},{16,18},{17,... | collective-permute-start | bytes 786440 | tf_op jit(solution)/shard_map/ppermute | solution.py:606
  29.3 14.6 %collective-permute-start.6 = (bf16[1,2,256,256]{3,2,1,0:T(8,128)(2,1)}, bf16[1,2,256,256]{3,2,1,0:T(8,128)(2,1)S(1)}, u32[]{:S(2)}, u32[]{:S(2)}) collective-permute-start(bf16[1,2,256,256]{3,2,1,0:T(8,128)(2,1)} %get-tuple-element.160), channel_id=1, source_target_pairs={{2,0},{3,1},{6,4},{7,5},{10,8},{11,9},{14,12},{15,13},{18,16},{19,... | collective-permute-start | bytes 786440 | tf_op jit(solution)/shard_map/ppermute | solution.py:618
  47.1 1.6 %collective-permute-start.8 = (bf16[2,256,256]{2,1,0:T(8,128)(2,1)S(1)}, bf16[2,256,256]{2,1,0:T(8,128)(2,1)S(1)}, u32[]{:S(2)}, u32[]{:S(2)}) collective-permute-start(bf16[2,256,256]{2,1,0:T(8,128)(2,1)S(1)} %constant_dynamic-slice_fusion.1), channel_id=1, source_target_pairs={{0,1},{1,0},{2,3},{3,2},{4,5},{5,4},{6,7},{7,6},{8,9},{9,8},{10,11... | collective-permute-start | bytes 786440 | tf_op jit(solution)/shard_map/ppermute | solution.py:625
  48.8 9.5 %collective-permute-start.9 = (bf16[2,256,256]{2,1,0:T(8,128)(2,1)S(1)}, bf16[2,256,256]{2,1,0:T(8,128)(2,1)S(1)}, u32[]{:S(2)}, u32[]{:S(2)}) collective-permute-start(bf16[2,256,256]{2,1,0:T(8,128)(2,1)S(1)} %add_convert_fusion), channel_id=1, source_target_pairs={{0,4},{4,8},{8,12},{1,5},{5,9},{9,13},{2,6},{6,10},{10,14},{3,7},{... | collective-permute-start | bytes 786440 | tf_op jit(solution)/shard_map/ppermute | solution.py:627
  52.4 5.8 %collective-permute-start.7 = (bf16[2,256,512]{2,1,0:T(8,128)(2,1)S(1)}, bf16[2,256,512]{2,1,0:T(8,128)(2,1)S(1)}, u32[]{:S(2)}, u32[]{:S(2)}) collective-permute-start(bf16[2,256,512]{2,1,0:T(8,128)(2,1)S(1)} %get-tuple-element.173), channel_id=1, source_target_pairs={{0,1},{1,0},{2,3},{3,2},{4,5},{5,4},{6,7},{7,6},{8,9},{9,8},{10,11... | collective-permute-start | bytes 1572872 | tf_op jit(solution)/shard_map/ppermute | solution.py:629
  58.3 1.5 %collective-permute-start.10 = (bf16[2,256,256]{2,1,0:T(8,128)(2,1)S(1)}, bf16[2,256,256]{2,1,0:T(8,128)(2,1)S(1)}, u32[]{:S(2)}, u32[]{:S(2)}) collective-permute-start(bf16[2,256,256]{2,1,0:T(8,128)(2,1)S(1)} %collective-permute-done.9), channel_id=1, source_target_pairs={{0,1},{1,0},{2,3},{3,2},{4,5},{5,4},{6,7},{7,6},{8,9},{9,8},{10,11... | collective-permute-start | bytes 786440 | tf_op jit(solution)/shard_map/ppermute | solution.py:630

commit v16 on v14

--- a/solution.py
+++ b/solution.py
@@ -557,7 +557,7 @@
         if turn > 0:
             carry = lax.ppermute(carry, "depth", [(turn - 1, turn)])
             inputs = jnp.where(segment == turn, carry, inputs)
-        carry = lax.cond(segment == turn, forward_all, silent, carry)
+        carry = forward_all(carry)
 
     measured, carry = lax.optimization_barrier((measured, carry))
     both_measured = lax.ppermute(measured, "batch", pairs)
@@ -575,7 +575,7 @@
 
     if depth_count > 1:
         carry = lax.ppermute(carry, "depth", [(depth_count - 2, depth_count - 1)])
-    carry, gradient = lax.cond(segment == depth_count - 1, last_pass, last_silent, carry)
+    carry, gradient = last_pass(carry)
 
     def back_pass(incoming, previous):
         return run_adjoint(

time: 59.4 us -> 63.9 us (1.076)
  Pallas kernels: 8.71 us -> 16.8 us
  waiting for transfers between devices: 30.4 us -> 24.5 us
  starting transfers between devices: 9.25 us -> 10.5 us
  local copies, waits for them, and re-layouts: 2.6 us -> 3.78 us
    ppermute x1, waiting for transfers between devices: 14 us -> 8.51 us  [local(): carry = lax.ppermute(carry, 'depth', [(turn + 1, turn)])]
    pallas_call x1 -> x2, Pallas kernels: 3.08 us -> 8.5 us  [run_adjoint(): pl.pallas_call(adjoint_kernel(last, number == 1), grid_spec=grid_spec, ou...]
    ppermute x1, starting transfers between devices: 1.98 us -> 3.56 us  [local(): carry = lax.ppermute(carry, 'depth', [(depth_count - 2, depth_count - 1)])]
    unnamed x6 -> x12, local copies, waits for them, and re-layouts: 0.02 us -> 1.41 us
    pallas_call x1, Pallas kernels: 3.98 us -> 5.32 us  [run_first(): pl.pallas_call(first_kernel, grid_spec=grid_spec, out_shape=jax.ShapeDtyp...]
    pallas_call x1, Pallas kernels: 1.65 us -> 2.94 us  [cut_patches(): pl.pallas_call(cut_kernel, grid_spec=grid_spec, out_shape=jax.ShapeDtypeS...]
  transfers between devices with their start and end apart: 11 -> 11, of which waited for: 7 -> 7; matrix products, arithmetic and copies ran while one was open for 9% -> 8% of each run, Pallas kernels for 3% -> 5%
where the time goes in v16:
time: 63.9 us; the launch traced here: 63.5 us
  waiting for transfers between devices  24.5 us (38%)
  Pallas kernels  16.8 us (26%)
  starting transfers between devices  10.5 us (16%)
  other arithmetic  4.13 us (6%)
  between operations  3.88 us (6%)
  local copies, waits for them, and re-layouts  3.78 us (6%)
    ppermute x1, waiting for transfers between devices, local(): carry = lax.ppermute(carry, 'depth', [(turn + 1, turn)])  8.51 us
    pallas_call x2, Pallas kernels, run_adjoint(): pl.pallas_call(adjoint_kernel(last, number == 1), grid_spec=grid_spec, ou...  8.5 us
    ppermute x1, waiting for transfers between devices, local(): lax.ppermute(spill_sum, 'tile', [(t, t + 1) for t in range(tile_count - 1)])  5.75 us
    pallas_call x1, Pallas kernels, run_first(): pl.pallas_call(first_kernel, grid_spec=grid_spec, out_shape=jax.ShapeDtyp...  5.32 us
    ppermute x1, waiting for transfers between devices, from_behind(): return lax.ppermute(block, axis, route)  4.66 us
    ppermute x1, starting transfers between devices, local(): carry = lax.ppermute(carry, 'depth', [(depth_count - 2, depth_count - 1)])  3.56 us
    ppermute x1, starting transfers between devices, local(): lax.ppermute(spill_sum, 'tile', [(t, t + 1) for t in range(tile_count - 1)])  3.5 us
    pallas_call x1, Pallas kernels, cut_patches(): pl.pallas_call(cut_kernel, grid_spec=grid_spec, out_shape=jax.ShapeDtypeS...  2.94 us
  transfers between devices with their start and end apart: 11, of which 7 were waited for; matrix products, arithmetic and copies ran while one was open for 8% of the time, Pallas kernels for 5%

profile of v16, /device:TPU:0, one launch (start us, length us, event | category | flops | bytes accessed | tf_op | source)
XLA Modules:
  0.0 63.5 jit_solution(10967653595057172769)
XLA Ops:
  0.0 0.5 collective-permute-start.1
  0.5 0.1 collective-permute-start
  0.5 1.1 %dynamic-slice_convert_fusion = bf16[1,2,256,256]{3,2,1,0:T(8,128)(2,1)S(1)} fusion(f32[1,2,256,512]{3,2,1,0:T(8,128)} %tile_ref.3, s32[]{:T(128)S(6)} %select_n.84), kind=kLoop, calls=%fused_computation.4 | loop fusion | bytes 524292 | tf_op jit(solution)/shard_map/convert_element_type | solution.py:505
  1.6 1.3 %collective-permute-start.2 = (bf16[1,2,256,256]{3,2,1,0:T(8,128)(2,1)S(1)}, bf16[1,2,256,256]{3,2,1,0:T(8,128)(2,1)S(1)}, u32[]{:S(2)}, u32[]{:S(2)}) collective-permute-start(bf16[1,2,256,256]{3,2,1,0:T(8,128)(2,1)S(1)} %dynamic-slice_convert_fusion), channel_id=1, source_target_pairs={{4,0},{8,4},{12,8},{5,1},{9,5},{13,9},{6,2},{10,6},{14,10},{7,3},{... | collective-permute-start | bytes 786440 | tf_op jit(solution)/shard_map/ppermute | solution.py:18
  2.9 1.1 %multiply_convert_fusion = (bf16[256,256]{1,0:T(8,128)(2,1)S(1)}, bf16[256,256]{1,0:T(8,128)(2,1)S(1)}) fusion(), kind=kLoop, calls=%fused_computation.13 | loop fusion | flops 1245184 | bytes 262144 | tf_op jit(solution)/shard_map/convert_element_type | solution.py:51
  4.0 1.0 %fusion.6 = (f32[1,256,256]{2,1,0:T(8,128)S(1)}, f32[1,256,256]{2,1,0:T(8,128)S(1)}) fusion(s32[256]{0:T(256)S(1)} %fusion.9, f32[]{:T(128)S(6)} %neg.8), kind=kLoop, calls=%fused_computation.19 | loop fusion | flops 196608 | bytes 525316 | tf_op jit(solution)/shard_map/cos | solution.py:61
  5.8 0.6 %broadcast_select_fusion = s32[2]{0:T(128)S(1)} fusion(pred[]{:T(512)} %eq.20, s32[1]{0:T(128)} %collective-permute-done.1, s32[1]{0:T(128)S(6)} %copy.8), kind=kLoop, calls=%fused_computation.30 | loop fusion | flops 6 | bytes 17 | tf_op jit(solution)/shard_map/jit(_where)/select_n | solution.py:518
  6.5 0.6 fusion.12
  8.3 4.7 %collective-permute-done.2.mine_ref = bf16[1,2,256,256]{3,2,1,0:T(8,128)(2,1)S(1)} collective-permute-done((bf16[1,2,256,256]{3,2,1,0:T(8,128)(2,1)S(1)}, bf16[1,2,256,256]{3,2,1,0:T(8,128)(2,1)S(1)}, u32[]{:S(2)}, u32[]{:S(2)}) %collective-permute-start.2) | collective-permute-done | bytes 262176 | tf_op jit(solution)/shard_map/ppermute | solution.py:18
  13.0 0.6 fusion.13
  14.2 0.3 collective-permute-done.3.partner_ref
  14.5 0.7 %copy-done.1 = bf16[1,2,256,256]{3,2,1,0:T(8,128)(2,1)} copy-done((bf16[1,2,256,256]{3,2,1,0:T(8,128)(2,1)}, bf16[1,2,256,256]{3,2,1,0:T(8,128)(2,1)S(1)}, u32[]{:S(2)}) %copy-start.1) | copy-done | bytes 262168
  15.2 5.3 %shard_map.60 = bf16[1,2,256,256]{3,2,1,0:T(8,128)(2,1)} custom-call(s32[1]{0:T(128)} %sub.17.rows_ref, s32[1]{0:T(128)} %bitcast.4.columns_ref, s32[1]{0:T(128)} %bitcast.order_ref, bf16[1,2,256,256]{3,2,1,0:T(8,128)(2,1)S(1)} %bitcast.9, f32[1,2,256,512]{3,2,1,0:T(8,128)} %tile_ref.3, bf16[1,2,256,256]{3,2,1,0:T(8,128)(2,1)} %copy-done, ...), custom_call_target="tpu_custom_call" | custom-call | tf_op jit(solution)/shard_map/pallas_call | solution.py:486
  20.5 0.2 collective-permute-start.5
  20.8 3.6 %collective-permute-start.4 = (bf16[1,2,256,256]{3,2,1,0:T(8,128)(2,1)}, bf16[1,2,256,256]{3,2,1,0:T(8,128)(2,1)S(1)}, u32[]{:S(2)}, u32[]{:S(2)}) collective-permute-start(bf16[1,2,256,256]{3,2,1,0:T(8,128)(2,1)} %shard_map.60), channel_id=1, source_target_pairs={{0,2},{1,3},{4,6},{5,7},{8,10},{9,11},{12,14},{13,15},{16,18},{17,... | collective-permute-start | bytes 786440 | tf_op jit(solution)/shard_map/ppermute | solution.py:577
  25.5 2.9 %shard_map.61.refs_1_ = f32[1,2,256,256]{3,2,1,0:T(8,128)S(1)} custom-call(s32[1]{0:T(128)} %sub.17.rows_ref, s32[1]{0:T(128)} %bitcast.4.columns_ref, s32[1]{0:T(128)} %bitcast.order_ref, f32[1,2,256,512]{3,2,1,0:T(8,128)} %tile_ref.3, bf16[1,2,256,256]{3,2,1,0:T(8,128)(2,1)} %copy-done, bf16[1,2,256,256]{3,2,1,0:T(8,128)(2,1)} %copy-done.1), custom_call_target="tpu_custom_call" | custom-call | tf_op jit(solution)/shard_map/pallas_call | solution.py:275
  28.4 2.2 %collective-permute-done.4.refs_0_ = bf16[1,2,256,256]{3,2,1,0:T(8,128)(2,1)S(1)} collective-permute-done((bf16[1,2,256,256]{3,2,1,0:T(8,128)(2,1)}, bf16[1,2,256,256]{3,2,1,0:T(8,128)(2,1)S(1)}, u32[]{:S(2)}, u32[]{:S(2)}) %collective-permute-start.4) | collective-permute-done | bytes 262176 | tf_op jit(solution)/shard_map/ppermute | solution.py:577
  30.6 0.7 %copy-done.4 = bf16[1,2,256,256]{3,2,1,0:T(8,128)(2,1)} copy-done((bf16[1,2,256,256]{3,2,1,0:T(8,128)(2,1)}, bf16[1,2,256,256]{3,2,1,0:T(8,128)(2,1)S(1)}, u32[]{:S(2)}) %copy-start.4) | copy-done | bytes 262168
  31.3 5.5 %shard_map.62 = (bf16[1,2,256,256]{3,2,1,0:T(8,128)(2,1)}, bf16[2,512,512]{2,1,0:T(8,128)(2,1)S(1)}) custom-call(s32[1]{0:T(128)} %sub.17.rows_ref, s32[1]{0:T(128)} %bitcast.4.columns_ref, s32[1]{0:T(128)} %convert_element_type.68.live_ref, s32[1]{0:T(128)} %min.6.slot_ref, s32[1]{0:T(128)} %convert_element_type.69.other_ref, ...), custom_call_target="tpu_custom_call" | custom-call | tf_op jit(solution)/shard_map/pallas_call | solution.py:429
  36.8 1.3 %collective-permute-start.6 = (bf16[1,2,256,256]{3,2,1,0:T(8,128)(2,1)}, bf16[1,2,256,256]{3,2,1,0:T(8,128)(2,1)S(1)}, u32[]{:S(2)}, u32[]{:S(2)}) collective-permute-start(bf16[1,2,256,256]{3,2,1,0:T(8,128)(2,1)} %get-tuple-element.88), channel_id=1, source_target_pairs={{2,0},{3,1},{6,4},{7,5},{10,8},{11,9},{14,12},{15,13},{18,16},{19,... | collective-permute-start | bytes 786440 | tf_op jit(solution)/shard_map/ppermute | solution.py:589
  38.1 8.5 %collective-permute-done.6 = bf16[1,2,256,256]{3,2,1,0:T(8,128)(2,1)S(1)} collective-permute-done((bf16[1,2,256,256]{3,2,1,0:T(8,128)(2,1)}, bf16[1,2,256,256]{3,2,1,0:T(8,128)(2,1)S(1)}, u32[]{:S(2)}, u32[]{:S(2)}) %collective-permute-start.6) | collective-permute-done | bytes 262176 | tf_op jit(solution)/shard_map/ppermute | solution.py:589
  46.6 3.0 %conditional.1 = (bf16[2,512,512]{2,1,0:T(8,128)(2,1)S(1)}) conditional(s32[]{:T(128)} %convert_element_type.67, bf16[2,512,512]{2,1,0:T(8,128)(2,1)S(1)} %get-tuple-element.87, (s32[1]{0:T(128)}, s32[1]{0:T(128)}, s32[1]{0:T(128)}, s32[1]{0:T(128)}, s32[1]{0:T(128)}, /*index=5*/bf16[1,2,256,256]{3,2,1,0:T(8,128)(2,1)S(1)}, ...), branch_computations={%region_0.1_spmd, %region_1.2_spmd} | conditional | bytes 8 | solution.py:590
  46.6 3.0 %branch_1_fun.3 = (bf16[1,2,256,256]{3,2,1,0:T(8,128)(2,1)}, bf16[2,512,512]{2,1,0:T(8,128)(2,1)S(1)}) custom-call(s32[1]{0:T(128)} %get-tuple-element.69.rows_ref, s32[1]{0:T(128)} %get-tuple-element.70.columns_ref, s32[1]{0:T(128)} %get-tuple-element.71.live_ref, s32[1]{0:T(128)} %get-tuple-element.72.slot_ref, s32[1]{0:T(128)} %get-tuple-element.73.other_ref, ...), custom_call_target="tpu_custom_call" | custom-call | tf_op jit(solution)/shard_map/cond/branch_1_fun/pallas_call | solution.py:429
  49.7 0.1 fusion.11
  49.8 0.1 collective-permute-start.8
  49.8 1.5 %collective-permute-done.8 = bf16[2,256,256]{2,1,0:T(8,128)(2,1)S(1)} collective-permute-done((bf16[2,256,256]{2,1,0:T(8,128)(2,1)S(1)}, bf16[2,256,256]{2,1,0:T(8,128)(2,1)S(1)}, u32[]{:S(2)}, u32[]{:S(2)}) %collective-permute-start.8) | collective-permute-done | bytes 262176 | tf_op jit(solution)/shard_map/ppermute | solution.py:596
  51.4 0.1 add_convert_fusion
  51.4 3.5 %collective-permute-start.9 = (bf16[2,256,256]{2,1,0:T(8,128)(2,1)S(1)}, bf16[2,256,256]{2,1,0:T(8,128)(2,1)S(1)}, u32[]{:S(2)}, u32[]{:S(2)}) collective-permute-start(bf16[2,256,256]{2,1,0:T(8,128)(2,1)S(1)} %add_convert_fusion), channel_id=1, source_target_pairs={{0,4},{4,8},{8,12},{1,5},{5,9},{9,13},{2,6},{6,10},{10,14},{3,7},{... | collective-permute-start | bytes 786440 | tf_op jit(solution)/shard_map/ppermute | solution.py:598
  55.0 0.1 collective-permute-start.7
  55.0 5.8 %collective-permute-done.9 = bf16[2,256,256]{2,1,0:T(8,128)(2,1)S(1)} collective-permute-done((bf16[2,256,256]{2,1,0:T(8,128)(2,1)S(1)}, bf16[2,256,256]{2,1,0:T(8,128)(2,1)S(1)}, u32[]{:S(2)}, u32[]{:S(2)}) %collective-permute-start.9) | collective-permute-done | bytes 262176 | tf_op jit(solution)/shard_map/ppermute | solution.py:598
  60.8 1.5 %collective-permute-done.10 = bf16[2,256,256]{2,1,0:T(8,128)(2,1)S(1)} collective-permute-done((bf16[2,256,256]{2,1,0:T(8,128)(2,1)S(1)}, bf16[2,256,256]{2,1,0:T(8,128)(2,1)S(1)}, u32[]{:S(2)}, u32[]{:S(2)}) %collective-permute-start.10) | collective-permute-done | bytes 262176 | tf_op jit(solution)/shard_map/ppermute | solution.py:601
  62.3 1.2 %add_bitcast_fusion = f32[1,2,256,512]{3,2,1,0:T(8,128)} fusion(bf16[2,256,512]{2,1,0:T(8,128)(2,1)S(1)} %collective-permute-done.7, bf16[2,256,256]{2,1,0:T(8,128)(2,1)S(1)} %collective-permute-done.10, bf16[2,256,256]{2,1,0:T(8,128)(2,1)S(1)} %collective-permute-done.9, pred[]{:T(512)} %eq.20, bf16[2,512,512]{2,1,0:T(8,128)(2,1)S(1)} %get-tuple-element.110), kind=kLoop, calls=%fused_computation | loop fusion | flops 3670016 | bytes 2621441 | tf_op jit(solution)/shard_map/broadcast_in_dim | solution.py:609
  (23 shorter events, 0.2 us)
Async XLA Ops:
  0.0 5.8 %collective-permute-start.1 = (s32[1]{0:T(128)}, s32[1]{0:T(128)}, u32[]{:S(2)}, u32[]{:S(2)}) collective-permute-start(s32[1]{0:T(128)} %param.14), channel_id=1, source_target_pairs={{0,1},{1,0},{2,3},{3,2},{4,5},{5,4},{6,7},{7,6},{8,9},{9,8},{10,11... | collective-permute-start | bytes 20 | tf_op jit(solution)/shard_map/ppermute | solution.py:512
  0.5 12.5 %collective-permute-start = (s32[2,2]{1,0:T(2,128)}, s32[2,2]{1,0:T(2,128)S(1)}, u32[]{:S(2)}, u32[]{:S(2)}) collective-permute-start(s32[2,2]{1,0:T(2,128)} %param.13), channel_id=1, source_target_pairs={{0,1},{1,0},{2,3},{3,2},{4,5},{5,4},{6,7},{7,6},{8,9},{9,8},{10,11... | collective-permute-start | bytes 56 | tf_op jit(solution)/shard_map/ppermute | solution.py:511
  1.6 11.4 %collective-permute-start.2 = (bf16[1,2,256,256]{3,2,1,0:T(8,128)(2,1)S(1)}, bf16[1,2,256,256]{3,2,1,0:T(8,128)(2,1)S(1)}, u32[]{:S(2)}, u32[]{:S(2)}) collective-permute-start(bf16[1,2,256,256]{3,2,1,0:T(8,128)(2,1)S(1)} %dynamic-slice_convert_fusion), channel_id=1, source_target_pairs={{4,0},{8,4},{12,8},{5,1},{9,5},{13,9},{6,2},{10,6},{14,10},{7,3},{... | collective-permute-start | bytes 786440 | tf_op jit(solution)/shard_map/ppermute | solution.py:18
  5.1 10.1 %copy-start.2 = (bf16[2,256,256]{2,1,0:T(8,128)(2,1)S(1)}, bf16[2,256,256]{2,1,0:T(8,128)(2,1)}, u32[]{:S(2)}) copy-start(bf16[2,256,256]{2,1,0:T(8,128)(2,1)} %param.12) | copy-start | bytes 786436
  8.3 4.7 %copy-start.5 = (s32[2,2]{1,0:T(2,128)S(1)}, s32[2,2]{1,0:T(2,128)}, u32[]{:S(2)}) copy-start(s32[2,2]{1,0:T(2,128)} %param.13) | copy-start | bytes 52
  13.0 1.5 %copy-start = (bf16[1,2,256,256]{3,2,1,0:T(8,128)(2,1)}, bf16[1,2,256,256]{3,2,1,0:T(8,128)(2,1)S(1)}, u32[]{:S(2)}) copy-start(bf16[1,2,256,256]{3,2,1,0:T(8,128)(2,1)S(1)} %collective-permute-done.2.mine_ref) | copy-start | bytes 786436
  13.0 1.5 %collective-permute-start.3 = (bf16[1,2,256,256]{3,2,1,0:T(8,128)(2,1)S(1)}, bf16[1,2,256,256]{3,2,1,0:T(8,128)(2,1)S(1)}, u32[]{:S(2)}, u32[]{:S(2)}) collective-permute-start(bf16[1,2,256,256]{3,2,1,0:T(8,128)(2,1)S(1)} %collective-permute-done.2.mine_ref), channel_id=1, source_target_pairs={{0,1},{1,0},{2,3},{3,2},{4,5},{5,4},{6,7},{7,6},{8,9},{9,8},{10,11... | collective-permute-start | bytes 786440 | tf_op jit(solution)/shard_map/ppermute | solution.py:507
  14.5 0.7 %copy-start.1 = (bf16[1,2,256,256]{3,2,1,0:T(8,128)(2,1)}, bf16[1,2,256,256]{3,2,1,0:T(8,128)(2,1)S(1)}, u32[]{:S(2)}) copy-start(bf16[1,2,256,256]{3,2,1,0:T(8,128)(2,1)S(1)} %collective-permute-done.3.partner_ref) | copy-start | bytes 786436
  15.2 5.3 %copy-start.3 = (f32[2,256,256]{2,1,0:T(8,128)S(1)}, f32[2,256,256]{2,1,0:T(8,128)}, u32[]{:S(2)}) copy-start(f32[2,256,256]{2,1,0:T(8,128)} %refs_5_) | copy-start | bytes 1572868
  20.5 10.8 %collective-permute-start.5 = (f32[2,256,256]{2,1,0:T(8,128)S(1)}, f32[2,256,256]{2,1,0:T(8,128)}, u32[]{:S(2)}, u32[]{:S(2)}) collective-permute-start(f32[2,256,256]{2,1,0:T(8,128)S(1)} %copy-done.3), channel_id=1, source_target_pairs={{0,1},{1,0},{2,3},{3,2},{4,5},{5,4},{6,7},{7,6},{8,9},{9,8},{10,11... | collective-permute-start | bytes 1572872 | tf_op jit(solution)/shard_map/ppermute | solution.py:563
  20.8 9.9 %collective-permute-start.4 = (bf16[1,2,256,256]{3,2,1,0:T(8,128)(2,1)}, bf16[1,2,256,256]{3,2,1,0:T(8,128)(2,1)S(1)}, u32[]{:S(2)}, u32[]{:S(2)}) collective-permute-start(bf16[1,2,256,256]{3,2,1,0:T(8,128)(2,1)} %shard_map.60), channel_id=1, source_target_pairs={{0,2},{1,3},{4,6},{5,7},{8,10},{9,11},{12,14},{13,15},{16,18},{17,... | collective-permute-start | bytes 786440 | tf_op jit(solution)/shard_map/ppermute | solution.py:577
  30.6 0.7 %copy-start.4 = (bf16[1,2,256,256]{3,2,1,0:T(8,128)(2,1)}, bf16[1,2,256,256]{3,2,1,0:T(8,128)(2,1)S(1)}, u32[]{:S(2)}) copy-start(bf16[1,2,256,256]{3,2,1,0:T(8,128)(2,1)S(1)} %collective-permute-done.4.refs_0_) | copy-start | bytes 786436
  36.8 9.8 %collective-permute-start.6 = (bf16[1,2,256,256]{3,2,1,0:T(8,128)(2,1)}, bf16[1,2,256,256]{3,2,1,0:T(8,128)(2,1)S(1)}, u32[]{:S(2)}, u32[]{:S(2)}) collective-permute-start(bf16[1,2,256,256]{3,2,1,0:T(8,128)(2,1)} %get-tuple-element.88), channel_id=1, source_target_pairs={{2,0},{3,1},{6,4},{7,5},{10,8},{11,9},{14,12},{15,13},{18,16},{19,... | collective-permute-start | bytes 786440 | tf_op jit(solution)/shard_map/ppermute | solution.py:589
  49.8 1.6 %collective-permute-start.8 = (bf16[2,256,256]{2,1,0:T(8,128)(2,1)S(1)}, bf16[2,256,256]{2,1,0:T(8,128)(2,1)S(1)}, u32[]{:S(2)}, u32[]{:S(2)}) collective-permute-start(bf16[2,256,256]{2,1,0:T(8,128)(2,1)S(1)} %constant_dynamic-slice_fusion.1), channel_id=1, source_target_pairs={{0,1},{1,0},{2,3},{3,2},{4,5},{5,4},{6,7},{7,6},{8,9},{9,8},{10,11... | collective-permute-start | bytes 786440 | tf_op jit(solution)/shard_map/ppermute | solution.py:596
  51.4 9.3 %collective-permute-start.9 = (bf16[2,256,256]{2,1,0:T(8,128)(2,1)S(1)}, bf16[2,256,256]{2,1,0:T(8,128)(2,1)S(1)}, u32[]{:S(2)}, u32[]{:S(2)}) collective-permute-start(bf16[2,256,256]{2,1,0:T(8,128)(2,1)S(1)} %add_convert_fusion), channel_id=1, source_target_pairs={{0,4},{4,8},{8,12},{1,5},{5,9},{9,13},{2,6},{6,10},{10,14},{3,7},{... | collective-permute-start | bytes 786440 | tf_op jit(solution)/shard_map/ppermute | solution.py:598
  55.0 5.8 %collective-permute-start.7 = (bf16[2,256,512]{2,1,0:T(8,128)(2,1)S(1)}, bf16[2,256,512]{2,1,0:T(8,128)(2,1)S(1)}, u32[]{:S(2)}, u32[]{:S(2)}) collective-permute-start(bf16[2,256,512]{2,1,0:T(8,128)(2,1)S(1)} %get-tuple-element.101), channel_id=1, source_target_pairs={{0,1},{1,0},{2,3},{3,2},{4,5},{5,4},{6,7},{7,6},{8,9},{9,8},{10,11... | collective-permute-start | bytes 1572872 | tf_op jit(solution)/shard_map/ppermute | solution.py:600
  60.8 1.5 %collective-permute-start.10 = (bf16[2,256,256]{2,1,0:T(8,128)(2,1)S(1)}, bf16[2,256,256]{2,1,0:T(8,128)(2,1)S(1)}, u32[]{:S(2)}, u32[]{:S(2)}) collective-permute-start(bf16[2,256,256]{2,1,0:T(8,128)(2,1)S(1)} %collective-permute-done.9), channel_id=1, source_target_pairs={{0,1},{1,0},{2,3},{3,2},{4,5},{5,4},{6,7},{7,6},{8,9},{9,8},{10,11... | collective-permute-start | bytes 786440 | tf_op jit(solution)/shard_map/ppermute | solution.py:601

commit v17 on v13

--- a/solution.py
+++ b/solution.py
@@ -551,7 +551,6 @@
     first_core = batch_index == 0
     both_positions = lax.ppermute(positions, "batch", pairs)
     both_counts = lax.ppermute(counts, "batch", pairs)
-    both_measured = lax.ppermute(measured, "batch", pairs)
     all_positions = jnp.where(
         first_core,
         jnp.concatenate([positions, both_positions]),
@@ -601,6 +600,8 @@
             inputs = jnp.where(segment == turn, carry, inputs)
         carry = lax.cond(segment == turn, forward_all, silent, carry)
 
+    measured, carry = lax.optimization_barrier((measured, carry))
+    both_measured = lax.ppermute(measured, "batch", pairs)
     height = tile_rows + width
     scalars = (local_rows, local_columns, live.astype(jnp.int32), slot, other)
 
@@ -617,7 +618,13 @@
         carry = lax.ppermute(carry, "depth", [(depth_count - 2, depth_count - 1)])
     arrived_last = carry
     carry, spread_last = lax.cond(segment == depth_count - 1, last_pass, last_silent, carry)
-    gradient = run_place(spread_last, arrived_last, scalars, height, columns_all)
+    gradient = lax.cond(
+        segment == depth_count - 1,
+        lambda s, a: run_place(s, a, scalars, height, columns_all),
+        lambda s, a: jnp.zeros((2, height, columns_all), jnp.bfloat16),
+        spread_last,
+        arrived_last,
+    )
 
     def back_pass(incoming, previous):
         return run_adjoint(

time: 59.7 us -> 59.5 us (level)
  Pallas kernels: 12.1 us -> 9.33 us
  waiting for transfers between devices: 27.2 us -> 29.8 us
    pallas_call x1 -> x0, Pallas kernels: 2.58 us -> none  [run_place(): pl.pallas_call(place_kernel, grid_spec=grid_spec, out_shape=jax.ShapeDtyp...]
    ppermute x1, waiting for transfers between devices: 11 us -> 13.3 us  [local(): carry = lax.ppermute(carry, 'depth', [(turn + 1, turn)])]
  transfers between devices with their start and end apart: 11 -> 11, of which waited for: 7 -> 7; matrix products, arithmetic and copies ran while one was open for 9% -> 9% of each run, Pallas kernels for 14% -> 3%
where the time goes in v17:
time: 59.5 us; the launch traced here: 59.2 us
  waiting for transfers between devices  29.8 us (50%)
  Pallas kernels  9.33 us (16%)
  starting transfers between devices  9.2 us (15%)
  other arithmetic  4.19 us (7%)
  between operations  4.11 us (7%)
  local copies, waits for them, and re-layouts  2.5 us (4%)
    ppermute x1, waiting for transfers between devices, local(): carry = lax.ppermute(carry, 'depth', [(turn + 1, turn)])  13.3 us
    ppermute x1, waiting for transfers between devices, local(): lax.ppermute(spill_sum, 'tile', [(t, t + 1) for t in range(tile_count - 1)])  5.75 us
    ppermute x1, waiting for transfers between devices, from_behind(): return lax.ppermute(block, axis, route)  4.47 us
    pallas_call x1, Pallas kernels, run_first(): pl.pallas_call(first_kernel, grid_spec=grid_spec, out_shape=jax.ShapeDtyp...  3.91 us
    pallas_call x1, Pallas kernels, run_adjoint(): pl.pallas_call(adjoint_kernel(last, number == 1), grid_spec=grid_spec, ou...  3.83 us
    ppermute x1, starting transfers between devices, local(): lax.ppermute(spill_sum, 'tile', [(t, t + 1) for t in range(tile_count - 1)])  3.66 us
    ppermute x1, waiting for transfers between devices, local(): carry = lax.ppermute(carry, 'depth', [(depth_count - 2, depth_count - 1)])  2.98 us
    ppermute x1, starting transfers between devices, local(): carry = lax.ppermute(carry, 'depth', [(depth_count - 2, depth_count - 1)])  2 us
  transfers between devices with their start and end apart: 11, of which 7 were waited for; matrix products, arithmetic and copies ran while one was open for 9% of the time, Pallas kernels for 3%

profile of v17, /device:TPU:0, one launch (start us, length us, event | category | flops | bytes accessed | tf_op | source)
XLA Modules:
  0.0 59.2 jit_solution(7856081948720912650)
XLA Ops:
  0.0 0.5 collective-permute-start
  0.5 0.1 collective-permute-start.1
  0.5 1.1 %dynamic-slice_convert_fusion = bf16[1,2,256,256]{3,2,1,0:T(8,128)(2,1)S(1)} fusion(f32[1,2,256,512]{3,2,1,0:T(8,128)} %tile_ref.1, s32[]{:T(128)S(6)} %select_n.84), kind=kLoop, calls=%fused_computation.4 | loop fusion | bytes 524292 | tf_op jit(solution)/shard_map/convert_element_type | solution.py:546
  1.6 1.3 %collective-permute-start.2 = (bf16[1,2,256,256]{3,2,1,0:T(8,128)(2,1)S(1)}, bf16[1,2,256,256]{3,2,1,0:T(8,128)(2,1)S(1)}, u32[]{:S(2)}, u32[]{:S(2)}) collective-permute-start(bf16[1,2,256,256]{3,2,1,0:T(8,128)(2,1)S(1)} %dynamic-slice_convert_fusion), channel_id=1, source_target_pairs={{4,0},{8,4},{12,8},{5,1},{9,5},{13,9},{6,2},{10,6},{14,10},{7,3},{... | collective-permute-start | bytes 786440 | tf_op jit(solution)/shard_map/ppermute | solution.py:18
  2.9 1.1 %multiply_convert_fusion = (bf16[256,256]{1,0:T(8,128)(2,1)S(1)}, bf16[256,256]{1,0:T(8,128)(2,1)S(1)}) fusion(), kind=kLoop, calls=%fused_computation.13 | loop fusion | flops 1245184 | bytes 262144 | tf_op jit(solution)/shard_map/convert_element_type | solution.py:51
  4.0 1.0 %fusion.6 = (f32[1,256,256]{2,1,0:T(8,128)S(1)}, f32[1,256,256]{2,1,0:T(8,128)S(1)}) fusion(s32[256]{0:T(256)S(1)} %fusion.9, f32[]{:T(128)S(6)} %neg.8), kind=kLoop, calls=%fused_computation.19 | loop fusion | flops 196608 | bytes 525316 | tf_op jit(solution)/shard_map/cos | solution.py:61
  5.9 0.7 %broadcast_select_fusion = s32[2]{0:T(128)S(1)} fusion(pred[]{:T(512)} %eq.24, s32[1]{0:T(128)} %collective-permute-done.1, s32[1]{0:T(128)S(6)} %copy.16), kind=kLoop, calls=%fused_computation.30 | loop fusion | flops 6 | bytes 17 | tf_op jit(solution)/shard_map/jit(_where)/select_n | solution.py:559
  6.6 0.6 %fusion.12 = (s32[1]{0:T(128)}, s32[1]{0:T(128)}) fusion(s32[2]{0:T(128)S(1)} %broadcast_select_fusion), kind=kLoop, calls=%fused_computation.32 | loop fusion | bytes 16 | tf_op jit(solution)/shard_map/slice | solution.py:563
  8.5 4.5 %collective-permute-done.2.mine_ref = bf16[1,2,256,256]{3,2,1,0:T(8,128)(2,1)S(1)} collective-permute-done((bf16[1,2,256,256]{3,2,1,0:T(8,128)(2,1)S(1)}, bf16[1,2,256,256]{3,2,1,0:T(8,128)(2,1)S(1)}, u32[]{:S(2)}, u32[]{:S(2)}) %collective-permute-start.2) | collective-permute-done | bytes 262176 | tf_op jit(solution)/shard_map/ppermute | solution.py:18
  13.0 0.6 %fusion.13 = (s32[1,1]{1,0:T(1,128)}, s32[1,1]{1,0:T(1,128)}) fusion(s32[1,2]{1,0:T(1,128)S(1)} %constant_dynamic-slice_fusion), kind=kLoop, calls=%fused_computation.33 | loop fusion | bytes 16 | tf_op jit(solution)/shard_map/slice | solution.py:570
  14.3 0.2 collective-permute-done.3.partner_ref
  14.5 3.9 %conditional.4 = (bf16[1,2,256,256]{3,2,1,0:T(8,128)(2,1)}) conditional(s32[]{:T(128)} %convert_element_type.72, () %tuple.58, (s32[1]{0:T(128)}, s32[1]{0:T(128)}, s32[1]{0:T(128)}, bf16[1,2,256,256]{3,2,1,0:T(8,128)(2,1)S(1)}, f32[1,2,256,512]{3,2,1,0:T(8,128)S(1)}, /*index=5*/bf16[1,2,256,256]{3,2,1,0:T(8,128)(2,1)S(1)}, ...), branch_computations={%region_0.1_spmd, %region_1.2_spmd} | conditional | bytes 262154 | solution.py:601
  14.5 3.9 %branch_1_fun.6 = bf16[1,2,256,256]{3,2,1,0:T(8,128)(2,1)} custom-call(s32[1]{0:T(128)} %get-tuple-element.129.rows_ref, s32[1]{0:T(128)} %get-tuple-element.130.columns_ref, s32[1]{0:T(128)} %get-tuple-element.131.order_ref, bf16[1,2,256,256]{3,2,1,0:T(8,128)(2,1)S(1)} %get-tuple-element.132.wave_ref, f32[1,2,256,512]{3,2,1,0:T(8,128)S(1)} %get-tuple-element.133.tile_ref, ...), custom_call_target="tpu_custom_call" | custom-call | tf_op jit(solution)/shard_map/cond/branch_1_fun/pallas_call | solution.py:527
  18.4 0.3 collective-permute-start.5
  18.7 2.0 %collective-permute-start.4 = (bf16[1,2,256,256]{3,2,1,0:T(8,128)(2,1)}, bf16[1,2,256,256]{3,2,1,0:T(8,128)(2,1)}, u32[]{:S(2)}, u32[]{:S(2)}) collective-permute-start(bf16[1,2,256,256]{3,2,1,0:T(8,128)(2,1)} %get-tuple-element.201), channel_id=1, source_target_pairs={{0,2},{1,3},{4,6},{5,7},{8,10},{9,11},{12,14},{13,15},{16,18},{17,... | collective-permute-start | bytes 786440 | tf_op jit(solution)/shard_map/ppermute | solution.py:618
  22.0 1.6 %shard_map.60 = f32[1,2,256,256]{3,2,1,0:T(8,128)S(1)} custom-call(s32[1]{0:T(128)} %sub.17.rows_ref, s32[1]{0:T(128)} %bitcast.4.columns_ref, s32[1]{0:T(128)} %bitcast.order_ref, f32[1,2,256,512]{3,2,1,0:T(8,128)S(1)} %copy-done, bf16[1,2,256,256]{3,2,1,0:T(8,128)(2,1)S(1)} %collective-permute-done.2.mine_ref, ...), custom_call_target="tpu_custom_call" | custom-call | tf_op jit(solution)/shard_map/pallas_call | solution.py:275
  23.6 3.0 %collective-permute-done.4 = bf16[1,2,256,256]{3,2,1,0:T(8,128)(2,1)} collective-permute-done((bf16[1,2,256,256]{3,2,1,0:T(8,128)(2,1)}, bf16[1,2,256,256]{3,2,1,0:T(8,128)(2,1)}, u32[]{:S(2)}, u32[]{:S(2)}) %collective-permute-start.4) | collective-permute-done | bytes 262176 | tf_op jit(solution)/shard_map/ppermute | solution.py:618
  26.6 1.3 %collective-permute-start.6 = (bf16[1,2,256,256]{3,2,1,0:T(8,128)(2,1)S(1)}, bf16[1,2,256,256]{3,2,1,0:T(8,128)(2,1)}, u32[]{:S(2)}, u32[]{:S(2)}) collective-permute-start(bf16[1,2,256,256]{3,2,1,0:T(8,128)(2,1)S(1)} %get-tuple-element.175), channel_id=1, source_target_pairs={{2,0},{3,1},{6,4},{7,5},{10,8},{11,9},{14,12},{15,13},{18,16},{19,... | collective-permute-start | bytes 786440 | tf_op jit(solution)/shard_map/ppermute | solution.py:638
  27.9 0.1 conditional.6
  27.9 0.1 broadcast.198
  28.0 13.3 %collective-permute-done.6 = bf16[1,2,256,256]{3,2,1,0:T(8,128)(2,1)} collective-permute-done((bf16[1,2,256,256]{3,2,1,0:T(8,128)(2,1)S(1)}, bf16[1,2,256,256]{3,2,1,0:T(8,128)(2,1)}, u32[]{:S(2)}, u32[]{:S(2)}) %collective-permute-start.6) | collective-permute-done | bytes 262176 | tf_op jit(solution)/shard_map/ppermute | solution.py:638
  41.3 3.8 %conditional.7 = (bf16[2,512,512]{2,1,0:T(8,128)(2,1)S(1)}) conditional(s32[]{:T(128)} %convert_element_type.72, bf16[2,512,512]{2,1,0:T(8,128)(2,1)S(1)} %get-tuple-element.203, (s32[1]{0:T(128)}, s32[1]{0:T(128)}, s32[1]{0:T(128)}, s32[1]{0:T(128)}, s32[1]{0:T(128)}, /*index=5*/bf16[1,2,256,256]{3,2,1,0:T(8,128)(2,1)}, ...), branch_computations={%region_6.7_spmd, %region_7.8_spmd} | conditional | bytes 8 | solution.py:639
  41.3 3.8 %branch_1_fun.9 = (bf16[1,2,256,256]{3,2,1,0:T(8,128)(2,1)}, bf16[2,512,512]{2,1,0:T(8,128)(2,1)S(1)}) custom-call(s32[1]{0:T(128)} %get-tuple-element.156.rows_ref, s32[1]{0:T(128)} %get-tuple-element.157.columns_ref, s32[1]{0:T(128)} %get-tuple-element.158.live_ref, s32[1]{0:T(128)} %get-tuple-element.159.slot_ref, s32[1]{0:T(128)} %get-tuple-element.160.other_ref, ...), custom_call_target="tpu_custom_call" | custom-call | tf_op jit(solution)/shard_map/cond/branch_1_fun/pallas_call | solution.py:436
  45.1 0.1 fusion.11
  45.3 0.1 collective-permute-start.8
  45.3 1.5 %collective-permute-done.8 = bf16[2,256,256]{2,1,0:T(8,128)(2,1)S(1)} collective-permute-done((bf16[2,256,256]{2,1,0:T(8,128)(2,1)S(1)}, bf16[2,256,256]{2,1,0:T(8,128)(2,1)S(1)}, u32[]{:S(2)}, u32[]{:S(2)}) %collective-permute-start.8) | collective-permute-done | bytes 262176 | tf_op jit(solution)/shard_map/ppermute | solution.py:645
  46.9 0.1 add_convert_fusion
  46.9 3.7 %collective-permute-start.9 = (bf16[2,256,256]{2,1,0:T(8,128)(2,1)S(1)}, bf16[2,256,256]{2,1,0:T(8,128)(2,1)S(1)}, u32[]{:S(2)}, u32[]{:S(2)}) collective-permute-start(bf16[2,256,256]{2,1,0:T(8,128)(2,1)S(1)} %add_convert_fusion), channel_id=1, source_target_pairs={{0,4},{4,8},{8,12},{1,5},{5,9},{9,13},{2,6},{6,10},{10,14},{3,7},{... | collective-permute-start | bytes 786440 | tf_op jit(solution)/shard_map/ppermute | solution.py:647
  50.6 0.1 collective-permute-start.7
  50.7 5.8 %collective-permute-done.9 = bf16[2,256,256]{2,1,0:T(8,128)(2,1)S(1)} collective-permute-done((bf16[2,256,256]{2,1,0:T(8,128)(2,1)S(1)}, bf16[2,256,256]{2,1,0:T(8,128)(2,1)S(1)}, u32[]{:S(2)}, u32[]{:S(2)}) %collective-permute-start.9) | collective-permute-done | bytes 262176 | tf_op jit(solution)/shard_map/ppermute | solution.py:647
  56.4 1.5 %collective-permute-done.10 = bf16[2,256,256]{2,1,0:T(8,128)(2,1)S(1)} collective-permute-done((bf16[2,256,256]{2,1,0:T(8,128)(2,1)S(1)}, bf16[2,256,256]{2,1,0:T(8,128)(2,1)S(1)}, u32[]{:S(2)}, u32[]{:S(2)}) %collective-permute-start.10) | collective-permute-done | bytes 262176 | tf_op jit(solution)/shard_map/ppermute | solution.py:650
  58.0 1.2 %add_bitcast_fusion = f32[1,2,256,512]{3,2,1,0:T(8,128)} fusion(bf16[2,256,512]{2,1,0:T(8,128)(2,1)S(1)} %collective-permute-done.7, bf16[2,256,256]{2,1,0:T(8,128)(2,1)S(1)} %collective-permute-done.10, bf16[2,256,256]{2,1,0:T(8,128)(2,1)S(1)} %collective-permute-done.9, pred[]{:T(512)} %eq.24, bf16[2,512,512]{2,1,0:T(8,128)(2,1)S(1)} %get-tuple-element.204), kind=kLoop, calls=%fused_computation | loop fusion | flops 3670016 | bytes 2621441 | tf_op jit(solution)/shard_map/broadcast_in_dim | solution.py:658
  (22 shorter events, 0.3 us)
Async XLA Ops:
  0.0 13.0 %collective-permute-start = (s32[2,2]{1,0:T(2,128)}, s32[2,2]{1,0:T(2,128)S(1)}, u32[]{:S(2)}, u32[]{:S(2)}) collective-permute-start(s32[2,2]{1,0:T(2,128)} %param.19), channel_id=1, source_target_pairs={{0,1},{1,0},{2,3},{3,2},{4,5},{5,4},{6,7},{7,6},{8,9},{9,8},{10,11... | collective-permute-start | bytes 56 | tf_op jit(solution)/shard_map/ppermute | solution.py:552
  0.5 5.4 %collective-permute-start.1 = (s32[1]{0:T(128)}, s32[1]{0:T(128)}, u32[]{:S(2)}, u32[]{:S(2)}) collective-permute-start(s32[1]{0:T(128)} %param.20), channel_id=1, source_target_pairs={{0,1},{1,0},{2,3},{3,2},{4,5},{5,4},{6,7},{7,6},{8,9},{9,8},{10,11... | collective-permute-start | bytes 20 | tf_op jit(solution)/shard_map/ppermute | solution.py:553
  1.6 11.4 %collective-permute-start.2 = (bf16[1,2,256,256]{3,2,1,0:T(8,128)(2,1)S(1)}, bf16[1,2,256,256]{3,2,1,0:T(8,128)(2,1)S(1)}, u32[]{:S(2)}, u32[]{:S(2)}) collective-permute-start(bf16[1,2,256,256]{3,2,1,0:T(8,128)(2,1)S(1)} %dynamic-slice_convert_fusion), channel_id=1, source_target_pairs={{4,0},{8,4},{12,8},{5,1},{9,5},{13,9},{6,2},{10,6},{14,10},{7,3},{... | collective-permute-start | bytes 786440 | tf_op jit(solution)/shard_map/ppermute | solution.py:18
  5.0 9.5 %copy-start = (f32[1,2,256,512]{3,2,1,0:T(8,128)S(1)}, f32[1,2,256,512]{3,2,1,0:T(8,128)}, u32[]{:S(2)}) copy-start(f32[1,2,256,512]{3,2,1,0:T(8,128)} %tile_ref.1) | copy-start | bytes 3145732
  5.1 9.4 %copy-start.1 = (bf16[2,256,256]{2,1,0:T(8,128)(2,1)S(1)}, bf16[2,256,256]{2,1,0:T(8,128)(2,1)}, u32[]{:S(2)}) copy-start(bf16[2,256,256]{2,1,0:T(8,128)(2,1)} %param.18) | copy-start | bytes 786436
  8.5 4.5 %copy-start.2 = (s32[2,2]{1,0:T(2,128)S(1)}, s32[2,2]{1,0:T(2,128)}, u32[]{:S(2)}) copy-start(s32[2,2]{1,0:T(2,128)} %param.19) | copy-start | bytes 52
  13.0 1.5 %collective-permute-start.3 = (bf16[1,2,256,256]{3,2,1,0:T(8,128)(2,1)S(1)}, bf16[1,2,256,256]{3,2,1,0:T(8,128)(2,1)S(1)}, u32[]{:S(2)}, u32[]{:S(2)}) collective-permute-start(bf16[1,2,256,256]{3,2,1,0:T(8,128)(2,1)S(1)} %collective-permute-done.2.mine_ref), channel_id=1, source_target_pairs={{0,1},{1,0},{2,3},{3,2},{4,5},{5,4},{6,7},{7,6},{8,9},{9,8},{10,11... | collective-permute-start | bytes 786440 | tf_op jit(solution)/shard_map/ppermute | solution.py:548
  18.4 8.1 %collective-permute-start.5 = (f32[2,256,256]{2,1,0:T(8,128)}, f32[2,256,256]{2,1,0:T(8,128)}, u32[]{:S(2)}, u32[]{:S(2)}) collective-permute-start(f32[2,256,256]{2,1,0:T(8,128)} %param.21), channel_id=1, source_target_pairs={{0,1},{1,0},{2,3},{3,2},{4,5},{5,4},{6,7},{7,6},{8,9},{9,8},{10,11... | collective-permute-start | bytes 1572872 | tf_op jit(solution)/shard_map/ppermute | solution.py:604
  18.7 7.8 %collective-permute-start.4 = (bf16[1,2,256,256]{3,2,1,0:T(8,128)(2,1)}, bf16[1,2,256,256]{3,2,1,0:T(8,128)(2,1)}, u32[]{:S(2)}, u32[]{:S(2)}) collective-permute-start(bf16[1,2,256,256]{3,2,1,0:T(8,128)(2,1)} %get-tuple-element.201), channel_id=1, source_target_pairs={{0,2},{1,3},{4,6},{5,7},{8,10},{9,11},{12,14},{13,15},{16,18},{17,... | collective-permute-start | bytes 786440 | tf_op jit(solution)/shard_map/ppermute | solution.py:618
  26.6 14.7 %collective-permute-start.6 = (bf16[1,2,256,256]{3,2,1,0:T(8,128)(2,1)S(1)}, bf16[1,2,256,256]{3,2,1,0:T(8,128)(2,1)}, u32[]{:S(2)}, u32[]{:S(2)}) collective-permute-start(bf16[1,2,256,256]{3,2,1,0:T(8,128)(2,1)S(1)} %get-tuple-element.175), channel_id=1, source_target_pairs={{2,0},{3,1},{6,4},{7,5},{10,8},{11,9},{14,12},{15,13},{18,16},{19,... | collective-permute-start | bytes 786440 | tf_op jit(solution)/shard_map/ppermute | solution.py:638
  45.3 1.6 %collective-permute-start.8 = (bf16[2,256,256]{2,1,0:T(8,128)(2,1)S(1)}, bf16[2,256,256]{2,1,0:T(8,128)(2,1)S(1)}, u32[]{:S(2)}, u32[]{:S(2)}) collective-permute-start(bf16[2,256,256]{2,1,0:T(8,128)(2,1)S(1)} %constant_dynamic-slice_fusion.1), channel_id=1, source_target_pairs={{0,1},{1,0},{2,3},{3,2},{4,5},{5,4},{6,7},{7,6},{8,9},{9,8},{10,11... | collective-permute-start | bytes 786440 | tf_op jit(solution)/shard_map/ppermute | solution.py:645
  46.9 9.5 %collective-permute-start.9 = (bf16[2,256,256]{2,1,0:T(8,128)(2,1)S(1)}, bf16[2,256,256]{2,1,0:T(8,128)(2,1)S(1)}, u32[]{:S(2)}, u32[]{:S(2)}) collective-permute-start(bf16[2,256,256]{2,1,0:T(8,128)(2,1)S(1)} %add_convert_fusion), channel_id=1, source_target_pairs={{0,4},{4,8},{8,12},{1,5},{5,9},{9,13},{2,6},{6,10},{10,14},{3,7},{... | collective-permute-start | bytes 786440 | tf_op jit(solution)/shard_map/ppermute | solution.py:647
  50.6 5.8 %collective-permute-start.7 = (bf16[2,256,512]{2,1,0:T(8,128)(2,1)S(1)}, bf16[2,256,512]{2,1,0:T(8,128)(2,1)S(1)}, u32[]{:S(2)}, u32[]{:S(2)}) collective-permute-start(bf16[2,256,512]{2,1,0:T(8,128)(2,1)S(1)} %get-tuple-element.188), channel_id=1, source_target_pairs={{0,1},{1,0},{2,3},{3,2},{4,5},{5,4},{6,7},{7,6},{8,9},{9,8},{10,11... | collective-permute-start | bytes 1572872 | tf_op jit(solution)/shard_map/ppermute | solution.py:649
  56.4 1.5 %collective-permute-start.10 = (bf16[2,256,256]{2,1,0:T(8,128)(2,1)S(1)}, bf16[2,256,256]{2,1,0:T(8,128)(2,1)S(1)}, u32[]{:S(2)}, u32[]{:S(2)}) collective-permute-start(bf16[2,256,256]{2,1,0:T(8,128)(2,1)S(1)} %collective-permute-done.9), channel_id=1, source_target_pairs={{0,1},{1,0},{2,3},{3,2},{4,5},{5,4},{6,7},{7,6},{8,9},{9,8},{10,11... | collective-permute-start | bytes 786440 | tf_op jit(solution)/shard_map/ppermute | solution.py:650

commit v18 on v14

--- a/solution.py
+++ b/solution.py
@@ -343,11 +343,11 @@
             direct_ref[part] = pltpu.roll(tall, row_shift, 0).astype(direct_ref.dtype)
 
 
-def adjoint_kernel(last, single):
+def adjoint_kernel(last, single, opening=False):
     def kernel(rows_ref, columns_ref, live_ref, slot_ref, other_ref, *refs):
         refs = list(refs)
         wave_ref = refs.pop(0)
-        patch_ref = refs.pop(0)
+        patch_ref = None if opening else refs.pop(0)
         chirp_ref = refs.pop(0)
         blocks = refs[:2]
         refs = refs[2:]
@@ -356,7 +356,11 @@
             partner_ref = refs.pop(0)
         else:
             source_ref = refs.pop(0)
-        passed_ref, grad_ref, total_ref = refs
+        if opening:
+            grad_ref, total_ref = refs
+            passed_ref = None
+        else:
+            passed_ref, grad_ref, total_ref = refs
         index = pl.program_id(0)
 
         if not single:
@@ -365,8 +369,9 @@
                 total_ref[...] = jnp.zeros(total_ref.shape, total_ref.dtype)
 
         wave = wave_ref[0].astype(jnp.float32)
-        patch_re = patch_ref[0, 0]
-        patch_im = patch_ref[0, 1]
+        if not opening:
+            patch_re = patch_ref[0, 0]
+            patch_im = patch_ref[0, 1]
         chirp_re = chirp_ref[0]
         chirp_im = chirp_ref[1]
         if last:
@@ -386,8 +391,9 @@
             in_re = wave[0]
             in_im = wave[1]
         spread_re, spread_im = propagate_block(in_re, in_im, blocks, chirp_re, -chirp_im)
-        passed_ref[0, 0] = (patch_re * spread_re + patch_im * spread_im).astype(jnp.bfloat16)
-        passed_ref[0, 1] = (patch_re * spread_im - patch_im * spread_re).astype(jnp.bfloat16)
+        if not opening:
+            passed_ref[0, 0] = (patch_re * spread_re + patch_im * spread_im).astype(jnp.bfloat16)
+            passed_ref[0, 1] = (patch_re * spread_im - patch_im * spread_re).astype(jnp.bfloat16)
         term_re = source_re * spread_re + source_im * spread_im
         term_im = source_re * spread_im - source_im * spread_re
         place_term(
@@ -403,11 +409,12 @@
     return kernel
 
 
-def run_adjoint(waves, patches, chirps, blocks, scalars, extra, height, columns_all, last):
+def run_adjoint(waves, patches, chirps, blocks, scalars, extra, height, columns_all, last,
+                opening=False):
     number, _, width, _ = waves.shape
     wave_spec = pl.BlockSpec((1, 2, width, width), lambda i, *s: (i, 0, 0, 0))
     chirp_spec = pl.BlockSpec((2, width, width), lambda i, *s: (0, 0, 0))
-    in_specs = [wave_spec, wave_spec, chirp_spec] + [
+    in_specs = [wave_spec] + ([] if opening else [wave_spec]) + [chirp_spec] + [
         pl.BlockSpec((2 * width, width), lambda i, *s: (0, 0)),
         pl.BlockSpec((width, 2 * width), lambda i, *s: (0, 0)),
     ]
@@ -420,20 +427,16 @@
         num_scalar_prefetch=5,
         grid=(number,),
         in_specs=in_specs,
-        out_specs=(
-            wave_spec,
-            pl.BlockSpec((2, height, columns_all), lambda i, *s: (0, 0, 0)),
-        ),
+        out_specs=((() if opening else (wave_spec,))
+                   + (pl.BlockSpec((2, height, columns_all), lambda i, *s: (0, 0, 0)),)),
         scratch_shapes=[pltpu.VMEM((2, height, columns_all), jnp.float32)],
     )
     return pl.pallas_call(
-        adjoint_kernel(last, number == 1),
+        adjoint_kernel(last, number == 1, opening),
         grid_spec=grid_spec,
-        out_shape=(
-            jax.ShapeDtypeStruct(waves.shape, jnp.bfloat16),
-            jax.ShapeDtypeStruct((2, height, columns_all), jnp.bfloat16),
-        ),
-    )(*scalars, waves, patches, chirps, *blocks, *extra)
+        out_shape=((() if opening else (jax.ShapeDtypeStruct(waves.shape, jnp.bfloat16),))
+                   + (jax.ShapeDtypeStruct((2, height, columns_all), jnp.bfloat16),)),
+    )(*scalars, waves, *(() if opening else (patches,)), chirps, *blocks, *extra)
 
 
 def first_kernel(rows_ref, columns_ref, order_ref, wave_ref, tile_ref, mine_ref, partner_ref,
@@ -582,12 +585,20 @@
             incoming, patches, chirps, blocks, scalars, (inputs,), height, columns_all, False
         )
 
+    def opening_pass(incoming, previous):
+        (gradient,) = run_adjoint(
+            incoming, patches, chirps, blocks, scalars, (inputs,), height, columns_all, False,
+            opening=True,
+        )
+        return (incoming, gradient)
+
     def back_silent(incoming, previous):
         return (jnp.zeros_like(incoming), previous)
 
     for turn in reversed(range(depth_count - 1)):
         carry = lax.ppermute(carry, "depth", [(turn + 1, turn)])
-        carry, gradient = lax.cond(segment == turn, back_pass, back_silent, carry, gradient)
+        step = opening_pass if turn == 0 else back_pass
+        carry, gradient = lax.cond(segment == turn, step, back_silent, carry, gradient)
 
     gradient = gradient.astype(jnp.bfloat16)
     spill = gradient[:, tile_rows:, :]

time: 59.4 us -> 59 us (level)
  no operation moved by 1% of the time
where the time goes in v18:
time: 59 us; the launch traced here: 58.7 us
  waiting for transfers between devices  30.4 us (52%)
  starting transfers between devices  9.16 us (16%)
  Pallas kernels  8.19 us (14%)
  other arithmetic  4.25 us (7%)
  between operations  4.24 us (7%)
  local copies, waits for them, and re-layouts  2.46 us (4%)
    ppermute x1, waiting for transfers between devices, local(): carry = lax.ppermute(carry, 'depth', [(turn + 1, turn)])  13.9 us
    ppermute x1, waiting for transfers between devices, local(): lax.ppermute(spill_sum, 'tile', [(t, t + 1) for t in range(tile_count - 1)])  5.75 us
    ppermute x1, waiting for transfers between devices, from_behind(): return lax.ppermute(block, axis, route)  4.37 us
    pallas_call x1, Pallas kernels, run_first(): pl.pallas_call(first_kernel, grid_spec=grid_spec, out_shape=jax.ShapeDtyp...  3.85 us
    ppermute x1, starting transfers between devices, local(): lax.ppermute(spill_sum, 'tile', [(t, t + 1) for t in range(tile_count - 1)])  3.65 us
    ppermute x1, waiting for transfers between devices, local(): carry = lax.ppermute(carry, 'depth', [(depth_count - 2, depth_count - 1)])  2.99 us
    pallas_call x1, Pallas kernels, run_adjoint(): pl.pallas_call(adjoint_kernel(last, number == 1, opening), grid_spec=grid...  2.81 us
    ppermute x1, starting transfers between devices, local(): carry = lax.ppermute(carry, 'depth', [(depth_count - 2, depth_count - 1)])  1.98 us
  transfers between devices with their start and end apart: 11, of which 7 were waited for; matrix products, arithmetic and copies ran while one was open for 9% of the time, Pallas kernels for 3%

profile of v18, /device:TPU:0, one launch (start us, length us, event | category | flops | bytes accessed | tf_op | source)
XLA Modules:
  0.0 58.7 jit_solution(114046873743570489)
XLA Ops:
  0.0 0.5 collective-permute-start.1
  0.5 0.1 collective-permute-start
  0.5 1.1 %dynamic-slice_convert_fusion = bf16[1,2,256,256]{3,2,1,0:T(8,128)(2,1)S(1)} fusion(f32[1,2,256,512]{3,2,1,0:T(8,128)} %tile_ref.1, s32[]{:T(128)S(6)} %select_n.84), kind=kLoop, calls=%fused_computation.4 | loop fusion | bytes 524292 | tf_op jit(solution)/shard_map/convert_element_type | solution.py:508
  1.6 1.3 %collective-permute-start.2 = (bf16[1,2,256,256]{3,2,1,0:T(8,128)(2,1)S(1)}, bf16[1,2,256,256]{3,2,1,0:T(8,128)(2,1)S(1)}, u32[]{:S(2)}, u32[]{:S(2)}) collective-permute-start(bf16[1,2,256,256]{3,2,1,0:T(8,128)(2,1)S(1)} %dynamic-slice_convert_fusion), channel_id=1, source_target_pairs={{4,0},{8,4},{12,8},{5,1},{9,5},{13,9},{6,2},{10,6},{14,10},{7,3},{... | collective-permute-start | bytes 786440 | tf_op jit(solution)/shard_map/ppermute | solution.py:18
  2.9 1.1 %multiply_convert_fusion = (bf16[256,256]{1,0:T(8,128)(2,1)S(1)}, bf16[256,256]{1,0:T(8,128)(2,1)S(1)}) fusion(), kind=kLoop, calls=%fused_computation.13 | loop fusion | flops 1245184 | bytes 262144 | tf_op jit(solution)/shard_map/convert_element_type | solution.py:51
  4.1 1.0 %fusion.6 = (f32[1,256,256]{2,1,0:T(8,128)S(1)}, f32[1,256,256]{2,1,0:T(8,128)S(1)}) fusion(s32[256]{0:T(256)S(1)} %fusion.9, f32[]{:T(128)S(6)} %neg.8), kind=kLoop, calls=%fused_computation.19 | loop fusion | flops 196608 | bytes 525316 | tf_op jit(solution)/shard_map/cos | solution.py:61
  5.9 0.8 %broadcast_select_fusion = s32[2]{0:T(128)S(1)} fusion(pred[]{:T(512)} %eq.23, s32[1]{0:T(128)} %collective-permute-done.1, s32[1]{0:T(128)S(6)} %copy.14), kind=kLoop, calls=%fused_computation.30 | loop fusion | flops 6 | bytes 17 | tf_op jit(solution)/shard_map/jit(_where)/select_n | solution.py:521
  6.6 0.6 %fusion.12 = (s32[1]{0:T(128)}, s32[1]{0:T(128)}) fusion(s32[2]{0:T(128)S(1)} %broadcast_select_fusion), kind=kLoop, calls=%fused_computation.32 | loop fusion | bytes 16 | tf_op jit(solution)/shard_map/slice | solution.py:525
  8.6 4.4 %collective-permute-done.2.mine_ref = bf16[1,2,256,256]{3,2,1,0:T(8,128)(2,1)S(1)} collective-permute-done((bf16[1,2,256,256]{3,2,1,0:T(8,128)(2,1)S(1)}, bf16[1,2,256,256]{3,2,1,0:T(8,128)(2,1)S(1)}, u32[]{:S(2)}, u32[]{:S(2)}) %collective-permute-start.2) | collective-permute-done | bytes 262176 | tf_op jit(solution)/shard_map/ppermute | solution.py:18
  13.0 0.6 fusion.13
  14.3 0.3 collective-permute-done.3.partner_ref
  14.5 3.9 %conditional.3 = (bf16[1,2,256,256]{3,2,1,0:T(8,128)(2,1)}) conditional(s32[]{:T(128)} %convert_element_type.71, () %tuple.55, (s32[1]{0:T(128)}, s32[1]{0:T(128)}, s32[1]{0:T(128)}, bf16[1,2,256,256]{3,2,1,0:T(8,128)(2,1)S(1)}, f32[1,2,256,512]{3,2,1,0:T(8,128)S(1)}, /*index=5*/bf16[1,2,256,256]{3,2,1,0:T(8,128)(2,1)S(1)}, ...), branch_computations={%region_0.1_spmd, %region_1.2_spmd} | conditional | bytes 262154 | solution.py:563
  14.5 3.9 %branch_1_fun.5 = bf16[1,2,256,256]{3,2,1,0:T(8,128)(2,1)} custom-call(s32[1]{0:T(128)} %get-tuple-element.117.rows_ref, s32[1]{0:T(128)} %get-tuple-element.118.columns_ref, s32[1]{0:T(128)} %get-tuple-element.119.order_ref, bf16[1,2,256,256]{3,2,1,0:T(8,128)(2,1)S(1)} %get-tuple-element.120.wave_ref, f32[1,2,256,512]{3,2,1,0:T(8,128)S(1)} %get-tuple-element.121.tile_ref, ...), custom_call_target="tpu_custom_call" | custom-call | tf_op jit(solution)/shard_map/cond/branch_1_fun/pallas_call | solution.py:489
  18.4 0.3 collective-permute-start.5
  18.7 2.0 %collective-permute-start.4 = (bf16[1,2,256,256]{3,2,1,0:T(8,128)(2,1)}, bf16[1,2,256,256]{3,2,1,0:T(8,128)(2,1)}, u32[]{:S(2)}, u32[]{:S(2)}) collective-permute-start(bf16[1,2,256,256]{3,2,1,0:T(8,128)(2,1)} %get-tuple-element.182), channel_id=1, source_target_pairs={{0,2},{1,3},{4,6},{5,7},{8,10},{9,11},{12,14},{13,15},{16,18},{17,... | collective-permute-start | bytes 786440 | tf_op jit(solution)/shard_map/ppermute | solution.py:580
  22.0 1.5 %shard_map.60 = f32[1,2,256,256]{3,2,1,0:T(8,128)S(1)} custom-call(s32[1]{0:T(128)} %sub.17.rows_ref, s32[1]{0:T(128)} %bitcast.4.columns_ref, s32[1]{0:T(128)} %bitcast.order_ref, f32[1,2,256,512]{3,2,1,0:T(8,128)S(1)} %copy-done, bf16[1,2,256,256]{3,2,1,0:T(8,128)(2,1)S(1)} %collective-permute-done.2.mine_ref, ...), custom_call_target="tpu_custom_call" | custom-call | tf_op jit(solution)/shard_map/pallas_call | solution.py:275
  23.5 3.0 %collective-permute-done.4 = bf16[1,2,256,256]{3,2,1,0:T(8,128)(2,1)} collective-permute-done((bf16[1,2,256,256]{3,2,1,0:T(8,128)(2,1)}, bf16[1,2,256,256]{3,2,1,0:T(8,128)(2,1)}, u32[]{:S(2)}, u32[]{:S(2)}) %collective-permute-start.4) | collective-permute-done | bytes 262176 | tf_op jit(solution)/shard_map/ppermute | solution.py:580
  26.5 0.1 conditional.4
  26.5 0.1 broadcast.198
  26.6 1.3 %collective-permute-start.6 = (bf16[1,2,256,256]{3,2,1,0:T(8,128)(2,1)S(1)}, bf16[1,2,256,256]{3,2,1,0:T(8,128)(2,1)S(1)}, u32[]{:S(2)}, u32[]{:S(2)}) collective-permute-start(bf16[1,2,256,256]{3,2,1,0:T(8,128)(2,1)S(1)} %get-tuple-element.156), channel_id=1, source_target_pairs={{2,0},{3,1},{6,4},{7,5},{10,8},{11,9},{14,12},{15,13},{18,16},{19,... | collective-permute-start | bytes 786440 | tf_op jit(solution)/shard_map/ppermute | solution.py:599
  27.9 13.9 %collective-permute-done.6 = bf16[1,2,256,256]{3,2,1,0:T(8,128)(2,1)S(1)} collective-permute-done((bf16[1,2,256,256]{3,2,1,0:T(8,128)(2,1)S(1)}, bf16[1,2,256,256]{3,2,1,0:T(8,128)(2,1)S(1)}, u32[]{:S(2)}, u32[]{:S(2)}) %collective-permute-start.6) | collective-permute-done | bytes 262176 | tf_op jit(solution)/shard_map/ppermute | solution.py:599
  41.8 2.8 %conditional.5 = (bf16[2,512,512]{2,1,0:T(8,128)(2,1)S(1)}) conditional(s32[]{:T(128)} %convert_element_type.71, bf16[2,512,512]{2,1,0:T(8,128)(2,1)S(1)} %get-tuple-element.155, (s32[1]{0:T(128)}, s32[1]{0:T(128)}, s32[1]{0:T(128)}, s32[1]{0:T(128)}, s32[1]{0:T(128)}, /*index=5*/bf16[1,2,256,256]{3,2,1,0:T(8,128)(2,1)S(1)}, ...), branch_computations={%region_4.5_spmd, %region_5.6_spmd} | conditional | bytes 8 | solution.py:601
  41.8 2.8 %branch_1_fun.7 = bf16[2,512,512]{2,1,0:T(8,128)(2,1)S(1)} custom-call(s32[1]{0:T(128)} %get-tuple-element.139.rows_ref, s32[1]{0:T(128)} %get-tuple-element.140.columns_ref, s32[1]{0:T(128)} %get-tuple-element.141.live_ref, s32[1]{0:T(128)} %get-tuple-element.142.slot_ref, s32[1]{0:T(128)} %get-tuple-element.143.other_ref, ...), custom_call_target="tpu_custom_call" | custom-call | tf_op jit(solution)/shard_map/cond/branch_1_fun/pallas_call | solution.py:434
  44.7 0.1 fusion.11
  44.8 0.1 collective-permute-start.8
  44.9 1.5 %collective-permute-done.8 = bf16[2,256,256]{2,1,0:T(8,128)(2,1)S(1)} collective-permute-done((bf16[2,256,256]{2,1,0:T(8,128)(2,1)S(1)}, bf16[2,256,256]{2,1,0:T(8,128)(2,1)S(1)}, u32[]{:S(2)}, u32[]{:S(2)}) %collective-permute-start.8) | collective-permute-done | bytes 262176 | tf_op jit(solution)/shard_map/ppermute | solution.py:607
  46.4 0.1 add_convert_fusion
  46.5 3.7 %collective-permute-start.9 = (bf16[2,256,256]{2,1,0:T(8,128)(2,1)S(1)}, bf16[2,256,256]{2,1,0:T(8,128)(2,1)S(1)}, u32[]{:S(2)}, u32[]{:S(2)}) collective-permute-start(bf16[2,256,256]{2,1,0:T(8,128)(2,1)S(1)} %add_convert_fusion), channel_id=1, source_target_pairs={{0,4},{4,8},{8,12},{1,5},{5,9},{9,13},{2,6},{6,10},{10,14},{3,7},{... | collective-permute-start | bytes 786440 | tf_op jit(solution)/shard_map/ppermute | solution.py:609
  50.1 0.1 collective-permute-start.7
  50.2 5.8 %collective-permute-done.9 = bf16[2,256,256]{2,1,0:T(8,128)(2,1)S(1)} collective-permute-done((bf16[2,256,256]{2,1,0:T(8,128)(2,1)S(1)}, bf16[2,256,256]{2,1,0:T(8,128)(2,1)S(1)}, u32[]{:S(2)}, u32[]{:S(2)}) %collective-permute-start.9) | collective-permute-done | bytes 262176 | tf_op jit(solution)/shard_map/ppermute | solution.py:609
  56.0 1.5 %collective-permute-done.10 = bf16[2,256,256]{2,1,0:T(8,128)(2,1)S(1)} collective-permute-done((bf16[2,256,256]{2,1,0:T(8,128)(2,1)S(1)}, bf16[2,256,256]{2,1,0:T(8,128)(2,1)S(1)}, u32[]{:S(2)}, u32[]{:S(2)}) %collective-permute-start.10) | collective-permute-done | bytes 262176 | tf_op jit(solution)/shard_map/ppermute | solution.py:612
  57.5 1.2 %add_bitcast_fusion = f32[1,2,256,512]{3,2,1,0:T(8,128)} fusion(bf16[2,256,512]{2,1,0:T(8,128)(2,1)S(1)} %collective-permute-done.7, bf16[2,256,256]{2,1,0:T(8,128)(2,1)S(1)} %collective-permute-done.10, bf16[2,256,256]{2,1,0:T(8,128)(2,1)S(1)} %collective-permute-done.9, pred[]{:T(512)} %eq.23, bf16[2,512,512]{2,1,0:T(8,128)(2,1)S(1)} %get-tuple-element.184), kind=kLoop, calls=%fused_computation | loop fusion | flops 3670016 | bytes 2621441 | tf_op jit(solution)/shard_map/broadcast_in_dim | solution.py:620
  (20 shorter events, 0.2 us)
Async XLA Ops:
  0.0 5.9 %collective-permute-start.1 = (s32[1]{0:T(128)}, s32[1]{0:T(128)}, u32[]{:S(2)}, u32[]{:S(2)}) collective-permute-start(s32[1]{0:T(128)} %param.18), channel_id=1, source_target_pairs={{0,1},{1,0},{2,3},{3,2},{4,5},{5,4},{6,7},{7,6},{8,9},{9,8},{10,11... | collective-permute-start | bytes 20 | tf_op jit(solution)/shard_map/ppermute | solution.py:515
  0.5 12.5 %collective-permute-start = (s32[2,2]{1,0:T(2,128)}, s32[2,2]{1,0:T(2,128)S(1)}, u32[]{:S(2)}, u32[]{:S(2)}) collective-permute-start(s32[2,2]{1,0:T(2,128)} %param.17), channel_id=1, source_target_pairs={{0,1},{1,0},{2,3},{3,2},{4,5},{5,4},{6,7},{7,6},{8,9},{9,8},{10,11... | collective-permute-start | bytes 56 | tf_op jit(solution)/shard_map/ppermute | solution.py:514
  1.6 11.4 %collective-permute-start.2 = (bf16[1,2,256,256]{3,2,1,0:T(8,128)(2,1)S(1)}, bf16[1,2,256,256]{3,2,1,0:T(8,128)(2,1)S(1)}, u32[]{:S(2)}, u32[]{:S(2)}) collective-permute-start(bf16[1,2,256,256]{3,2,1,0:T(8,128)(2,1)S(1)} %dynamic-slice_convert_fusion), channel_id=1, source_target_pairs={{4,0},{8,4},{12,8},{5,1},{9,5},{13,9},{6,2},{10,6},{14,10},{7,3},{... | collective-permute-start | bytes 786440 | tf_op jit(solution)/shard_map/ppermute | solution.py:18
  4.0 10.5 %copy-start = (f32[1,2,256,512]{3,2,1,0:T(8,128)S(1)}, f32[1,2,256,512]{3,2,1,0:T(8,128)}, u32[]{:S(2)}) copy-start(f32[1,2,256,512]{3,2,1,0:T(8,128)} %tile_ref.1) | copy-start | bytes 3145732
  5.1 9.4 %copy-start.1 = (bf16[2,256,256]{2,1,0:T(8,128)(2,1)S(1)}, bf16[2,256,256]{2,1,0:T(8,128)(2,1)}, u32[]{:S(2)}) copy-start(bf16[2,256,256]{2,1,0:T(8,128)(2,1)} %param.16) | copy-start | bytes 786436
  8.6 4.4 %copy-start.2 = (s32[2,2]{1,0:T(2,128)S(1)}, s32[2,2]{1,0:T(2,128)}, u32[]{:S(2)}) copy-start(s32[2,2]{1,0:T(2,128)} %param.17) | copy-start | bytes 52
  13.0 1.5 %collective-permute-start.3 = (bf16[1,2,256,256]{3,2,1,0:T(8,128)(2,1)S(1)}, bf16[1,2,256,256]{3,2,1,0:T(8,128)(2,1)S(1)}, u32[]{:S(2)}, u32[]{:S(2)}) collective-permute-start(bf16[1,2,256,256]{3,2,1,0:T(8,128)(2,1)S(1)} %collective-permute-done.2.mine_ref), channel_id=1, source_target_pairs={{0,1},{1,0},{2,3},{3,2},{4,5},{5,4},{6,7},{7,6},{8,9},{9,8},{10,11... | collective-permute-start | bytes 786440 | tf_op jit(solution)/shard_map/ppermute | solution.py:510
  18.4 8.1 %collective-permute-start.5 = (f32[2,256,256]{2,1,0:T(8,128)}, f32[2,256,256]{2,1,0:T(8,128)}, u32[]{:S(2)}, u32[]{:S(2)}) collective-permute-start(f32[2,256,256]{2,1,0:T(8,128)} %param.19), channel_id=1, source_target_pairs={{0,1},{1,0},{2,3},{3,2},{4,5},{5,4},{6,7},{7,6},{8,9},{9,8},{10,11... | collective-permute-start | bytes 1572872 | tf_op jit(solution)/shard_map/ppermute | solution.py:566
  18.7 7.8 %collective-permute-start.4 = (bf16[1,2,256,256]{3,2,1,0:T(8,128)(2,1)}, bf16[1,2,256,256]{3,2,1,0:T(8,128)(2,1)}, u32[]{:S(2)}, u32[]{:S(2)}) collective-permute-start(bf16[1,2,256,256]{3,2,1,0:T(8,128)(2,1)} %get-tuple-element.182), channel_id=1, source_target_pairs={{0,2},{1,3},{4,6},{5,7},{8,10},{9,11},{12,14},{13,15},{16,18},{17,... | collective-permute-start | bytes 786440 | tf_op jit(solution)/shard_map/ppermute | solution.py:580
  26.6 15.2 %collective-permute-start.6 = (bf16[1,2,256,256]{3,2,1,0:T(8,128)(2,1)S(1)}, bf16[1,2,256,256]{3,2,1,0:T(8,128)(2,1)S(1)}, u32[]{:S(2)}, u32[]{:S(2)}) collective-permute-start(bf16[1,2,256,256]{3,2,1,0:T(8,128)(2,1)S(1)} %get-tuple-element.156), channel_id=1, source_target_pairs={{2,0},{3,1},{6,4},{7,5},{10,8},{11,9},{14,12},{15,13},{18,16},{19,... | collective-permute-start | bytes 786440 | tf_op jit(solution)/shard_map/ppermute | solution.py:599
  44.8 1.6 %collective-permute-start.8 = (bf16[2,256,256]{2,1,0:T(8,128)(2,1)S(1)}, bf16[2,256,256]{2,1,0:T(8,128)(2,1)S(1)}, u32[]{:S(2)}, u32[]{:S(2)}) collective-permute-start(bf16[2,256,256]{2,1,0:T(8,128)(2,1)S(1)} %constant_dynamic-slice_fusion.1), channel_id=1, source_target_pairs={{0,1},{1,0},{2,3},{3,2},{4,5},{5,4},{6,7},{7,6},{8,9},{9,8},{10,11... | collective-permute-start | bytes 786440 | tf_op jit(solution)/shard_map/ppermute | solution.py:607
  46.5 9.5 %collective-permute-start.9 = (bf16[2,256,256]{2,1,0:T(8,128)(2,1)S(1)}, bf16[2,256,256]{2,1,0:T(8,128)(2,1)S(1)}, u32[]{:S(2)}, u32[]{:S(2)}) collective-permute-start(bf16[2,256,256]{2,1,0:T(8,128)(2,1)S(1)} %add_convert_fusion), channel_id=1, source_target_pairs={{0,4},{4,8},{8,12},{1,5},{5,9},{9,13},{2,6},{6,10},{10,14},{3,7},{... | collective-permute-start | bytes 786440 | tf_op jit(solution)/shard_map/ppermute | solution.py:609
  50.1 5.8 %collective-permute-start.7 = (bf16[2,256,512]{2,1,0:T(8,128)(2,1)S(1)}, bf16[2,256,512]{2,1,0:T(8,128)(2,1)S(1)}, u32[]{:S(2)}, u32[]{:S(2)}) collective-permute-start(bf16[2,256,512]{2,1,0:T(8,128)(2,1)S(1)} %get-tuple-element.169), channel_id=1, source_target_pairs={{0,1},{1,0},{2,3},{3,2},{4,5},{5,4},{6,7},{7,6},{8,9},{9,8},{10,11... | collective-permute-start | bytes 1572872 | tf_op jit(solution)/shard_map/ppermute | solution.py:611
  55.9 1.5 %collective-permute-start.10 = (bf16[2,256,256]{2,1,0:T(8,128)(2,1)S(1)}, bf16[2,256,256]{2,1,0:T(8,128)(2,1)S(1)}, u32[]{:S(2)}, u32[]{:S(2)}) collective-permute-start(bf16[2,256,256]{2,1,0:T(8,128)(2,1)S(1)} %collective-permute-done.9), channel_id=1, source_target_pairs={{0,1},{1,0},{2,3},{3,2},{4,5},{5,4},{6,7},{7,6},{8,9},{9,8},{10,11... | collective-permute-start | bytes 786440 | tf_op jit(solution)/shard_map/ppermute | solution.py:612

commit v19 on v18

--- a/solution.py
+++ b/solution.py
@@ -394,6 +394,10 @@
         if not opening:
             passed_ref[0, 0] = (patch_re * spread_re + patch_im * spread_im).astype(jnp.bfloat16)
             passed_ref[0, 1] = (patch_re * spread_im - patch_im * spread_re).astype(jnp.bfloat16)
+        if last:
+            grad_ref[0, 0] = spread_re.astype(jnp.bfloat16)
+            grad_ref[0, 1] = spread_im.astype(jnp.bfloat16)
+            return
         term_re = source_re * spread_re + source_im * spread_im
         term_im = source_re * spread_im - source_im * spread_re
         place_term(
@@ -428,15 +432,54 @@
         grid=(number,),
         in_specs=in_specs,
         out_specs=((() if opening else (wave_spec,))
-                   + (pl.BlockSpec((2, height, columns_all), lambda i, *s: (0, 0, 0)),)),
+                   + ((wave_spec,) if last else
+                      (pl.BlockSpec((2, height, columns_all), lambda i, *s: (0, 0, 0)),))),
         scratch_shapes=[pltpu.VMEM((2, height, columns_all), jnp.float32)],
     )
     return pl.pallas_call(
         adjoint_kernel(last, number == 1, opening),
         grid_spec=grid_spec,
         out_shape=((() if opening else (jax.ShapeDtypeStruct(waves.shape, jnp.bfloat16),))
-                   + (jax.ShapeDtypeStruct((2, height, columns_all), jnp.bfloat16),)),
+                   + ((jax.ShapeDtypeStruct(waves.shape, jnp.bfloat16),) if last else
+                      (jax.ShapeDtypeStruct((2, height, columns_all), jnp.bfloat16),))),
     )(*scalars, waves, *(() if opening else (patches,)), chirps, *blocks, *extra)
+
+
+def place_kernel(rows_ref, columns_ref, live_ref, spread_ref, source_ref, grad_ref, total_ref):
+    index = pl.program_id(0)
+
+    @pl.when(index == 0)
+    def _():
+        total_ref[...] = jnp.zeros(total_ref.shape, total_ref.dtype)
+
+    spread = spread_ref[0].astype(jnp.float32)
+    source = source_ref[0].astype(jnp.float32)
+    term_re = source[0] * spread[0] + source[1] * spread[1]
+    term_im = source[0] * spread[1] - source[1] * spread[0]
+    place_term(
+        term_re, term_im, rows_ref[index], columns_ref[index], live_ref[index] > 0, total_ref
+    )
+
+    @pl.when(index == pl.num_programs(0) - 1)
+    def _():
+        grad_ref[...] = total_ref[...].astype(grad_ref.dtype)
+
+
+def run_place(spread, source, scalars, height, columns_all):
+    number, _, width, _ = spread.shape
+    wave_spec = pl.BlockSpec((1, 2, width, width), lambda i, *s: (i, 0, 0, 0))
+    grid_spec = pltpu.PrefetchScalarGridSpec(
+        num_scalar_prefetch=3,
+        grid=(number,),
+        in_specs=[wave_spec, wave_spec],
+        out_specs=pl.BlockSpec((2, height, columns_all), lambda i, *s: (0, 0, 0)),
+        scratch_shapes=[pltpu.VMEM((2, height, columns_all), jnp.float32)],
+    )
+    return pl.pallas_call(
+        place_kernel,
+        grid_spec=grid_spec,
+        out_shape=jax.ShapeDtypeStruct((2, height, columns_all), jnp.bfloat16),
+    )(*scalars[:3], spread, source)
 
 
 def first_kernel(rows_ref, columns_ref, order_ref, wave_ref, tile_ref, mine_ref, partner_ref,
@@ -574,11 +617,19 @@
         )
 
     def last_silent(incoming):
-        return (jnp.zeros_like(incoming), jnp.zeros((2, height, columns_all), jnp.bfloat16))
+        return (jnp.zeros_like(incoming), jnp.zeros_like(incoming))
 
     if depth_count > 1:
         carry = lax.ppermute(carry, "depth", [(depth_count - 2, depth_count - 1)])
-    carry, gradient = lax.cond(segment == depth_count - 1, last_pass, last_silent, carry)
+    arrived_last = carry
+    carry, spread_last = lax.cond(segment == depth_count - 1, last_pass, last_silent, carry)
+    gradient = lax.cond(
+        segment == depth_count - 1,
+        lambda s, a: run_place(s, a, scalars, height, columns_all),
+        lambda s, a: jnp.zeros((2, height, columns_all), jnp.bfloat16),
+        spread_last,
+        arrived_last,
+    )
 
     def back_pass(incoming, previous):
         return run_adjoint(

time: 59 us -> 58.4 us (0.990)
  waiting for transfers between devices: 30.4 us -> 29.6 us
    ppermute x1, waiting for transfers between devices: 13.9 us -> 13.2 us  [local(): carry = lax.ppermute(carry, 'depth', [(turn + 1, turn)])]
where the time goes in v19:
time: 58.4 us; the launch traced here: 58.1 us
  waiting for transfers between devices  29.6 us (51%)
  starting transfers between devices  9.21 us (16%)
  Pallas kernels  8.38 us (14%)
  other arithmetic  4.25 us (7%)
  between operations  4.04 us (7%)
  local copies, waits for them, and re-layouts  2.58 us (4%)
    ppermute x1, waiting for transfers between devices, local(): carry = lax.ppermute(carry, 'depth', [(turn + 1, turn)])  13.2 us
    ppermute x1, waiting for transfers between devices, local(): lax.ppermute(spill_sum, 'tile', [(t, t + 1) for t in range(tile_count - 1)])  5.75 us
    ppermute x1, waiting for transfers between devices, from_behind(): return lax.ppermute(block, axis, route)  4.48 us
    pallas_call x1, Pallas kernels, run_first(): pl.pallas_call(first_kernel, grid_spec=grid_spec, out_shape=jax.ShapeDtyp...  3.91 us
    ppermute x1, starting transfers between devices, local(): lax.ppermute(spill_sum, 'tile', [(t, t + 1) for t in range(tile_count - 1)])  3.65 us
    ppermute x1, waiting for transfers between devices, local(): carry = lax.ppermute(carry, 'depth', [(depth_count - 2, depth_count - 1)])  2.93 us
    pallas_call x1, Pallas kernels, run_adjoint(): pl.pallas_call(adjoint_kernel(last, number == 1, opening), grid_spec=grid...  2.87 us
    ppermute x1, starting transfers between devices, local(): carry = lax.ppermute(carry, 'depth', [(depth_count - 2, depth_count - 1)])  1.99 us
  transfers between devices with their start and end apart: 11, of which 7 were waited for; matrix products, arithmetic and copies ran while one was open for 9% of the time, Pallas kernels for 3%

profile of v19, /device:TPU:0, one launch (start us, length us, event | category | flops | bytes accessed | tf_op | source)
XLA Modules:
  0.0 58.1 jit_solution(6956817216030261030)
XLA Ops:
  0.0 0.5 collective-permute-start
  0.5 0.1 collective-permute-start.1
  0.5 1.1 %dynamic-slice_convert_fusion = bf16[1,2,256,256]{3,2,1,0:T(8,128)(2,1)S(1)} fusion(f32[1,2,256,512]{3,2,1,0:T(8,128)} %tile_ref.1, s32[]{:T(128)S(6)} %select_n.84), kind=kLoop, calls=%fused_computation.4 | loop fusion | bytes 524292 | tf_op jit(solution)/shard_map/convert_element_type | solution.py:551
  1.6 1.3 %collective-permute-start.2 = (bf16[1,2,256,256]{3,2,1,0:T(8,128)(2,1)S(1)}, bf16[1,2,256,256]{3,2,1,0:T(8,128)(2,1)S(1)}, u32[]{:S(2)}, u32[]{:S(2)}) collective-permute-start(bf16[1,2,256,256]{3,2,1,0:T(8,128)(2,1)S(1)} %dynamic-slice_convert_fusion), channel_id=1, source_target_pairs={{4,0},{8,4},{12,8},{5,1},{9,5},{13,9},{6,2},{10,6},{14,10},{7,3},{... | collective-permute-start | bytes 786440 | tf_op jit(solution)/shard_map/ppermute | solution.py:18
  2.9 1.1 %multiply_convert_fusion = (bf16[256,256]{1,0:T(8,128)(2,1)S(1)}, bf16[256,256]{1,0:T(8,128)(2,1)S(1)}) fusion(), kind=kLoop, calls=%fused_computation.13 | loop fusion | flops 1245184 | bytes 262144 | tf_op jit(solution)/shard_map/convert_element_type | solution.py:51
  4.0 1.0 %fusion.6 = (f32[1,256,256]{2,1,0:T(8,128)S(1)}, f32[1,256,256]{2,1,0:T(8,128)S(1)}) fusion(s32[256]{0:T(256)S(1)} %fusion.9, f32[]{:T(128)S(6)} %neg.8), kind=kLoop, calls=%fused_computation.19 | loop fusion | flops 196608 | bytes 525316 | tf_op jit(solution)/shard_map/cos | solution.py:61
  5.9 0.8 %broadcast_select_fusion = s32[2]{0:T(128)S(1)} fusion(pred[]{:T(512)} %eq.24, s32[1]{0:T(128)} %collective-permute-done.1, s32[1]{0:T(128)S(6)} %copy.16), kind=kLoop, calls=%fused_computation.30 | loop fusion | flops 6 | bytes 17 | tf_op jit(solution)/shard_map/jit(_where)/select_n | solution.py:564
  6.7 0.7 %fusion.12 = (s32[1]{0:T(128)}, s32[1]{0:T(128)}) fusion(s32[2]{0:T(128)S(1)} %broadcast_select_fusion), kind=kLoop, calls=%fused_computation.32 | loop fusion | bytes 16 | tf_op jit(solution)/shard_map/slice | solution.py:568
  8.5 4.5 %collective-permute-done.2.mine_ref = bf16[1,2,256,256]{3,2,1,0:T(8,128)(2,1)S(1)} collective-permute-done((bf16[1,2,256,256]{3,2,1,0:T(8,128)(2,1)S(1)}, bf16[1,2,256,256]{3,2,1,0:T(8,128)(2,1)S(1)}, u32[]{:S(2)}, u32[]{:S(2)}) %collective-permute-start.2) | collective-permute-done | bytes 262176 | tf_op jit(solution)/shard_map/ppermute | solution.py:18
  13.0 0.6 %fusion.13 = (s32[1,1]{1,0:T(1,128)}, s32[1,1]{1,0:T(1,128)}) fusion(s32[1,2]{1,0:T(1,128)S(1)} %constant_dynamic-slice_fusion), kind=kLoop, calls=%fused_computation.33 | loop fusion | bytes 16 | tf_op jit(solution)/shard_map/slice | solution.py:575
  14.3 0.2 collective-permute-done.3.partner_ref
  14.5 3.9 %conditional.4 = (bf16[1,2,256,256]{3,2,1,0:T(8,128)(2,1)}) conditional(s32[]{:T(128)} %convert_element_type.72, () %tuple.58, (s32[1]{0:T(128)}, s32[1]{0:T(128)}, s32[1]{0:T(128)}, bf16[1,2,256,256]{3,2,1,0:T(8,128)(2,1)S(1)}, f32[1,2,256,512]{3,2,1,0:T(8,128)S(1)}, /*index=5*/bf16[1,2,256,256]{3,2,1,0:T(8,128)(2,1)S(1)}, ...), branch_computations={%region_0.1_spmd, %region_1.2_spmd} | conditional | bytes 262154 | solution.py:606
  14.5 3.9 %branch_1_fun.6 = bf16[1,2,256,256]{3,2,1,0:T(8,128)(2,1)} custom-call(s32[1]{0:T(128)} %get-tuple-element.127.rows_ref, s32[1]{0:T(128)} %get-tuple-element.128.columns_ref, s32[1]{0:T(128)} %get-tuple-element.129.order_ref, bf16[1,2,256,256]{3,2,1,0:T(8,128)(2,1)S(1)} %get-tuple-element.130.wave_ref, f32[1,2,256,512]{3,2,1,0:T(8,128)S(1)} %get-tuple-element.131.tile_ref, ...), custom_call_target="tpu_custom_call" | custom-call | tf_op jit(solution)/shard_map/cond/branch_1_fun/pallas_call | solution.py:532
  18.4 0.3 collective-permute-start.5
  18.8 2.0 %collective-permute-start.4 = (bf16[1,2,256,256]{3,2,1,0:T(8,128)(2,1)}, bf16[1,2,256,256]{3,2,1,0:T(8,128)(2,1)}, u32[]{:S(2)}, u32[]{:S(2)}) collective-permute-start(bf16[1,2,256,256]{3,2,1,0:T(8,128)(2,1)} %get-tuple-element.197), channel_id=1, source_target_pairs={{0,2},{1,3},{4,6},{5,7},{8,10},{9,11},{12,14},{13,15},{16,18},{17,... | collective-permute-start | bytes 786440 | tf_op jit(solution)/shard_map/ppermute | solution.py:623
  22.0 1.6 %shard_map.60 = f32[1,2,256,256]{3,2,1,0:T(8,128)S(1)} custom-call(s32[1]{0:T(128)} %sub.17.rows_ref, s32[1]{0:T(128)} %bitcast.4.columns_ref, s32[1]{0:T(128)} %bitcast.order_ref, f32[1,2,256,512]{3,2,1,0:T(8,128)S(1)} %copy-done, bf16[1,2,256,256]{3,2,1,0:T(8,128)(2,1)S(1)} %collective-permute-done.2.mine_ref, ...), custom_call_target="tpu_custom_call" | custom-call | tf_op jit(solution)/shard_map/pallas_call | solution.py:275
  23.6 2.9 %collective-permute-done.4 = bf16[1,2,256,256]{3,2,1,0:T(8,128)(2,1)} collective-permute-done((bf16[1,2,256,256]{3,2,1,0:T(8,128)(2,1)}, bf16[1,2,256,256]{3,2,1,0:T(8,128)(2,1)}, u32[]{:S(2)}, u32[]{:S(2)}) %collective-permute-start.4) | collective-permute-done | bytes 262176 | tf_op jit(solution)/shard_map/ppermute | solution.py:623
  26.6 1.3 %collective-permute-start.6 = (bf16[1,2,256,256]{3,2,1,0:T(8,128)(2,1)S(1)}, bf16[1,2,256,256]{3,2,1,0:T(8,128)(2,1)S(1)}, u32[]{:S(2)}, u32[]{:S(2)}) collective-permute-start(bf16[1,2,256,256]{3,2,1,0:T(8,128)(2,1)S(1)} %get-tuple-element.171), channel_id=1, source_target_pairs={{2,0},{3,1},{6,4},{7,5},{10,8},{11,9},{14,12},{15,13},{18,16},{19,... | collective-permute-start | bytes 786440 | tf_op jit(solution)/shard_map/ppermute | solution.py:650
  27.9 0.1 conditional.6
  27.9 0.1 broadcast.198
  28.0 13.2 %collective-permute-done.6 = bf16[1,2,256,256]{3,2,1,0:T(8,128)(2,1)S(1)} collective-permute-done((bf16[1,2,256,256]{3,2,1,0:T(8,128)(2,1)S(1)}, bf16[1,2,256,256]{3,2,1,0:T(8,128)(2,1)S(1)}, u32[]{:S(2)}, u32[]{:S(2)}) %collective-permute-start.6) | collective-permute-done | bytes 262176 | tf_op jit(solution)/shard_map/ppermute | solution.py:650
  41.2 2.9 %conditional.7 = (bf16[2,512,512]{2,1,0:T(8,128)(2,1)S(1)}) conditional(s32[]{:T(128)} %convert_element_type.72, bf16[2,512,512]{2,1,0:T(8,128)(2,1)S(1)} %get-tuple-element.199, (s32[1]{0:T(128)}, s32[1]{0:T(128)}, s32[1]{0:T(128)}, s32[1]{0:T(128)}, s32[1]{0:T(128)}, /*index=5*/bf16[1,2,256,256]{3,2,1,0:T(8,128)(2,1)S(1)}, ...), branch_computations={%region_6.7_spmd, %region_7.8_spmd} | conditional | bytes 8 | solution.py:652
  41.2 2.9 %branch_1_fun.9 = bf16[2,512,512]{2,1,0:T(8,128)(2,1)S(1)} custom-call(s32[1]{0:T(128)} %get-tuple-element.154.rows_ref, s32[1]{0:T(128)} %get-tuple-element.155.columns_ref, s32[1]{0:T(128)} %get-tuple-element.156.live_ref, s32[1]{0:T(128)} %get-tuple-element.157.slot_ref, s32[1]{0:T(128)} %get-tuple-element.158.other_ref, ...), custom_call_target="tpu_custom_call" | custom-call | tf_op jit(solution)/shard_map/cond/branch_1_fun/pallas_call | solution.py:439
  44.1 0.1 fusion.11
  44.2 0.1 collective-permute-start.8
  44.3 1.5 %collective-permute-done.8 = bf16[2,256,256]{2,1,0:T(8,128)(2,1)S(1)} collective-permute-done((bf16[2,256,256]{2,1,0:T(8,128)(2,1)S(1)}, bf16[2,256,256]{2,1,0:T(8,128)(2,1)S(1)}, u32[]{:S(2)}, u32[]{:S(2)}) %collective-permute-start.8) | collective-permute-done | bytes 262176 | tf_op jit(solution)/shard_map/ppermute | solution.py:658
  45.8 0.1 add_convert_fusion
  45.9 3.7 %collective-permute-start.9 = (bf16[2,256,256]{2,1,0:T(8,128)(2,1)S(1)}, bf16[2,256,256]{2,1,0:T(8,128)(2,1)S(1)}, u32[]{:S(2)}, u32[]{:S(2)}) collective-permute-start(bf16[2,256,256]{2,1,0:T(8,128)(2,1)S(1)} %add_convert_fusion), channel_id=1, source_target_pairs={{0,4},{4,8},{8,12},{1,5},{5,9},{9,13},{2,6},{6,10},{10,14},{3,7},{... | collective-permute-start | bytes 786440 | tf_op jit(solution)/shard_map/ppermute | solution.py:660
  49.5 0.1 collective-permute-start.7
  49.6 5.8 %collective-permute-done.9 = bf16[2,256,256]{2,1,0:T(8,128)(2,1)S(1)} collective-permute-done((bf16[2,256,256]{2,1,0:T(8,128)(2,1)S(1)}, bf16[2,256,256]{2,1,0:T(8,128)(2,1)S(1)}, u32[]{:S(2)}, u32[]{:S(2)}) %collective-permute-start.9) | collective-permute-done | bytes 262176 | tf_op jit(solution)/shard_map/ppermute | solution.py:660
  55.4 1.5 %collective-permute-done.10 = bf16[2,256,256]{2,1,0:T(8,128)(2,1)S(1)} collective-permute-done((bf16[2,256,256]{2,1,0:T(8,128)(2,1)S(1)}, bf16[2,256,256]{2,1,0:T(8,128)(2,1)S(1)}, u32[]{:S(2)}, u32[]{:S(2)}) %collective-permute-start.10) | collective-permute-done | bytes 262176 | tf_op jit(solution)/shard_map/ppermute | solution.py:663
  56.9 1.2 %add_bitcast_fusion = f32[1,2,256,512]{3,2,1,0:T(8,128)} fusion(bf16[2,256,512]{2,1,0:T(8,128)(2,1)S(1)} %collective-permute-done.7, bf16[2,256,256]{2,1,0:T(8,128)(2,1)S(1)} %collective-permute-done.10, bf16[2,256,256]{2,1,0:T(8,128)(2,1)S(1)} %collective-permute-done.9, pred[]{:T(512)} %eq.24, bf16[2,512,512]{2,1,0:T(8,128)(2,1)S(1)} %get-tuple-element.200), kind=kLoop, calls=%fused_computation | loop fusion | flops 3670016 | bytes 2621441 | tf_op jit(solution)/shard_map/broadcast_in_dim | solution.py:671
  (22 shorter events, 0.3 us)
Async XLA Ops:
  0.0 13.0 %collective-permute-start = (s32[2,2]{1,0:T(2,128)}, s32[2,2]{1,0:T(2,128)S(1)}, u32[]{:S(2)}, u32[]{:S(2)}) collective-permute-start(s32[2,2]{1,0:T(2,128)} %param.19), channel_id=1, source_target_pairs={{0,1},{1,0},{2,3},{3,2},{4,5},{5,4},{6,7},{7,6},{8,9},{9,8},{10,11... | collective-permute-start | bytes 56 | tf_op jit(solution)/shard_map/ppermute | solution.py:557
  0.5 5.4 %collective-permute-start.1 = (s32[1]{0:T(128)}, s32[1]{0:T(128)}, u32[]{:S(2)}, u32[]{:S(2)}) collective-permute-start(s32[1]{0:T(128)} %param.20), channel_id=1, source_target_pairs={{0,1},{1,0},{2,3},{3,2},{4,5},{5,4},{6,7},{7,6},{8,9},{9,8},{10,11... | collective-permute-start | bytes 20 | tf_op jit(solution)/shard_map/ppermute | solution.py:558
  1.6 11.4 %collective-permute-start.2 = (bf16[1,2,256,256]{3,2,1,0:T(8,128)(2,1)S(1)}, bf16[1,2,256,256]{3,2,1,0:T(8,128)(2,1)S(1)}, u32[]{:S(2)}, u32[]{:S(2)}) collective-permute-start(bf16[1,2,256,256]{3,2,1,0:T(8,128)(2,1)S(1)} %dynamic-slice_convert_fusion), channel_id=1, source_target_pairs={{4,0},{8,4},{12,8},{5,1},{9,5},{13,9},{6,2},{10,6},{14,10},{7,3},{... | collective-permute-start | bytes 786440 | tf_op jit(solution)/shard_map/ppermute | solution.py:18
  5.0 9.5 %copy-start = (f32[1,2,256,512]{3,2,1,0:T(8,128)S(1)}, f32[1,2,256,512]{3,2,1,0:T(8,128)}, u32[]{:S(2)}) copy-start(f32[1,2,256,512]{3,2,1,0:T(8,128)} %tile_ref.1) | copy-start | bytes 3145732
  5.1 9.4 %copy-start.1 = (bf16[2,256,256]{2,1,0:T(8,128)(2,1)S(1)}, bf16[2,256,256]{2,1,0:T(8,128)(2,1)}, u32[]{:S(2)}) copy-start(bf16[2,256,256]{2,1,0:T(8,128)(2,1)} %param.18) | copy-start | bytes 786436
  8.5 4.5 %copy-start.2 = (s32[2,2]{1,0:T(2,128)S(1)}, s32[2,2]{1,0:T(2,128)}, u32[]{:S(2)}) copy-start(s32[2,2]{1,0:T(2,128)} %param.19) | copy-start | bytes 52
  13.0 1.5 %collective-permute-start.3 = (bf16[1,2,256,256]{3,2,1,0:T(8,128)(2,1)S(1)}, bf16[1,2,256,256]{3,2,1,0:T(8,128)(2,1)S(1)}, u32[]{:S(2)}, u32[]{:S(2)}) collective-permute-start(bf16[1,2,256,256]{3,2,1,0:T(8,128)(2,1)S(1)} %collective-permute-done.2.mine_ref), channel_id=1, source_target_pairs={{0,1},{1,0},{2,3},{3,2},{4,5},{5,4},{6,7},{7,6},{8,9},{9,8},{10,11... | collective-permute-start | bytes 786440 | tf_op jit(solution)/shard_map/ppermute | solution.py:553
  18.4 8.1 %collective-permute-start.5 = (f32[2,256,256]{2,1,0:T(8,128)}, f32[2,256,256]{2,1,0:T(8,128)}, u32[]{:S(2)}, u32[]{:S(2)}) collective-permute-start(f32[2,256,256]{2,1,0:T(8,128)} %param.21), channel_id=1, source_target_pairs={{0,1},{1,0},{2,3},{3,2},{4,5},{5,4},{6,7},{7,6},{8,9},{9,8},{10,11... | collective-permute-start | bytes 1572872 | tf_op jit(solution)/shard_map/ppermute | solution.py:609
  18.8 7.8 %collective-permute-start.4 = (bf16[1,2,256,256]{3,2,1,0:T(8,128)(2,1)}, bf16[1,2,256,256]{3,2,1,0:T(8,128)(2,1)}, u32[]{:S(2)}, u32[]{:S(2)}) collective-permute-start(bf16[1,2,256,256]{3,2,1,0:T(8,128)(2,1)} %get-tuple-element.197), channel_id=1, source_target_pairs={{0,2},{1,3},{4,6},{5,7},{8,10},{9,11},{12,14},{13,15},{16,18},{17,... | collective-permute-start | bytes 786440 | tf_op jit(solution)/shard_map/ppermute | solution.py:623
  26.6 14.6 %collective-permute-start.6 = (bf16[1,2,256,256]{3,2,1,0:T(8,128)(2,1)S(1)}, bf16[1,2,256,256]{3,2,1,0:T(8,128)(2,1)S(1)}, u32[]{:S(2)}, u32[]{:S(2)}) collective-permute-start(bf16[1,2,256,256]{3,2,1,0:T(8,128)(2,1)S(1)} %get-tuple-element.171), channel_id=1, source_target_pairs={{2,0},{3,1},{6,4},{7,5},{10,8},{11,9},{14,12},{15,13},{18,16},{19,... | collective-permute-start | bytes 786440 | tf_op jit(solution)/shard_map/ppermute | solution.py:650
  44.2 1.6 %collective-permute-start.8 = (bf16[2,256,256]{2,1,0:T(8,128)(2,1)S(1)}, bf16[2,256,256]{2,1,0:T(8,128)(2,1)S(1)}, u32[]{:S(2)}, u32[]{:S(2)}) collective-permute-start(bf16[2,256,256]{2,1,0:T(8,128)(2,1)S(1)} %constant_dynamic-slice_fusion.1), channel_id=1, source_target_pairs={{0,1},{1,0},{2,3},{3,2},{4,5},{5,4},{6,7},{7,6},{8,9},{9,8},{10,11... | collective-permute-start | bytes 786440 | tf_op jit(solution)/shard_map/ppermute | solution.py:658
  45.9 9.5 %collective-permute-start.9 = (bf16[2,256,256]{2,1,0:T(8,128)(2,1)S(1)}, bf16[2,256,256]{2,1,0:T(8,128)(2,1)S(1)}, u32[]{:S(2)}, u32[]{:S(2)}) collective-permute-start(bf16[2,256,256]{2,1,0:T(8,128)(2,1)S(1)} %add_convert_fusion), channel_id=1, source_target_pairs={{0,4},{4,8},{8,12},{1,5},{5,9},{9,13},{2,6},{6,10},{10,14},{3,7},{... | collective-permute-start | bytes 786440 | tf_op jit(solution)/shard_map/ppermute | solution.py:660
  49.5 5.8 %collective-permute-start.7 = (bf16[2,256,512]{2,1,0:T(8,128)(2,1)S(1)}, bf16[2,256,512]{2,1,0:T(8,128)(2,1)S(1)}, u32[]{:S(2)}, u32[]{:S(2)}) collective-permute-start(bf16[2,256,512]{2,1,0:T(8,128)(2,1)S(1)} %get-tuple-element.184), channel_id=1, source_target_pairs={{0,1},{1,0},{2,3},{3,2},{4,5},{5,4},{6,7},{7,6},{8,9},{9,8},{10,11... | collective-permute-start | bytes 1572872 | tf_op jit(solution)/shard_map/ppermute | solution.py:662
  55.3 1.5 %collective-permute-start.10 = (bf16[2,256,256]{2,1,0:T(8,128)(2,1)S(1)}, bf16[2,256,256]{2,1,0:T(8,128)(2,1)S(1)}, u32[]{:S(2)}, u32[]{:S(2)}) collective-permute-start(bf16[2,256,256]{2,1,0:T(8,128)(2,1)S(1)} %collective-permute-done.9), channel_id=1, source_target_pairs={{0,1},{1,0},{2,3},{3,2},{4,5},{5,4},{6,7},{7,6},{8,9},{9,8},{10,11... | collective-permute-start | bytes 786440 | tf_op jit(solution)/shard_map/ppermute | solution.py:663

commit v20 on v19

--- a/solution.py
+++ b/solution.py
@@ -536,6 +536,11 @@
     )(rows, columns, order, waves, tile, mine, partner, chirps, *blocks)
 
 
+def hop(block, axis, route):
+    parts = [lax.ppermute(block[:, k], axis, route) for k in range(block.shape[1])]
+    return jnp.stack(parts, axis=1)
+
+
 def local(object_field, probe, positions, counts, measured):
     width = probe.shape[1]
     tile_rows = object_field.shape[2]
@@ -601,7 +606,7 @@
     inputs = start
     for turn in range(depth_count - 1):
         if turn > 0:
-            carry = lax.ppermute(carry, "depth", [(turn - 1, turn)])
+            carry = hop(carry, "depth", [(turn - 1, turn)])
             inputs = jnp.where(segment == turn, carry, inputs)
         carry = lax.cond(segment == turn, forward_all, silent, carry)
 
@@ -620,7 +625,7 @@
         return (jnp.zeros_like(incoming), jnp.zeros_like(incoming))
 
     if depth_count > 1:
-        carry = lax.ppermute(carry, "depth", [(depth_count - 2, depth_count - 1)])
+        carry = hop(carry, "depth", [(depth_count - 2, depth_count - 1)])
     arrived_last = carry
     carry, spread_last = lax.cond(segment == depth_count - 1, last_pass, last_silent, carry)
     gradient = lax.cond(
@@ -647,7 +652,7 @@
         return (jnp.zeros_like(incoming), previous)
 
     for turn in reversed(range(depth_count - 1)):
-        carry = lax.ppermute(carry, "depth", [(turn + 1, turn)])
+        carry = hop(carry, "depth", [(turn + 1, turn)])
         step = opening_pass if turn == 0 else back_pass
         carry, gradient = lax.cond(segment == turn, step, back_silent, carry, gradient)
 

time: 58.4 us -> 59.5 us (1.019)
  waiting for transfers between devices: 29.6 us -> 26 us
  starting transfers between devices: 9.21 us -> 12.5 us
  other arithmetic: 4.25 us -> 5.24 us
  local copies, waits for them, and re-layouts: 2.58 us -> 3.31 us
  Pallas kernels: 8.38 us -> 7.69 us
    ppermute x2 -> x4, waiting for transfers between devices: 16.1 us -> 12.6 us  [hop(): lax.ppermute(block[:, k], axis, route)]
    ppermute x2 -> x4, starting transfers between devices: 3.28 us -> 6.47 us  [hop(): lax.ppermute(block[:, k], axis, route)]
    another operation x0 -> x2, other arithmetic: none -> 1.02 us  [hop(): return jnp.stack(parts, axis=1)]
    pallas_call x1, Pallas kernels: 3.91 us -> 3.21 us  [run_first(): pl.pallas_call(first_kernel, grid_spec=grid_spec, out_shape=jax.ShapeDtyp...]
    squeeze x0 -> x2, local copies, waits for them, and re-layouts: none -> 0.69 us  [hop(): block[:, k]]
  transfers between devices with their start and end apart: 11 -> 13, of which waited for: 7 -> 8; matrix products, arithmetic and copies ran while one was open for 9% -> 12% of each run, Pallas kernels for 3% -> 3%
where the time goes in v20:
time: 59.5 us; the launch traced here: 59.1 us
  waiting for transfers between devices  26 us (44%)
  starting transfers between devices  12.5 us (21%)
  Pallas kernels  7.69 us (13%)
  other arithmetic  5.24 us (9%)
  between operations  4.27 us (7%)
  local copies, waits for them, and re-layouts  3.31 us (6%)
    ppermute x4, waiting for transfers between devices, hop(): lax.ppermute(block[:, k], axis, route)  12.6 us
    ppermute x4, starting transfers between devices, hop(): lax.ppermute(block[:, k], axis, route)  6.47 us
    ppermute x1, waiting for transfers between devices, local(): lax.ppermute(spill_sum, 'tile', [(t, t + 1) for t in range(tile_count - 1)])  5.75 us
    ppermute x1, waiting for transfers between devices, from_behind(): return lax.ppermute(block, axis, route)  4.41 us
    ppermute x1, starting transfers between devices, local(): lax.ppermute(spill_sum, 'tile', [(t, t + 1) for t in range(tile_count - 1)])  3.65 us
    pallas_call x1, Pallas kernels, run_first(): pl.pallas_call(first_kernel, grid_spec=grid_spec, out_shape=jax.ShapeDtyp...  3.21 us
    pallas_call x1, Pallas kernels, run_adjoint(): pl.pallas_call(adjoint_kernel(last, number == 1, opening), grid_spec=grid...  2.87 us
    pallas_call x1, Pallas kernels, cut_patches(): pl.pallas_call(cut_kernel, grid_spec=grid_spec, out_shape=jax.ShapeDtypeS...  1.6 us
  transfers between devices with their start and end apart: 13, of which 8 were waited for; matrix products, arithmetic and copies ran while one was open for 12% of the time, Pallas kernels for 3%

profile of v20, /device:TPU:0, one launch (start us, length us, event | category | flops | bytes accessed | tf_op | source)
XLA Modules:
  0.0 59.1 jit_solution(5937432108491623361)
XLA Ops:
  0.0 0.5 collective-permute-start
  0.5 1.1 %dynamic-slice_convert_fusion = bf16[1,2,256,256]{3,2,1,0:T(8,128)(2,1)S(1)} fusion(f32[1,2,256,512]{3,2,1,0:T(8,128)} %tile_ref.1, s32[]{:T(128)S(6)} %select_n.84), kind=kLoop, calls=%fused_computation.4 | loop fusion | bytes 524292 | tf_op jit(solution)/shard_map/convert_element_type | solution.py:556
  1.6 1.3 %collective-permute-start.2 = (bf16[1,2,256,256]{3,2,1,0:T(8,128)(2,1)S(1)}, bf16[1,2,256,256]{3,2,1,0:T(8,128)(2,1)S(1)}, u32[]{:S(2)}, u32[]{:S(2)}) collective-permute-start(bf16[1,2,256,256]{3,2,1,0:T(8,128)(2,1)S(1)} %dynamic-slice_convert_fusion), channel_id=1, source_target_pairs={{4,0},{8,4},{12,8},{5,1},{9,5},{13,9},{6,2},{10,6},{14,10},{7,3},{... | collective-permute-start | bytes 786440 | tf_op jit(solution)/shard_map/ppermute | solution.py:18
  2.9 1.1 %multiply_convert_fusion = (bf16[256,256]{1,0:T(8,128)(2,1)S(1)}, bf16[256,256]{1,0:T(8,128)(2,1)S(1)}) fusion(), kind=kLoop, calls=%fused_computation.15 | loop fusion | flops 1245184 | bytes 262144 | tf_op jit(solution)/shard_map/convert_element_type | solution.py:51
  4.0 1.0 %fusion.6 = (f32[1,256,256]{2,1,0:T(8,128)S(1)}, f32[1,256,256]{2,1,0:T(8,128)S(1)}) fusion(s32[256]{0:T(256)S(1)} %fusion.9, f32[]{:T(128)S(6)} %neg.8), kind=kLoop, calls=%fused_computation.21 | loop fusion | flops 196608 | bytes 525316 | tf_op jit(solution)/shard_map/cos | solution.py:61
  5.9 0.7 %broadcast_select_fusion = s32[2]{0:T(128)S(1)} fusion(pred[]{:T(512)} %eq.24, s32[1]{0:T(128)} %collective-permute-done.1, s32[1]{0:T(128)S(6)} %copy.16), kind=kLoop, calls=%fused_computation.36 | loop fusion | flops 6 | bytes 17 | tf_op jit(solution)/shard_map/jit(_where)/select_n | solution.py:569
  6.6 0.7 %fusion.12 = (s32[1]{0:T(128)}, s32[1]{0:T(128)}) fusion(s32[2]{0:T(128)S(1)} %broadcast_select_fusion), kind=kLoop, calls=%fused_computation.38 | loop fusion | bytes 16 | tf_op jit(solution)/shard_map/slice | solution.py:573
  8.6 4.4 %collective-permute-done.2.mine_ref = bf16[1,2,256,256]{3,2,1,0:T(8,128)(2,1)S(1)} collective-permute-done((bf16[1,2,256,256]{3,2,1,0:T(8,128)(2,1)S(1)}, bf16[1,2,256,256]{3,2,1,0:T(8,128)(2,1)S(1)}, u32[]{:S(2)}, u32[]{:S(2)}) %collective-permute-start.2) | collective-permute-done | bytes 262176 | tf_op jit(solution)/shard_map/ppermute | solution.py:18
  13.0 0.7 %fusion.13 = (s32[1,1]{1,0:T(1,128)}, s32[1,1]{1,0:T(1,128)}) fusion(s32[1,2]{1,0:T(1,128)S(1)} %constant_dynamic-slice_fusion), kind=kLoop, calls=%fused_computation.39 | loop fusion | bytes 16 | tf_op jit(solution)/shard_map/slice | solution.py:580
  14.3 0.2 collective-permute-done.3.partner_ref
  14.5 3.2 %conditional.4 = (bf16[1,2,256,256]{3,2,1,0:T(8,128)(2,1)S(1)}) conditional(s32[]{:T(128)} %convert_element_type.72, () %tuple.58, (s32[1]{0:T(128)}, s32[1]{0:T(128)}, s32[1]{0:T(128)}, bf16[1,2,256,256]{3,2,1,0:T(8,128)(2,1)S(1)}, f32[1,2,256,512]{3,2,1,0:T(8,128)S(1)}, /*index=5*/bf16[1,2,256,256]{3,2,1,0:T(8,128)(2,1)S(1)}, ...), branch_computations={%region_0.1_spmd, %region_1.2_spmd} | conditional | bytes 262154 | solution.py:611
  14.5 3.2 %branch_1_fun.6 = bf16[1,2,256,256]{3,2,1,0:T(8,128)(2,1)S(1)} custom-call(s32[1]{0:T(128)} %get-tuple-element.127.rows_ref, s32[1]{0:T(128)} %get-tuple-element.128.columns_ref, s32[1]{0:T(128)} %get-tuple-element.129.order_ref, bf16[1,2,256,256]{3,2,1,0:T(8,128)(2,1)S(1)} %get-tuple-element.130.wave_ref, ...), custom_call_target="tpu_custom_call" | custom-call | tf_op jit(solution)/shard_map/cond/branch_1_fun/pallas_call | solution.py:532
  17.7 0.4 collective-permute-start.6
  18.2 0.7 %slice_bitcast_fusion.3 = (bf16[1,256,256]{2,1,0:T(8,128)(2,1)S(1)}, bf16[1,256,256]{2,1,0:T(8,128)(2,1)}) fusion(bf16[1,2,256,256]{3,2,1,0:T(8,128)(2,1)S(1)} %get-tuple-element.201), kind=kLoop, calls=%fused_computation.26 | loop fusion | bytes 524288 | tf_op jit(solution)/shard_map/squeeze | solution.py:540
  18.8 1.9 %collective-permute-start.5 = (bf16[1,256,256]{2,1,0:T(8,128)(2,1)}, bf16[1,256,256]{2,1,0:T(8,128)(2,1)}, u32[]{:S(2)}, u32[]{:S(2)}) collective-permute-start(bf16[1,256,256]{2,1,0:T(8,128)(2,1)} %get-tuple-element.188), channel_id=1, source_target_pairs={{0,2},{1,3},{4,6},{5,7},{8,10},{9,11},{12,14},{13,15},{16,18},{17,... | collective-permute-start | bytes 393224 | tf_op jit(solution)/shard_map/ppermute | solution.py:540
  20.8 1.9 %collective-permute-start.4 = (bf16[1,256,256]{2,1,0:T(8,128)(2,1)S(1)}, bf16[1,256,256]{2,1,0:T(8,128)(2,1)}, u32[]{:S(2)}, u32[]{:S(2)}) collective-permute-start(bf16[1,256,256]{2,1,0:T(8,128)(2,1)S(1)} %get-tuple-element.187), channel_id=1, source_target_pairs={{0,2},{1,3},{4,6},{5,7},{8,10},{9,11},{12,14},{13,15},{16,18},{17,... | collective-permute-start | bytes 393224 | tf_op jit(solution)/shard_map/ppermute | solution.py:540
  24.0 1.6 %shard_map.60 = f32[1,2,256,256]{3,2,1,0:T(8,128)S(1)} custom-call(s32[1]{0:T(128)} %sub.17.rows_ref, s32[1]{0:T(128)} %bitcast.4.columns_ref, s32[1]{0:T(128)} %bitcast.order_ref, f32[1,2,256,512]{3,2,1,0:T(8,128)S(1)} %copy-done, bf16[1,2,256,256]{3,2,1,0:T(8,128)(2,1)S(1)} %collective-permute-done.2.mine_ref, ...), custom_call_target="tpu_custom_call" | custom-call | tf_op jit(solution)/shard_map/pallas_call | solution.py:275
  25.7 0.8 %collective-permute-done.4 = bf16[1,256,256]{2,1,0:T(8,128)(2,1)} collective-permute-done((bf16[1,256,256]{2,1,0:T(8,128)(2,1)S(1)}, bf16[1,256,256]{2,1,0:T(8,128)(2,1)}, u32[]{:S(2)}, u32[]{:S(2)}) %collective-permute-start.4) | collective-permute-done | bytes 131104 | tf_op jit(solution)/shard_map/ppermute | solution.py:540
  26.5 1.0 %pad_maximum_fusion.3 = bf16[1,2,256,256]{3,2,1,0:T(8,128)(2,1)S(1)} fusion(bf16[1,1,256,256]{3,2,1,0:T(8,128)(2,1)} %bitcast.10, bf16[1,1,256,256]{3,2,1,0:T(8,128)(2,1)} %bitcast.8), kind=kLoop, calls=%fused_computation.13 | loop fusion | flops 131072 | bytes 524288 | tf_op jit(solution)/shard_map/stack | solution.py:541
  27.6 1.3 %collective-permute-start.8 = (bf16[1,256,256]{2,1,0:T(8,128)(2,1)S(1)}, bf16[1,256,256]{2,1,0:T(8,128)(2,1)S(1)}, u32[]{:S(2)}, u32[]{:S(2)}) collective-permute-start(bf16[1,256,256]{2,1,0:T(8,128)(2,1)S(1)} %get-tuple-element.186), channel_id=1, source_target_pairs={{2,0},{3,1},{6,4},{7,5},{10,8},{11,9},{14,12},{15,13},{18,16},{19,... | collective-permute-start | bytes 393224 | tf_op jit(solution)/shard_map/ppermute | solution.py:540
  28.9 1.3 %collective-permute-start.7 = (bf16[1,256,256]{2,1,0:T(8,128)(2,1)S(1)}, bf16[1,256,256]{2,1,0:T(8,128)(2,1)S(1)}, u32[]{:S(2)}, u32[]{:S(2)}) collective-permute-start(bf16[1,256,256]{2,1,0:T(8,128)(2,1)S(1)} %get-tuple-element.185), channel_id=1, source_target_pairs={{2,0},{3,1},{6,4},{7,5},{10,8},{11,9},{14,12},{15,13},{18,16},{19,... | collective-permute-start | bytes 393224 | tf_op jit(solution)/shard_map/ppermute | solution.py:540
  30.2 0.1 conditional.6
  30.2 0.1 broadcast.198
  30.3 10.0 %collective-permute-done.8 = bf16[1,256,256]{2,1,0:T(8,128)(2,1)S(1)} collective-permute-done((bf16[1,256,256]{2,1,0:T(8,128)(2,1)S(1)}, bf16[1,256,256]{2,1,0:T(8,128)(2,1)S(1)}, u32[]{:S(2)}, u32[]{:S(2)}) %collective-permute-start.8) | collective-permute-done | bytes 131104 | tf_op jit(solution)/shard_map/ppermute | solution.py:540
  40.3 1.8 %collective-permute-done.7 = bf16[1,256,256]{2,1,0:T(8,128)(2,1)S(1)} collective-permute-done((bf16[1,256,256]{2,1,0:T(8,128)(2,1)S(1)}, bf16[1,256,256]{2,1,0:T(8,128)(2,1)S(1)}, u32[]{:S(2)}, u32[]{:S(2)}) %collective-permute-start.7) | collective-permute-done | bytes 131104 | tf_op jit(solution)/shard_map/ppermute | solution.py:540
  42.1 2.9 %conditional.7 = (bf16[2,512,512]{2,1,0:T(8,128)(2,1)S(1)}) conditional(s32[]{:T(128)} %convert_element_type.72, bf16[2,512,512]{2,1,0:T(8,128)(2,1)S(1)} %get-tuple-element.203, (s32[1]{0:T(128)}, s32[1]{0:T(128)}, s32[1]{0:T(128)}, s32[1]{0:T(128)}, s32[1]{0:T(128)}, /*index=5*/bf16[1,2,256,256]{3,2,1,0:T(8,128)(2,1)S(1)}, ...), branch_computations={%region_6.7_spmd, %region_7.8_spmd} | conditional | bytes 8 | solution.py:657
  42.1 2.9 %branch_1_fun.9 = bf16[2,512,512]{2,1,0:T(8,128)(2,1)S(1)} custom-call(s32[1]{0:T(128)} %get-tuple-element.154.rows_ref, s32[1]{0:T(128)} %get-tuple-element.155.columns_ref, s32[1]{0:T(128)} %get-tuple-element.156.live_ref, s32[1]{0:T(128)} %get-tuple-element.157.slot_ref, s32[1]{0:T(128)} %get-tuple-element.158.other_ref, ...), custom_call_target="tpu_custom_call" | custom-call | tf_op jit(solution)/shard_map/cond/branch_1_fun/pallas_call | solution.py:439
  45.2 1.5 %collective-permute-done.10 = bf16[2,256,256]{2,1,0:T(8,128)(2,1)S(1)} collective-permute-done((bf16[2,256,256]{2,1,0:T(8,128)(2,1)S(1)}, bf16[2,256,256]{2,1,0:T(8,128)(2,1)S(1)}, u32[]{:S(2)}, u32[]{:S(2)}) %collective-permute-start.10) | collective-permute-done | bytes 262176 | tf_op jit(solution)/shard_map/ppermute | solution.py:663
  46.8 3.7 %collective-permute-start.11 = (bf16[2,256,256]{2,1,0:T(8,128)(2,1)S(1)}, bf16[2,256,256]{2,1,0:T(8,128)(2,1)S(1)}, u32[]{:S(2)}, u32[]{:S(2)}) collective-permute-start(bf16[2,256,256]{2,1,0:T(8,128)(2,1)S(1)} %add_convert_fusion), channel_id=1, source_target_pairs={{0,4},{4,8},{8,12},{1,5},{5,9},{9,13},{2,6},{6,10},{10,14},{3,7},{... | collective-permute-start | bytes 786440 | tf_op jit(solution)/shard_map/ppermute | solution.py:665
  50.6 5.8 %collective-permute-done.11 = bf16[2,256,256]{2,1,0:T(8,128)(2,1)S(1)} collective-permute-done((bf16[2,256,256]{2,1,0:T(8,128)(2,1)S(1)}, bf16[2,256,256]{2,1,0:T(8,128)(2,1)S(1)}, u32[]{:S(2)}, u32[]{:S(2)}) %collective-permute-start.11) | collective-permute-done | bytes 262176 | tf_op jit(solution)/shard_map/ppermute | solution.py:665
  56.3 1.5 %collective-permute-done.12 = bf16[2,256,256]{2,1,0:T(8,128)(2,1)S(1)} collective-permute-done((bf16[2,256,256]{2,1,0:T(8,128)(2,1)S(1)}, bf16[2,256,256]{2,1,0:T(8,128)(2,1)S(1)}, u32[]{:S(2)}, u32[]{:S(2)}) %collective-permute-start.12) | collective-permute-done | bytes 262176 | tf_op jit(solution)/shard_map/ppermute | solution.py:668
  57.8 1.2 %add_bitcast_fusion = f32[1,2,256,512]{3,2,1,0:T(8,128)} fusion(bf16[2,256,512]{2,1,0:T(8,128)(2,1)S(1)} %collective-permute-done.9, bf16[2,256,256]{2,1,0:T(8,128)(2,1)S(1)} %collective-permute-done.12, bf16[2,256,256]{2,1,0:T(8,128)(2,1)S(1)} %collective-permute-done.11, pred[]{:T(512)} %eq.24, bf16[2,512,512]{2,1,0:T(8,128)(2,1)S(1)} %get-tuple-element.204), kind=kLoop, calls=%fused_computation | loop fusion | flops 3670016 | bytes 2621441 | tf_op jit(solution)/shard_map/broadcast_in_dim | solution.py:676
  (32 shorter events, 0.7 us)
Async XLA Ops:
  0.0 13.0 %collective-permute-start = (s32[2,2]{1,0:T(2,128)}, s32[2,2]{1,0:T(2,128)S(1)}, u32[]{:S(2)}, u32[]{:S(2)}) collective-permute-start(s32[2,2]{1,0:T(2,128)} %param.19), channel_id=1, source_target_pairs={{0,1},{1,0},{2,3},{3,2},{4,5},{5,4},{6,7},{7,6},{8,9},{9,8},{10,11... | collective-permute-start | bytes 56 | tf_op jit(solution)/shard_map/ppermute | solution.py:562
  0.5 5.4 %collective-permute-start.1 = (s32[1]{0:T(128)}, s32[1]{0:T(128)}, u32[]{:S(2)}, u32[]{:S(2)}) collective-permute-start(s32[1]{0:T(128)} %param.20), channel_id=1, source_target_pairs={{0,1},{1,0},{2,3},{3,2},{4,5},{5,4},{6,7},{7,6},{8,9},{9,8},{10,11... | collective-permute-start | bytes 20 | tf_op jit(solution)/shard_map/ppermute | solution.py:563
  1.6 11.4 %collective-permute-start.2 = (bf16[1,2,256,256]{3,2,1,0:T(8,128)(2,1)S(1)}, bf16[1,2,256,256]{3,2,1,0:T(8,128)(2,1)S(1)}, u32[]{:S(2)}, u32[]{:S(2)}) collective-permute-start(bf16[1,2,256,256]{3,2,1,0:T(8,128)(2,1)S(1)} %dynamic-slice_convert_fusion), channel_id=1, source_target_pairs={{4,0},{8,4},{12,8},{5,1},{9,5},{13,9},{6,2},{10,6},{14,10},{7,3},{... | collective-permute-start | bytes 786440 | tf_op jit(solution)/shard_map/ppermute | solution.py:18
  5.0 9.5 %copy-start = (f32[1,2,256,512]{3,2,1,0:T(8,128)S(1)}, f32[1,2,256,512]{3,2,1,0:T(8,128)}, u32[]{:S(2)}) copy-start(f32[1,2,256,512]{3,2,1,0:T(8,128)} %tile_ref.1) | copy-start | bytes 3145732
  5.1 9.4 %copy-start.1 = (bf16[2,256,256]{2,1,0:T(8,128)(2,1)S(1)}, bf16[2,256,256]{2,1,0:T(8,128)(2,1)}, u32[]{:S(2)}) copy-start(bf16[2,256,256]{2,1,0:T(8,128)(2,1)} %param.18) | copy-start | bytes 786436
  8.6 4.4 %copy-start.3 = (s32[2,2]{1,0:T(2,128)S(1)}, s32[2,2]{1,0:T(2,128)}, u32[]{:S(2)}) copy-start(s32[2,2]{1,0:T(2,128)} %param.19) | copy-start | bytes 52
  13.0 1.5 %collective-permute-start.3 = (bf16[1,2,256,256]{3,2,1,0:T(8,128)(2,1)S(1)}, bf16[1,2,256,256]{3,2,1,0:T(8,128)(2,1)S(1)}, u32[]{:S(2)}, u32[]{:S(2)}) collective-permute-start(bf16[1,2,256,256]{3,2,1,0:T(8,128)(2,1)S(1)} %collective-permute-done.2.mine_ref), channel_id=1, source_target_pairs={{0,1},{1,0},{2,3},{3,2},{4,5},{5,4},{6,7},{7,6},{8,9},{9,8},{10,11... | collective-permute-start | bytes 786440 | tf_op jit(solution)/shard_map/ppermute | solution.py:558
  17.7 9.7 %collective-permute-start.6 = (f32[2,256,256]{2,1,0:T(8,128)}, f32[2,256,256]{2,1,0:T(8,128)}, u32[]{:S(2)}, u32[]{:S(2)}) collective-permute-start(f32[2,256,256]{2,1,0:T(8,128)} %param.21), channel_id=1, source_target_pairs={{0,1},{1,0},{2,3},{3,2},{4,5},{5,4},{6,7},{7,6},{8,9},{9,8},{10,11... | collective-permute-start | bytes 1572872 | tf_op jit(solution)/shard_map/ppermute | solution.py:614
  18.8 6.8 %collective-permute-start.5 = (bf16[1,256,256]{2,1,0:T(8,128)(2,1)}, bf16[1,256,256]{2,1,0:T(8,128)(2,1)}, u32[]{:S(2)}, u32[]{:S(2)}) collective-permute-start(bf16[1,256,256]{2,1,0:T(8,128)(2,1)} %get-tuple-element.188), channel_id=1, source_target_pairs={{0,2},{1,3},{4,6},{5,7},{8,10},{9,11},{12,14},{13,15},{16,18},{17,... | collective-permute-start | bytes 393224 | tf_op jit(solution)/shard_map/ppermute | solution.py:540
  20.8 5.7 %collective-permute-start.4 = (bf16[1,256,256]{2,1,0:T(8,128)(2,1)S(1)}, bf16[1,256,256]{2,1,0:T(8,128)(2,1)}, u32[]{:S(2)}, u32[]{:S(2)}) collective-permute-start(bf16[1,256,256]{2,1,0:T(8,128)(2,1)S(1)} %get-tuple-element.187), channel_id=1, source_target_pairs={{0,2},{1,3},{4,6},{5,7},{8,10},{9,11},{12,14},{13,15},{16,18},{17,... | collective-permute-start | bytes 393224 | tf_op jit(solution)/shard_map/ppermute | solution.py:540
  25.6 1.8 %copy-start.2 = (f32[2,256,256]{2,1,0:T(8,128)S(1)}, f32[2,256,256]{2,1,0:T(8,128)}, u32[]{:S(2)}) copy-start(f32[2,256,256]{2,1,0:T(8,128)} %param.21) | copy-start | bytes 1572868
  27.6 12.7 %collective-permute-start.8 = (bf16[1,256,256]{2,1,0:T(8,128)(2,1)S(1)}, bf16[1,256,256]{2,1,0:T(8,128)(2,1)S(1)}, u32[]{:S(2)}, u32[]{:S(2)}) collective-permute-start(bf16[1,256,256]{2,1,0:T(8,128)(2,1)S(1)} %get-tuple-element.186), channel_id=1, source_target_pairs={{2,0},{3,1},{6,4},{7,5},{10,8},{11,9},{14,12},{15,13},{18,16},{19,... | collective-permute-start | bytes 393224 | tf_op jit(solution)/shard_map/ppermute | solution.py:540
  28.9 13.2 %collective-permute-start.7 = (bf16[1,256,256]{2,1,0:T(8,128)(2,1)S(1)}, bf16[1,256,256]{2,1,0:T(8,128)(2,1)S(1)}, u32[]{:S(2)}, u32[]{:S(2)}) collective-permute-start(bf16[1,256,256]{2,1,0:T(8,128)(2,1)S(1)} %get-tuple-element.185), channel_id=1, source_target_pairs={{2,0},{3,1},{6,4},{7,5},{10,8},{11,9},{14,12},{15,13},{18,16},{19,... | collective-permute-start | bytes 393224 | tf_op jit(solution)/shard_map/ppermute | solution.py:540
  45.1 1.6 %collective-permute-start.10 = (bf16[2,256,256]{2,1,0:T(8,128)(2,1)S(1)}, bf16[2,256,256]{2,1,0:T(8,128)(2,1)S(1)}, u32[]{:S(2)}, u32[]{:S(2)}) collective-permute-start(bf16[2,256,256]{2,1,0:T(8,128)(2,1)S(1)} %constant_dynamic-slice_fusion.1), channel_id=1, source_target_pairs={{0,1},{1,0},{2,3},{3,2},{4,5},{5,4},{6,7},{7,6},{8,9},{9,8},{10,11... | collective-permute-start | bytes 786440 | tf_op jit(solution)/shard_map/ppermute | solution.py:663
  46.8 9.5 %collective-permute-start.11 = (bf16[2,256,256]{2,1,0:T(8,128)(2,1)S(1)}, bf16[2,256,256]{2,1,0:T(8,128)(2,1)S(1)}, u32[]{:S(2)}, u32[]{:S(2)}) collective-permute-start(bf16[2,256,256]{2,1,0:T(8,128)(2,1)S(1)} %add_convert_fusion), channel_id=1, source_target_pairs={{0,4},{4,8},{8,12},{1,5},{5,9},{9,13},{2,6},{6,10},{10,14},{3,7},{... | collective-permute-start | bytes 786440 | tf_op jit(solution)/shard_map/ppermute | solution.py:665
  50.5 5.8 %collective-permute-start.9 = (bf16[2,256,512]{2,1,0:T(8,128)(2,1)S(1)}, bf16[2,256,512]{2,1,0:T(8,128)(2,1)S(1)}, u32[]{:S(2)}, u32[]{:S(2)}) collective-permute-start(bf16[2,256,512]{2,1,0:T(8,128)(2,1)S(1)} %get-tuple-element.184), channel_id=1, source_target_pairs={{0,1},{1,0},{2,3},{3,2},{4,5},{5,4},{6,7},{7,6},{8,9},{9,8},{10,11... | collective-permute-start | bytes 1572872 | tf_op jit(solution)/shard_map/ppermute | solution.py:667
  56.3 1.5 %collective-permute-start.12 = (bf16[2,256,256]{2,1,0:T(8,128)(2,1)S(1)}, bf16[2,256,256]{2,1,0:T(8,128)(2,1)S(1)}, u32[]{:S(2)}, u32[]{:S(2)}) collective-permute-start(bf16[2,256,256]{2,1,0:T(8,128)(2,1)S(1)} %collective-permute-done.11), channel_id=1, source_target_pairs={{0,1},{1,0},{2,3},{3,2},{4,5},{5,4},{6,7},{7,6},{8,9},{9,8},{10,11... | collective-permute-start | bytes 786440 | tf_op jit(solution)/shard_map/ppermute | solution.py:668

commit v21 on v19

--- a/solution.py
+++ b/solution.py
@@ -483,12 +483,11 @@
 
 
 def first_kernel(rows_ref, columns_ref, order_ref, wave_ref, tile_ref, mine_ref, partner_ref,
-                 chirp_ref, dft_rows_ref, dft_cols_ref, result_ref):
+                 chirp_ref, dft_rows_ref, dft_cols_ref, result_ref, rows_scratch):
     index = pl.program_id(0)
     width = wave_ref.shape[2]
     height = tile_ref.shape[2] + mine_ref.shape[2]
     columns_all = tile_ref.shape[3]
-    row_shift = (height - rows_ref[index]) % height
     column_shift = (columns_all - columns_ref[index]) % columns_all
     first = order_ref[0] == 0
     patch = []
@@ -498,8 +497,13 @@
         rim = jnp.concatenate(
             [jnp.where(first, mine, partner), jnp.where(first, partner, mine)], axis=1
         )
-        full = jnp.concatenate([tile_ref[0, part], rim], axis=0)
-        full = pltpu.roll(full, row_shift, 0)[:width]
+        rows_tile = tile_ref.shape[2]
+        rows_scratch[:rows_tile, :] = tile_ref[0, part]
+        rows_scratch[rows_tile:, :] = rim
+        row = rows_ref[index]
+        aligned = pl.multiple_of((row // 8) * 8, 8)
+        full = rows_scratch[pl.ds(aligned, width + 8), :]
+        full = pltpu.roll(full, (width + 8 - row % 8) % (width + 8), 0)[:width]
         patch.append(pltpu.roll(full, column_shift, 1)[:, :width])
     wave = wave_ref[0].astype(jnp.float32)
     wave_re = patch[0] * wave[0] - patch[1] * wave[1]
@@ -528,6 +532,7 @@
             whole(blocks[1].shape),
         ],
         out_specs=wave_spec,
+        scratch_shapes=[pltpu.VMEM((tile.shape[2] + mine.shape[2], tile.shape[3]), jnp.float32)],
     )
     return pl.pallas_call(
         first_kernel,

time: 58.4 us -> 58.1 us (level)
  no operation moved by 1% of the time
where the time goes in v21:
time: 58.1 us; the launch traced here: 57.7 us
  waiting for transfers between devices  29.6 us (51%)
  starting transfers between devices  9.21 us (16%)
  Pallas kernels  8 us (14%)
  other arithmetic  4.25 us (7%)
  between operations  4.04 us (7%)
  local copies, waits for them, and re-layouts  2.58 us (4%)
    ppermute x1, waiting for transfers between devices, local(): carry = lax.ppermute(carry, 'depth', [(turn + 1, turn)])  13.2 us
    ppermute x1, waiting for transfers between devices, local(): lax.ppermute(spill_sum, 'tile', [(t, t + 1) for t in range(tile_count - 1)])  5.75 us
    ppermute x1, waiting for transfers between devices, from_behind(): return lax.ppermute(block, axis, route)  4.48 us
    ppermute x1, starting transfers between devices, local(): lax.ppermute(spill_sum, 'tile', [(t, t + 1) for t in range(tile_count - 1)])  3.65 us
    pallas_call x1, Pallas kernels, run_first(): pl.pallas_call(first_kernel, grid_spec=grid_spec, out_shape=jax.ShapeDtyp...  3.54 us
    ppermute x1, waiting for transfers between devices, local(): carry = lax.ppermute(carry, 'depth', [(depth_count - 2, depth_count - 1)])  2.93 us
    pallas_call x1, Pallas kernels, run_adjoint(): pl.pallas_call(adjoint_kernel(last, number == 1, opening), grid_spec=grid...  2.87 us
    ppermute x1, starting transfers between devices, local(): carry = lax.ppermute(carry, 'depth', [(depth_count - 2, depth_count - 1)])  1.99 us
  transfers between devices with their start and end apart: 11, of which 7 were waited for; matrix products, arithmetic and copies ran while one was open for 9% of the time, Pallas kernels for 3%

profile of v21, /device:TPU:0, one launch (start us, length us, event | category | flops | bytes accessed | tf_op | source)
XLA Modules:
  0.0 57.7 jit_solution(6434718734357588018)
XLA Ops:
  0.0 0.5 collective-permute-start
  0.5 0.1 collective-permute-start.1
  0.5 1.1 %dynamic-slice_convert_fusion = bf16[1,2,256,256]{3,2,1,0:T(8,128)(2,1)S(1)} fusion(f32[1,2,256,512]{3,2,1,0:T(8,128)} %tile_ref.1, s32[]{:T(128)S(6)} %select_n.84), kind=kLoop, calls=%fused_computation.4 | loop fusion | bytes 524292 | tf_op jit(solution)/shard_map/convert_element_type | solution.py:556
  1.6 1.3 %collective-permute-start.2 = (bf16[1,2,256,256]{3,2,1,0:T(8,128)(2,1)S(1)}, bf16[1,2,256,256]{3,2,1,0:T(8,128)(2,1)S(1)}, u32[]{:S(2)}, u32[]{:S(2)}) collective-permute-start(bf16[1,2,256,256]{3,2,1,0:T(8,128)(2,1)S(1)} %dynamic-slice_convert_fusion), channel_id=1, source_target_pairs={{4,0},{8,4},{12,8},{5,1},{9,5},{13,9},{6,2},{10,6},{14,10},{7,3},{... | collective-permute-start | bytes 786440 | tf_op jit(solution)/shard_map/ppermute | solution.py:18
  2.9 1.1 %multiply_convert_fusion = (bf16[256,256]{1,0:T(8,128)(2,1)S(1)}, bf16[256,256]{1,0:T(8,128)(2,1)S(1)}) fusion(), kind=kLoop, calls=%fused_computation.13 | loop fusion | flops 1245184 | bytes 262144 | tf_op jit(solution)/shard_map/convert_element_type | solution.py:51
  4.0 1.0 %fusion.6 = (f32[1,256,256]{2,1,0:T(8,128)S(1)}, f32[1,256,256]{2,1,0:T(8,128)S(1)}) fusion(s32[256]{0:T(256)S(1)} %fusion.9, f32[]{:T(128)S(6)} %neg.8), kind=kLoop, calls=%fused_computation.19 | loop fusion | flops 196608 | bytes 525316 | tf_op jit(solution)/shard_map/cos | solution.py:61
  5.9 0.8 %broadcast_select_fusion = s32[2]{0:T(128)S(1)} fusion(pred[]{:T(512)} %eq.24, s32[1]{0:T(128)} %collective-permute-done.1, s32[1]{0:T(128)S(6)} %copy.16), kind=kLoop, calls=%fused_computation.30 | loop fusion | flops 6 | bytes 17 | tf_op jit(solution)/shard_map/jit(_where)/select_n | solution.py:569
  6.7 0.7 %fusion.12 = (s32[1]{0:T(128)}, s32[1]{0:T(128)}) fusion(s32[2]{0:T(128)S(1)} %broadcast_select_fusion), kind=kLoop, calls=%fused_computation.32 | loop fusion | bytes 16 | tf_op jit(solution)/shard_map/slice | solution.py:573
  8.5 4.5 %collective-permute-done.2.mine_ref = bf16[1,2,256,256]{3,2,1,0:T(8,128)(2,1)S(1)} collective-permute-done((bf16[1,2,256,256]{3,2,1,0:T(8,128)(2,1)S(1)}, bf16[1,2,256,256]{3,2,1,0:T(8,128)(2,1)S(1)}, u32[]{:S(2)}, u32[]{:S(2)}) %collective-permute-start.2) | collective-permute-done | bytes 262176 | tf_op jit(solution)/shard_map/ppermute | solution.py:18
  13.0 0.6 %fusion.13 = (s32[1,1]{1,0:T(1,128)}, s32[1,1]{1,0:T(1,128)}) fusion(s32[1,2]{1,0:T(1,128)S(1)} %constant_dynamic-slice_fusion), kind=kLoop, calls=%fused_computation.33 | loop fusion | bytes 16 | tf_op jit(solution)/shard_map/slice | solution.py:580
  14.3 0.2 collective-permute-done.3.partner_ref
  14.5 3.5 %conditional.4 = (bf16[1,2,256,256]{3,2,1,0:T(8,128)(2,1)}) conditional(s32[]{:T(128)} %convert_element_type.72, () %tuple.58, (s32[1]{0:T(128)}, s32[1]{0:T(128)}, s32[1]{0:T(128)}, bf16[1,2,256,256]{3,2,1,0:T(8,128)(2,1)S(1)}, f32[1,2,256,512]{3,2,1,0:T(8,128)S(1)}, /*index=5*/bf16[1,2,256,256]{3,2,1,0:T(8,128)(2,1)S(1)}, ...), branch_computations={%region_0.1_spmd, %region_1.2_spmd} | conditional | bytes 262154 | solution.py:611
  14.5 3.5 %branch_1_fun.6 = bf16[1,2,256,256]{3,2,1,0:T(8,128)(2,1)} custom-call(s32[1]{0:T(128)} %get-tuple-element.127.rows_ref, s32[1]{0:T(128)} %get-tuple-element.128.columns_ref, s32[1]{0:T(128)} %get-tuple-element.129.order_ref, bf16[1,2,256,256]{3,2,1,0:T(8,128)(2,1)S(1)} %get-tuple-element.130.wave_ref, f32[1,2,256,512]{3,2,1,0:T(8,128)S(1)} %get-tuple-element.131.tile_ref, ...), custom_call_target="tpu_custom_call" | custom-call | tf_op jit(solution)/shard_map/cond/branch_1_fun/pallas_call | solution.py:537
  18.1 0.3 collective-permute-start.5
  18.4 2.0 %collective-permute-start.4 = (bf16[1,2,256,256]{3,2,1,0:T(8,128)(2,1)}, bf16[1,2,256,256]{3,2,1,0:T(8,128)(2,1)}, u32[]{:S(2)}, u32[]{:S(2)}) collective-permute-start(bf16[1,2,256,256]{3,2,1,0:T(8,128)(2,1)} %get-tuple-element.197), channel_id=1, source_target_pairs={{0,2},{1,3},{4,6},{5,7},{8,10},{9,11},{12,14},{13,15},{16,18},{17,... | collective-permute-start | bytes 786440 | tf_op jit(solution)/shard_map/ppermute | solution.py:628
  21.6 1.6 %shard_map.60 = f32[1,2,256,256]{3,2,1,0:T(8,128)S(1)} custom-call(s32[1]{0:T(128)} %sub.17.rows_ref, s32[1]{0:T(128)} %bitcast.4.columns_ref, s32[1]{0:T(128)} %bitcast.order_ref, f32[1,2,256,512]{3,2,1,0:T(8,128)S(1)} %copy-done, bf16[1,2,256,256]{3,2,1,0:T(8,128)(2,1)S(1)} %collective-permute-done.2.mine_ref, ...), custom_call_target="tpu_custom_call" | custom-call | tf_op jit(solution)/shard_map/pallas_call | solution.py:275
  23.2 2.9 %collective-permute-done.4 = bf16[1,2,256,256]{3,2,1,0:T(8,128)(2,1)} collective-permute-done((bf16[1,2,256,256]{3,2,1,0:T(8,128)(2,1)}, bf16[1,2,256,256]{3,2,1,0:T(8,128)(2,1)}, u32[]{:S(2)}, u32[]{:S(2)}) %collective-permute-start.4) | collective-permute-done | bytes 262176 | tf_op jit(solution)/shard_map/ppermute | solution.py:628
  26.2 1.3 %collective-permute-start.6 = (bf16[1,2,256,256]{3,2,1,0:T(8,128)(2,1)S(1)}, bf16[1,2,256,256]{3,2,1,0:T(8,128)(2,1)S(1)}, u32[]{:S(2)}, u32[]{:S(2)}) collective-permute-start(bf16[1,2,256,256]{3,2,1,0:T(8,128)(2,1)S(1)} %get-tuple-element.171), channel_id=1, source_target_pairs={{2,0},{3,1},{6,4},{7,5},{10,8},{11,9},{14,12},{15,13},{18,16},{19,... | collective-permute-start | bytes 786440 | tf_op jit(solution)/shard_map/ppermute | solution.py:655
  27.5 0.1 conditional.6
  27.6 0.1 broadcast.198
  27.6 13.2 %collective-permute-done.6 = bf16[1,2,256,256]{3,2,1,0:T(8,128)(2,1)S(1)} collective-permute-done((bf16[1,2,256,256]{3,2,1,0:T(8,128)(2,1)S(1)}, bf16[1,2,256,256]{3,2,1,0:T(8,128)(2,1)S(1)}, u32[]{:S(2)}, u32[]{:S(2)}) %collective-permute-start.6) | collective-permute-done | bytes 262176 | tf_op jit(solution)/shard_map/ppermute | solution.py:655
  40.8 2.9 %conditional.7 = (bf16[2,512,512]{2,1,0:T(8,128)(2,1)S(1)}) conditional(s32[]{:T(128)} %convert_element_type.72, bf16[2,512,512]{2,1,0:T(8,128)(2,1)S(1)} %get-tuple-element.199, (s32[1]{0:T(128)}, s32[1]{0:T(128)}, s32[1]{0:T(128)}, s32[1]{0:T(128)}, s32[1]{0:T(128)}, /*index=5*/bf16[1,2,256,256]{3,2,1,0:T(8,128)(2,1)S(1)}, ...), branch_computations={%region_6.7_spmd, %region_7.8_spmd} | conditional | bytes 8 | solution.py:657
  40.8 2.9 %branch_1_fun.9 = bf16[2,512,512]{2,1,0:T(8,128)(2,1)S(1)} custom-call(s32[1]{0:T(128)} %get-tuple-element.154.rows_ref, s32[1]{0:T(128)} %get-tuple-element.155.columns_ref, s32[1]{0:T(128)} %get-tuple-element.156.live_ref, s32[1]{0:T(128)} %get-tuple-element.157.slot_ref, s32[1]{0:T(128)} %get-tuple-element.158.other_ref, ...), custom_call_target="tpu_custom_call" | custom-call | tf_op jit(solution)/shard_map/cond/branch_1_fun/pallas_call | solution.py:439
  43.7 0.1 fusion.11
  43.8 0.1 collective-permute-start.8
  43.9 1.5 %collective-permute-done.8 = bf16[2,256,256]{2,1,0:T(8,128)(2,1)S(1)} collective-permute-done((bf16[2,256,256]{2,1,0:T(8,128)(2,1)S(1)}, bf16[2,256,256]{2,1,0:T(8,128)(2,1)S(1)}, u32[]{:S(2)}, u32[]{:S(2)}) %collective-permute-start.8) | collective-permute-done | bytes 262176 | tf_op jit(solution)/shard_map/ppermute | solution.py:663
  45.4 0.1 add_convert_fusion
  45.5 3.7 %collective-permute-start.9 = (bf16[2,256,256]{2,1,0:T(8,128)(2,1)S(1)}, bf16[2,256,256]{2,1,0:T(8,128)(2,1)S(1)}, u32[]{:S(2)}, u32[]{:S(2)}) collective-permute-start(bf16[2,256,256]{2,1,0:T(8,128)(2,1)S(1)} %add_convert_fusion), channel_id=1, source_target_pairs={{0,4},{4,8},{8,12},{1,5},{5,9},{9,13},{2,6},{6,10},{10,14},{3,7},{... | collective-permute-start | bytes 786440 | tf_op jit(solution)/shard_map/ppermute | solution.py:665
  49.1 0.1 collective-permute-start.7
  49.2 5.8 %collective-permute-done.9 = bf16[2,256,256]{2,1,0:T(8,128)(2,1)S(1)} collective-permute-done((bf16[2,256,256]{2,1,0:T(8,128)(2,1)S(1)}, bf16[2,256,256]{2,1,0:T(8,128)(2,1)S(1)}, u32[]{:S(2)}, u32[]{:S(2)}) %collective-permute-start.9) | collective-permute-done | bytes 262176 | tf_op jit(solution)/shard_map/ppermute | solution.py:665
  55.0 1.5 %collective-permute-done.10 = bf16[2,256,256]{2,1,0:T(8,128)(2,1)S(1)} collective-permute-done((bf16[2,256,256]{2,1,0:T(8,128)(2,1)S(1)}, bf16[2,256,256]{2,1,0:T(8,128)(2,1)S(1)}, u32[]{:S(2)}, u32[]{:S(2)}) %collective-permute-start.10) | collective-permute-done | bytes 262176 | tf_op jit(solution)/shard_map/ppermute | solution.py:668
  56.5 1.2 %add_bitcast_fusion = f32[1,2,256,512]{3,2,1,0:T(8,128)} fusion(bf16[2,256,512]{2,1,0:T(8,128)(2,1)S(1)} %collective-permute-done.7, bf16[2,256,256]{2,1,0:T(8,128)(2,1)S(1)} %collective-permute-done.10, bf16[2,256,256]{2,1,0:T(8,128)(2,1)S(1)} %collective-permute-done.9, pred[]{:T(512)} %eq.24, bf16[2,512,512]{2,1,0:T(8,128)(2,1)S(1)} %get-tuple-element.200), kind=kLoop, calls=%fused_computation | loop fusion | flops 3670016 | bytes 2621441 | tf_op jit(solution)/shard_map/broadcast_in_dim | solution.py:676
  (22 shorter events, 0.3 us)
Async XLA Ops:
  0.0 13.0 %collective-permute-start = (s32[2,2]{1,0:T(2,128)}, s32[2,2]{1,0:T(2,128)S(1)}, u32[]{:S(2)}, u32[]{:S(2)}) collective-permute-start(s32[2,2]{1,0:T(2,128)} %param.19), channel_id=1, source_target_pairs={{0,1},{1,0},{2,3},{3,2},{4,5},{5,4},{6,7},{7,6},{8,9},{9,8},{10,11... | collective-permute-start | bytes 56 | tf_op jit(solution)/shard_map/ppermute | solution.py:562
  0.5 5.4 %collective-permute-start.1 = (s32[1]{0:T(128)}, s32[1]{0:T(128)}, u32[]{:S(2)}, u32[]{:S(2)}) collective-permute-start(s32[1]{0:T(128)} %param.20), channel_id=1, source_target_pairs={{0,1},{1,0},{2,3},{3,2},{4,5},{5,4},{6,7},{7,6},{8,9},{9,8},{10,11... | collective-permute-start | bytes 20 | tf_op jit(solution)/shard_map/ppermute | solution.py:563
  1.6 11.4 %collective-permute-start.2 = (bf16[1,2,256,256]{3,2,1,0:T(8,128)(2,1)S(1)}, bf16[1,2,256,256]{3,2,1,0:T(8,128)(2,1)S(1)}, u32[]{:S(2)}, u32[]{:S(2)}) collective-permute-start(bf16[1,2,256,256]{3,2,1,0:T(8,128)(2,1)S(1)} %dynamic-slice_convert_fusion), channel_id=1, source_target_pairs={{4,0},{8,4},{12,8},{5,1},{9,5},{13,9},{6,2},{10,6},{14,10},{7,3},{... | collective-permute-start | bytes 786440 | tf_op jit(solution)/shard_map/ppermute | solution.py:18
  5.0 9.5 %copy-start = (f32[1,2,256,512]{3,2,1,0:T(8,128)S(1)}, f32[1,2,256,512]{3,2,1,0:T(8,128)}, u32[]{:S(2)}) copy-start(f32[1,2,256,512]{3,2,1,0:T(8,128)} %tile_ref.1) | copy-start | bytes 3145732
  5.1 9.4 %copy-start.1 = (bf16[2,256,256]{2,1,0:T(8,128)(2,1)S(1)}, bf16[2,256,256]{2,1,0:T(8,128)(2,1)}, u32[]{:S(2)}) copy-start(bf16[2,256,256]{2,1,0:T(8,128)(2,1)} %param.18) | copy-start | bytes 786436
  8.5 4.5 %copy-start.2 = (s32[2,2]{1,0:T(2,128)S(1)}, s32[2,2]{1,0:T(2,128)}, u32[]{:S(2)}) copy-start(s32[2,2]{1,0:T(2,128)} %param.19) | copy-start | bytes 52
  13.0 1.5 %collective-permute-start.3 = (bf16[1,2,256,256]{3,2,1,0:T(8,128)(2,1)S(1)}, bf16[1,2,256,256]{3,2,1,0:T(8,128)(2,1)S(1)}, u32[]{:S(2)}, u32[]{:S(2)}) collective-permute-start(bf16[1,2,256,256]{3,2,1,0:T(8,128)(2,1)S(1)} %collective-permute-done.2.mine_ref), channel_id=1, source_target_pairs={{0,1},{1,0},{2,3},{3,2},{4,5},{5,4},{6,7},{7,6},{8,9},{9,8},{10,11... | collective-permute-start | bytes 786440 | tf_op jit(solution)/shard_map/ppermute | solution.py:558
  18.1 8.1 %collective-permute-start.5 = (f32[2,256,256]{2,1,0:T(8,128)}, f32[2,256,256]{2,1,0:T(8,128)}, u32[]{:S(2)}, u32[]{:S(2)}) collective-permute-start(f32[2,256,256]{2,1,0:T(8,128)} %param.21), channel_id=1, source_target_pairs={{0,1},{1,0},{2,3},{3,2},{4,5},{5,4},{6,7},{7,6},{8,9},{9,8},{10,11... | collective-permute-start | bytes 1572872 | tf_op jit(solution)/shard_map/ppermute | solution.py:614
  18.4 7.8 %collective-permute-start.4 = (bf16[1,2,256,256]{3,2,1,0:T(8,128)(2,1)}, bf16[1,2,256,256]{3,2,1,0:T(8,128)(2,1)}, u32[]{:S(2)}, u32[]{:S(2)}) collective-permute-start(bf16[1,2,256,256]{3,2,1,0:T(8,128)(2,1)} %get-tuple-element.197), channel_id=1, source_target_pairs={{0,2},{1,3},{4,6},{5,7},{8,10},{9,11},{12,14},{13,15},{16,18},{17,... | collective-permute-start | bytes 786440 | tf_op jit(solution)/shard_map/ppermute | solution.py:628
  26.2 14.6 %collective-permute-start.6 = (bf16[1,2,256,256]{3,2,1,0:T(8,128)(2,1)S(1)}, bf16[1,2,256,256]{3,2,1,0:T(8,128)(2,1)S(1)}, u32[]{:S(2)}, u32[]{:S(2)}) collective-permute-start(bf16[1,2,256,256]{3,2,1,0:T(8,128)(2,1)S(1)} %get-tuple-element.171), channel_id=1, source_target_pairs={{2,0},{3,1},{6,4},{7,5},{10,8},{11,9},{14,12},{15,13},{18,16},{19,... | collective-permute-start | bytes 786440 | tf_op jit(solution)/shard_map/ppermute | solution.py:655
  43.8 1.6 %collective-permute-start.8 = (bf16[2,256,256]{2,1,0:T(8,128)(2,1)S(1)}, bf16[2,256,256]{2,1,0:T(8,128)(2,1)S(1)}, u32[]{:S(2)}, u32[]{:S(2)}) collective-permute-start(bf16[2,256,256]{2,1,0:T(8,128)(2,1)S(1)} %constant_dynamic-slice_fusion.1), channel_id=1, source_target_pairs={{0,1},{1,0},{2,3},{3,2},{4,5},{5,4},{6,7},{7,6},{8,9},{9,8},{10,11... | collective-permute-start | bytes 786440 | tf_op jit(solution)/shard_map/ppermute | solution.py:663
  45.5 9.5 %collective-permute-start.9 = (bf16[2,256,256]{2,1,0:T(8,128)(2,1)S(1)}, bf16[2,256,256]{2,1,0:T(8,128)(2,1)S(1)}, u32[]{:S(2)}, u32[]{:S(2)}) collective-permute-start(bf16[2,256,256]{2,1,0:T(8,128)(2,1)S(1)} %add_convert_fusion), channel_id=1, source_target_pairs={{0,4},{4,8},{8,12},{1,5},{5,9},{9,13},{2,6},{6,10},{10,14},{3,7},{... | collective-permute-start | bytes 786440 | tf_op jit(solution)/shard_map/ppermute | solution.py:665
  49.1 5.8 %collective-permute-start.7 = (bf16[2,256,512]{2,1,0:T(8,128)(2,1)S(1)}, bf16[2,256,512]{2,1,0:T(8,128)(2,1)S(1)}, u32[]{:S(2)}, u32[]{:S(2)}) collective-permute-start(bf16[2,256,512]{2,1,0:T(8,128)(2,1)S(1)} %get-tuple-element.184), channel_id=1, source_target_pairs={{0,1},{1,0},{2,3},{3,2},{4,5},{5,4},{6,7},{7,6},{8,9},{9,8},{10,11... | collective-permute-start | bytes 1572872 | tf_op jit(solution)/shard_map/ppermute | solution.py:667
  55.0 1.5 %collective-permute-start.10 = (bf16[2,256,256]{2,1,0:T(8,128)(2,1)S(1)}, bf16[2,256,256]{2,1,0:T(8,128)(2,1)S(1)}, u32[]{:S(2)}, u32[]{:S(2)}) collective-permute-start(bf16[2,256,256]{2,1,0:T(8,128)(2,1)S(1)} %collective-permute-done.9), channel_id=1, source_target_pairs={{0,1},{1,0},{2,3},{3,2},{4,5},{5,4},{6,7},{7,6},{8,9},{9,8},{10,11... | collective-permute-start | bytes 786440 | tf_op jit(solution)/shard_map/ppermute | solution.py:668

commit v22 on v21

--- a/solution.py
+++ b/solution.py
@@ -488,7 +488,6 @@
     width = wave_ref.shape[2]
     height = tile_ref.shape[2] + mine_ref.shape[2]
     columns_all = tile_ref.shape[3]
-    column_shift = (columns_all - columns_ref[index]) % columns_all
     first = order_ref[0] == 0
     patch = []
     for part in range(2):
@@ -498,13 +497,19 @@
             [jnp.where(first, mine, partner), jnp.where(first, partner, mine)], axis=1
         )
         rows_tile = tile_ref.shape[2]
-        rows_scratch[:rows_tile, :] = tile_ref[0, part]
-        rows_scratch[rows_tile:, :] = rim
+        rows_scratch[:, columns_all:] = jnp.zeros(
+            (rows_scratch.shape[0], rows_scratch.shape[1] - columns_all), jnp.float32
+        )
+        rows_scratch[:rows_tile, :columns_all] = tile_ref[0, part]
+        rows_scratch[rows_tile:, :columns_all] = rim
         row = rows_ref[index]
+        column = columns_ref[index]
         aligned = pl.multiple_of((row // 8) * 8, 8)
-        full = rows_scratch[pl.ds(aligned, width + 8), :]
+        across = pl.multiple_of((column // 128) * 128, 128)
+        full = rows_scratch[pl.ds(aligned, width + 8), pl.ds(across, width + 128)]
         full = pltpu.roll(full, (width + 8 - row % 8) % (width + 8), 0)[:width]
-        patch.append(pltpu.roll(full, column_shift, 1)[:, :width])
+        full = pltpu.roll(full, (width + 128 - column % 128) % (width + 128), 1)
+        patch.append(full[:, :width])
     wave = wave_ref[0].astype(jnp.float32)
     wave_re = patch[0] * wave[0] - patch[1] * wave[1]
     wave_im = patch[0] * wave[1] + patch[1] * wave[0]
@@ -532,7 +537,9 @@
             whole(blocks[1].shape),
         ],
         out_specs=wave_spec,
-        scratch_shapes=[pltpu.VMEM((tile.shape[2] + mine.shape[2], tile.shape[3]), jnp.float32)],
+        scratch_shapes=[
+            pltpu.VMEM((tile.shape[2] + mine.shape[2], tile.shape[3] + 128), jnp.float32)
+        ],
     )
     return pl.pallas_call(
         first_kernel,

time: 58.1 us -> 57.9 us (level)
  no operation moved by 1% of the time
where the time goes in v22:
time: 57.9 us; the launch traced here: 57.6 us
  waiting for transfers between devices  29.6 us (51%)
  starting transfers between devices  9.21 us (16%)
  Pallas kernels  7.86 us (14%)
  other arithmetic  4.25 us (7%)
  between operations  4.04 us (7%)
  local copies, waits for them, and re-layouts  2.58 us (4%)
    ppermute x1, waiting for transfers between devices, local(): carry = lax.ppermute(carry, 'depth', [(turn + 1, turn)])  13.2 us
    ppermute x1, waiting for transfers between devices, local(): lax.ppermute(spill_sum, 'tile', [(t, t + 1) for t in range(tile_count - 1)])  5.75 us
    ppermute x1, waiting for transfers between devices, from_behind(): return lax.ppermute(block, axis, route)  4.48 us
    ppermute x1, starting transfers between devices, local(): lax.ppermute(spill_sum, 'tile', [(t, t + 1) for t in range(tile_count - 1)])  3.65 us
    pallas_call x1, Pallas kernels, run_first(): pl.pallas_call(first_kernel, grid_spec=grid_spec, out_shape=jax.ShapeDtyp...  3.4 us
    ppermute x1, waiting for transfers between devices, local(): carry = lax.ppermute(carry, 'depth', [(depth_count - 2, depth_count - 1)])  2.93 us
    pallas_call x1, Pallas kernels, run_adjoint(): pl.pallas_call(adjoint_kernel(last, number == 1, opening), grid_spec=grid...  2.87 us
    ppermute x1, starting transfers between devices, local(): carry = lax.ppermute(carry, 'depth', [(depth_count - 2, depth_count - 1)])  1.99 us
  transfers between devices with their start and end apart: 11, of which 7 were waited for; matrix products, arithmetic and copies ran while one was open for 9% of the time, Pallas kernels for 3%

profile of v22, /device:TPU:0, one launch (start us, length us, event | category | flops | bytes accessed | tf_op | source)
XLA Modules:
  0.0 57.6 jit_solution(2463865284847917462)
XLA Ops:
  0.0 0.5 collective-permute-start
  0.5 0.1 collective-permute-start.1
  0.5 1.1 %dynamic-slice_convert_fusion = bf16[1,2,256,256]{3,2,1,0:T(8,128)(2,1)S(1)} fusion(f32[1,2,256,512]{3,2,1,0:T(8,128)} %tile_ref.1, s32[]{:T(128)S(6)} %select_n.84), kind=kLoop, calls=%fused_computation.4 | loop fusion | bytes 524292 | tf_op jit(solution)/shard_map/convert_element_type | solution.py:563
  1.6 1.3 %collective-permute-start.2 = (bf16[1,2,256,256]{3,2,1,0:T(8,128)(2,1)S(1)}, bf16[1,2,256,256]{3,2,1,0:T(8,128)(2,1)S(1)}, u32[]{:S(2)}, u32[]{:S(2)}) collective-permute-start(bf16[1,2,256,256]{3,2,1,0:T(8,128)(2,1)S(1)} %dynamic-slice_convert_fusion), channel_id=1, source_target_pairs={{4,0},{8,4},{12,8},{5,1},{9,5},{13,9},{6,2},{10,6},{14,10},{7,3},{... | collective-permute-start | bytes 786440 | tf_op jit(solution)/shard_map/ppermute | solution.py:18
  2.9 1.1 %multiply_convert_fusion = (bf16[256,256]{1,0:T(8,128)(2,1)S(1)}, bf16[256,256]{1,0:T(8,128)(2,1)S(1)}) fusion(), kind=kLoop, calls=%fused_computation.13 | loop fusion | flops 1245184 | bytes 262144 | tf_op jit(solution)/shard_map/convert_element_type | solution.py:51
  4.0 1.0 %fusion.6 = (f32[1,256,256]{2,1,0:T(8,128)S(1)}, f32[1,256,256]{2,1,0:T(8,128)S(1)}) fusion(s32[256]{0:T(256)S(1)} %fusion.9, f32[]{:T(128)S(6)} %neg.8), kind=kLoop, calls=%fused_computation.19 | loop fusion | flops 196608 | bytes 525316 | tf_op jit(solution)/shard_map/cos | solution.py:61
  5.9 0.8 %broadcast_select_fusion = s32[2]{0:T(128)S(1)} fusion(pred[]{:T(512)} %eq.24, s32[1]{0:T(128)} %collective-permute-done.1, s32[1]{0:T(128)S(6)} %copy.16), kind=kLoop, calls=%fused_computation.30 | loop fusion | flops 6 | bytes 17 | tf_op jit(solution)/shard_map/jit(_where)/select_n | solution.py:576
  6.7 0.7 %fusion.12 = (s32[1]{0:T(128)}, s32[1]{0:T(128)}) fusion(s32[2]{0:T(128)S(1)} %broadcast_select_fusion), kind=kLoop, calls=%fused_computation.32 | loop fusion | bytes 16 | tf_op jit(solution)/shard_map/slice | solution.py:580
  8.5 4.5 %collective-permute-done.2.mine_ref = bf16[1,2,256,256]{3,2,1,0:T(8,128)(2,1)S(1)} collective-permute-done((bf16[1,2,256,256]{3,2,1,0:T(8,128)(2,1)S(1)}, bf16[1,2,256,256]{3,2,1,0:T(8,128)(2,1)S(1)}, u32[]{:S(2)}, u32[]{:S(2)}) %collective-permute-start.2) | collective-permute-done | bytes 262176 | tf_op jit(solution)/shard_map/ppermute | solution.py:18
  13.0 0.6 %fusion.13 = (s32[1,1]{1,0:T(1,128)}, s32[1,1]{1,0:T(1,128)}) fusion(s32[1,2]{1,0:T(1,128)S(1)} %constant_dynamic-slice_fusion), kind=kLoop, calls=%fused_computation.33 | loop fusion | bytes 16 | tf_op jit(solution)/shard_map/slice | solution.py:587
  14.3 0.2 collective-permute-done.3.partner_ref
  14.5 3.4 %conditional.4 = (bf16[1,2,256,256]{3,2,1,0:T(8,128)(2,1)}) conditional(s32[]{:T(128)} %convert_element_type.72, () %tuple.58, (s32[1]{0:T(128)}, s32[1]{0:T(128)}, s32[1]{0:T(128)}, bf16[1,2,256,256]{3,2,1,0:T(8,128)(2,1)S(1)}, f32[1,2,256,512]{3,2,1,0:T(8,128)S(1)}, /*index=5*/bf16[1,2,256,256]{3,2,1,0:T(8,128)(2,1)S(1)}, ...), branch_computations={%region_0.1_spmd, %region_1.2_spmd} | conditional | bytes 262154 | solution.py:618
  14.5 3.4 %branch_1_fun.6 = bf16[1,2,256,256]{3,2,1,0:T(8,128)(2,1)} custom-call(s32[1]{0:T(128)} %get-tuple-element.127.rows_ref, s32[1]{0:T(128)} %get-tuple-element.128.columns_ref, s32[1]{0:T(128)} %get-tuple-element.129.order_ref, bf16[1,2,256,256]{3,2,1,0:T(8,128)(2,1)S(1)} %get-tuple-element.130.wave_ref, f32[1,2,256,512]{3,2,1,0:T(8,128)S(1)} %get-tuple-element.131.tile_ref, ...), custom_call_target="tpu_custom_call" | custom-call | tf_op jit(solution)/shard_map/cond/branch_1_fun/pallas_call | solution.py:544
  17.9 0.3 collective-permute-start.5
  18.3 2.0 %collective-permute-start.4 = (bf16[1,2,256,256]{3,2,1,0:T(8,128)(2,1)}, bf16[1,2,256,256]{3,2,1,0:T(8,128)(2,1)}, u32[]{:S(2)}, u32[]{:S(2)}) collective-permute-start(bf16[1,2,256,256]{3,2,1,0:T(8,128)(2,1)} %get-tuple-element.197), channel_id=1, source_target_pairs={{0,2},{1,3},{4,6},{5,7},{8,10},{9,11},{12,14},{13,15},{16,18},{17,... | collective-permute-start | bytes 786440 | tf_op jit(solution)/shard_map/ppermute | solution.py:635
  21.5 1.6 %shard_map.60 = f32[1,2,256,256]{3,2,1,0:T(8,128)S(1)} custom-call(s32[1]{0:T(128)} %sub.17.rows_ref, s32[1]{0:T(128)} %bitcast.4.columns_ref, s32[1]{0:T(128)} %bitcast.order_ref, f32[1,2,256,512]{3,2,1,0:T(8,128)S(1)} %copy-done, bf16[1,2,256,256]{3,2,1,0:T(8,128)(2,1)S(1)} %collective-permute-done.2.mine_ref, ...), custom_call_target="tpu_custom_call" | custom-call | tf_op jit(solution)/shard_map/pallas_call | solution.py:275
  23.1 2.9 %collective-permute-done.4 = bf16[1,2,256,256]{3,2,1,0:T(8,128)(2,1)} collective-permute-done((bf16[1,2,256,256]{3,2,1,0:T(8,128)(2,1)}, bf16[1,2,256,256]{3,2,1,0:T(8,128)(2,1)}, u32[]{:S(2)}, u32[]{:S(2)}) %collective-permute-start.4) | collective-permute-done | bytes 262176 | tf_op jit(solution)/shard_map/ppermute | solution.py:635
  26.1 1.3 %collective-permute-start.6 = (bf16[1,2,256,256]{3,2,1,0:T(8,128)(2,1)S(1)}, bf16[1,2,256,256]{3,2,1,0:T(8,128)(2,1)S(1)}, u32[]{:S(2)}, u32[]{:S(2)}) collective-permute-start(bf16[1,2,256,256]{3,2,1,0:T(8,128)(2,1)S(1)} %get-tuple-element.171), channel_id=1, source_target_pairs={{2,0},{3,1},{6,4},{7,5},{10,8},{11,9},{14,12},{15,13},{18,16},{19,... | collective-permute-start | bytes 786440 | tf_op jit(solution)/shard_map/ppermute | solution.py:662
  27.4 0.1 conditional.6
  27.4 0.1 broadcast.198
  27.5 13.2 %collective-permute-done.6 = bf16[1,2,256,256]{3,2,1,0:T(8,128)(2,1)S(1)} collective-permute-done((bf16[1,2,256,256]{3,2,1,0:T(8,128)(2,1)S(1)}, bf16[1,2,256,256]{3,2,1,0:T(8,128)(2,1)S(1)}, u32[]{:S(2)}, u32[]{:S(2)}) %collective-permute-start.6) | collective-permute-done | bytes 262176 | tf_op jit(solution)/shard_map/ppermute | solution.py:662
  40.7 2.9 %conditional.7 = (bf16[2,512,512]{2,1,0:T(8,128)(2,1)S(1)}) conditional(s32[]{:T(128)} %convert_element_type.72, bf16[2,512,512]{2,1,0:T(8,128)(2,1)S(1)} %get-tuple-element.199, (s32[1]{0:T(128)}, s32[1]{0:T(128)}, s32[1]{0:T(128)}, s32[1]{0:T(128)}, s32[1]{0:T(128)}, /*index=5*/bf16[1,2,256,256]{3,2,1,0:T(8,128)(2,1)S(1)}, ...), branch_computations={%region_6.7_spmd, %region_7.8_spmd} | conditional | bytes 8 | solution.py:664
  40.7 2.9 %branch_1_fun.9 = bf16[2,512,512]{2,1,0:T(8,128)(2,1)S(1)} custom-call(s32[1]{0:T(128)} %get-tuple-element.154.rows_ref, s32[1]{0:T(128)} %get-tuple-element.155.columns_ref, s32[1]{0:T(128)} %get-tuple-element.156.live_ref, s32[1]{0:T(128)} %get-tuple-element.157.slot_ref, s32[1]{0:T(128)} %get-tuple-element.158.other_ref, ...), custom_call_target="tpu_custom_call" | custom-call | tf_op jit(solution)/shard_map/cond/branch_1_fun/pallas_call | solution.py:439
  43.5 0.1 fusion.11
  43.7 0.1 collective-permute-start.8
  43.7 1.5 %collective-permute-done.8 = bf16[2,256,256]{2,1,0:T(8,128)(2,1)S(1)} collective-permute-done((bf16[2,256,256]{2,1,0:T(8,128)(2,1)S(1)}, bf16[2,256,256]{2,1,0:T(8,128)(2,1)S(1)}, u32[]{:S(2)}, u32[]{:S(2)}) %collective-permute-start.8) | collective-permute-done | bytes 262176 | tf_op jit(solution)/shard_map/ppermute | solution.py:670
  45.3 0.1 add_convert_fusion
  45.3 3.7 %collective-permute-start.9 = (bf16[2,256,256]{2,1,0:T(8,128)(2,1)S(1)}, bf16[2,256,256]{2,1,0:T(8,128)(2,1)S(1)}, u32[]{:S(2)}, u32[]{:S(2)}) collective-permute-start(bf16[2,256,256]{2,1,0:T(8,128)(2,1)S(1)} %add_convert_fusion), channel_id=1, source_target_pairs={{0,4},{4,8},{8,12},{1,5},{5,9},{9,13},{2,6},{6,10},{10,14},{3,7},{... | collective-permute-start | bytes 786440 | tf_op jit(solution)/shard_map/ppermute | solution.py:672
  49.0 0.1 collective-permute-start.7
  49.1 5.8 %collective-permute-done.9 = bf16[2,256,256]{2,1,0:T(8,128)(2,1)S(1)} collective-permute-done((bf16[2,256,256]{2,1,0:T(8,128)(2,1)S(1)}, bf16[2,256,256]{2,1,0:T(8,128)(2,1)S(1)}, u32[]{:S(2)}, u32[]{:S(2)}) %collective-permute-start.9) | collective-permute-done | bytes 262176 | tf_op jit(solution)/shard_map/ppermute | solution.py:672
  54.8 1.5 %collective-permute-done.10 = bf16[2,256,256]{2,1,0:T(8,128)(2,1)S(1)} collective-permute-done((bf16[2,256,256]{2,1,0:T(8,128)(2,1)S(1)}, bf16[2,256,256]{2,1,0:T(8,128)(2,1)S(1)}, u32[]{:S(2)}, u32[]{:S(2)}) %collective-permute-start.10) | collective-permute-done | bytes 262176 | tf_op jit(solution)/shard_map/ppermute | solution.py:675
  56.4 1.2 %add_bitcast_fusion = f32[1,2,256,512]{3,2,1,0:T(8,128)} fusion(bf16[2,256,512]{2,1,0:T(8,128)(2,1)S(1)} %collective-permute-done.7, bf16[2,256,256]{2,1,0:T(8,128)(2,1)S(1)} %collective-permute-done.10, bf16[2,256,256]{2,1,0:T(8,128)(2,1)S(1)} %collective-permute-done.9, pred[]{:T(512)} %eq.24, bf16[2,512,512]{2,1,0:T(8,128)(2,1)S(1)} %get-tuple-element.200), kind=kLoop, calls=%fused_computation | loop fusion | flops 3670016 | bytes 2621441 | tf_op jit(solution)/shard_map/broadcast_in_dim | solution.py:683
  (22 shorter events, 0.3 us)
Async XLA Ops:
  0.0 13.0 %collective-permute-start = (s32[2,2]{1,0:T(2,128)}, s32[2,2]{1,0:T(2,128)S(1)}, u32[]{:S(2)}, u32[]{:S(2)}) collective-permute-start(s32[2,2]{1,0:T(2,128)} %param.19), channel_id=1, source_target_pairs={{0,1},{1,0},{2,3},{3,2},{4,5},{5,4},{6,7},{7,6},{8,9},{9,8},{10,11... | collective-permute-start | bytes 56 | tf_op jit(solution)/shard_map/ppermute | solution.py:569
  0.5 5.4 %collective-permute-start.1 = (s32[1]{0:T(128)}, s32[1]{0:T(128)}, u32[]{:S(2)}, u32[]{:S(2)}) collective-permute-start(s32[1]{0:T(128)} %param.20), channel_id=1, source_target_pairs={{0,1},{1,0},{2,3},{3,2},{4,5},{5,4},{6,7},{7,6},{8,9},{9,8},{10,11... | collective-permute-start | bytes 20 | tf_op jit(solution)/shard_map/ppermute | solution.py:570
  1.6 11.4 %collective-permute-start.2 = (bf16[1,2,256,256]{3,2,1,0:T(8,128)(2,1)S(1)}, bf16[1,2,256,256]{3,2,1,0:T(8,128)(2,1)S(1)}, u32[]{:S(2)}, u32[]{:S(2)}) collective-permute-start(bf16[1,2,256,256]{3,2,1,0:T(8,128)(2,1)S(1)} %dynamic-slice_convert_fusion), channel_id=1, source_target_pairs={{4,0},{8,4},{12,8},{5,1},{9,5},{13,9},{6,2},{10,6},{14,10},{7,3},{... | collective-permute-start | bytes 786440 | tf_op jit(solution)/shard_map/ppermute | solution.py:18
  5.0 9.5 %copy-start = (f32[1,2,256,512]{3,2,1,0:T(8,128)S(1)}, f32[1,2,256,512]{3,2,1,0:T(8,128)}, u32[]{:S(2)}) copy-start(f32[1,2,256,512]{3,2,1,0:T(8,128)} %tile_ref.1) | copy-start | bytes 3145732
  5.1 9.4 %copy-start.1 = (bf16[2,256,256]{2,1,0:T(8,128)(2,1)S(1)}, bf16[2,256,256]{2,1,0:T(8,128)(2,1)}, u32[]{:S(2)}) copy-start(bf16[2,256,256]{2,1,0:T(8,128)(2,1)} %param.18) | copy-start | bytes 786436
  8.5 4.5 %copy-start.2 = (s32[2,2]{1,0:T(2,128)S(1)}, s32[2,2]{1,0:T(2,128)}, u32[]{:S(2)}) copy-start(s32[2,2]{1,0:T(2,128)} %param.19) | copy-start | bytes 52
  13.0 1.5 %collective-permute-start.3 = (bf16[1,2,256,256]{3,2,1,0:T(8,128)(2,1)S(1)}, bf16[1,2,256,256]{3,2,1,0:T(8,128)(2,1)S(1)}, u32[]{:S(2)}, u32[]{:S(2)}) collective-permute-start(bf16[1,2,256,256]{3,2,1,0:T(8,128)(2,1)S(1)} %collective-permute-done.2.mine_ref), channel_id=1, source_target_pairs={{0,1},{1,0},{2,3},{3,2},{4,5},{5,4},{6,7},{7,6},{8,9},{9,8},{10,11... | collective-permute-start | bytes 786440 | tf_op jit(solution)/shard_map/ppermute | solution.py:565
  17.9 8.1 %collective-permute-start.5 = (f32[2,256,256]{2,1,0:T(8,128)}, f32[2,256,256]{2,1,0:T(8,128)}, u32[]{:S(2)}, u32[]{:S(2)}) collective-permute-start(f32[2,256,256]{2,1,0:T(8,128)} %param.21), channel_id=1, source_target_pairs={{0,1},{1,0},{2,3},{3,2},{4,5},{5,4},{6,7},{7,6},{8,9},{9,8},{10,11... | collective-permute-start | bytes 1572872 | tf_op jit(solution)/shard_map/ppermute | solution.py:621
  18.3 7.8 %collective-permute-start.4 = (bf16[1,2,256,256]{3,2,1,0:T(8,128)(2,1)}, bf16[1,2,256,256]{3,2,1,0:T(8,128)(2,1)}, u32[]{:S(2)}, u32[]{:S(2)}) collective-permute-start(bf16[1,2,256,256]{3,2,1,0:T(8,128)(2,1)} %get-tuple-element.197), channel_id=1, source_target_pairs={{0,2},{1,3},{4,6},{5,7},{8,10},{9,11},{12,14},{13,15},{16,18},{17,... | collective-permute-start | bytes 786440 | tf_op jit(solution)/shard_map/ppermute | solution.py:635
  26.1 14.6 %collective-permute-start.6 = (bf16[1,2,256,256]{3,2,1,0:T(8,128)(2,1)S(1)}, bf16[1,2,256,256]{3,2,1,0:T(8,128)(2,1)S(1)}, u32[]{:S(2)}, u32[]{:S(2)}) collective-permute-start(bf16[1,2,256,256]{3,2,1,0:T(8,128)(2,1)S(1)} %get-tuple-element.171), channel_id=1, source_target_pairs={{2,0},{3,1},{6,4},{7,5},{10,8},{11,9},{14,12},{15,13},{18,16},{19,... | collective-permute-start | bytes 786440 | tf_op jit(solution)/shard_map/ppermute | solution.py:662
  43.7 1.6 %collective-permute-start.8 = (bf16[2,256,256]{2,1,0:T(8,128)(2,1)S(1)}, bf16[2,256,256]{2,1,0:T(8,128)(2,1)S(1)}, u32[]{:S(2)}, u32[]{:S(2)}) collective-permute-start(bf16[2,256,256]{2,1,0:T(8,128)(2,1)S(1)} %constant_dynamic-slice_fusion.1), channel_id=1, source_target_pairs={{0,1},{1,0},{2,3},{3,2},{4,5},{5,4},{6,7},{7,6},{8,9},{9,8},{10,11... | collective-permute-start | bytes 786440 | tf_op jit(solution)/shard_map/ppermute | solution.py:670
  45.3 9.5 %collective-permute-start.9 = (bf16[2,256,256]{2,1,0:T(8,128)(2,1)S(1)}, bf16[2,256,256]{2,1,0:T(8,128)(2,1)S(1)}, u32[]{:S(2)}, u32[]{:S(2)}) collective-permute-start(bf16[2,256,256]{2,1,0:T(8,128)(2,1)S(1)} %add_convert_fusion), channel_id=1, source_target_pairs={{0,4},{4,8},{8,12},{1,5},{5,9},{9,13},{2,6},{6,10},{10,14},{3,7},{... | collective-permute-start | bytes 786440 | tf_op jit(solution)/shard_map/ppermute | solution.py:672
  49.0 5.8 %collective-permute-start.7 = (bf16[2,256,512]{2,1,0:T(8,128)(2,1)S(1)}, bf16[2,256,512]{2,1,0:T(8,128)(2,1)S(1)}, u32[]{:S(2)}, u32[]{:S(2)}) collective-permute-start(bf16[2,256,512]{2,1,0:T(8,128)(2,1)S(1)} %get-tuple-element.184), channel_id=1, source_target_pairs={{0,1},{1,0},{2,3},{3,2},{4,5},{5,4},{6,7},{7,6},{8,9},{9,8},{10,11... | collective-permute-start | bytes 1572872 | tf_op jit(solution)/shard_map/ppermute | solution.py:674
  54.8 1.5 %collective-permute-start.10 = (bf16[2,256,256]{2,1,0:T(8,128)(2,1)S(1)}, bf16[2,256,256]{2,1,0:T(8,128)(2,1)S(1)}, u32[]{:S(2)}, u32[]{:S(2)}) collective-permute-start(bf16[2,256,256]{2,1,0:T(8,128)(2,1)S(1)} %collective-permute-done.9), channel_id=1, source_target_pairs={{0,1},{1,0},{2,3},{3,2},{4,5},{5,4},{6,7},{7,6},{8,9},{9,8},{10,11... | collective-permute-start | bytes 786440 | tf_op jit(solution)/shard_map/ppermute | solution.py:675

commit v23 on v22

--- a/solution.py
+++ b/solution.py
@@ -310,7 +310,7 @@
     return (out_re.astype(jnp.float32), out_im.astype(jnp.float32))
 
 
-def place_term(term_re, term_im, row, column, alive, total_ref, direct_ref=None):
+def place_term(term_re, term_im, row, column, alive, total_ref, direct_ref=None, pad_ref=None):
     width = term_re.shape[0]
     height = total_ref.shape[1]
     columns_all = total_ref.shape[2]
@@ -318,6 +318,16 @@
     column_shift = column % columns_all
     for part, term in enumerate((term_re, term_im)):
         term = jnp.where(alive, term, 0.0)
+        if direct_ref is not None and pad_ref is not None:
+            pad_ref[...] = jnp.zeros(pad_ref.shape, jnp.float32)
+            block = jnp.concatenate([term, jnp.zeros((width, 128), jnp.float32)], axis=1)
+            block = jnp.concatenate([block, jnp.zeros((8, width + 128), jnp.float32)], axis=0)
+            block = pltpu.roll(pltpu.roll(block, row % 8, 0), column % 128, 1)
+            aligned = pl.multiple_of((row // 8) * 8, 8)
+            across = pl.multiple_of((column // 128) * 128, 128)
+            pad_ref[pl.ds(aligned, width + 8), pl.ds(across, width + 128)] = block
+            direct_ref[part] = pad_ref[:height, :columns_all].astype(direct_ref.dtype)
+            continue
         wide = jnp.concatenate(
             [term, jnp.zeros((width, columns_all - width), jnp.float32)], axis=1
         )
@@ -357,10 +367,10 @@
         else:
             source_ref = refs.pop(0)
         if opening:
-            grad_ref, total_ref = refs
+            grad_ref, total_ref, pad_ref = refs
             passed_ref = None
         else:
-            passed_ref, grad_ref, total_ref = refs
+            passed_ref, grad_ref, total_ref, pad_ref = refs
         index = pl.program_id(0)
 
         if not single:
@@ -402,7 +412,7 @@
         term_im = source_re * spread_im - source_im * spread_re
         place_term(
             term_re, term_im, rows_ref[index], columns_ref[index], live_ref[index] > 0,
-            total_ref, grad_ref if single else None,
+            total_ref, grad_ref if single else None, pad_ref,
         )
 
         if not single:
@@ -434,7 +444,10 @@
         out_specs=((() if opening else (wave_spec,))
                    + ((wave_spec,) if last else
                       (pl.BlockSpec((2, height, columns_all), lambda i, *s: (0, 0, 0)),))),
-        scratch_shapes=[pltpu.VMEM((2, height, columns_all), jnp.float32)],
+        scratch_shapes=[
+            pltpu.VMEM((2, height, columns_all), jnp.float32),
+            pltpu.VMEM((height + 8, columns_all + 128), jnp.float32),
+        ],
     )
     return pl.pallas_call(
         adjoint_kernel(last, number == 1, opening),

time: 57.9 us -> 57.7 us (level)
  no operation moved by 1% of the time
where the time goes in v23:
time: 57.7 us; the launch traced here: 57.3 us
  waiting for transfers between devices  29.6 us (51%)
  starting transfers between devices  9.21 us (16%)
  Pallas kernels  7.61 us (13%)
  other arithmetic  4.25 us (7%)
  between operations  4.04 us (7%)
  local copies, waits for them, and re-layouts  2.58 us (4%)
    ppermute x1, waiting for transfers between devices, local(): carry = lax.ppermute(carry, 'depth', [(turn + 1, turn)])  13.2 us
    ppermute x1, waiting for transfers between devices, local(): lax.ppermute(spill_sum, 'tile', [(t, t + 1) for t in range(tile_count - 1)])  5.75 us
    ppermute x1, waiting for transfers between devices, from_behind(): return lax.ppermute(block, axis, route)  4.48 us
    ppermute x1, starting transfers between devices, local(): lax.ppermute(spill_sum, 'tile', [(t, t + 1) for t in range(tile_count - 1)])  3.65 us
    pallas_call x1, Pallas kernels, run_first(): pl.pallas_call(first_kernel, grid_spec=grid_spec, out_shape=jax.ShapeDtyp...  3.4 us
    ppermute x1, waiting for transfers between devices, local(): carry = lax.ppermute(carry, 'depth', [(depth_count - 2, depth_count - 1)])  2.92 us
    pallas_call x1, Pallas kernels, run_adjoint(): pl.pallas_call(adjoint_kernel(last, number == 1, opening), grid_spec=grid...  2.62 us
    ppermute x1, starting transfers between devices, local(): carry = lax.ppermute(carry, 'depth', [(depth_count - 2, depth_count - 1)])  1.99 us
  transfers between devices with their start and end apart: 11, of which 7 were waited for; matrix products, arithmetic and copies ran while one was open for 9% of the time, Pallas kernels for 3%

profile of v23, /device:TPU:0, one launch (start us, length us, event | category | flops | bytes accessed | tf_op | source)
XLA Modules:
  0.0 57.3 jit_solution(10648373204594919575)
XLA Ops:
  0.0 0.5 collective-permute-start
  0.5 0.1 collective-permute-start.1
  0.5 1.1 %dynamic-slice_convert_fusion = bf16[1,2,256,256]{3,2,1,0:T(8,128)(2,1)S(1)} fusion(f32[1,2,256,512]{3,2,1,0:T(8,128)} %tile_ref.1, s32[]{:T(128)S(6)} %select_n.84), kind=kLoop, calls=%fused_computation.4 | loop fusion | bytes 524292 | tf_op jit(solution)/shard_map/convert_element_type | solution.py:576
  1.6 1.3 %collective-permute-start.2 = (bf16[1,2,256,256]{3,2,1,0:T(8,128)(2,1)S(1)}, bf16[1,2,256,256]{3,2,1,0:T(8,128)(2,1)S(1)}, u32[]{:S(2)}, u32[]{:S(2)}) collective-permute-start(bf16[1,2,256,256]{3,2,1,0:T(8,128)(2,1)S(1)} %dynamic-slice_convert_fusion), channel_id=1, source_target_pairs={{4,0},{8,4},{12,8},{5,1},{9,5},{13,9},{6,2},{10,6},{14,10},{7,3},{... | collective-permute-start | bytes 786440 | tf_op jit(solution)/shard_map/ppermute | solution.py:18
  2.9 1.1 %multiply_convert_fusion = (bf16[256,256]{1,0:T(8,128)(2,1)S(1)}, bf16[256,256]{1,0:T(8,128)(2,1)S(1)}) fusion(), kind=kLoop, calls=%fused_computation.13 | loop fusion | flops 1245184 | bytes 262144 | tf_op jit(solution)/shard_map/convert_element_type | solution.py:51
  4.0 1.0 %fusion.6 = (f32[1,256,256]{2,1,0:T(8,128)S(1)}, f32[1,256,256]{2,1,0:T(8,128)S(1)}) fusion(s32[256]{0:T(256)S(1)} %fusion.9, f32[]{:T(128)S(6)} %neg.8), kind=kLoop, calls=%fused_computation.19 | loop fusion | flops 196608 | bytes 525316 | tf_op jit(solution)/shard_map/cos | solution.py:61
  5.9 0.8 %broadcast_select_fusion = s32[2]{0:T(128)S(1)} fusion(pred[]{:T(512)} %eq.24, s32[1]{0:T(128)} %collective-permute-done.1, s32[1]{0:T(128)S(6)} %copy.16), kind=kLoop, calls=%fused_computation.30 | loop fusion | flops 6 | bytes 17 | tf_op jit(solution)/shard_map/jit(_where)/select_n | solution.py:589
  6.7 0.7 %fusion.12 = (s32[1]{0:T(128)}, s32[1]{0:T(128)}) fusion(s32[2]{0:T(128)S(1)} %broadcast_select_fusion), kind=kLoop, calls=%fused_computation.32 | loop fusion | bytes 16 | tf_op jit(solution)/shard_map/slice | solution.py:593
  8.5 4.5 %collective-permute-done.2.mine_ref = bf16[1,2,256,256]{3,2,1,0:T(8,128)(2,1)S(1)} collective-permute-done((bf16[1,2,256,256]{3,2,1,0:T(8,128)(2,1)S(1)}, bf16[1,2,256,256]{3,2,1,0:T(8,128)(2,1)S(1)}, u32[]{:S(2)}, u32[]{:S(2)}) %collective-permute-start.2) | collective-permute-done | bytes 262176 | tf_op jit(solution)/shard_map/ppermute | solution.py:18
  13.0 0.6 %fusion.13 = (s32[1,1]{1,0:T(1,128)}, s32[1,1]{1,0:T(1,128)}) fusion(s32[1,2]{1,0:T(1,128)S(1)} %constant_dynamic-slice_fusion), kind=kLoop, calls=%fused_computation.33 | loop fusion | bytes 16 | tf_op jit(solution)/shard_map/slice | solution.py:600
  14.3 0.2 collective-permute-done.3.partner_ref
  14.5 3.4 %conditional.4 = (bf16[1,2,256,256]{3,2,1,0:T(8,128)(2,1)}) conditional(s32[]{:T(128)} %convert_element_type.72, () %tuple.58, (s32[1]{0:T(128)}, s32[1]{0:T(128)}, s32[1]{0:T(128)}, bf16[1,2,256,256]{3,2,1,0:T(8,128)(2,1)S(1)}, f32[1,2,256,512]{3,2,1,0:T(8,128)S(1)}, /*index=5*/bf16[1,2,256,256]{3,2,1,0:T(8,128)(2,1)S(1)}, ...), branch_computations={%region_0.1_spmd, %region_1.2_spmd} | conditional | bytes 262154 | solution.py:631
  14.5 3.4 %branch_1_fun.6 = bf16[1,2,256,256]{3,2,1,0:T(8,128)(2,1)} custom-call(s32[1]{0:T(128)} %get-tuple-element.127.rows_ref, s32[1]{0:T(128)} %get-tuple-element.128.columns_ref, s32[1]{0:T(128)} %get-tuple-element.129.order_ref, bf16[1,2,256,256]{3,2,1,0:T(8,128)(2,1)S(1)} %get-tuple-element.130.wave_ref, f32[1,2,256,512]{3,2,1,0:T(8,128)S(1)} %get-tuple-element.131.tile_ref, ...), custom_call_target="tpu_custom_call" | custom-call | tf_op jit(solution)/shard_map/cond/branch_1_fun/pallas_call | solution.py:557
  17.9 0.3 collective-permute-start.5
  18.3 2.0 %collective-permute-start.4 = (bf16[1,2,256,256]{3,2,1,0:T(8,128)(2,1)}, bf16[1,2,256,256]{3,2,1,0:T(8,128)(2,1)}, u32[]{:S(2)}, u32[]{:S(2)}) collective-permute-start(bf16[1,2,256,256]{3,2,1,0:T(8,128)(2,1)} %get-tuple-element.197), channel_id=1, source_target_pairs={{0,2},{1,3},{4,6},{5,7},{8,10},{9,11},{12,14},{13,15},{16,18},{17,... | collective-permute-start | bytes 786440 | tf_op jit(solution)/shard_map/ppermute | solution.py:648
  21.5 1.6 %shard_map.60 = f32[1,2,256,256]{3,2,1,0:T(8,128)S(1)} custom-call(s32[1]{0:T(128)} %sub.17.rows_ref, s32[1]{0:T(128)} %bitcast.4.columns_ref, s32[1]{0:T(128)} %bitcast.order_ref, f32[1,2,256,512]{3,2,1,0:T(8,128)S(1)} %copy-done, bf16[1,2,256,256]{3,2,1,0:T(8,128)(2,1)S(1)} %collective-permute-done.2.mine_ref, ...), custom_call_target="tpu_custom_call" | custom-call | tf_op jit(solution)/shard_map/pallas_call | solution.py:275
  23.1 2.9 %collective-permute-done.4 = bf16[1,2,256,256]{3,2,1,0:T(8,128)(2,1)} collective-permute-done((bf16[1,2,256,256]{3,2,1,0:T(8,128)(2,1)}, bf16[1,2,256,256]{3,2,1,0:T(8,128)(2,1)}, u32[]{:S(2)}, u32[]{:S(2)}) %collective-permute-start.4) | collective-permute-done | bytes 262176 | tf_op jit(solution)/shard_map/ppermute | solution.py:648
  26.1 1.3 %collective-permute-start.6 = (bf16[1,2,256,256]{3,2,1,0:T(8,128)(2,1)S(1)}, bf16[1,2,256,256]{3,2,1,0:T(8,128)(2,1)S(1)}, u32[]{:S(2)}, u32[]{:S(2)}) collective-permute-start(bf16[1,2,256,256]{3,2,1,0:T(8,128)(2,1)S(1)} %get-tuple-element.171), channel_id=1, source_target_pairs={{2,0},{3,1},{6,4},{7,5},{10,8},{11,9},{14,12},{15,13},{18,16},{19,... | collective-permute-start | bytes 786440 | tf_op jit(solution)/shard_map/ppermute | solution.py:675
  27.4 0.1 conditional.6
  27.4 0.1 broadcast.198
  27.5 13.2 %collective-permute-done.6 = bf16[1,2,256,256]{3,2,1,0:T(8,128)(2,1)S(1)} collective-permute-done((bf16[1,2,256,256]{3,2,1,0:T(8,128)(2,1)S(1)}, bf16[1,2,256,256]{3,2,1,0:T(8,128)(2,1)S(1)}, u32[]{:S(2)}, u32[]{:S(2)}) %collective-permute-start.6) | collective-permute-done | bytes 262176 | tf_op jit(solution)/shard_map/ppermute | solution.py:675
  40.7 2.6 %conditional.7 = (bf16[2,512,512]{2,1,0:T(8,128)(2,1)S(1)}) conditional(s32[]{:T(128)} %convert_element_type.72, bf16[2,512,512]{2,1,0:T(8,128)(2,1)S(1)} %get-tuple-element.199, (s32[1]{0:T(128)}, s32[1]{0:T(128)}, s32[1]{0:T(128)}, s32[1]{0:T(128)}, s32[1]{0:T(128)}, /*index=5*/bf16[1,2,256,256]{3,2,1,0:T(8,128)(2,1)S(1)}, ...), branch_computations={%region_6.7_spmd, %region_7.8_spmd} | conditional | bytes 8 | solution.py:677
  40.7 2.6 %branch_1_fun.9 = bf16[2,512,512]{2,1,0:T(8,128)(2,1)S(1)} custom-call(s32[1]{0:T(128)} %get-tuple-element.154.rows_ref, s32[1]{0:T(128)} %get-tuple-element.155.columns_ref, s32[1]{0:T(128)} %get-tuple-element.156.live_ref, s32[1]{0:T(128)} %get-tuple-element.157.slot_ref, s32[1]{0:T(128)} %get-tuple-element.158.other_ref, ...), custom_call_target="tpu_custom_call" | custom-call | tf_op jit(solution)/shard_map/cond/branch_1_fun/pallas_call | solution.py:452
  43.3 0.1 fusion.11
  43.4 0.1 collective-permute-start.8
  43.5 1.5 %collective-permute-done.8 = bf16[2,256,256]{2,1,0:T(8,128)(2,1)S(1)} collective-permute-done((bf16[2,256,256]{2,1,0:T(8,128)(2,1)S(1)}, bf16[2,256,256]{2,1,0:T(8,128)(2,1)S(1)}, u32[]{:S(2)}, u32[]{:S(2)}) %collective-permute-start.8) | collective-permute-done | bytes 262176 | tf_op jit(solution)/shard_map/ppermute | solution.py:683
  45.0 0.1 add_convert_fusion
  45.1 3.7 %collective-permute-start.9 = (bf16[2,256,256]{2,1,0:T(8,128)(2,1)S(1)}, bf16[2,256,256]{2,1,0:T(8,128)(2,1)S(1)}, u32[]{:S(2)}, u32[]{:S(2)}) collective-permute-start(bf16[2,256,256]{2,1,0:T(8,128)(2,1)S(1)} %add_convert_fusion), channel_id=1, source_target_pairs={{0,4},{4,8},{8,12},{1,5},{5,9},{9,13},{2,6},{6,10},{10,14},{3,7},{... | collective-permute-start | bytes 786440 | tf_op jit(solution)/shard_map/ppermute | solution.py:685
  48.7 0.1 collective-permute-start.7
  48.8 5.8 %collective-permute-done.9 = bf16[2,256,256]{2,1,0:T(8,128)(2,1)S(1)} collective-permute-done((bf16[2,256,256]{2,1,0:T(8,128)(2,1)S(1)}, bf16[2,256,256]{2,1,0:T(8,128)(2,1)S(1)}, u32[]{:S(2)}, u32[]{:S(2)}) %collective-permute-start.9) | collective-permute-done | bytes 262176 | tf_op jit(solution)/shard_map/ppermute | solution.py:685
  54.6 1.5 %collective-permute-done.10 = bf16[2,256,256]{2,1,0:T(8,128)(2,1)S(1)} collective-permute-done((bf16[2,256,256]{2,1,0:T(8,128)(2,1)S(1)}, bf16[2,256,256]{2,1,0:T(8,128)(2,1)S(1)}, u32[]{:S(2)}, u32[]{:S(2)}) %collective-permute-start.10) | collective-permute-done | bytes 262176 | tf_op jit(solution)/shard_map/ppermute | solution.py:688
  56.1 1.2 %add_bitcast_fusion = f32[1,2,256,512]{3,2,1,0:T(8,128)} fusion(bf16[2,256,512]{2,1,0:T(8,128)(2,1)S(1)} %collective-permute-done.7, bf16[2,256,256]{2,1,0:T(8,128)(2,1)S(1)} %collective-permute-done.10, bf16[2,256,256]{2,1,0:T(8,128)(2,1)S(1)} %collective-permute-done.9, pred[]{:T(512)} %eq.24, bf16[2,512,512]{2,1,0:T(8,128)(2,1)S(1)} %get-tuple-element.200), kind=kLoop, calls=%fused_computation | loop fusion | flops 3670016 | bytes 2621441 | tf_op jit(solution)/shard_map/broadcast_in_dim | solution.py:696
  (22 shorter events, 0.3 us)
Async XLA Ops:
  0.0 13.0 %collective-permute-start = (s32[2,2]{1,0:T(2,128)}, s32[2,2]{1,0:T(2,128)S(1)}, u32[]{:S(2)}, u32[]{:S(2)}) collective-permute-start(s32[2,2]{1,0:T(2,128)} %param.19), channel_id=1, source_target_pairs={{0,1},{1,0},{2,3},{3,2},{4,5},{5,4},{6,7},{7,6},{8,9},{9,8},{10,11... | collective-permute-start | bytes 56 | tf_op jit(solution)/shard_map/ppermute | solution.py:582
  0.5 5.4 %collective-permute-start.1 = (s32[1]{0:T(128)}, s32[1]{0:T(128)}, u32[]{:S(2)}, u32[]{:S(2)}) collective-permute-start(s32[1]{0:T(128)} %param.20), channel_id=1, source_target_pairs={{0,1},{1,0},{2,3},{3,2},{4,5},{5,4},{6,7},{7,6},{8,9},{9,8},{10,11... | collective-permute-start | bytes 20 | tf_op jit(solution)/shard_map/ppermute | solution.py:583
  1.6 11.4 %collective-permute-start.2 = (bf16[1,2,256,256]{3,2,1,0:T(8,128)(2,1)S(1)}, bf16[1,2,256,256]{3,2,1,0:T(8,128)(2,1)S(1)}, u32[]{:S(2)}, u32[]{:S(2)}) collective-permute-start(bf16[1,2,256,256]{3,2,1,0:T(8,128)(2,1)S(1)} %dynamic-slice_convert_fusion), channel_id=1, source_target_pairs={{4,0},{8,4},{12,8},{5,1},{9,5},{13,9},{6,2},{10,6},{14,10},{7,3},{... | collective-permute-start | bytes 786440 | tf_op jit(solution)/shard_map/ppermute | solution.py:18
  5.0 9.5 %copy-start = (f32[1,2,256,512]{3,2,1,0:T(8,128)S(1)}, f32[1,2,256,512]{3,2,1,0:T(8,128)}, u32[]{:S(2)}) copy-start(f32[1,2,256,512]{3,2,1,0:T(8,128)} %tile_ref.1) | copy-start | bytes 3145732
  5.1 9.4 %copy-start.1 = (bf16[2,256,256]{2,1,0:T(8,128)(2,1)S(1)}, bf16[2,256,256]{2,1,0:T(8,128)(2,1)}, u32[]{:S(2)}) copy-start(bf16[2,256,256]{2,1,0:T(8,128)(2,1)} %param.18) | copy-start | bytes 786436
  8.5 4.5 %copy-start.2 = (s32[2,2]{1,0:T(2,128)S(1)}, s32[2,2]{1,0:T(2,128)}, u32[]{:S(2)}) copy-start(s32[2,2]{1,0:T(2,128)} %param.19) | copy-start | bytes 52
  13.0 1.5 %collective-permute-start.3 = (bf16[1,2,256,256]{3,2,1,0:T(8,128)(2,1)S(1)}, bf16[1,2,256,256]{3,2,1,0:T(8,128)(2,1)S(1)}, u32[]{:S(2)}, u32[]{:S(2)}) collective-permute-start(bf16[1,2,256,256]{3,2,1,0:T(8,128)(2,1)S(1)} %collective-permute-done.2.mine_ref), channel_id=1, source_target_pairs={{0,1},{1,0},{2,3},{3,2},{4,5},{5,4},{6,7},{7,6},{8,9},{9,8},{10,11... | collective-permute-start | bytes 786440 | tf_op jit(solution)/shard_map/ppermute | solution.py:578
  17.9 8.1 %collective-permute-start.5 = (f32[2,256,256]{2,1,0:T(8,128)}, f32[2,256,256]{2,1,0:T(8,128)}, u32[]{:S(2)}, u32[]{:S(2)}) collective-permute-start(f32[2,256,256]{2,1,0:T(8,128)} %param.21), channel_id=1, source_target_pairs={{0,1},{1,0},{2,3},{3,2},{4,5},{5,4},{6,7},{7,6},{8,9},{9,8},{10,11... | collective-permute-start | bytes 1572872 | tf_op jit(solution)/shard_map/ppermute | solution.py:634
  18.3 7.8 %collective-permute-start.4 = (bf16[1,2,256,256]{3,2,1,0:T(8,128)(2,1)}, bf16[1,2,256,256]{3,2,1,0:T(8,128)(2,1)}, u32[]{:S(2)}, u32[]{:S(2)}) collective-permute-start(bf16[1,2,256,256]{3,2,1,0:T(8,128)(2,1)} %get-tuple-element.197), channel_id=1, source_target_pairs={{0,2},{1,3},{4,6},{5,7},{8,10},{9,11},{12,14},{13,15},{16,18},{17,... | collective-permute-start | bytes 786440 | tf_op jit(solution)/shard_map/ppermute | solution.py:648
  26.1 14.6 %collective-permute-start.6 = (bf16[1,2,256,256]{3,2,1,0:T(8,128)(2,1)S(1)}, bf16[1,2,256,256]{3,2,1,0:T(8,128)(2,1)S(1)}, u32[]{:S(2)}, u32[]{:S(2)}) collective-permute-start(bf16[1,2,256,256]{3,2,1,0:T(8,128)(2,1)S(1)} %get-tuple-element.171), channel_id=1, source_target_pairs={{2,0},{3,1},{6,4},{7,5},{10,8},{11,9},{14,12},{15,13},{18,16},{19,... | collective-permute-start | bytes 786440 | tf_op jit(solution)/shard_map/ppermute | solution.py:675
  43.4 1.6 %collective-permute-start.8 = (bf16[2,256,256]{2,1,0:T(8,128)(2,1)S(1)}, bf16[2,256,256]{2,1,0:T(8,128)(2,1)S(1)}, u32[]{:S(2)}, u32[]{:S(2)}) collective-permute-start(bf16[2,256,256]{2,1,0:T(8,128)(2,1)S(1)} %constant_dynamic-slice_fusion.1), channel_id=1, source_target_pairs={{0,1},{1,0},{2,3},{3,2},{4,5},{5,4},{6,7},{7,6},{8,9},{9,8},{10,11... | collective-permute-start | bytes 786440 | tf_op jit(solution)/shard_map/ppermute | solution.py:683
  45.1 9.5 %collective-permute-start.9 = (bf16[2,256,256]{2,1,0:T(8,128)(2,1)S(1)}, bf16[2,256,256]{2,1,0:T(8,128)(2,1)S(1)}, u32[]{:S(2)}, u32[]{:S(2)}) collective-permute-start(bf16[2,256,256]{2,1,0:T(8,128)(2,1)S(1)} %add_convert_fusion), channel_id=1, source_target_pairs={{0,4},{4,8},{8,12},{1,5},{5,9},{9,13},{2,6},{6,10},{10,14},{3,7},{... | collective-permute-start | bytes 786440 | tf_op jit(solution)/shard_map/ppermute | solution.py:685
  48.7 5.8 %collective-permute-start.7 = (bf16[2,256,512]{2,1,0:T(8,128)(2,1)S(1)}, bf16[2,256,512]{2,1,0:T(8,128)(2,1)S(1)}, u32[]{:S(2)}, u32[]{:S(2)}) collective-permute-start(bf16[2,256,512]{2,1,0:T(8,128)(2,1)S(1)} %get-tuple-element.184), channel_id=1, source_target_pairs={{0,1},{1,0},{2,3},{3,2},{4,5},{5,4},{6,7},{7,6},{8,9},{9,8},{10,11... | collective-permute-start | bytes 1572872 | tf_op jit(solution)/shard_map/ppermute | solution.py:687
  54.6 1.5 %collective-permute-start.10 = (bf16[2,256,256]{2,1,0:T(8,128)(2,1)S(1)}, bf16[2,256,256]{2,1,0:T(8,128)(2,1)S(1)}, u32[]{:S(2)}, u32[]{:S(2)}) collective-permute-start(bf16[2,256,256]{2,1,0:T(8,128)(2,1)S(1)} %collective-permute-done.9), channel_id=1, source_target_pairs={{0,1},{1,0},{2,3},{3,2},{4,5},{5,4},{6,7},{7,6},{8,9},{9,8},{10,11... | collective-permute-start | bytes 786440 | tf_op jit(solution)/shard_map/ppermute | solution.py:688

commit v24 on v23

--- a/solution.py
+++ b/solution.py
@@ -579,8 +579,10 @@
     capacity = positions.shape[0]
     share = -(-capacity // batch_count)
     first_core = batch_index == 0
-    both_positions = lax.ppermute(positions, "batch", pairs)
-    both_counts = lax.ppermute(counts, "batch", pairs)
+    packed = jnp.concatenate([positions, jnp.broadcast_to(counts[:, None], (1, 2))])
+    both_packed = lax.ppermute(packed, "batch", pairs)
+    both_positions = both_packed[:-1]
+    both_counts = both_packed[-1, :1]
     all_positions = jnp.where(
         first_core,
         jnp.concatenate([positions, both_positions]),

time: 57.7 us -> 60.1 us (1.042)
  local copies, waits for them, and re-layouts: 2.58 us -> 3.84 us
  waiting for transfers between devices: 29.6 us -> 30.4 us
    ppermute x1, waiting for transfers between devices: 4.48 us -> 5.87 us  [from_behind(): return lax.ppermute(block, axis, route)]
    unnamed x6 -> x8, local copies, waits for them, and re-layouts: 0.02 us -> 0.69 us
  transfers between devices with their start and end apart: 11 -> 10, of which waited for: 7 -> 6; matrix products, arithmetic and copies ran while one was open for 9% -> 10% of each run, Pallas kernels for 3% -> 3%
where the time goes in v24:
time: 60.1 us; the launch traced here: 59.7 us
  waiting for transfers between devices  30.4 us (51%)
  starting transfers between devices  9.35 us (16%)
  Pallas kernels  7.75 us (13%)
  other arithmetic  4.25 us (7%)
  between operations  4.12 us (7%)
  local copies, waits for them, and re-layouts  3.84 us (6%)
    ppermute x1, waiting for transfers between devices, local(): carry = lax.ppermute(carry, 'depth', [(turn + 1, turn)])  13 us
    ppermute x1, waiting for transfers between devices, from_behind(): return lax.ppermute(block, axis, route)  5.87 us
    ppermute x1, waiting for transfers between devices, local(): lax.ppermute(spill_sum, 'tile', [(t, t + 1) for t in range(tile_count - 1)])  5.75 us
    ppermute x1, starting transfers between devices, local(): lax.ppermute(spill_sum, 'tile', [(t, t + 1) for t in range(tile_count - 1)])  3.66 us
    pallas_call x1, Pallas kernels, run_first(): pl.pallas_call(first_kernel, grid_spec=grid_spec, out_shape=jax.ShapeDtyp...  3.45 us
    ppermute x1, waiting for transfers between devices, local(): carry = lax.ppermute(carry, 'depth', [(depth_count - 2, depth_count - 1)])  2.67 us
    pallas_call x1, Pallas kernels, run_adjoint(): pl.pallas_call(adjoint_kernel(last, number == 1, opening), grid_spec=grid...  2.67 us
    ppermute x1, starting transfers between devices, local(): carry = lax.ppermute(carry, 'depth', [(depth_count - 2, depth_count - 1)])  2 us
  transfers between devices with their start and end apart: 10, of which 6 were waited for; matrix products, arithmetic and copies ran while one was open for 10% of the time, Pallas kernels for 3%

profile of v24, /device:TPU:0, one launch (start us, length us, event | category | flops | bytes accessed | tf_op | source)
XLA Modules:
  0.0 59.7 jit_solution(10504774199887675249)
XLA Ops:
  0.7 0.7 %copy-done.2 = s32[2,2]{1,0:T(2,128)S(1)} copy-done((s32[2,2]{1,0:T(2,128)S(1)}, s32[2,2]{1,0:T(2,128)}, u32[]{:S(2)}) %copy-start.2) | copy-done | bytes 40
  1.3 0.5 collective-permute-start
  1.8 1.1 %dynamic-slice_convert_fusion = bf16[1,2,256,256]{3,2,1,0:T(8,128)(2,1)S(1)} fusion(f32[1,2,256,512]{3,2,1,0:T(8,128)} %tile_ref.1, s32[]{:T(128)S(6)} %select_n.84), kind=kLoop, calls=%fused_computation.4 | loop fusion | bytes 524292 | tf_op jit(solution)/shard_map/convert_element_type | solution.py:576
  2.9 1.3 %collective-permute-start.1 = (bf16[1,2,256,256]{3,2,1,0:T(8,128)(2,1)S(1)}, bf16[1,2,256,256]{3,2,1,0:T(8,128)(2,1)S(1)}, u32[]{:S(2)}, u32[]{:S(2)}) collective-permute-start(bf16[1,2,256,256]{3,2,1,0:T(8,128)(2,1)S(1)} %dynamic-slice_convert_fusion), channel_id=1, source_target_pairs={{4,0},{8,4},{12,8},{5,1},{9,5},{13,9},{6,2},{10,6},{14,10},{7,3},{... | collective-permute-start | bytes 786440 | tf_op jit(solution)/shard_map/ppermute | solution.py:18
  4.2 1.1 %multiply_convert_fusion = (bf16[256,256]{1,0:T(8,128)(2,1)S(1)}, bf16[256,256]{1,0:T(8,128)(2,1)S(1)}) fusion(), kind=kLoop, calls=%fused_computation.13 | loop fusion | flops 1245184 | bytes 262144 | tf_op jit(solution)/shard_map/convert_element_type | solution.py:51
  5.3 1.0 %fusion.6 = (f32[1,256,256]{2,1,0:T(8,128)S(1)}, f32[1,256,256]{2,1,0:T(8,128)S(1)}) fusion(s32[256]{0:T(256)S(1)} %fusion.9, f32[]{:T(128)S(6)} %neg.8), kind=kLoop, calls=%fused_computation.19 | loop fusion | flops 196608 | bytes 525316 | tf_op jit(solution)/shard_map/cos | solution.py:61
  6.5 0.6 slice.66
  7.1 0.8 %broadcast_select_fusion = s32[2]{0:T(128)S(1)} fusion(pred[]{:T(512)} %eq.24, s32[1]{0:T(128)} %bitcast.2, s32[1]{0:T(128)} %copy.16), kind=kLoop, calls=%fused_computation.30 | loop fusion | flops 6 | bytes 17 | tf_op jit(solution)/shard_map/jit(_where)/select_n | solution.py:591
  7.8 0.6 %fusion.12 = (s32[1]{0:T(128)}, s32[1]{0:T(128)}) fusion(s32[2]{0:T(128)S(1)} %broadcast_select_fusion), kind=kLoop, calls=%fused_computation.32 | loop fusion | bytes 16 | tf_op jit(solution)/shard_map/slice | solution.py:595
  8.4 5.9 %collective-permute-done.1.mine_ref = bf16[1,2,256,256]{3,2,1,0:T(8,128)(2,1)S(1)} collective-permute-done((bf16[1,2,256,256]{3,2,1,0:T(8,128)(2,1)S(1)}, bf16[1,2,256,256]{3,2,1,0:T(8,128)(2,1)S(1)}, u32[]{:S(2)}, u32[]{:S(2)}) %collective-permute-start.1) | collective-permute-done | bytes 262176 | tf_op jit(solution)/shard_map/ppermute | solution.py:18
  15.6 0.7 %fusion.13 = (s32[1,1]{1,0:T(1,128)}, s32[1,1]{1,0:T(1,128)}) fusion(s32[1,2]{1,0:T(1,128)S(1)} %constant_dynamic-slice_fusion), kind=kLoop, calls=%fused_computation.33 | loop fusion | bytes 16 | tf_op jit(solution)/shard_map/slice | solution.py:602
  17.0 3.5 %conditional.4 = (bf16[1,2,256,256]{3,2,1,0:T(8,128)(2,1)}) conditional(s32[]{:T(128)} %convert_element_type.72, () %tuple.58, (s32[1]{0:T(128)}, s32[1]{0:T(128)}, s32[1]{0:T(128)}, bf16[1,2,256,256]{3,2,1,0:T(8,128)(2,1)S(1)}, f32[1,2,256,512]{3,2,1,0:T(8,128)S(1)}, /*index=5*/bf16[1,2,256,256]{3,2,1,0:T(8,128)(2,1)S(1)}, ...), branch_computations={%region_0.1_spmd, %region_1.2_spmd} | conditional | bytes 262154 | solution.py:633
  17.0 3.4 %branch_1_fun.6 = bf16[1,2,256,256]{3,2,1,0:T(8,128)(2,1)} custom-call(s32[1]{0:T(128)} %get-tuple-element.127.rows_ref, s32[1]{0:T(128)} %get-tuple-element.128.columns_ref, s32[1]{0:T(128)} %get-tuple-element.129.order_ref, bf16[1,2,256,256]{3,2,1,0:T(8,128)(2,1)S(1)} %get-tuple-element.130.wave_ref, f32[1,2,256,512]{3,2,1,0:T(8,128)S(1)} %get-tuple-element.131.tile_ref, ...), custom_call_target="tpu_custom_call" | custom-call | tf_op jit(solution)/shard_map/cond/branch_1_fun/pallas_call | solution.py:557
  20.4 0.5 collective-permute-start.4
  20.9 2.0 %collective-permute-start.3 = (bf16[1,2,256,256]{3,2,1,0:T(8,128)(2,1)}, bf16[1,2,256,256]{3,2,1,0:T(8,128)(2,1)}, u32[]{:S(2)}, u32[]{:S(2)}) collective-permute-start(bf16[1,2,256,256]{3,2,1,0:T(8,128)(2,1)} %get-tuple-element.197), channel_id=1, source_target_pairs={{0,2},{1,3},{4,6},{5,7},{8,10},{9,11},{12,14},{13,15},{16,18},{17,... | collective-permute-start | bytes 786440 | tf_op jit(solution)/shard_map/ppermute | solution.py:650
  24.2 1.6 %shard_map.60 = f32[1,2,256,256]{3,2,1,0:T(8,128)S(1)} custom-call(s32[1]{0:T(128)} %sub.17.rows_ref, s32[1]{0:T(128)} %bitcast.6.columns_ref, s32[1]{0:T(128)} %bitcast.1.order_ref, f32[1,2,256,512]{3,2,1,0:T(8,128)S(1)} %copy-done, bf16[1,2,256,256]{3,2,1,0:T(8,128)(2,1)S(1)} %collective-permute-done.1.mine_ref, ...), custom_call_target="tpu_custom_call" | custom-call | tf_op jit(solution)/shard_map/pallas_call | solution.py:275
  25.9 2.7 %collective-permute-done.3 = bf16[1,2,256,256]{3,2,1,0:T(8,128)(2,1)} collective-permute-done((bf16[1,2,256,256]{3,2,1,0:T(8,128)(2,1)}, bf16[1,2,256,256]{3,2,1,0:T(8,128)(2,1)}, u32[]{:S(2)}, u32[]{:S(2)}) %collective-permute-start.3) | collective-permute-done | bytes 262176 | tf_op jit(solution)/shard_map/ppermute | solution.py:650
  28.6 1.3 %collective-permute-start.5 = (bf16[1,2,256,256]{3,2,1,0:T(8,128)(2,1)S(1)}, bf16[1,2,256,256]{3,2,1,0:T(8,128)(2,1)S(1)}, u32[]{:S(2)}, u32[]{:S(2)}) collective-permute-start(bf16[1,2,256,256]{3,2,1,0:T(8,128)(2,1)S(1)} %get-tuple-element.171), channel_id=1, source_target_pairs={{2,0},{3,1},{6,4},{7,5},{10,8},{11,9},{14,12},{15,13},{18,16},{19,... | collective-permute-start | bytes 786440 | tf_op jit(solution)/shard_map/ppermute | solution.py:677
  29.9 0.1 conditional.6
  29.9 0.1 broadcast.199
  30.0 13.0 %collective-permute-done.5 = bf16[1,2,256,256]{3,2,1,0:T(8,128)(2,1)S(1)} collective-permute-done((bf16[1,2,256,256]{3,2,1,0:T(8,128)(2,1)S(1)}, bf16[1,2,256,256]{3,2,1,0:T(8,128)(2,1)S(1)}, u32[]{:S(2)}, u32[]{:S(2)}) %collective-permute-start.5) | collective-permute-done | bytes 262176 | tf_op jit(solution)/shard_map/ppermute | solution.py:677
  43.0 2.7 %conditional.7 = (bf16[2,512,512]{2,1,0:T(8,128)(2,1)S(1)}) conditional(s32[]{:T(128)} %convert_element_type.72, bf16[2,512,512]{2,1,0:T(8,128)(2,1)S(1)} %get-tuple-element.199, (s32[1]{0:T(128)}, s32[1]{0:T(128)}, s32[1]{0:T(128)}, s32[1]{0:T(128)}, s32[1]{0:T(128)}, /*index=5*/bf16[1,2,256,256]{3,2,1,0:T(8,128)(2,1)S(1)}, ...), branch_computations={%region_6.7_spmd, %region_7.8_spmd} | conditional | bytes 8 | solution.py:679
  43.0 2.7 %branch_1_fun.9 = bf16[2,512,512]{2,1,0:T(8,128)(2,1)S(1)} custom-call(s32[1]{0:T(128)} %get-tuple-element.154.rows_ref, s32[1]{0:T(128)} %get-tuple-element.155.columns_ref, s32[1]{0:T(128)} %get-tuple-element.156.live_ref, s32[1]{0:T(128)} %get-tuple-element.157.slot_ref, s32[1]{0:T(128)} %get-tuple-element.158.other_ref, ...), custom_call_target="tpu_custom_call" | custom-call | tf_op jit(solution)/shard_map/cond/branch_1_fun/pallas_call | solution.py:452
  45.7 0.1 fusion.11
  45.8 0.1 collective-permute-start.7
  45.9 1.5 %collective-permute-done.7 = bf16[2,256,256]{2,1,0:T(8,128)(2,1)S(1)} collective-permute-done((bf16[2,256,256]{2,1,0:T(8,128)(2,1)S(1)}, bf16[2,256,256]{2,1,0:T(8,128)(2,1)S(1)}, u32[]{:S(2)}, u32[]{:S(2)}) %collective-permute-start.7) | collective-permute-done | bytes 262176 | tf_op jit(solution)/shard_map/ppermute | solution.py:685
  47.4 0.1 add_convert_fusion
  47.5 3.7 %collective-permute-start.8 = (bf16[2,256,256]{2,1,0:T(8,128)(2,1)S(1)}, bf16[2,256,256]{2,1,0:T(8,128)(2,1)S(1)}, u32[]{:S(2)}, u32[]{:S(2)}) collective-permute-start(bf16[2,256,256]{2,1,0:T(8,128)(2,1)S(1)} %add_convert_fusion), channel_id=1, source_target_pairs={{0,4},{4,8},{8,12},{1,5},{5,9},{9,13},{2,6},{6,10},{10,14},{3,7},{... | collective-permute-start | bytes 786440 | tf_op jit(solution)/shard_map/ppermute | solution.py:687
  51.2 0.1 collective-permute-start.6
  51.2 5.8 %collective-permute-done.8 = bf16[2,256,256]{2,1,0:T(8,128)(2,1)S(1)} collective-permute-done((bf16[2,256,256]{2,1,0:T(8,128)(2,1)S(1)}, bf16[2,256,256]{2,1,0:T(8,128)(2,1)S(1)}, u32[]{:S(2)}, u32[]{:S(2)}) %collective-permute-start.8) | collective-permute-done | bytes 262176 | tf_op jit(solution)/shard_map/ppermute | solution.py:687
  57.0 1.5 %collective-permute-done.9 = bf16[2,256,256]{2,1,0:T(8,128)(2,1)S(1)} collective-permute-done((bf16[2,256,256]{2,1,0:T(8,128)(2,1)S(1)}, bf16[2,256,256]{2,1,0:T(8,128)(2,1)S(1)}, u32[]{:S(2)}, u32[]{:S(2)}) %collective-permute-start.9) | collective-permute-done | bytes 262176 | tf_op jit(solution)/shard_map/ppermute | solution.py:690
  58.5 1.2 %add_bitcast_fusion = f32[1,2,256,512]{3,2,1,0:T(8,128)} fusion(bf16[2,256,512]{2,1,0:T(8,128)(2,1)S(1)} %collective-permute-done.6, bf16[2,256,256]{2,1,0:T(8,128)(2,1)S(1)} %collective-permute-done.9, bf16[2,256,256]{2,1,0:T(8,128)(2,1)S(1)} %collective-permute-done.8, pred[]{:T(512)} %eq.24, bf16[2,512,512]{2,1,0:T(8,128)(2,1)S(1)} %get-tuple-element.200), kind=kLoop, calls=%fused_computation | loop fusion | flops 3670016 | bytes 2621441 | tf_op jit(solution)/shard_map/broadcast_in_dim | solution.py:698
  (26 shorter events, 0.3 us)
Async XLA Ops:
  0.7 0.7 %copy-start.2 = (s32[2,2]{1,0:T(2,128)S(1)}, s32[2,2]{1,0:T(2,128)}, u32[]{:S(2)}) copy-start(s32[2,2]{1,0:T(2,128)} %param.19) | copy-start | bytes 52
  1.3 5.1 %collective-permute-start = (s32[3,2]{1,0:T(4,128)S(1)}, s32[3,2]{1,0:T(4,128)S(1)}, u32[]{:S(2)}, u32[]{:S(2)}) collective-permute-start(s32[3,2]{1,0:T(4,128)S(1)} %concatenate.37), channel_id=1, source_target_pairs={{0,1},{1,0},{2,3},{3,2},{4,5},{5,4},{6,7},{7,6},{8,9},{9,8},{10,11... | collective-permute-start | bytes 80 | tf_op jit(solution)/shard_map/ppermute | solution.py:583
  2.9 11.5 %collective-permute-start.1 = (bf16[1,2,256,256]{3,2,1,0:T(8,128)(2,1)S(1)}, bf16[1,2,256,256]{3,2,1,0:T(8,128)(2,1)S(1)}, u32[]{:S(2)}, u32[]{:S(2)}) collective-permute-start(bf16[1,2,256,256]{3,2,1,0:T(8,128)(2,1)S(1)} %dynamic-slice_convert_fusion), channel_id=1, source_target_pairs={{4,0},{8,4},{12,8},{5,1},{9,5},{13,9},{6,2},{10,6},{14,10},{7,3},{... | collective-permute-start | bytes 786440 | tf_op jit(solution)/shard_map/ppermute | solution.py:18
  6.3 10.6 %copy-start = (f32[1,2,256,512]{3,2,1,0:T(8,128)S(1)}, f32[1,2,256,512]{3,2,1,0:T(8,128)}, u32[]{:S(2)}) copy-start(f32[1,2,256,512]{3,2,1,0:T(8,128)} %tile_ref.1) | copy-start | bytes 3145732
  6.4 10.6 %copy-start.1 = (bf16[2,256,256]{2,1,0:T(8,128)(2,1)S(1)}, bf16[2,256,256]{2,1,0:T(8,128)(2,1)}, u32[]{:S(2)}) copy-start(bf16[2,256,256]{2,1,0:T(8,128)(2,1)} %param.18) | copy-start | bytes 786436
  6.5 0.6 %copy-start.3 = (s32[3,2]{1,0:T(4,128)}, s32[3,2]{1,0:T(4,128)S(1)}, u32[]{:S(2)}) copy-start(s32[3,2]{1,0:T(4,128)S(1)} %collective-permute-done) | copy-start | bytes 76
  7.8 6.5 %slice-start = ((s32[3,2]{1,0:T(4,128)}), s32[2,2]{1,0:T(2,128)S(1)}, s32[]{:S(2)}) async-start(s32[3,2]{1,0:T(4,128)} %copy-done.3), calls=%async_computation | async-start | bytes 2048 | tf_op jit(solution)/shard_map/slice | solution.py:584
  14.3 2.6 %collective-permute-start.2 = (bf16[1,2,256,256]{3,2,1,0:T(8,128)(2,1)S(1)}, bf16[1,2,256,256]{3,2,1,0:T(8,128)(2,1)S(1)}, u32[]{:S(2)}, u32[]{:S(2)}) collective-permute-start(bf16[1,2,256,256]{3,2,1,0:T(8,128)(2,1)S(1)} %collective-permute-done.1.mine_ref), channel_id=1, source_target_pairs={{0,1},{1,0},{2,3},{3,2},{4,5},{5,4},{6,7},{7,6},{8,9},{9,8},{10,11... | collective-permute-start | bytes 786440 | tf_op jit(solution)/shard_map/ppermute | solution.py:578
  20.4 8.1 %collective-permute-start.4 = (f32[2,256,256]{2,1,0:T(8,128)}, f32[2,256,256]{2,1,0:T(8,128)}, u32[]{:S(2)}, u32[]{:S(2)}) collective-permute-start(f32[2,256,256]{2,1,0:T(8,128)} %param.21), channel_id=1, source_target_pairs={{0,1},{1,0},{2,3},{3,2},{4,5},{5,4},{6,7},{7,6},{8,9},{9,8},{10,11... | collective-permute-start | bytes 1572872 | tf_op jit(solution)/shard_map/ppermute | solution.py:636
  20.9 7.6 %collective-permute-start.3 = (bf16[1,2,256,256]{3,2,1,0:T(8,128)(2,1)}, bf16[1,2,256,256]{3,2,1,0:T(8,128)(2,1)}, u32[]{:S(2)}, u32[]{:S(2)}) collective-permute-start(bf16[1,2,256,256]{3,2,1,0:T(8,128)(2,1)} %get-tuple-element.197), channel_id=1, source_target_pairs={{0,2},{1,3},{4,6},{5,7},{8,10},{9,11},{12,14},{13,15},{16,18},{17,... | collective-permute-start | bytes 786440 | tf_op jit(solution)/shard_map/ppermute | solution.py:650
  28.6 14.4 %collective-permute-start.5 = (bf16[1,2,256,256]{3,2,1,0:T(8,128)(2,1)S(1)}, bf16[1,2,256,256]{3,2,1,0:T(8,128)(2,1)S(1)}, u32[]{:S(2)}, u32[]{:S(2)}) collective-permute-start(bf16[1,2,256,256]{3,2,1,0:T(8,128)(2,1)S(1)} %get-tuple-element.171), channel_id=1, source_target_pairs={{2,0},{3,1},{6,4},{7,5},{10,8},{11,9},{14,12},{15,13},{18,16},{19,... | collective-permute-start | bytes 786440 | tf_op jit(solution)/shard_map/ppermute | solution.py:677
  45.8 1.6 %collective-permute-start.7 = (bf16[2,256,256]{2,1,0:T(8,128)(2,1)S(1)}, bf16[2,256,256]{2,1,0:T(8,128)(2,1)S(1)}, u32[]{:S(2)}, u32[]{:S(2)}) collective-permute-start(bf16[2,256,256]{2,1,0:T(8,128)(2,1)S(1)} %constant_dynamic-slice_fusion.1), channel_id=1, source_target_pairs={{0,1},{1,0},{2,3},{3,2},{4,5},{5,4},{6,7},{7,6},{8,9},{9,8},{10,11... | collective-permute-start | bytes 786440 | tf_op jit(solution)/shard_map/ppermute | solution.py:685
  47.5 9.5 %collective-permute-start.8 = (bf16[2,256,256]{2,1,0:T(8,128)(2,1)S(1)}, bf16[2,256,256]{2,1,0:T(8,128)(2,1)S(1)}, u32[]{:S(2)}, u32[]{:S(2)}) collective-permute-start(bf16[2,256,256]{2,1,0:T(8,128)(2,1)S(1)} %add_convert_fusion), channel_id=1, source_target_pairs={{0,4},{4,8},{8,12},{1,5},{5,9},{9,13},{2,6},{6,10},{10,14},{3,7},{... | collective-permute-start | bytes 786440 | tf_op jit(solution)/shard_map/ppermute | solution.py:687
  51.2 5.8 %collective-permute-start.6 = (bf16[2,256,512]{2,1,0:T(8,128)(2,1)S(1)}, bf16[2,256,512]{2,1,0:T(8,128)(2,1)S(1)}, u32[]{:S(2)}, u32[]{:S(2)}) collective-permute-start(bf16[2,256,512]{2,1,0:T(8,128)(2,1)S(1)} %get-tuple-element.184), channel_id=1, source_target_pairs={{0,1},{1,0},{2,3},{3,2},{4,5},{5,4},{6,7},{7,6},{8,9},{9,8},{10,11... | collective-permute-start | bytes 1572872 | tf_op jit(solution)/shard_map/ppermute | solution.py:689
  57.0 1.5 %collective-permute-start.9 = (bf16[2,256,256]{2,1,0:T(8,128)(2,1)S(1)}, bf16[2,256,256]{2,1,0:T(8,128)(2,1)S(1)}, u32[]{:S(2)}, u32[]{:S(2)}) collective-permute-start(bf16[2,256,256]{2,1,0:T(8,128)(2,1)S(1)} %collective-permute-done.8), channel_id=1, source_target_pairs={{0,1},{1,0},{2,3},{3,2},{4,5},{5,4},{6,7},{7,6},{8,9},{9,8},{10,11... | collective-permute-start | bytes 786440 | tf_op jit(solution)/shard_map/ppermute | solution.py:690

commit v25 on v23

--- a/solution.py
+++ b/solution.py
@@ -630,7 +630,6 @@
             inputs = jnp.where(segment == turn, carry, inputs)
         carry = lax.cond(segment == turn, forward_all, silent, carry)
 
-    measured, carry = lax.optimization_barrier((measured, carry))
     both_measured = lax.ppermute(measured, "batch", pairs)
     height = tile_rows + width
     scalars = (local_rows, local_columns, live.astype(jnp.int32), slot, other)

time: 57.7 us -> 57.7 us (level)
  transfers between devices with their start and end apart: 11 -> 11, of which waited for: 7 -> 7; matrix products, arithmetic and copies ran while one was open for 9% -> 9% of each run, Pallas kernels for 3% -> 9%
where the time goes in v25:
time: 57.7 us; the launch traced here: 57.3 us
  waiting for transfers between devices  29.5 us (51%)
  starting transfers between devices  9.4 us (16%)
  Pallas kernels  7.61 us (13%)
  other arithmetic  4.11 us (7%)
  between operations  4.04 us (7%)
  local copies, waits for them, and re-layouts  2.58 us (4%)
    ppermute x1, waiting for transfers between devices, local(): carry = lax.ppermute(carry, 'depth', [(turn + 1, turn)])  13.3 us
    ppermute x1, waiting for transfers between devices, local(): lax.ppermute(spill_sum, 'tile', [(t, t + 1) for t in range(tile_count - 1)])  5.75 us
    ppermute x1, waiting for transfers between devices, from_behind(): return lax.ppermute(block, axis, route)  4.11 us
    ppermute x1, starting transfers between devices, local(): lax.ppermute(spill_sum, 'tile', [(t, t + 1) for t in range(tile_count - 1)])  3.65 us
    pallas_call x1, Pallas kernels, run_first(): pl.pallas_call(first_kernel, grid_spec=grid_spec, out_shape=jax.ShapeDtyp...  3.4 us
    ppermute x1, waiting for transfers between devices, local(): carry = lax.ppermute(carry, 'depth', [(depth_count - 2, depth_count - 1)])  3.06 us
    pallas_call x1, Pallas kernels, run_adjoint(): pl.pallas_call(adjoint_kernel(last, number == 1, opening), grid_spec=grid...  2.62 us
    ppermute x1, starting transfers between devices, local(): carry = lax.ppermute(carry, 'depth', [(depth_count - 2, depth_count - 1)])  1.99 us
  transfers between devices with their start and end apart: 11, of which 7 were waited for; matrix products, arithmetic and copies ran while one was open for 9% of the time, Pallas kernels for 9%

profile of v25, /device:TPU:0, one launch (start us, length us, event | category | flops | bytes accessed | tf_op | source)
XLA Modules:
  0.0 57.3 jit_solution(12336532233951347509)
XLA Ops:
  0.0 0.5 collective-permute-start
  0.5 0.1 collective-permute-start.1
  0.5 1.1 %dynamic-slice_convert_fusion = bf16[1,2,256,256]{3,2,1,0:T(8,128)(2,1)S(1)} fusion(f32[1,2,256,512]{3,2,1,0:T(8,128)} %tile_ref.1, s32[]{:T(128)S(6)} %select_n.84), kind=kLoop, calls=%fused_computation.4 | loop fusion | bytes 524292 | tf_op jit(solution)/shard_map/convert_element_type | solution.py:576
  1.6 1.3 %collective-permute-start.2 = (bf16[1,2,256,256]{3,2,1,0:T(8,128)(2,1)S(1)}, bf16[1,2,256,256]{3,2,1,0:T(8,128)(2,1)S(1)}, u32[]{:S(2)}, u32[]{:S(2)}) collective-permute-start(bf16[1,2,256,256]{3,2,1,0:T(8,128)(2,1)S(1)} %dynamic-slice_convert_fusion), channel_id=1, source_target_pairs={{4,0},{8,4},{12,8},{5,1},{9,5},{13,9},{6,2},{10,6},{14,10},{7,3},{... | collective-permute-start | bytes 786440 | tf_op jit(solution)/shard_map/ppermute | solution.py:18
  2.9 0.5 collective-permute-start.5
  3.4 1.1 %multiply_convert_fusion = (bf16[256,256]{1,0:T(8,128)(2,1)S(1)}, bf16[256,256]{1,0:T(8,128)(2,1)S(1)}) fusion(), kind=kLoop, calls=%fused_computation.13 | loop fusion | flops 1245184 | bytes 262144 | tf_op jit(solution)/shard_map/convert_element_type | solution.py:51
  4.5 1.0 %fusion.6 = (f32[1,256,256]{2,1,0:T(8,128)S(1)}, f32[1,256,256]{2,1,0:T(8,128)S(1)}) fusion(s32[256]{0:T(256)S(1)} %fusion.9, f32[]{:T(128)S(6)} %neg.8), kind=kLoop, calls=%fused_computation.19 | loop fusion | flops 196608 | bytes 525316 | tf_op jit(solution)/shard_map/cos | solution.py:61
  6.4 0.6 %broadcast_select_fusion = s32[2]{0:T(128)S(1)} fusion(pred[]{:T(512)} %eq.24, s32[1]{0:T(128)} %collective-permute-done.1, s32[1]{0:T(128)S(6)} %copy.16), kind=kLoop, calls=%fused_computation.30 | loop fusion | flops 6 | bytes 17 | tf_op jit(solution)/shard_map/jit(_where)/select_n | solution.py:589
  7.0 0.7 %fusion.12 = (s32[1]{0:T(128)}, s32[1]{0:T(128)}) fusion(s32[2]{0:T(128)S(1)} %broadcast_select_fusion), kind=kLoop, calls=%fused_computation.32 | loop fusion | bytes 16 | tf_op jit(solution)/shard_map/slice | solution.py:593
  8.9 4.1 %collective-permute-done.2.mine_ref = bf16[1,2,256,256]{3,2,1,0:T(8,128)(2,1)S(1)} collective-permute-done((bf16[1,2,256,256]{3,2,1,0:T(8,128)(2,1)S(1)}, bf16[1,2,256,256]{3,2,1,0:T(8,128)(2,1)S(1)}, u32[]{:S(2)}, u32[]{:S(2)}) %collective-permute-start.2) | collective-permute-done | bytes 262176 | tf_op jit(solution)/shard_map/ppermute | solution.py:18
  13.0 0.6 %fusion.13 = (s32[1,1]{1,0:T(1,128)}, s32[1,1]{1,0:T(1,128)}) fusion(s32[1,2]{1,0:T(1,128)S(1)} %constant_dynamic-slice_fusion), kind=kLoop, calls=%fused_computation.33 | loop fusion | bytes 16 | tf_op jit(solution)/shard_map/slice | solution.py:600
  14.3 0.2 collective-permute-done.3.partner_ref
  14.5 3.4 %conditional.4 = (bf16[1,2,256,256]{3,2,1,0:T(8,128)(2,1)}) conditional(s32[]{:T(128)} %convert_element_type.72, () %tuple.57, (s32[1]{0:T(128)}, s32[1]{0:T(128)}, s32[1]{0:T(128)}, bf16[1,2,256,256]{3,2,1,0:T(8,128)(2,1)S(1)}, f32[1,2,256,512]{3,2,1,0:T(8,128)S(1)}, /*index=5*/bf16[1,2,256,256]{3,2,1,0:T(8,128)(2,1)S(1)}, ...), branch_computations={%region_0.1_spmd, %region_1.2_spmd} | conditional | bytes 262154 | solution.py:631
  14.5 3.4 %branch_1_fun.6 = bf16[1,2,256,256]{3,2,1,0:T(8,128)(2,1)} custom-call(s32[1]{0:T(128)} %get-tuple-element.127.rows_ref, s32[1]{0:T(128)} %get-tuple-element.128.columns_ref, s32[1]{0:T(128)} %get-tuple-element.129.order_ref, bf16[1,2,256,256]{3,2,1,0:T(8,128)(2,1)S(1)} %get-tuple-element.130.wave_ref, f32[1,2,256,512]{3,2,1,0:T(8,128)S(1)} %get-tuple-element.131.tile_ref, ...), custom_call_target="tpu_custom_call" | custom-call | tf_op jit(solution)/shard_map/cond/branch_1_fun/pallas_call | solution.py:557
  17.9 2.0 %collective-permute-start.4 = (bf16[1,2,256,256]{3,2,1,0:T(8,128)(2,1)}, bf16[1,2,256,256]{3,2,1,0:T(8,128)(2,1)}, u32[]{:S(2)}, u32[]{:S(2)}) collective-permute-start(bf16[1,2,256,256]{3,2,1,0:T(8,128)(2,1)} %get-tuple-element.193), channel_id=1, source_target_pairs={{0,2},{1,3},{4,6},{5,7},{8,10},{9,11},{12,14},{13,15},{16,18},{17,... | collective-permute-start | bytes 786440 | tf_op jit(solution)/shard_map/ppermute | solution.py:647
  21.2 1.6 %shard_map.60 = f32[1,2,256,256]{3,2,1,0:T(8,128)S(1)} custom-call(s32[1]{0:T(128)} %sub.17.rows_ref, s32[1]{0:T(128)} %bitcast.4.columns_ref, s32[1]{0:T(128)} %bitcast.order_ref, f32[1,2,256,512]{3,2,1,0:T(8,128)S(1)} %copy-done, bf16[1,2,256,256]{3,2,1,0:T(8,128)(2,1)S(1)} %collective-permute-done.2.mine_ref, ...), custom_call_target="tpu_custom_call" | custom-call | tf_op jit(solution)/shard_map/pallas_call | solution.py:275
  22.8 3.1 %collective-permute-done.4 = bf16[1,2,256,256]{3,2,1,0:T(8,128)(2,1)} collective-permute-done((bf16[1,2,256,256]{3,2,1,0:T(8,128)(2,1)}, bf16[1,2,256,256]{3,2,1,0:T(8,128)(2,1)}, u32[]{:S(2)}, u32[]{:S(2)}) %collective-permute-start.4) | collective-permute-done | bytes 262176 | tf_op jit(solution)/shard_map/ppermute | solution.py:647
  25.9 1.3 %collective-permute-start.6 = (bf16[1,2,256,256]{3,2,1,0:T(8,128)(2,1)S(1)}, bf16[1,2,256,256]{3,2,1,0:T(8,128)(2,1)S(1)}, u32[]{:S(2)}, u32[]{:S(2)}) collective-permute-start(bf16[1,2,256,256]{3,2,1,0:T(8,128)(2,1)S(1)} %get-tuple-element.167), channel_id=1, source_target_pairs={{2,0},{3,1},{6,4},{7,5},{10,8},{11,9},{14,12},{15,13},{18,16},{19,... | collective-permute-start | bytes 786440 | tf_op jit(solution)/shard_map/ppermute | solution.py:674
  27.2 0.1 conditional.6
  27.2 0.1 broadcast.198
  27.3 13.3 %collective-permute-done.6 = bf16[1,2,256,256]{3,2,1,0:T(8,128)(2,1)S(1)} collective-permute-done((bf16[1,2,256,256]{3,2,1,0:T(8,128)(2,1)S(1)}, bf16[1,2,256,256]{3,2,1,0:T(8,128)(2,1)S(1)}, u32[]{:S(2)}, u32[]{:S(2)}) %collective-permute-start.6) | collective-permute-done | bytes 262176 | tf_op jit(solution)/shard_map/ppermute | solution.py:674
  40.6 2.6 %conditional.7 = (bf16[2,512,512]{2,1,0:T(8,128)(2,1)S(1)}) conditional(s32[]{:T(128)} %convert_element_type.72, bf16[2,512,512]{2,1,0:T(8,128)(2,1)S(1)} %get-tuple-element.195, (s32[1]{0:T(128)}, s32[1]{0:T(128)}, s32[1]{0:T(128)}, s32[1]{0:T(128)}, s32[1]{0:T(128)}, /*index=5*/bf16[1,2,256,256]{3,2,1,0:T(8,128)(2,1)S(1)}, ...), branch_computations={%region_6.7_spmd, %region_7.8_spmd} | conditional | bytes 8 | solution.py:676
  40.6 2.6 %branch_1_fun.9 = bf16[2,512,512]{2,1,0:T(8,128)(2,1)S(1)} custom-call(s32[1]{0:T(128)} %get-tuple-element.154.rows_ref, s32[1]{0:T(128)} %get-tuple-element.155.columns_ref, s32[1]{0:T(128)} %get-tuple-element.156.live_ref, s32[1]{0:T(128)} %get-tuple-element.157.slot_ref, s32[1]{0:T(128)} %get-tuple-element.158.other_ref, ...), custom_call_target="tpu_custom_call" | custom-call | tf_op jit(solution)/shard_map/cond/branch_1_fun/pallas_call | solution.py:452
  43.3 0.1 fusion.11
  43.4 0.1 collective-permute-start.8
  43.5 1.5 %collective-permute-done.8 = bf16[2,256,256]{2,1,0:T(8,128)(2,1)S(1)} collective-permute-done((bf16[2,256,256]{2,1,0:T(8,128)(2,1)S(1)}, bf16[2,256,256]{2,1,0:T(8,128)(2,1)S(1)}, u32[]{:S(2)}, u32[]{:S(2)}) %collective-permute-start.8) | collective-permute-done | bytes 262176 | tf_op jit(solution)/shard_map/ppermute | solution.py:682
  45.0 0.1 add_convert_fusion
  45.1 3.7 %collective-permute-start.9 = (bf16[2,256,256]{2,1,0:T(8,128)(2,1)S(1)}, bf16[2,256,256]{2,1,0:T(8,128)(2,1)S(1)}, u32[]{:S(2)}, u32[]{:S(2)}) collective-permute-start(bf16[2,256,256]{2,1,0:T(8,128)(2,1)S(1)} %add_convert_fusion), channel_id=1, source_target_pairs={{0,4},{4,8},{8,12},{1,5},{5,9},{9,13},{2,6},{6,10},{10,14},{3,7},{... | collective-permute-start | bytes 786440 | tf_op jit(solution)/shard_map/ppermute | solution.py:684
  48.7 0.1 collective-permute-start.7
  48.8 5.8 %collective-permute-done.9 = bf16[2,256,256]{2,1,0:T(8,128)(2,1)S(1)} collective-permute-done((bf16[2,256,256]{2,1,0:T(8,128)(2,1)S(1)}, bf16[2,256,256]{2,1,0:T(8,128)(2,1)S(1)}, u32[]{:S(2)}, u32[]{:S(2)}) %collective-permute-start.9) | collective-permute-done | bytes 262176 | tf_op jit(solution)/shard_map/ppermute | solution.py:684
  54.6 1.5 %collective-permute-done.10 = bf16[2,256,256]{2,1,0:T(8,128)(2,1)S(1)} collective-permute-done((bf16[2,256,256]{2,1,0:T(8,128)(2,1)S(1)}, bf16[2,256,256]{2,1,0:T(8,128)(2,1)S(1)}, u32[]{:S(2)}, u32[]{:S(2)}) %collective-permute-start.10) | collective-permute-done | bytes 262176 | tf_op jit(solution)/shard_map/ppermute | solution.py:687
  56.1 1.2 %add_bitcast_fusion = f32[1,2,256,512]{3,2,1,0:T(8,128)} fusion(bf16[2,256,512]{2,1,0:T(8,128)(2,1)S(1)} %collective-permute-done.7, bf16[2,256,256]{2,1,0:T(8,128)(2,1)S(1)} %collective-permute-done.10, bf16[2,256,256]{2,1,0:T(8,128)(2,1)S(1)} %collective-permute-done.9, pred[]{:T(512)} %eq.24, bf16[2,512,512]{2,1,0:T(8,128)(2,1)S(1)} %get-tuple-element.196), kind=kLoop, calls=%fused_computation | loop fusion | flops 3670016 | bytes 2621441 | tf_op jit(solution)/shard_map/broadcast_in_dim | solution.py:695
  (22 shorter events, 0.3 us)
Async XLA Ops:
  0.0 13.0 %collective-permute-start = (s32[2,2]{1,0:T(2,128)}, s32[2,2]{1,0:T(2,128)S(1)}, u32[]{:S(2)}, u32[]{:S(2)}) collective-permute-start(s32[2,2]{1,0:T(2,128)} %param.19), channel_id=1, source_target_pairs={{0,1},{1,0},{2,3},{3,2},{4,5},{5,4},{6,7},{7,6},{8,9},{9,8},{10,11... | collective-permute-start | bytes 56 | tf_op jit(solution)/shard_map/ppermute | solution.py:582
  0.5 6.0 %collective-permute-start.1 = (s32[1]{0:T(128)}, s32[1]{0:T(128)}, u32[]{:S(2)}, u32[]{:S(2)}) collective-permute-start(s32[1]{0:T(128)} %param.20), channel_id=1, source_target_pairs={{0,1},{1,0},{2,3},{3,2},{4,5},{5,4},{6,7},{7,6},{8,9},{9,8},{10,11... | collective-permute-start | bytes 20 | tf_op jit(solution)/shard_map/ppermute | solution.py:583
  1.6 11.4 %collective-permute-start.2 = (bf16[1,2,256,256]{3,2,1,0:T(8,128)(2,1)S(1)}, bf16[1,2,256,256]{3,2,1,0:T(8,128)(2,1)S(1)}, u32[]{:S(2)}, u32[]{:S(2)}) collective-permute-start(bf16[1,2,256,256]{3,2,1,0:T(8,128)(2,1)S(1)} %dynamic-slice_convert_fusion), channel_id=1, source_target_pairs={{4,0},{8,4},{12,8},{5,1},{9,5},{13,9},{6,2},{10,6},{14,10},{7,3},{... | collective-permute-start | bytes 786440 | tf_op jit(solution)/shard_map/ppermute | solution.py:18
  2.9 19.9 %collective-permute-start.5 = (f32[2,256,256]{2,1,0:T(8,128)}, f32[2,256,256]{2,1,0:T(8,128)}, u32[]{:S(2)}, u32[]{:S(2)}) collective-permute-start(f32[2,256,256]{2,1,0:T(8,128)} %param.21), channel_id=1, source_target_pairs={{0,1},{1,0},{2,3},{3,2},{4,5},{5,4},{6,7},{7,6},{8,9},{9,8},{10,11... | collective-permute-start | bytes 1572872 | tf_op jit(solution)/shard_map/ppermute | solution.py:633
  5.5 9.0 %copy-start = (f32[1,2,256,512]{3,2,1,0:T(8,128)S(1)}, f32[1,2,256,512]{3,2,1,0:T(8,128)}, u32[]{:S(2)}) copy-start(f32[1,2,256,512]{3,2,1,0:T(8,128)} %tile_ref.1) | copy-start | bytes 3145732
  5.6 8.9 %copy-start.1 = (bf16[2,256,256]{2,1,0:T(8,128)(2,1)S(1)}, bf16[2,256,256]{2,1,0:T(8,128)(2,1)}, u32[]{:S(2)}) copy-start(bf16[2,256,256]{2,1,0:T(8,128)(2,1)} %param.18) | copy-start | bytes 786436
  8.9 4.1 %copy-start.2 = (s32[2,2]{1,0:T(2,128)S(1)}, s32[2,2]{1,0:T(2,128)}, u32[]{:S(2)}) copy-start(s32[2,2]{1,0:T(2,128)} %param.19) | copy-start | bytes 52
  13.0 1.5 %collective-permute-start.3 = (bf16[1,2,256,256]{3,2,1,0:T(8,128)(2,1)S(1)}, bf16[1,2,256,256]{3,2,1,0:T(8,128)(2,1)S(1)}, u32[]{:S(2)}, u32[]{:S(2)}) collective-permute-start(bf16[1,2,256,256]{3,2,1,0:T(8,128)(2,1)S(1)} %collective-permute-done.2.mine_ref), channel_id=1, source_target_pairs={{0,1},{1,0},{2,3},{3,2},{4,5},{5,4},{6,7},{7,6},{8,9},{9,8},{10,11... | collective-permute-start | bytes 786440 | tf_op jit(solution)/shard_map/ppermute | solution.py:578
  17.9 7.9 %collective-permute-start.4 = (bf16[1,2,256,256]{3,2,1,0:T(8,128)(2,1)}, bf16[1,2,256,256]{3,2,1,0:T(8,128)(2,1)}, u32[]{:S(2)}, u32[]{:S(2)}) collective-permute-start(bf16[1,2,256,256]{3,2,1,0:T(8,128)(2,1)} %get-tuple-element.193), channel_id=1, source_target_pairs={{0,2},{1,3},{4,6},{5,7},{8,10},{9,11},{12,14},{13,15},{16,18},{17,... | collective-permute-start | bytes 786440 | tf_op jit(solution)/shard_map/ppermute | solution.py:647
  25.9 14.7 %collective-permute-start.6 = (bf16[1,2,256,256]{3,2,1,0:T(8,128)(2,1)S(1)}, bf16[1,2,256,256]{3,2,1,0:T(8,128)(2,1)S(1)}, u32[]{:S(2)}, u32[]{:S(2)}) collective-permute-start(bf16[1,2,256,256]{3,2,1,0:T(8,128)(2,1)S(1)} %get-tuple-element.167), channel_id=1, source_target_pairs={{2,0},{3,1},{6,4},{7,5},{10,8},{11,9},{14,12},{15,13},{18,16},{19,... | collective-permute-start | bytes 786440 | tf_op jit(solution)/shard_map/ppermute | solution.py:674
  43.4 1.6 %collective-permute-start.8 = (bf16[2,256,256]{2,1,0:T(8,128)(2,1)S(1)}, bf16[2,256,256]{2,1,0:T(8,128)(2,1)S(1)}, u32[]{:S(2)}, u32[]{:S(2)}) collective-permute-start(bf16[2,256,256]{2,1,0:T(8,128)(2,1)S(1)} %constant_dynamic-slice_fusion.1), channel_id=1, source_target_pairs={{0,1},{1,0},{2,3},{3,2},{4,5},{5,4},{6,7},{7,6},{8,9},{9,8},{10,11... | collective-permute-start | bytes 786440 | tf_op jit(solution)/shard_map/ppermute | solution.py:682
  45.1 9.5 %collective-permute-start.9 = (bf16[2,256,256]{2,1,0:T(8,128)(2,1)S(1)}, bf16[2,256,256]{2,1,0:T(8,128)(2,1)S(1)}, u32[]{:S(2)}, u32[]{:S(2)}) collective-permute-start(bf16[2,256,256]{2,1,0:T(8,128)(2,1)S(1)} %add_convert_fusion), channel_id=1, source_target_pairs={{0,4},{4,8},{8,12},{1,5},{5,9},{9,13},{2,6},{6,10},{10,14},{3,7},{... | collective-permute-start | bytes 786440 | tf_op jit(solution)/shard_map/ppermute | solution.py:684
  48.7 5.8 %collective-permute-start.7 = (bf16[2,256,512]{2,1,0:T(8,128)(2,1)S(1)}, bf16[2,256,512]{2,1,0:T(8,128)(2,1)S(1)}, u32[]{:S(2)}, u32[]{:S(2)}) collective-permute-start(bf16[2,256,512]{2,1,0:T(8,128)(2,1)S(1)} %get-tuple-element.180), channel_id=1, source_target_pairs={{0,1},{1,0},{2,3},{3,2},{4,5},{5,4},{6,7},{7,6},{8,9},{9,8},{10,11... | collective-permute-start | bytes 1572872 | tf_op jit(solution)/shard_map/ppermute | solution.py:686
  54.6 1.5 %collective-permute-start.10 = (bf16[2,256,256]{2,1,0:T(8,128)(2,1)S(1)}, bf16[2,256,256]{2,1,0:T(8,128)(2,1)S(1)}, u32[]{:S(2)}, u32[]{:S(2)}) collective-permute-start(bf16[2,256,256]{2,1,0:T(8,128)(2,1)S(1)} %collective-permute-done.9), channel_id=1, source_target_pairs={{0,1},{1,0},{2,3},{3,2},{4,5},{5,4},{6,7},{7,6},{8,9},{9,8},{10,11... | collective-permute-start | bytes 786440 | tf_op jit(solution)/shard_map/ppermute | solution.py:687

commit v26 on v25

--- a/solution.py
+++ b/solution.py
@@ -363,7 +363,6 @@
         refs = refs[2:]
         if last:
             own_ref = refs.pop(0)
-            partner_ref = refs.pop(0)
         else:
             source_ref = refs.pop(0)
         if opening:
@@ -390,7 +389,7 @@
             lit_re = patch_re * wave[0] - patch_im * wave[1]
             lit_im = patch_re * wave[1] + patch_im * wave[0]
             out_re, out_im = propagate_block(lit_re, lit_im, blocks, chirp_re, chirp_im)
-            measured = jnp.where(other_ref[index] > 0, partner_ref[0], own_ref[0])
+            measured = own_ref[0]
             weight = RESIDUAL_SCALE * (out_re * out_re + out_im * out_im - measured)
             in_re = (weight * out_re).astype(jnp.bfloat16).astype(jnp.float32)
             in_im = (weight * out_im).astype(jnp.bfloat16).astype(jnp.float32)
@@ -433,8 +432,7 @@
         pl.BlockSpec((width, 2 * width), lambda i, *s: (0, 0)),
     ]
     if last:
-        slot_spec = pl.BlockSpec((1, width, width), lambda i, r, c, a, s, o: (s[i], 0, 0))
-        in_specs += [slot_spec, slot_spec]
+        in_specs += [pl.BlockSpec((1, width, width), lambda i, *s: (i, 0, 0))]
     else:
         in_specs += [wave_spec]
     grid_spec = pltpu.PrefetchScalarGridSpec(
@@ -631,12 +629,15 @@
         carry = lax.cond(segment == turn, forward_all, silent, carry)
 
     both_measured = lax.ppermute(measured, "batch", pairs)
+    chosen_measured = jnp.where(
+        (other > 0)[:, None, None], both_measured[slot], measured[slot]
+    )
     height = tile_rows + width
     scalars = (local_rows, local_columns, live.astype(jnp.int32), slot, other)
 
     def last_pass(incoming):
         return run_adjoint(
-            incoming, patches, chirps, blocks, scalars, (measured, both_measured),
+            incoming, patches, chirps, blocks, scalars, (chosen_measured,),
             height, columns_all, True,
         )
 

time: 57.7 us -> 59.9 us (1.038)
  waiting for transfers between devices: 29.5 us -> 31.7 us
    ppermute x1, waiting for transfers between devices: 13.3 us -> 15 us  [local(): carry = lax.ppermute(carry, 'depth', [(turn + 1, turn)])]
  transfers between devices with their start and end apart: 11 -> 11, of which waited for: 7 -> 7; matrix products, arithmetic and copies ran while one was open for 9% -> 9% of each run, Pallas kernels for 9% -> 8%
where the time goes in v26:
time: 59.9 us; the launch traced here: 59.5 us
  waiting for transfers between devices  31.7 us (53%)
  starting transfers between devices  9.34 us (16%)
  Pallas kernels  7.61 us (13%)
  other arithmetic  4.13 us (7%)
  between operations  4.05 us (7%)
  local copies, waits for them, and re-layouts  2.58 us (4%)
    ppermute x1, waiting for transfers between devices, local(): carry = lax.ppermute(carry, 'depth', [(turn + 1, turn)])  15 us
    ppermute x1, waiting for transfers between devices, local(): lax.ppermute(spill_sum, 'tile', [(t, t + 1) for t in range(tile_count - 1)])  5.75 us
    ppermute x1, waiting for transfers between devices, from_behind(): return lax.ppermute(block, axis, route)  4.67 us
    ppermute x1, starting transfers between devices, local(): lax.ppermute(spill_sum, 'tile', [(t, t + 1) for t in range(tile_count - 1)])  3.65 us
    pallas_call x1, Pallas kernels, run_first(): pl.pallas_call(first_kernel, grid_spec=grid_spec, out_shape=jax.ShapeDtyp...  3.4 us
    ppermute x1, waiting for transfers between devices, local(): carry = lax.ppermute(carry, 'depth', [(depth_count - 2, depth_count - 1)])  3.06 us
    pallas_call x1, Pallas kernels, run_adjoint(): pl.pallas_call(adjoint_kernel(last, number == 1, opening), grid_spec=grid...  2.62 us
    ppermute x1, starting transfers between devices, local(): carry = lax.ppermute(carry, 'depth', [(depth_count - 2, depth_count - 1)])  1.99 us
  transfers between devices with their start and end apart: 11, of which 7 were waited for; matrix products, arithmetic and copies ran while one was open for 9% of the time, Pallas kernels for 8%

profile of v26, /device:TPU:0, one launch (start us, length us, event | category | flops | bytes accessed | tf_op | source)
XLA Modules:
  0.0 59.5 jit_solution(9825290486205451987)
XLA Ops:
  0.0 0.5 collective-permute-start
  0.5 0.1 collective-permute-start.1
  0.5 0.5 collective-permute-start.2
  1.0 1.1 %dynamic-slice_convert_fusion = bf16[1,2,256,256]{3,2,1,0:T(8,128)(2,1)S(1)} fusion(f32[1,2,256,512]{3,2,1,0:T(8,128)} %tile_ref.1, s32[]{:T(128)S(6)} %select_n.100), kind=kLoop, calls=%fused_computation.5 | loop fusion | bytes 524292 | tf_op jit(solution)/shard_map/convert_element_type | solution.py:574
  2.0 1.3 %collective-permute-start.3 = (bf16[1,2,256,256]{3,2,1,0:T(8,128)(2,1)S(1)}, bf16[1,2,256,256]{3,2,1,0:T(8,128)(2,1)S(1)}, u32[]{:S(2)}, u32[]{:S(2)}) collective-permute-start(bf16[1,2,256,256]{3,2,1,0:T(8,128)(2,1)S(1)} %dynamic-slice_convert_fusion), channel_id=1, source_target_pairs={{4,0},{8,4},{12,8},{5,1},{9,5},{13,9},{6,2},{10,6},{14,10},{7,3},{... | collective-permute-start | bytes 786440 | tf_op jit(solution)/shard_map/ppermute | solution.py:18
  3.3 1.1 %multiply_convert_fusion = (bf16[256,256]{1,0:T(8,128)(2,1)S(1)}, bf16[256,256]{1,0:T(8,128)(2,1)S(1)}) fusion(), kind=kLoop, calls=%fused_computation.14 | loop fusion | flops 1245184 | bytes 262144 | tf_op jit(solution)/shard_map/convert_element_type | solution.py:51
  4.5 1.0 %fusion.6 = (f32[1,256,256]{2,1,0:T(8,128)S(1)}, f32[1,256,256]{2,1,0:T(8,128)S(1)}) fusion(s32[256]{0:T(256)S(1)} %fusion.9, f32[]{:T(128)S(6)} %neg.8), kind=kLoop, calls=%fused_computation.20 | loop fusion | flops 196608 | bytes 525316 | tf_op jit(solution)/shard_map/cos | solution.py:61
  6.4 0.6 %broadcast_select_fusion = s32[2]{0:T(128)S(1)} fusion(pred[]{:T(512)} %eq.24, s32[1]{0:T(128)} %collective-permute-done.1, s32[1]{0:T(128)S(6)} %copy.16), kind=kLoop, calls=%fused_computation.31 | loop fusion | flops 6 | bytes 17 | tf_op jit(solution)/shard_map/jit(_where)/select_n | solution.py:587
  7.0 0.7 %fusion.12 = (s32[1]{0:T(128)}, s32[1]{0:T(128)}) fusion(s32[2]{0:T(128)S(1)} %broadcast_select_fusion), kind=kLoop, calls=%fused_computation.33 | loop fusion | bytes 16 | tf_op jit(solution)/shard_map/slice | solution.py:591
  8.8 4.7 %collective-permute-done.3.mine_ref = bf16[1,2,256,256]{3,2,1,0:T(8,128)(2,1)S(1)} collective-permute-done((bf16[1,2,256,256]{3,2,1,0:T(8,128)(2,1)S(1)}, bf16[1,2,256,256]{3,2,1,0:T(8,128)(2,1)S(1)}, u32[]{:S(2)}, u32[]{:S(2)}) %collective-permute-start.3) | collective-permute-done | bytes 262176 | tf_op jit(solution)/shard_map/ppermute | solution.py:18
  13.5 0.6 %fusion.13 = (s32[1,1]{1,0:T(1,128)}, s32[1,1]{1,0:T(1,128)}) fusion(s32[1,2]{1,0:T(1,128)S(1)} %constant_dynamic-slice_fusion), kind=kLoop, calls=%fused_computation.34 | loop fusion | bytes 16 | tf_op jit(solution)/shard_map/slice | solution.py:598
  14.8 0.2 collective-permute-done.4.partner_ref
  15.0 3.4 %conditional.4 = (bf16[1,2,256,256]{3,2,1,0:T(8,128)(2,1)}) conditional(s32[]{:T(128)} %convert_element_type.72, () %tuple.58, (s32[1]{0:T(128)}, s32[1]{0:T(128)}, s32[1]{0:T(128)}, bf16[1,2,256,256]{3,2,1,0:T(8,128)(2,1)S(1)}, f32[1,2,256,512]{3,2,1,0:T(8,128)S(1)}, /*index=5*/bf16[1,2,256,256]{3,2,1,0:T(8,128)(2,1)S(1)}, ...), branch_computations={%region_0.1_spmd, %region_1.2_spmd} | conditional | bytes 262154 | solution.py:629
  15.0 3.4 %branch_1_fun.7 = bf16[1,2,256,256]{3,2,1,0:T(8,128)(2,1)} custom-call(s32[1]{0:T(128)} %get-tuple-element.159.rows_ref, s32[1]{0:T(128)} %get-tuple-element.160.columns_ref, s32[1]{0:T(128)} %get-tuple-element.161.order_ref, bf16[1,2,256,256]{3,2,1,0:T(8,128)(2,1)S(1)} %get-tuple-element.162.wave_ref, f32[1,2,256,512]{3,2,1,0:T(8,128)S(1)} %get-tuple-element.163.tile_ref, ...), custom_call_target="tpu_custom_call" | custom-call | tf_op jit(solution)/shard_map/cond/branch_1_fun/pallas_call | solution.py:555
  18.4 2.0 %collective-permute-start.5 = (bf16[1,2,256,256]{3,2,1,0:T(8,128)(2,1)}, bf16[1,2,256,256]{3,2,1,0:T(8,128)(2,1)}, u32[]{:S(2)}, u32[]{:S(2)}) collective-permute-start(bf16[1,2,256,256]{3,2,1,0:T(8,128)(2,1)} %get-tuple-element.247), channel_id=1, source_target_pairs={{0,2},{1,3},{4,6},{5,7},{8,10},{9,11},{12,14},{13,15},{16,18},{17,... | collective-permute-start | bytes 786440 | tf_op jit(solution)/shard_map/ppermute | solution.py:648
  21.7 1.6 %shard_map.60 = f32[1,2,256,256]{3,2,1,0:T(8,128)S(1)} custom-call(s32[1]{0:T(128)} %sub.17.rows_ref, s32[1]{0:T(128)} %bitcast.6.columns_ref, s32[1]{0:T(128)} %bitcast.2.order_ref, f32[1,2,256,512]{3,2,1,0:T(8,128)S(1)} %copy-done, bf16[1,2,256,256]{3,2,1,0:T(8,128)(2,1)S(1)} %collective-permute-done.3.mine_ref, ...), custom_call_target="tpu_custom_call" | custom-call | tf_op jit(solution)/shard_map/pallas_call | solution.py:275
  23.3 3.1 %collective-permute-done.5 = bf16[1,2,256,256]{3,2,1,0:T(8,128)(2,1)} collective-permute-done((bf16[1,2,256,256]{3,2,1,0:T(8,128)(2,1)}, bf16[1,2,256,256]{3,2,1,0:T(8,128)(2,1)}, u32[]{:S(2)}, u32[]{:S(2)}) %collective-permute-start.5) | collective-permute-done | bytes 262176 | tf_op jit(solution)/shard_map/ppermute | solution.py:648
  26.4 1.3 %collective-permute-start.6 = (bf16[1,2,256,256]{3,2,1,0:T(8,128)(2,1)S(1)}, bf16[1,2,256,256]{3,2,1,0:T(8,128)(2,1)S(1)}, u32[]{:S(2)}, u32[]{:S(2)}) collective-permute-start(bf16[1,2,256,256]{3,2,1,0:T(8,128)(2,1)S(1)} %get-tuple-element.199), channel_id=1, source_target_pairs={{2,0},{3,1},{6,4},{7,5},{10,8},{11,9},{14,12},{15,13},{18,16},{19,... | collective-permute-start | bytes 786440 | tf_op jit(solution)/shard_map/ppermute | solution.py:675
  27.7 0.1 conditional.6
  27.7 0.1 broadcast.210
  27.8 15.0 %collective-permute-done.6 = bf16[1,2,256,256]{3,2,1,0:T(8,128)(2,1)S(1)} collective-permute-done((bf16[1,2,256,256]{3,2,1,0:T(8,128)(2,1)S(1)}, bf16[1,2,256,256]{3,2,1,0:T(8,128)(2,1)S(1)}, u32[]{:S(2)}, u32[]{:S(2)}) %collective-permute-start.6) | collective-permute-done | bytes 262176 | tf_op jit(solution)/shard_map/ppermute | solution.py:675
  42.8 2.6 %conditional.7 = (bf16[2,512,512]{2,1,0:T(8,128)(2,1)S(1)}) conditional(s32[]{:T(128)} %convert_element_type.72, bf16[2,512,512]{2,1,0:T(8,128)(2,1)S(1)} %get-tuple-element.249, (s32[1]{0:T(128)}, s32[1]{0:T(128)}, s32[1]{0:T(128)}, s32[1]{0:T(128)}, s32[1]{0:T(128)}, /*index=5*/bf16[1,2,256,256]{3,2,1,0:T(8,128)(2,1)S(1)}, ...), branch_computations={%region_6.7_spmd, %region_7.8_spmd} | conditional | bytes 8 | solution.py:677
  42.8 2.6 %branch_1_fun.10 = bf16[2,512,512]{2,1,0:T(8,128)(2,1)S(1)} custom-call(s32[1]{0:T(128)} %get-tuple-element.186.rows_ref, s32[1]{0:T(128)} %get-tuple-element.187.columns_ref, s32[1]{0:T(128)} %get-tuple-element.188.live_ref, s32[1]{0:T(128)} %get-tuple-element.189.slot_ref, s32[1]{0:T(128)} %get-tuple-element.190.other_ref, ...), custom_call_target="tpu_custom_call" | custom-call | tf_op jit(solution)/shard_map/cond/branch_1_fun/pallas_call | solution.py:450
  45.4 0.1 fusion.11
  45.5 0.1 collective-permute-start.8
  45.6 1.5 %collective-permute-done.8 = bf16[2,256,256]{2,1,0:T(8,128)(2,1)S(1)} collective-permute-done((bf16[2,256,256]{2,1,0:T(8,128)(2,1)S(1)}, bf16[2,256,256]{2,1,0:T(8,128)(2,1)S(1)}, u32[]{:S(2)}, u32[]{:S(2)}) %collective-permute-start.8) | collective-permute-done | bytes 262176 | tf_op jit(solution)/shard_map/ppermute | solution.py:683
  47.1 0.1 add_convert_fusion
  47.2 3.7 %collective-permute-start.9 = (bf16[2,256,256]{2,1,0:T(8,128)(2,1)S(1)}, bf16[2,256,256]{2,1,0:T(8,128)(2,1)S(1)}, u32[]{:S(2)}, u32[]{:S(2)}) collective-permute-start(bf16[2,256,256]{2,1,0:T(8,128)(2,1)S(1)} %add_convert_fusion), channel_id=1, source_target_pairs={{0,4},{4,8},{8,12},{1,5},{5,9},{9,13},{2,6},{6,10},{10,14},{3,7},{... | collective-permute-start | bytes 786440 | tf_op jit(solution)/shard_map/ppermute | solution.py:685
  50.9 0.1 collective-permute-start.7
  51.0 5.8 %collective-permute-done.9 = bf16[2,256,256]{2,1,0:T(8,128)(2,1)S(1)} collective-permute-done((bf16[2,256,256]{2,1,0:T(8,128)(2,1)S(1)}, bf16[2,256,256]{2,1,0:T(8,128)(2,1)S(1)}, u32[]{:S(2)}, u32[]{:S(2)}) %collective-permute-start.9) | collective-permute-done | bytes 262176 | tf_op jit(solution)/shard_map/ppermute | solution.py:685
  56.7 1.5 %collective-permute-done.10 = bf16[2,256,256]{2,1,0:T(8,128)(2,1)S(1)} collective-permute-done((bf16[2,256,256]{2,1,0:T(8,128)(2,1)S(1)}, bf16[2,256,256]{2,1,0:T(8,128)(2,1)S(1)}, u32[]{:S(2)}, u32[]{:S(2)}) %collective-permute-start.10) | collective-permute-done | bytes 262176 | tf_op jit(solution)/shard_map/ppermute | solution.py:688
  58.3 1.2 %add_bitcast_fusion = f32[1,2,256,512]{3,2,1,0:T(8,128)} fusion(bf16[2,256,512]{2,1,0:T(8,128)(2,1)S(1)} %collective-permute-done.7, bf16[2,256,256]{2,1,0:T(8,128)(2,1)S(1)} %collective-permute-done.10, bf16[2,256,256]{2,1,0:T(8,128)(2,1)S(1)} %collective-permute-done.9, pred[]{:T(512)} %eq.24, bf16[2,512,512]{2,1,0:T(8,128)(2,1)S(1)} %get-tuple-element.250), kind=kLoop, calls=%fused_computation.1 | loop fusion | flops 3670016 | bytes 2621441 | tf_op jit(solution)/shard_map/broadcast_in_dim | solution.py:696
  (22 shorter events, 0.3 us)
Async XLA Ops:
  0.0 13.5 %collective-permute-start = (s32[2,2]{1,0:T(2,128)}, s32[2,2]{1,0:T(2,128)S(1)}, u32[]{:S(2)}, u32[]{:S(2)}) collective-permute-start(s32[2,2]{1,0:T(2,128)} %param.19), channel_id=1, source_target_pairs={{0,1},{1,0},{2,3},{3,2},{4,5},{5,4},{6,7},{7,6},{8,9},{9,8},{10,11... | collective-permute-start | bytes 56 | tf_op jit(solution)/shard_map/ppermute | solution.py:580
  0.5 5.9 %collective-permute-start.1 = (s32[1]{0:T(128)}, s32[1]{0:T(128)}, u32[]{:S(2)}, u32[]{:S(2)}) collective-permute-start(s32[1]{0:T(128)} %param.20), channel_id=1, source_target_pairs={{0,1},{1,0},{2,3},{3,2},{4,5},{5,4},{6,7},{7,6},{8,9},{9,8},{10,11... | collective-permute-start | bytes 20 | tf_op jit(solution)/shard_map/ppermute | solution.py:581
  0.5 22.8 %collective-permute-start.2 = (f32[2,256,256]{2,1,0:T(8,128)}, f32[2,256,256]{2,1,0:T(8,128)}, u32[]{:S(2)}, u32[]{:S(2)}) collective-permute-start(f32[2,256,256]{2,1,0:T(8,128)} %param.21), channel_id=1, source_target_pairs={{0,1},{1,0},{2,3},{3,2},{4,5},{5,4},{6,7},{7,6},{8,9},{9,8},{10,11... | collective-permute-start | bytes 1572872 | tf_op jit(solution)/shard_map/ppermute | solution.py:631
  2.0 11.5 %collective-permute-start.3 = (bf16[1,2,256,256]{3,2,1,0:T(8,128)(2,1)S(1)}, bf16[1,2,256,256]{3,2,1,0:T(8,128)(2,1)S(1)}, u32[]{:S(2)}, u32[]{:S(2)}) collective-permute-start(bf16[1,2,256,256]{3,2,1,0:T(8,128)(2,1)S(1)} %dynamic-slice_convert_fusion), channel_id=1, source_target_pairs={{4,0},{8,4},{12,8},{5,1},{9,5},{13,9},{6,2},{10,6},{14,10},{7,3},{... | collective-permute-start | bytes 786440 | tf_op jit(solution)/shard_map/ppermute | solution.py:18
  5.5 9.5 %copy-start = (f32[1,2,256,512]{3,2,1,0:T(8,128)S(1)}, f32[1,2,256,512]{3,2,1,0:T(8,128)}, u32[]{:S(2)}) copy-start(f32[1,2,256,512]{3,2,1,0:T(8,128)} %tile_ref.1) | copy-start | bytes 3145732
  5.6 9.5 %copy-start.1 = (bf16[2,256,256]{2,1,0:T(8,128)(2,1)S(1)}, bf16[2,256,256]{2,1,0:T(8,128)(2,1)}, u32[]{:S(2)}) copy-start(bf16[2,256,256]{2,1,0:T(8,128)(2,1)} %param.18) | copy-start | bytes 786436
  8.8 4.7 %copy-start.2 = (s32[2,2]{1,0:T(2,128)S(1)}, s32[2,2]{1,0:T(2,128)}, u32[]{:S(2)}) copy-start(s32[2,2]{1,0:T(2,128)} %param.19) | copy-start | bytes 52
  13.5 1.5 %collective-permute-start.4 = (bf16[1,2,256,256]{3,2,1,0:T(8,128)(2,1)S(1)}, bf16[1,2,256,256]{3,2,1,0:T(8,128)(2,1)S(1)}, u32[]{:S(2)}, u32[]{:S(2)}) collective-permute-start(bf16[1,2,256,256]{3,2,1,0:T(8,128)(2,1)S(1)} %collective-permute-done.3.mine_ref), channel_id=1, source_target_pairs={{0,1},{1,0},{2,3},{3,2},{4,5},{5,4},{6,7},{7,6},{8,9},{9,8},{10,11... | collective-permute-start | bytes 786440 | tf_op jit(solution)/shard_map/ppermute | solution.py:576
  18.4 7.9 %collective-permute-start.5 = (bf16[1,2,256,256]{3,2,1,0:T(8,128)(2,1)}, bf16[1,2,256,256]{3,2,1,0:T(8,128)(2,1)}, u32[]{:S(2)}, u32[]{:S(2)}) collective-permute-start(bf16[1,2,256,256]{3,2,1,0:T(8,128)(2,1)} %get-tuple-element.247), channel_id=1, source_target_pairs={{0,2},{1,3},{4,6},{5,7},{8,10},{9,11},{12,14},{13,15},{16,18},{17,... | collective-permute-start | bytes 786440 | tf_op jit(solution)/shard_map/ppermute | solution.py:648
  26.4 16.4 %collective-permute-start.6 = (bf16[1,2,256,256]{3,2,1,0:T(8,128)(2,1)S(1)}, bf16[1,2,256,256]{3,2,1,0:T(8,128)(2,1)S(1)}, u32[]{:S(2)}, u32[]{:S(2)}) collective-permute-start(bf16[1,2,256,256]{3,2,1,0:T(8,128)(2,1)S(1)} %get-tuple-element.199), channel_id=1, source_target_pairs={{2,0},{3,1},{6,4},{7,5},{10,8},{11,9},{14,12},{15,13},{18,16},{19,... | collective-permute-start | bytes 786440 | tf_op jit(solution)/shard_map/ppermute | solution.py:675
  45.5 1.6 %collective-permute-start.8 = (bf16[2,256,256]{2,1,0:T(8,128)(2,1)S(1)}, bf16[2,256,256]{2,1,0:T(8,128)(2,1)S(1)}, u32[]{:S(2)}, u32[]{:S(2)}) collective-permute-start(bf16[2,256,256]{2,1,0:T(8,128)(2,1)S(1)} %constant_dynamic-slice_fusion.1), channel_id=1, source_target_pairs={{0,1},{1,0},{2,3},{3,2},{4,5},{5,4},{6,7},{7,6},{8,9},{9,8},{10,11... | collective-permute-start | bytes 786440 | tf_op jit(solution)/shard_map/ppermute | solution.py:683
  47.2 9.5 %collective-permute-start.9 = (bf16[2,256,256]{2,1,0:T(8,128)(2,1)S(1)}, bf16[2,256,256]{2,1,0:T(8,128)(2,1)S(1)}, u32[]{:S(2)}, u32[]{:S(2)}) collective-permute-start(bf16[2,256,256]{2,1,0:T(8,128)(2,1)S(1)} %add_convert_fusion), channel_id=1, source_target_pairs={{0,4},{4,8},{8,12},{1,5},{5,9},{9,13},{2,6},{6,10},{10,14},{3,7},{... | collective-permute-start | bytes 786440 | tf_op jit(solution)/shard_map/ppermute | solution.py:685
  50.9 5.8 %collective-permute-start.7 = (bf16[2,256,512]{2,1,0:T(8,128)(2,1)S(1)}, bf16[2,256,512]{2,1,0:T(8,128)(2,1)S(1)}, u32[]{:S(2)}, u32[]{:S(2)}) collective-permute-start(bf16[2,256,512]{2,1,0:T(8,128)(2,1)S(1)} %get-tuple-element.234), channel_id=1, source_target_pairs={{0,1},{1,0},{2,3},{3,2},{4,5},{5,4},{6,7},{7,6},{8,9},{9,8},{10,11... | collective-permute-start | bytes 1572872 | tf_op jit(solution)/shard_map/ppermute | solution.py:687
  56.7 1.5 %collective-permute-start.10 = (bf16[2,256,256]{2,1,0:T(8,128)(2,1)S(1)}, bf16[2,256,256]{2,1,0:T(8,128)(2,1)S(1)}, u32[]{:S(2)}, u32[]{:S(2)}) collective-permute-start(bf16[2,256,256]{2,1,0:T(8,128)(2,1)S(1)} %collective-permute-done.9), channel_id=1, source_target_pairs={{0,1},{1,0},{2,3},{3,2},{4,5},{5,4},{6,7},{7,6},{8,9},{9,8},{10,11... | collective-permute-start | bytes 786440 | tf_op jit(solution)/shard_map/ppermute | solution.py:688
